TPU v7x, 32 devices: a whole 2x2x4 slice. The times are simulated.
32 devices in a mesh: ctx: 8 (over z, y), tp: 4 (over x, core).
Axes of the slice: x: 2, y: 2, z: 4, core: 2. Of those that a mesh axis runs over, the one named last changes fastest.
Arguments:
- queries: bfloat16 [2048, 16, 128], P('ctx', 'tp'), may hold values from -12 to 12
- keys: bfloat16 [2048, 8, 128], P('ctx', 'tp'), may hold values from -6 to 6
- values: bfloat16 [2048, 8, 128], P('ctx', 'tp'), may hold values from -6 to 6
- residual: bfloat16 [2048, 3072], P('ctx', 'tp'), may hold values from -6 to 6
- out_weight: bfloat16 [16, 128, 3072], P(None, None, 'tp'), may hold values from -1 to 1
- post_gain: bfloat16 [3072], P('tp'), may hold values from 0.099609375 to 1.8984375
Outputs:
- mixed: bfloat16 [2048, 3072], P('ctx', 'tp')
All inputs are finite; a program needn't handle non-finite values.
Results may differ from a plain program's by a relative error of at most 0.015.
Values may be sent and summed in bfloat16 or wider, within the bound.
No kernel may reach another device: no remote copies, remote signals or barrier semaphores. Data moves between devices by JAX's collectives and lax.ppermute only.
A program may use at most 64 MiB of HBM per device.

v0:
```python
import jax
import jax.numpy as jnp
from jax import lax
from jax.sharding import PartitionSpec as P

WINDOW_TOKENS = 4096
D = 3072


softcap_value = 50.0
query_scale = 1.0 / 12.0
rope_base = 10000.0


def passed_along(value, axis, steps):
    count = lax.axis_size(axis)
    first, last = (max(0, -steps), min(count, count - steps))
    return lax.ppermute(value, axis, [(source, source + steps) for source in range(first, last)])


def rotate(values_in, positions):
    half_width = values_in.shape[-1] // 2
    steps_half = jnp.arange(half_width, dtype=jnp.float32)
    inverse = rope_base ** (-2.0 * steps_half / values_in.shape[-1])
    angles = positions.astype(jnp.float32)[..., None] * inverse
    cosine = jnp.cos(angles)
    sine_part = jnp.sin(angles)
    first_half = values_in[..., :half_width]
    second_half = values_in[..., half_width:]
    return jnp.concatenate(
        [
            first_half * cosine - second_half * sine_part,
            second_half * cosine + first_half * sine_part,
        ],
        axis=-1,
    )


def attend_block(state, key_block, value_block, source, rotary_queries, device_index):
    numerators, denominators = state
    rows = key_block.shape[0]
    scores = (
        jnp.einsum("sgrh,kgh->grsk", rotary_queries, key_block, preferred_element_type=jnp.float32)
        * query_scale
    )
    capped = softcap_value * jnp.tanh(scores / softcap_value)
    offsets = jnp.arange(rows, dtype=jnp.int32)
    query_pos = device_index * rows + offsets
    key_pos = source * rows + offsets
    distance = query_pos[:, None] - key_pos[None, :]
    allowed = (distance >= 0) & (distance < WINDOW_TOKENS) & (key_pos[None, :] >= 0)
    weights = jnp.where(allowed[None, None], jnp.exp(capped), 0.0)
    denominators = denominators + jnp.sum(weights, axis=-1)
    numerators = numerators + jnp.einsum(
        "grsk,kgh->grsh",
        weights.astype(jnp.bfloat16),
        value_block,
        preferred_element_type=jnp.float32,
    )
    return (numerators, denominators)


def local(queries, keys, values, residual, out_weight, post_gain):
    rows = queries.shape[0]
    q_heads = queries.shape[1]
    head_size = queries.shape[2]
    kv_heads = keys.shape[1]
    heads_per_group = q_heads // kv_heads
    cycle_size = lax.axis_size("ctx")
    device_index = lax.axis_index("ctx")
    positions = (device_index * rows + jnp.arange(rows, dtype=jnp.int32))[:, None]
    rotary_queries = rotate(queries.astype(jnp.float32), positions).astype(jnp.bfloat16)
    rotary_queries = rotary_queries.reshape(rows, kv_heads, heads_per_group, head_size)
    rotary_keys = rotate(keys.astype(jnp.float32), positions).astype(jnp.bfloat16)
    reach = min(WINDOW_TOKENS // rows, cycle_size - 1)
    state = (
        jnp.zeros((kv_heads, heads_per_group, rows, head_size), jnp.float32),
        jnp.zeros((kv_heads, heads_per_group, rows), jnp.float32),
    )
    state = attend_block(state, rotary_keys, values, device_index, rotary_queries, device_index)

    def advance(step_index, carried):
        running, key_block, value_block = carried
        key_block, value_block = passed_along((key_block, value_block), "ctx", 1)
        running = attend_block(
            running,
            key_block,
            value_block,
            device_index - step_index - 1,
            rotary_queries,
            device_index,
        )
        return (running, key_block, value_block)

    state, unused_keys, unused_values = lax.fori_loop(
        0, reach, advance, (state, rotary_keys, values)
    )
    numerators, denominators = state
    attended = (numerators / denominators[..., None]).astype(jnp.bfloat16)
    attended = jnp.transpose(attended, (2, 0, 1, 3)).reshape(rows, q_heads, head_size)
    local_cols = out_weight.shape[2]
    piece = lax.all_gather(attended, "tp", axis=1, tiled=True)
    heads_in = piece.shape[1]
    weight_rows = out_weight.reshape(heads_in * head_size, local_cols)
    projected = jnp.dot(
        piece.reshape(rows, heads_in * head_size), weight_rows, preferred_element_type=jnp.float32
    )
    square_sums = lax.psum(jnp.sum(projected * projected, axis=1), "tp")
    normed = projected * lax.rsqrt(square_sums / D + 1e-06)[:, None] * post_gain.astype(jnp.float32)
    mixed = residual.astype(jnp.float32) + normed
    return mixed.astype(jnp.bfloat16)


def solution(mesh):
    in_specs = (
        P("ctx", "tp", None),
        P("ctx", "tp", None),
        P("ctx", "tp", None),
        P("ctx", "tp"),
        P(None, None, "tp"),
        P("tp"),
    )
    out_specs = P("ctx", "tp")
    return jax.shard_map(local, mesh=mesh, in_specs=in_specs, out_specs=out_specs, check_vma=False)
```

profile of v0, /device:TPU:24, one launch (start us, length us, event | category | flops | bytes accessed | tf_op | source)
XLA Modules:
  0.0 135.7 jit_solution(11933492602181658960)
XLA Ops:
  6.6 1.1 copy_convert_fusion
  7.7 1.0 convert_element_type.47
  8.7 0.5 multiply_cosine_fusion
  9.2 0.8 subtract_convert_fusion.1
  10.1 0.5 subtract_convert_fusion
  10.6 0.7 copy.17
  11.4 0.7 copy.20
  12.1 1.1 pad_maximum_fusion.1
  13.1 1.1 pad_maximum_fusion
  14.5 0.5 fusion.24
  15.0 1.2 fusion.15
  16.1 81.8 %while.21 = (s32[]{:T(128)}, f32[2,2,256,128]{3,2,1,0:T(8,128)}, f32[2,2,256]{2,1,0:T(2,128)S(1)}, bf16[256,2,128]{2,0,1:T(8,128)(2,1)}, bf16[256,2,128]{2,0,1:T...) while((s32[]{:T(128)}, f32[2,2,256,128]{3,2,1,0:T(8,128)}, ...), condition=%wide.region_3.4_spmd, body=%wide.region_1.3_spmd.sunk | while | flops 135988224 | bytes 8540965 | solution.py:95
  16.1 3.4 %collective-permute-start = (bf16[256,2,128]{2,0,1:T(8,128)(2,1)}, bf16[256,2,128]{2,0,1:T(8,128)(2,1)S(1)}, u32[]{:S(2)}, u32[]{:S(2)}) collective-permute-start(bf16[256,2,128]{2,0,1:T(8,128)(2,1)} %get-tuple-element.308), channel_id=1, source_target_pairs={{0,4},{4,8},{8,12},{12,16},{16,20},{20,24},{24,28},{1,5},{5,9},{9,... | collective-permute-start | bytes 393224 | tf_op jit(solution)/shard_map/while/body/eval_jaxpr/ppermute | solution.py:18
  19.6 1.9 %collective-permute-start.1 = (bf16[256,2,128]{2,0,1:T(8,128)(2,1)S(1)}, bf16[256,2,128]{2,0,1:T(8,128)(2,1)S(1)}, u32[]{:S(2)}, u32[]{:S(2)}) collective-permute-start(bf16[256,2,128]{2,0,1:T(8,128)(2,1)S(1)} %get-tuple-element.309), channel_id=1, source_target_pairs={{0,4},{4,8},{8,12},{12,16},{16,20},{20,24},{24,28},{1,5},{5,9},{9,... | collective-permute-start | bytes 393224 | tf_op jit(solution)/shard_map/while/body/eval_jaxpr/ppermute | solution.py:18
  21.7 2.7 %collective-permute-done = bf16[256,2,128]{2,0,1:T(8,128)(2,1)S(1)} collective-permute-done((bf16[256,2,128]{2,0,1:T(8,128)(2,1)}, bf16[256,2,128]{2,0,1:T(8,128)(2,1)S(1)}, u32[]{:S(2)}, u32[]{:S(2)}) %collective-permute-start) | collective-permute-done | bytes 131104 | tf_op jit(solution)/shard_map/while/body/eval_jaxpr/ppermute | solution.py:18
  24.4 1.4 %fusion.40 = (f32[2,2,256]{2,1,0:T(2,128)S(1)}, bf16[2,2,256,256]{2,3,1,0:T(8,128)(2,1)S(1)}) fusion(bf16[256,2,2,128]{3,0,2,1:T(8,128)(2,1)} %get-tuple-element.323, bf16[256,2,128]{2,0,1:T(8,128)(2,1)S(1)} %collective-permute-done, pred[256,256]{0,1:T(8,128)(4,1)S(1)} %fusion.39), kind=kOutput, calls=%fused_computation.49.clone.1 | convolution fusion | flops 68418560 | bytes 987136 | tf_op jit(solution)/shard_map/while/body/eval_jaxpr/sgrh,kgh->grsk/dot_general | solution.py:43
  25.8 0.6 copy.45
  26.5 0.9 collective-permute-done.1
  27.3 0.4 convolution_add_fusion.2
  27.8 0.8 copy-done.2
  28.6 2.8 %collective-permute-start = (bf16[256,2,128]{2,0,1:T(8,128)(2,1)}, bf16[256,2,128]{2,0,1:T(8,128)(2,1)S(1)}, u32[]{:S(2)}, u32[]{:S(2)}) collective-permute-start(bf16[256,2,128]{2,0,1:T(8,128)(2,1)} %get-tuple-element.308), channel_id=1, source_target_pairs={{0,4},{4,8},{8,12},{12,16},{16,20},{20,24},{24,28},{1,5},{5,9},{9,... | collective-permute-start | bytes 393224 | tf_op jit(solution)/shard_map/while/body/eval_jaxpr/ppermute | solution.py:18
  31.3 1.9 %collective-permute-start.1 = (bf16[256,2,128]{2,0,1:T(8,128)(2,1)S(1)}, bf16[256,2,128]{2,0,1:T(8,128)(2,1)S(1)}, u32[]{:S(2)}, u32[]{:S(2)}) collective-permute-start(bf16[256,2,128]{2,0,1:T(8,128)(2,1)S(1)} %get-tuple-element.309), channel_id=1, source_target_pairs={{0,4},{4,8},{8,12},{12,16},{16,20},{20,24},{24,28},{1,5},{5,9},{9,... | collective-permute-start | bytes 393224 | tf_op jit(solution)/shard_map/while/body/eval_jaxpr/ppermute | solution.py:18
  33.5 4.4 %collective-permute-done = bf16[256,2,128]{2,0,1:T(8,128)(2,1)S(1)} collective-permute-done((bf16[256,2,128]{2,0,1:T(8,128)(2,1)}, bf16[256,2,128]{2,0,1:T(8,128)(2,1)S(1)}, u32[]{:S(2)}, u32[]{:S(2)}) %collective-permute-start) | collective-permute-done | bytes 131104 | tf_op jit(solution)/shard_map/while/body/eval_jaxpr/ppermute | solution.py:18
  37.9 1.4 %fusion.40 = (f32[2,2,256]{2,1,0:T(2,128)S(1)}, bf16[2,2,256,256]{2,3,1,0:T(8,128)(2,1)S(1)}) fusion(bf16[256,2,2,128]{3,0,2,1:T(8,128)(2,1)} %get-tuple-element.323, bf16[256,2,128]{2,0,1:T(8,128)(2,1)S(1)} %collective-permute-done, pred[256,256]{0,1:T(8,128)(4,1)S(1)} %fusion.39), kind=kOutput, calls=%fused_computation.49.clone.1 | convolution fusion | flops 68418560 | bytes 987136 | tf_op jit(solution)/shard_map/while/body/eval_jaxpr/sgrh,kgh->grsk/dot_general | solution.py:43
  39.3 0.6 copy.45
  40.5 0.8 copy-done.2
  41.2 1.9 %collective-permute-start = (bf16[256,2,128]{2,0,1:T(8,128)(2,1)}, bf16[256,2,128]{2,0,1:T(8,128)(2,1)S(1)}, u32[]{:S(2)}, u32[]{:S(2)}) collective-permute-start(bf16[256,2,128]{2,0,1:T(8,128)(2,1)} %get-tuple-element.308), channel_id=1, source_target_pairs={{0,4},{4,8},{8,12},{12,16},{16,20},{20,24},{24,28},{1,5},{5,9},{9,... | collective-permute-start | bytes 393224 | tf_op jit(solution)/shard_map/while/body/eval_jaxpr/ppermute | solution.py:18
  43.2 1.9 %collective-permute-start.1 = (bf16[256,2,128]{2,0,1:T(8,128)(2,1)S(1)}, bf16[256,2,128]{2,0,1:T(8,128)(2,1)S(1)}, u32[]{:S(2)}, u32[]{:S(2)}) collective-permute-start(bf16[256,2,128]{2,0,1:T(8,128)(2,1)S(1)} %get-tuple-element.309), channel_id=1, source_target_pairs={{0,4},{4,8},{8,12},{12,16},{16,20},{20,24},{24,28},{1,5},{5,9},{9,... | collective-permute-start | bytes 393224 | tf_op jit(solution)/shard_map/while/body/eval_jaxpr/ppermute | solution.py:18
  45.3 4.0 %collective-permute-done = bf16[256,2,128]{2,0,1:T(8,128)(2,1)S(1)} collective-permute-done((bf16[256,2,128]{2,0,1:T(8,128)(2,1)}, bf16[256,2,128]{2,0,1:T(8,128)(2,1)S(1)}, u32[]{:S(2)}, u32[]{:S(2)}) %collective-permute-start) | collective-permute-done | bytes 131104 | tf_op jit(solution)/shard_map/while/body/eval_jaxpr/ppermute | solution.py:18
  49.3 1.4 %fusion.40 = (f32[2,2,256]{2,1,0:T(2,128)S(1)}, bf16[2,2,256,256]{2,3,1,0:T(8,128)(2,1)S(1)}) fusion(bf16[256,2,2,128]{3,0,2,1:T(8,128)(2,1)} %get-tuple-element.323, bf16[256,2,128]{2,0,1:T(8,128)(2,1)S(1)} %collective-permute-done, pred[256,256]{0,1:T(8,128)(4,1)S(1)} %fusion.39), kind=kOutput, calls=%fused_computation.49.clone.1 | convolution fusion | flops 68418560 | bytes 987136 | tf_op jit(solution)/shard_map/while/body/eval_jaxpr/sgrh,kgh->grsk/dot_general | solution.py:43
  50.8 0.6 copy.45
  51.4 0.4 convolution_add_fusion.2
  51.9 0.8 copy-done.2
  52.7 1.9 %collective-permute-start = (bf16[256,2,128]{2,0,1:T(8,128)(2,1)}, bf16[256,2,128]{2,0,1:T(8,128)(2,1)S(1)}, u32[]{:S(2)}, u32[]{:S(2)}) collective-permute-start(bf16[256,2,128]{2,0,1:T(8,128)(2,1)} %get-tuple-element.308), channel_id=1, source_target_pairs={{0,4},{4,8},{8,12},{12,16},{16,20},{20,24},{24,28},{1,5},{5,9},{9,... | collective-permute-start | bytes 393224 | tf_op jit(solution)/shard_map/while/body/eval_jaxpr/ppermute | solution.py:18
  54.6 1.9 %collective-permute-start.1 = (bf16[256,2,128]{2,0,1:T(8,128)(2,1)S(1)}, bf16[256,2,128]{2,0,1:T(8,128)(2,1)S(1)}, u32[]{:S(2)}, u32[]{:S(2)}) collective-permute-start(bf16[256,2,128]{2,0,1:T(8,128)(2,1)S(1)} %get-tuple-element.309), channel_id=1, source_target_pairs={{0,4},{4,8},{8,12},{12,16},{16,20},{20,24},{24,28},{1,5},{5,9},{9,... | collective-permute-start | bytes 393224 | tf_op jit(solution)/shard_map/while/body/eval_jaxpr/ppermute | solution.py:18
  56.7 3.9 %collective-permute-done = bf16[256,2,128]{2,0,1:T(8,128)(2,1)S(1)} collective-permute-done((bf16[256,2,128]{2,0,1:T(8,128)(2,1)}, bf16[256,2,128]{2,0,1:T(8,128)(2,1)S(1)}, u32[]{:S(2)}, u32[]{:S(2)}) %collective-permute-start) | collective-permute-done | bytes 131104 | tf_op jit(solution)/shard_map/while/body/eval_jaxpr/ppermute | solution.py:18
  60.6 1.4 %fusion.40 = (f32[2,2,256]{2,1,0:T(2,128)S(1)}, bf16[2,2,256,256]{2,3,1,0:T(8,128)(2,1)S(1)}) fusion(bf16[256,2,2,128]{3,0,2,1:T(8,128)(2,1)} %get-tuple-element.323, bf16[256,2,128]{2,0,1:T(8,128)(2,1)S(1)} %collective-permute-done, pred[256,256]{0,1:T(8,128)(4,1)S(1)} %fusion.39), kind=kOutput, calls=%fused_computation.49.clone.1 | convolution fusion | flops 68418560 | bytes 987136 | tf_op jit(solution)/shard_map/while/body/eval_jaxpr/sgrh,kgh->grsk/dot_general | solution.py:43
  62.1 0.6 copy.45
  62.8 0.4 convolution_add_fusion.2
  63.2 0.8 copy-done.2
  64.0 1.9 %collective-permute-start = (bf16[256,2,128]{2,0,1:T(8,128)(2,1)}, bf16[256,2,128]{2,0,1:T(8,128)(2,1)S(1)}, u32[]{:S(2)}, u32[]{:S(2)}) collective-permute-start(bf16[256,2,128]{2,0,1:T(8,128)(2,1)} %get-tuple-element.308), channel_id=1, source_target_pairs={{0,4},{4,8},{8,12},{12,16},{16,20},{20,24},{24,28},{1,5},{5,9},{9,... | collective-permute-start | bytes 393224 | tf_op jit(solution)/shard_map/while/body/eval_jaxpr/ppermute | solution.py:18
  65.9 1.9 %collective-permute-start.1 = (bf16[256,2,128]{2,0,1:T(8,128)(2,1)S(1)}, bf16[256,2,128]{2,0,1:T(8,128)(2,1)S(1)}, u32[]{:S(2)}, u32[]{:S(2)}) collective-permute-start(bf16[256,2,128]{2,0,1:T(8,128)(2,1)S(1)} %get-tuple-element.309), channel_id=1, source_target_pairs={{0,4},{4,8},{8,12},{12,16},{16,20},{20,24},{24,28},{1,5},{5,9},{9,... | collective-permute-start | bytes 393224 | tf_op jit(solution)/shard_map/while/body/eval_jaxpr/ppermute | solution.py:18
  68.0 3.9 %collective-permute-done = bf16[256,2,128]{2,0,1:T(8,128)(2,1)S(1)} collective-permute-done((bf16[256,2,128]{2,0,1:T(8,128)(2,1)}, bf16[256,2,128]{2,0,1:T(8,128)(2,1)S(1)}, u32[]{:S(2)}, u32[]{:S(2)}) %collective-permute-start) | collective-permute-done | bytes 131104 | tf_op jit(solution)/shard_map/while/body/eval_jaxpr/ppermute | solution.py:18
  71.9 1.4 %fusion.40 = (f32[2,2,256]{2,1,0:T(2,128)S(1)}, bf16[2,2,256,256]{2,3,1,0:T(8,128)(2,1)S(1)}) fusion(bf16[256,2,2,128]{3,0,2,1:T(8,128)(2,1)} %get-tuple-element.323, bf16[256,2,128]{2,0,1:T(8,128)(2,1)S(1)} %collective-permute-done, pred[256,256]{0,1:T(8,128)(4,1)S(1)} %fusion.39), kind=kOutput, calls=%fused_computation.49.clone.1 | convolution fusion | flops 68418560 | bytes 987136 | tf_op jit(solution)/shard_map/while/body/eval_jaxpr/sgrh,kgh->grsk/dot_general | solution.py:43
  73.4 0.6 copy.45
  74.5 0.8 copy-done.2
  75.3 1.9 %collective-permute-start = (bf16[256,2,128]{2,0,1:T(8,128)(2,1)}, bf16[256,2,128]{2,0,1:T(8,128)(2,1)S(1)}, u32[]{:S(2)}, u32[]{:S(2)}) collective-permute-start(bf16[256,2,128]{2,0,1:T(8,128)(2,1)} %get-tuple-element.308), channel_id=1, source_target_pairs={{0,4},{4,8},{8,12},{12,16},{16,20},{20,24},{24,28},{1,5},{5,9},{9,... | collective-permute-start | bytes 393224 | tf_op jit(solution)/shard_map/while/body/eval_jaxpr/ppermute | solution.py:18
  77.2 1.9 %collective-permute-start.1 = (bf16[256,2,128]{2,0,1:T(8,128)(2,1)S(1)}, bf16[256,2,128]{2,0,1:T(8,128)(2,1)S(1)}, u32[]{:S(2)}, u32[]{:S(2)}) collective-permute-start(bf16[256,2,128]{2,0,1:T(8,128)(2,1)S(1)} %get-tuple-element.309), channel_id=1, source_target_pairs={{0,4},{4,8},{8,12},{12,16},{16,20},{20,24},{24,28},{1,5},{5,9},{9,... | collective-permute-start | bytes 393224 | tf_op jit(solution)/shard_map/while/body/eval_jaxpr/ppermute | solution.py:18
  79.3 3.9 %collective-permute-done = bf16[256,2,128]{2,0,1:T(8,128)(2,1)S(1)} collective-permute-done((bf16[256,2,128]{2,0,1:T(8,128)(2,1)}, bf16[256,2,128]{2,0,1:T(8,128)(2,1)S(1)}, u32[]{:S(2)}, u32[]{:S(2)}) %collective-permute-start) | collective-permute-done | bytes 131104 | tf_op jit(solution)/shard_map/while/body/eval_jaxpr/ppermute | solution.py:18
  83.3 1.4 %fusion.40 = (f32[2,2,256]{2,1,0:T(2,128)S(1)}, bf16[2,2,256,256]{2,3,1,0:T(8,128)(2,1)S(1)}) fusion(bf16[256,2,2,128]{3,0,2,1:T(8,128)(2,1)} %get-tuple-element.323, bf16[256,2,128]{2,0,1:T(8,128)(2,1)S(1)} %collective-permute-done, pred[256,256]{0,1:T(8,128)(4,1)S(1)} %fusion.39), kind=kOutput, calls=%fused_computation.49.clone.1 | convolution fusion | flops 68418560 | bytes 987136 | tf_op jit(solution)/shard_map/while/body/eval_jaxpr/sgrh,kgh->grsk/dot_general | solution.py:43
  84.7 0.6 copy.45
  85.8 0.8 copy-done.2
  86.6 1.9 %collective-permute-start = (bf16[256,2,128]{2,0,1:T(8,128)(2,1)}, bf16[256,2,128]{2,0,1:T(8,128)(2,1)S(1)}, u32[]{:S(2)}, u32[]{:S(2)}) collective-permute-start(bf16[256,2,128]{2,0,1:T(8,128)(2,1)} %get-tuple-element.308), channel_id=1, source_target_pairs={{0,4},{4,8},{8,12},{12,16},{16,20},{20,24},{24,28},{1,5},{5,9},{9,... | collective-permute-start | bytes 393224 | tf_op jit(solution)/shard_map/while/body/eval_jaxpr/ppermute | solution.py:18
  88.5 1.9 %collective-permute-start.1 = (bf16[256,2,128]{2,0,1:T(8,128)(2,1)S(1)}, bf16[256,2,128]{2,0,1:T(8,128)(2,1)S(1)}, u32[]{:S(2)}, u32[]{:S(2)}) collective-permute-start(bf16[256,2,128]{2,0,1:T(8,128)(2,1)S(1)} %get-tuple-element.309), channel_id=1, source_target_pairs={{0,4},{4,8},{8,12},{12,16},{16,20},{20,24},{24,28},{1,5},{5,9},{9,... | collective-permute-start | bytes 393224 | tf_op jit(solution)/shard_map/while/body/eval_jaxpr/ppermute | solution.py:18
  90.7 3.9 %collective-permute-done = bf16[256,2,128]{2,0,1:T(8,128)(2,1)S(1)} collective-permute-done((bf16[256,2,128]{2,0,1:T(8,128)(2,1)}, bf16[256,2,128]{2,0,1:T(8,128)(2,1)S(1)}, u32[]{:S(2)}, u32[]{:S(2)}) %collective-permute-start) | collective-permute-done | bytes 131104 | tf_op jit(solution)/shard_map/while/body/eval_jaxpr/ppermute | solution.py:18
  94.6 1.4 %fusion.40 = (f32[2,2,256]{2,1,0:T(2,128)S(1)}, bf16[2,2,256,256]{2,3,1,0:T(8,128)(2,1)S(1)}) fusion(bf16[256,2,2,128]{3,0,2,1:T(8,128)(2,1)} %get-tuple-element.323, bf16[256,2,128]{2,0,1:T(8,128)(2,1)S(1)} %collective-permute-done, pred[256,256]{0,1:T(8,128)(4,1)S(1)} %fusion.39), kind=kOutput, calls=%fused_computation.49.clone.1 | convolution fusion | flops 68418560 | bytes 987136 | tf_op jit(solution)/shard_map/while/body/eval_jaxpr/sgrh,kgh->grsk/dot_general | solution.py:43
  96.0 0.6 copy.45
  97.1 0.8 copy-done.2
  97.9 2.0 %divide_convert_fusion = bf16[2,2,256,128]{3,2,1,0:T(8,128)(2,1)} fusion(f32[2,2,256,128]{3,2,1,0:T(8,128)} %get-tuple-element.189, f32[2,2,256]{2,1,0:T(2,128)S(1)} %get-tuple-element.190), kind=kLoop, calls=%fused_computation.26 | loop fusion | flops 262144 | bytes 790528 | tf_op jit(solution)/shard_map/convert_element_type | solution.py:99
  100.0 0.7 convert_element_type.50
  100.6 16.9 %all-gather.2.cloned.1.call-done = bf16[256,16,128]{2,0,1:T(8,128)(2,1)} async-done(((bf16[256,4,128]{2,0,1:T(8,128)(2,1)}), bf16[256,16,128]{2,0,1:T(8,128)(2,1)}) %all-gather.2.cloned.1.call-update) | async-done | bytes 1048592 | tf_op jit(solution)/shard_map/all_gather | solution.py:102
  117.6 3.1 %multiply_reduce_fusion = (f32[256]{0:T(256)S(1)}, f32[256,768]{1,0:T(8,128)}) fusion(bf16[256,16,128]{2,0,1:T(8,128)(2,1)} %all-gather.2.cloned.1.call-done, bf16[16,128,768]{2,1,0:T(8,128)(2,1)S(1)} %copy-done), kind=kOutput, calls=%fused_computation.25 | convolution fusion | flops 805699328 | bytes 4981760 | tf_op jit(solution)/shard_map/dot_general | solution.py:105
  120.7 6.0 %psum.7 = f32[256]{0:T(256)S(1)} all-reduce(f32[256]{0:T(256)S(1)} %get-tuple-element.233), channel_id=1, replica_groups=mesh['ctx'=8,'tp'=4] {'tp'}, use_global_device_ids=true, to_apply=%region_5.6 | all-reduce | flops 256 | bytes 2048 | tf_op jit(solution)/shard_map/psum | solution.py:108
  126.7 2.1 %add_convert_fusion = bf16[256,768]{1,0:T(8,128)(2,1)} fusion(f32[256,768]{1,0:T(8,128)} %get-tuple-element.234, bf16[256,768]{1,0:T(8,128)(2,1)S(1)} %copy-done.4, f32[768]{0:T(1024)S(1)} %convert_element_type.50, f32[256]{0:T(256)S(1)} %add_rsqrt_fusion), kind=kLoop, calls=%fused_computation.24 | loop fusion | flops 983040 | bytes 1576960 | tf_op jit(solution)/shard_map/convert_element_type | solution.py:111
  (93 shorter events, 3.2 us)
Async XLA Ops:
  6.5 111.0 %copy-start = (bf16[16,128,768]{2,1,0:T(8,128)(2,1)S(1)}, bf16[16,128,768]{2,1,0:T(8,128)(2,1)}, u32[]{:S(2)}) copy-start(bf16[16,128,768]{2,1,0:T(8,128)(2,1)} %param.12) | copy-start | bytes 9437188
  6.5 4.8 %copy-start.3 = (bf16[256,2,128]{2,1,0:T(2,128)(2,1)S(1)}, bf16[256,2,128]{2,1,0:T(2,128)(2,1)}, u32[]{:S(2)}) copy-start(bf16[256,2,128]{2,1,0:T(2,128)(2,1)} %param.10) | copy-start | bytes 393220
  6.5 111.0 %all-gather.2.cloned.1.call-start = ((), (), s32[]{:S(2)}) async-start(), calls=%async_computation | async-start | bytes 1310720 | tf_op jit(solution)/shard_map/all_gather | solution.py:102
  13.1 3.0 %copy-start.6 = (bf16[256,2,128]{2,0,1:T(8,128)(2,1)}, bf16[256,2,128]{2,0,1:T(8,128)(2,1)S(1)}, u32[]{:S(2)}) copy-start(bf16[256,2,128]{2,0,1:T(8,128)(2,1)S(1)} %pad_maximum_fusion.1) | copy-start | bytes 393220
  14.3 1.8 %copy-start.5 = (bf16[256,2,2,128]{3,0,2,1:T(8,128)(2,1)}, bf16[256,2,2,128]{3,0,2,1:T(8,128)(2,1)S(1)}, u32[]{:S(2)}) copy-start(bf16[256,2,2,128]{3,0,2,1:T(8,128)(2,1)S(1)} %pad_maximum_fusion) | copy-start | bytes 786436
  14.3 1.8 %copy-start.7 = (bf16[256,2,128]{2,0,1:T(8,128)(2,1)S(1)}, bf16[256,2,128]{2,0,1:T(8,128)(2,1)}, u32[]{:S(2)}) copy-start(bf16[256,2,128]{2,0,1:T(8,128)(2,1)} %copy.20) | copy-start | bytes 393220
  16.1 8.2 %collective-permute-start = (bf16[256,2,128]{2,0,1:T(8,128)(2,1)}, bf16[256,2,128]{2,0,1:T(8,128)(2,1)S(1)}, u32[]{:S(2)}, u32[]{:S(2)}) collective-permute-start(bf16[256,2,128]{2,0,1:T(8,128)(2,1)} %get-tuple-element.308), channel_id=1, source_target_pairs={{0,4},{4,8},{8,12},{12,16},{16,20},{20,24},{24,28},{1,5},{5,9},{9,... | collective-permute-start | bytes 393224 | tf_op jit(solution)/shard_map/while/body/eval_jaxpr/ppermute | solution.py:18
  19.6 7.8 %collective-permute-start.1 = (bf16[256,2,128]{2,0,1:T(8,128)(2,1)S(1)}, bf16[256,2,128]{2,0,1:T(8,128)(2,1)S(1)}, u32[]{:S(2)}, u32[]{:S(2)}) collective-permute-start(bf16[256,2,128]{2,0,1:T(8,128)(2,1)S(1)} %get-tuple-element.309), channel_id=1, source_target_pairs={{0,4},{4,8},{8,12},{12,16},{16,20},{20,24},{24,28},{1,5},{5,9},{9,... | collective-permute-start | bytes 393224 | tf_op jit(solution)/shard_map/while/body/eval_jaxpr/ppermute | solution.py:18
  21.5 5.8 %copy-start.1 = (f32[2,2,256,128]{3,2,1,0:T(8,128)S(1)}, f32[2,2,256,128]{3,2,1,0:T(8,128)}, u32[]{:S(2)}) copy-start(f32[2,2,256,128]{3,2,1,0:T(8,128)} %get-tuple-element.306) | copy-start | bytes 1572868 | tf_op jit(solution)/shard_map/while
  27.8 0.8 copy-start.2
  28.6 9.3 %collective-permute-start = (bf16[256,2,128]{2,0,1:T(8,128)(2,1)}, bf16[256,2,128]{2,0,1:T(8,128)(2,1)S(1)}, u32[]{:S(2)}, u32[]{:S(2)}) collective-permute-start(bf16[256,2,128]{2,0,1:T(8,128)(2,1)} %get-tuple-element.308), channel_id=1, source_target_pairs={{0,4},{4,8},{8,12},{12,16},{16,20},{20,24},{24,28},{1,5},{5,9},{9,... | collective-permute-start | bytes 393224 | tf_op jit(solution)/shard_map/while/body/eval_jaxpr/ppermute | solution.py:18
  31.3 8.7 %collective-permute-start.1 = (bf16[256,2,128]{2,0,1:T(8,128)(2,1)S(1)}, bf16[256,2,128]{2,0,1:T(8,128)(2,1)S(1)}, u32[]{:S(2)}, u32[]{:S(2)}) collective-permute-start(bf16[256,2,128]{2,0,1:T(8,128)(2,1)S(1)} %get-tuple-element.309), channel_id=1, source_target_pairs={{0,4},{4,8},{8,12},{12,16},{16,20},{20,24},{24,28},{1,5},{5,9},{9,... | collective-permute-start | bytes 393224 | tf_op jit(solution)/shard_map/while/body/eval_jaxpr/ppermute | solution.py:18
  33.3 6.7 %copy-start.1 = (f32[2,2,256,128]{3,2,1,0:T(8,128)S(1)}, f32[2,2,256,128]{3,2,1,0:T(8,128)}, u32[]{:S(2)}) copy-start(f32[2,2,256,128]{3,2,1,0:T(8,128)} %get-tuple-element.306) | copy-start | bytes 1572868 | tf_op jit(solution)/shard_map/while
  40.4 0.8 copy-start.2
  41.2 8.1 %collective-permute-start = (bf16[256,2,128]{2,0,1:T(8,128)(2,1)}, bf16[256,2,128]{2,0,1:T(8,128)(2,1)S(1)}, u32[]{:S(2)}, u32[]{:S(2)}) collective-permute-start(bf16[256,2,128]{2,0,1:T(8,128)(2,1)} %get-tuple-element.308), channel_id=1, source_target_pairs={{0,4},{4,8},{8,12},{12,16},{16,20},{20,24},{24,28},{1,5},{5,9},{9,... | collective-permute-start | bytes 393224 | tf_op jit(solution)/shard_map/while/body/eval_jaxpr/ppermute | solution.py:18
  43.2 8.3 %collective-permute-start.1 = (bf16[256,2,128]{2,0,1:T(8,128)(2,1)S(1)}, bf16[256,2,128]{2,0,1:T(8,128)(2,1)S(1)}, u32[]{:S(2)}, u32[]{:S(2)}) collective-permute-start(bf16[256,2,128]{2,0,1:T(8,128)(2,1)S(1)} %get-tuple-element.309), channel_id=1, source_target_pairs={{0,4},{4,8},{8,12},{12,16},{16,20},{20,24},{24,28},{1,5},{5,9},{9,... | collective-permute-start | bytes 393224 | tf_op jit(solution)/shard_map/while/body/eval_jaxpr/ppermute | solution.py:18
  45.1 6.3 %copy-start.1 = (f32[2,2,256,128]{3,2,1,0:T(8,128)S(1)}, f32[2,2,256,128]{3,2,1,0:T(8,128)}, u32[]{:S(2)}) copy-start(f32[2,2,256,128]{3,2,1,0:T(8,128)} %get-tuple-element.306) | copy-start | bytes 1572868 | tf_op jit(solution)/shard_map/while
  51.9 0.8 copy-start.2
  52.7 8.0 %collective-permute-start = (bf16[256,2,128]{2,0,1:T(8,128)(2,1)}, bf16[256,2,128]{2,0,1:T(8,128)(2,1)S(1)}, u32[]{:S(2)}, u32[]{:S(2)}) collective-permute-start(bf16[256,2,128]{2,0,1:T(8,128)(2,1)} %get-tuple-element.308), channel_id=1, source_target_pairs={{0,4},{4,8},{8,12},{12,16},{16,20},{20,24},{24,28},{1,5},{5,9},{9,... | collective-permute-start | bytes 393224 | tf_op jit(solution)/shard_map/while/body/eval_jaxpr/ppermute | solution.py:18
  54.6 8.2 %collective-permute-start.1 = (bf16[256,2,128]{2,0,1:T(8,128)(2,1)S(1)}, bf16[256,2,128]{2,0,1:T(8,128)(2,1)S(1)}, u32[]{:S(2)}, u32[]{:S(2)}) collective-permute-start(bf16[256,2,128]{2,0,1:T(8,128)(2,1)S(1)} %get-tuple-element.309), channel_id=1, source_target_pairs={{0,4},{4,8},{8,12},{12,16},{16,20},{20,24},{24,28},{1,5},{5,9},{9,... | collective-permute-start | bytes 393224 | tf_op jit(solution)/shard_map/while/body/eval_jaxpr/ppermute | solution.py:18
  56.5 6.2 %copy-start.1 = (f32[2,2,256,128]{3,2,1,0:T(8,128)S(1)}, f32[2,2,256,128]{3,2,1,0:T(8,128)}, u32[]{:S(2)}) copy-start(f32[2,2,256,128]{3,2,1,0:T(8,128)} %get-tuple-element.306) | copy-start | bytes 1572868 | tf_op jit(solution)/shard_map/while
  63.2 0.8 copy-start.2
  64.0 8.0 %collective-permute-start = (bf16[256,2,128]{2,0,1:T(8,128)(2,1)}, bf16[256,2,128]{2,0,1:T(8,128)(2,1)S(1)}, u32[]{:S(2)}, u32[]{:S(2)}) collective-permute-start(bf16[256,2,128]{2,0,1:T(8,128)(2,1)} %get-tuple-element.308), channel_id=1, source_target_pairs={{0,4},{4,8},{8,12},{12,16},{16,20},{20,24},{24,28},{1,5},{5,9},{9,... | collective-permute-start | bytes 393224 | tf_op jit(solution)/shard_map/while/body/eval_jaxpr/ppermute | solution.py:18
  65.9 8.2 %collective-permute-start.1 = (bf16[256,2,128]{2,0,1:T(8,128)(2,1)S(1)}, bf16[256,2,128]{2,0,1:T(8,128)(2,1)S(1)}, u32[]{:S(2)}, u32[]{:S(2)}) collective-permute-start(bf16[256,2,128]{2,0,1:T(8,128)(2,1)S(1)} %get-tuple-element.309), channel_id=1, source_target_pairs={{0,4},{4,8},{8,12},{12,16},{16,20},{20,24},{24,28},{1,5},{5,9},{9,... | collective-permute-start | bytes 393224 | tf_op jit(solution)/shard_map/while/body/eval_jaxpr/ppermute | solution.py:18
  67.9 6.2 %copy-start.1 = (f32[2,2,256,128]{3,2,1,0:T(8,128)S(1)}, f32[2,2,256,128]{3,2,1,0:T(8,128)}, u32[]{:S(2)}) copy-start(f32[2,2,256,128]{3,2,1,0:T(8,128)} %get-tuple-element.306) | copy-start | bytes 1572868 | tf_op jit(solution)/shard_map/while
  74.5 0.8 copy-start.2
  75.3 8.0 %collective-permute-start = (bf16[256,2,128]{2,0,1:T(8,128)(2,1)}, bf16[256,2,128]{2,0,1:T(8,128)(2,1)S(1)}, u32[]{:S(2)}, u32[]{:S(2)}) collective-permute-start(bf16[256,2,128]{2,0,1:T(8,128)(2,1)} %get-tuple-element.308), channel_id=1, source_target_pairs={{0,4},{4,8},{8,12},{12,16},{16,20},{20,24},{24,28},{1,5},{5,9},{9,... | collective-permute-start | bytes 393224 | tf_op jit(solution)/shard_map/while/body/eval_jaxpr/ppermute | solution.py:18
  77.2 8.2 %collective-permute-start.1 = (bf16[256,2,128]{2,0,1:T(8,128)(2,1)S(1)}, bf16[256,2,128]{2,0,1:T(8,128)(2,1)S(1)}, u32[]{:S(2)}, u32[]{:S(2)}) collective-permute-start(bf16[256,2,128]{2,0,1:T(8,128)(2,1)S(1)} %get-tuple-element.309), channel_id=1, source_target_pairs={{0,4},{4,8},{8,12},{12,16},{16,20},{20,24},{24,28},{1,5},{5,9},{9,... | collective-permute-start | bytes 393224 | tf_op jit(solution)/shard_map/while/body/eval_jaxpr/ppermute | solution.py:18
  79.2 6.2 %copy-start.1 = (f32[2,2,256,128]{3,2,1,0:T(8,128)S(1)}, f32[2,2,256,128]{3,2,1,0:T(8,128)}, u32[]{:S(2)}) copy-start(f32[2,2,256,128]{3,2,1,0:T(8,128)} %get-tuple-element.306) | copy-start | bytes 1572868 | tf_op jit(solution)/shard_map/while
  85.8 0.8 copy-start.2
  86.6 8.0 %collective-permute-start = (bf16[256,2,128]{2,0,1:T(8,128)(2,1)}, bf16[256,2,128]{2,0,1:T(8,128)(2,1)S(1)}, u32[]{:S(2)}, u32[]{:S(2)}) collective-permute-start(bf16[256,2,128]{2,0,1:T(8,128)(2,1)} %get-tuple-element.308), channel_id=1, source_target_pairs={{0,4},{4,8},{8,12},{12,16},{16,20},{20,24},{24,28},{1,5},{5,9},{9,... | collective-permute-start | bytes 393224 | tf_op jit(solution)/shard_map/while/body/eval_jaxpr/ppermute | solution.py:18
  88.5 8.2 %collective-permute-start.1 = (bf16[256,2,128]{2,0,1:T(8,128)(2,1)S(1)}, bf16[256,2,128]{2,0,1:T(8,128)(2,1)S(1)}, u32[]{:S(2)}, u32[]{:S(2)}) collective-permute-start(bf16[256,2,128]{2,0,1:T(8,128)(2,1)S(1)} %get-tuple-element.309), channel_id=1, source_target_pairs={{0,4},{4,8},{8,12},{12,16},{16,20},{20,24},{24,28},{1,5},{5,9},{9,... | collective-permute-start | bytes 393224 | tf_op jit(solution)/shard_map/while/body/eval_jaxpr/ppermute | solution.py:18
  90.5 6.2 %copy-start.1 = (f32[2,2,256,128]{3,2,1,0:T(8,128)S(1)}, f32[2,2,256,128]{3,2,1,0:T(8,128)}, u32[]{:S(2)}) copy-start(f32[2,2,256,128]{3,2,1,0:T(8,128)} %get-tuple-element.306) | copy-start | bytes 1572868 | tf_op jit(solution)/shard_map/while
  97.1 0.8 copy-start.2
  97.9 28.8 %copy-start.4 = (bf16[256,768]{1,0:T(8,128)(2,1)S(1)}, bf16[256,768]{1,0:T(8,128)(2,1)}, u32[]{:S(2)}) copy-start(bf16[256,768]{1,0:T(8,128)(2,1)} %param.11) | copy-start | bytes 1179652
Sparse Core Ops, SparseCore 0:
  100.1 17.4 all-gather.1
where the time goes:
time: 138 us; the launch traced here: 136 us
  waiting for transfers between devices  44.6 us (32%)
  starting transfers between devices  29.2 us (21%)
  matrix products  17.8 us (13%)
  between operations  13.5 us (10%)
  other arithmetic  12.3 us (9%)
  local copies, waits for them, and re-layouts  11.6 us (8%)
  blocking collectives  6.02 us (4%)
    ppermute x14, starting transfers between devices, passed_along(): lax.ppermute(value, axis, [(source, source + steps) for source in range(f...  29.2 us
    ppermute x14, waiting for transfers between devices, passed_along(): lax.ppermute(value, axis, [(source, source + steps) for source in range(f...  27.6 us
    all_gather x1, waiting for transfers between devices, local(): piece = lax.all_gather(attended, 'tp', axis=1, tiled=True)  16.9 us
    dot_general x8, matrix products, attend_block(): jnp.einsum('sgrh,kgh->grsk', rotary_queries, key_block, preferred_element...  10.6 us
    while x42, local copies, waits for them, and re-layouts  10.1 us
    psum x1, blocking collectives, local(): square_sums = lax.psum(jnp.sum(projected * projected, axis=1), 'tp')  6.02 us
    dot_general x8, matrix products, attend_block(): jnp.einsum('grsk,kgh->grsh', weights.astype(jnp.bfloat16), value_block, p...  4.09 us
    dot_general x1, matrix products, local(): jnp.dot(piece.reshape(rows, heads_in * head_size), weight_rows, preferred...  3.14 us
  transfers between devices with their start and end apart: 15, of which 9 were waited for; matrix products, arithmetic and copies ran while one was open for 12% of the time, Pallas kernels for 0%

commit v1 on v0

--- a/solution.py
+++ b/solution.py
@@ -36,19 +36,17 @@
     )
 
 
-def attend_block(state, key_block, value_block, source, rotary_queries, device_index):
+def attend_keys(state, key_block, value_block, query_pos, key_pos, rotary_queries, extra=None):
     numerators, denominators = state
-    rows = key_block.shape[0]
     scores = (
         jnp.einsum("sgrh,kgh->grsk", rotary_queries, key_block, preferred_element_type=jnp.float32)
         * query_scale
     )
     capped = softcap_value * jnp.tanh(scores / softcap_value)
-    offsets = jnp.arange(rows, dtype=jnp.int32)
-    query_pos = device_index * rows + offsets
-    key_pos = source * rows + offsets
     distance = query_pos[:, None] - key_pos[None, :]
     allowed = (distance >= 0) & (distance < WINDOW_TOKENS) & (key_pos[None, :] >= 0)
+    if extra is not None:
+        allowed = allowed & extra
     weights = jnp.where(allowed[None, None], jnp.exp(capped), 0.0)
     denominators = denominators + jnp.sum(weights, axis=-1)
     numerators = numerators + jnp.einsum(
@@ -68,33 +66,41 @@
     heads_per_group = q_heads // kv_heads
     cycle_size = lax.axis_size("ctx")
     device_index = lax.axis_index("ctx")
-    positions = (device_index * rows + jnp.arange(rows, dtype=jnp.int32))[:, None]
+    reach = min((WINDOW_TOKENS + rows - 2) // rows, cycle_size - 1)
+    offsets = jnp.arange(rows, dtype=jnp.int32)
+    query_pos = device_index * rows + offsets
+    gather_all = reach == cycle_size - 1
+    if gather_all and reach > 0:
+        stacked = jnp.concatenate([keys, values], axis=1)
+        gathered = lax.all_gather(stacked, "ctx", axis=0, tiled=True)
+    positions = query_pos[:, None]
     rotary_queries = rotate(queries.astype(jnp.float32), positions).astype(jnp.bfloat16)
     rotary_queries = rotary_queries.reshape(rows, kv_heads, heads_per_group, head_size)
     rotary_keys = rotate(keys.astype(jnp.float32), positions).astype(jnp.bfloat16)
-    reach = min(WINDOW_TOKENS // rows, cycle_size - 1)
     state = (
         jnp.zeros((kv_heads, heads_per_group, rows, head_size), jnp.float32),
         jnp.zeros((kv_heads, heads_per_group, rows), jnp.float32),
     )
-    state = attend_block(state, rotary_keys, values, device_index, rotary_queries, device_index)
+    state = attend_keys(state, rotary_keys, values, query_pos, query_pos, rotary_queries)
+    if gather_all and reach > 0:
+        earlier = reach * rows
+        key_pos = jnp.arange(earlier, dtype=jnp.int32)
+        far_keys = rotate(gathered[:earlier, :kv_heads].astype(jnp.float32), key_pos[:, None]).astype(jnp.bfloat16)
+        far_values = gathered[:earlier, kv_heads:]
+        before = (key_pos < device_index * rows)[None, :]
+        state = attend_keys(state, far_keys, far_values, query_pos, key_pos, rotary_queries, before)
+    elif reach > 0:
 
-    def advance(step_index, carried):
-        running, key_block, value_block = carried
-        key_block, value_block = passed_along((key_block, value_block), "ctx", 1)
-        running = attend_block(
-            running,
-            key_block,
-            value_block,
-            device_index - step_index - 1,
-            rotary_queries,
-            device_index,
+        def advance(step_index, carried):
+            running, key_block, value_block = carried
+            key_block, value_block = passed_along((key_block, value_block), "ctx", 1)
+            key_pos = (device_index - step_index - 1) * rows + offsets
+            running = attend_keys(running, key_block, value_block, query_pos, key_pos, rotary_queries)
+            return (running, key_block, value_block)
+
+        state, unused_keys, unused_values = lax.fori_loop(
+            0, reach, advance, (state, rotary_keys, values)
         )
-        return (running, key_block, value_block)
-
-    state, unused_keys, unused_values = lax.fori_loop(
-        0, reach, advance, (state, rotary_keys, values)
-    )
     numerators, denominators = state
     attended = (numerators / denominators[..., None]).astype(jnp.bfloat16)
     attended = jnp.transpose(attended, (2, 0, 1, 3)).reshape(rows, q_heads, head_size)

time: 138 us -> 106 us (0.77)
  starting transfers between devices: 29.2 us -> 0.04 us
  local copies, waits for them, and re-layouts: 11.6 us -> 1.99 us
  waiting for transfers between devices: 44.6 us -> 53.4 us
  matrix products: 17.8 us -> 12.2 us
  other arithmetic: 12.3 us -> 16.9 us
    all_gather x0 -> x1, waiting for transfers between devices: none -> 36.5 us  [local(): gathered = lax.all_gather(stacked, 'ctx', axis=0, tiled=True)]
    ppermute x14 -> x0, starting transfers between devices: 29.2 us -> none  [passed_along(): lax.ppermute(value, axis, [(source, source + steps) for source in range(f...]
    ppermute x14 -> x0, waiting for transfers between devices: 27.6 us -> none  [passed_along(): lax.ppermute(value, axis, [(source, source + steps) for source in range(f...]
    while x43 -> x0, local copies, waits for them, and re-layouts: 10.8 us -> none
    dot_general x16 -> x4, matrix products: 14.7 us -> 9.1 us  [the longest x2 5.03 us: attend_keys(): jnp.einsum('grsk,kgh->grsh', weights.astype(jnp.bfloat16), value_block, p...]
    cos x1 -> x2, other arithmetic: 0.53 us -> 5.5 us  [rotate(): cosine = jnp.cos(angles)]
    unnamed x12 -> x25, local copies, waits for them, and re-layouts: 0.03 us -> 1.92 us
    concatenate x2 -> x1, other arithmetic: 2.22 us -> 0.73 us  [local(): stacked = jnp.concatenate([keys, values], axis=1)]
  transfers between devices with their start and end apart: 15 -> 2, of which waited for: 9 -> 2; matrix products, arithmetic and copies ran while one was open for 12% -> 12% of each run, Pallas kernels for 0% -> 0%
where the time goes in v1:
time: 106 us; the launch traced here: 104 us
  waiting for transfers between devices  53.4 us (50%)
  other arithmetic  16.9 us (16%)
  between operations  13.6 us (13%)
  matrix products  12.2 us (12%)
  blocking collectives  6.01 us (6%)
  local copies, waits for them, and re-layouts  1.99 us (2%)
    all_gather x1, waiting for transfers between devices, local(): gathered = lax.all_gather(stacked, 'ctx', axis=0, tiled=True)  36.5 us
    all_gather x1, waiting for transfers between devices, local(): piece = lax.all_gather(attended, 'tp', axis=1, tiled=True)  16.8 us
    psum x1, blocking collectives, local(): square_sums = lax.psum(jnp.sum(projected * projected, axis=1), 'tp')  6.01 us
    cos x2, other arithmetic, rotate(): cosine = jnp.cos(angles)  5.5 us
    dot_general x2, matrix products, attend_keys(): jnp.einsum('grsk,kgh->grsh', weights.astype(jnp.bfloat16), value_block, p...  5.03 us
    dot_general x2, matrix products, attend_keys(): jnp.einsum('sgrh,kgh->grsk', rotary_queries, key_block, preferred_element...  4.07 us
    dot_general x1, matrix products, local(): jnp.dot(piece.reshape(rows, heads_in * head_size), weight_rows, preferred...  3.14 us
    another operation x3, other arithmetic  2.52 us
  transfers between devices with their start and end apart: 2, of which 2 were waited for; matrix products, arithmetic and copies ran while one was open for 12% of the time, Pallas kernels for 0%

profile of v1, /device:TPU:24, one launch (start us, length us, event | category | flops | bytes accessed | tf_op | source)
XLA Modules:
  0.0 104.2 jit_solution(11553782713327237204)
XLA Ops:
  6.5 0.0 copy-start
  6.5 0.0 all-gather.3.cloned.1.call-start
  6.5 1.1 %copy.21 = bf16[256,2,128]{2,0,1:T(8,128)(2,1)S(1)} copy(bf16[256,2,128]{2,1,0:T(2,128)(2,1)} %param.8) | data formatting | bytes 262144 | tf_op args[2]
  7.6 0.9 copy_convert_fusion
  8.6 0.7 pad_maximum_fusion.1
  9.3 0.0 all-gather.3.cloned.1.call-update
  9.3 0.0 all-gather.5.cloned.1.call-start
  9.4 1.8 %convert_element_type.60 = f32[256,4,128]{2,1,0:T(4,128)} convert(bf16[256,4,128]{2,1,0:T(4,128)(2,1)} %param.6) | non-fusion elementwise | flops 131072 | bytes 786432 | tf_op jit(solution)/shard_map/convert_element_type | solution.py:77
  11.2 0.5 multiply_cosine_fusion.1
  11.7 1.7 %subtract_convert_fusion.1 = (bf16[256,4,64]{2,1,0:T(4,128)(2,1)S(1)}, bf16[256,4,64]{2,1,0:T(4,128)(2,1)S(1)}) fusion(f32[256,4,128]{2,1,0:T(4,128)} %convert_element_type.60, f32[256,64]{1,0:T(8,128)S(1)} %get-tuple-element.16, f32[256,64]{1,0:T(8,128)S(1)} %get-tuple-element.15), kind=kLoop, calls=%fused_computation.35 | loop fusion | flops 524288 | bytes 917504 | tf_op jit(solution)/shard_map/convert.5
  13.5 0.0 copy-start.5
  13.6 0.0 copy-start.7
  13.6 0.1 fusion.22
  13.8 0.2 subtract_convert_fusion.2
  13.9 1.4 %fusion.33 = (f32[2,2,256]{2,1,0:T(2,128)S(1)}, bf16[2,2,256,256]{2,3,1,0:T(8,128)(2,1)}) fusion(bf16[256,2,2,64]{3,0,2,1:T(8,128)(2,1)S(1)} %bitcast.47, bf16[256,2,2,64]{3,0,2,1:T(8,128)(2,1)S(1)} %bitcast.49, bf16[256,2,64]{2,0,1:T(8,128)(2,1)S(1)} %get-tuple-element.10, bf16[256,2,64]{2,0,1:T(8,128)(2,1)S(1)} %get-tuple-element.9, ...), kind=kOutput, calls=%fused_computation.64 | convolution fusion | flops 69204992 | bytes 987136 | tf_op jit(solution)/shard_map/sgrh,kgh->grsk/dot_general | solution.py:42
  15.3 0.0 copy-done.5
  15.3 1.7 %fusion.8 = pred[256,1792]{0,1:T(8,128)(4,1)} fusion(s32[256]{0:T(256)S(1)} %iota_add_fusion, pred[1792]{0:T(1024)(128)(4,1)S(1)} %iota_compare_fusion), kind=kLoop, calls=%fused_computation.11 | loop fusion | flops 2293760 | bytes 461568 | tf_op jit(solution)/shard_map/and | solution.py:49
  17.0 0.0 copy-done.7
  17.0 5.0 %multiply_cosine_fusion = (f32[1792,64]{1,0:T(8,128)}, f32[1792,64]{1,0:T(8,128)}) fusion(f32[64]{0:T(128)S(1)} %multiply_power_fusion, f32[1792]{0:T(1024)S(1)} %iota_convert_fusion), kind=kLoop, calls=%fused_computation.19 | loop fusion | flops 114688 | bytes 924928 | tf_op jit(solution)/shard_map/cos | solution.py:26
  22.0 36.5 %all-gather.3.cloned.1.call-done = bf16[2048,4,128]{2,0,1:T(8,128)(2,1)} async-done(((bf16[256,4,128]{2,0,1:T(8,128)(2,1)}), bf16[2048,4,128]{2,0,1:T(8,128)(2,1)}) %all-gather.3.cloned.1.call-update) | async-done | bytes 2097168 | tf_op jit(solution)/shard_map/all_gather | solution.py:75
  58.5 0.0 copy-start.1
  58.5 0.0 copy-start.2
  58.5 1.4 %slice_convert_fusion = f32[1792,2,128]{2,0,1:T(8,128)S(1)} fusion(bf16[2048,4,128]{2,0,1:T(8,128)(2,1)} %all-gather.3.cloned.1.call-done), kind=kLoop, calls=%fused_computation.26 | loop fusion | flops 458752 | bytes 2752512 | tf_op jit(solution)/shard_map/convert_element_type | solution.py:88
  59.9 0.0 copy-done.1
  59.9 0.3 copy-done.2
  60.2 0.0 copy-start.3
  60.2 0.0 copy-start.6
  60.2 0.0 copy-start.8
  60.2 0.6 subtract_convert_fusion
  60.9 0.4 copy-done.3
  61.2 0.1 copy-done.6
  61.3 0.1 copy-done.8
  61.4 2.7 %fusion = (f32[2,2,256]{2,1,0:T(2,128)S(1)}, f32[2,1792,256,2]{2,1,3,0:T(8,128)S(1)}) fusion(pred[256,1792]{0,1:T(8,128)(4,1)S(1)} %copy-done.3, bf16[256,2,2,64]{3,0,2,1:T(8,128)(2,1)S(1)} %bitcast.48, bf16[256,2,2,64]{3,0,2,1:T(8,128)(2,1)S(1)} %bitcast.50, bf16[1792,2,64]{2,0,1:T(8,128)(2,1)S(1)} %get-tuple-element.6, ...), kind=kOutput, calls=%fused_computation.1 | convolution fusion | flops 479460352 | bytes 8982528 | tf_op jit(solution)/shard_map/sgrh,kgh->grsk/dot_general | solution.py:42
  64.1 0.0 copy-start.9
  64.1 0.0 copy-start.11
  64.1 3.9 %fusion.2 = f32[2,2,256,128]{3,2,1,0:T(8,128)S(1)} fusion(f32[2,1792,256,2]{2,1,3,0:T(8,128)S(1)} %get-tuple-element.20, pred[256,1792]{0,1:T(8,128)(4,1)S(1)} %copy-done.3, bf16[2048,4,128]{2,0,1:T(8,128)(2,1)} %all-gather.3.cloned.1.call-done), kind=kOutput, calls=%fused_computation.3 | convolution fusion | flops 477102080 | bytes 9240576 | tf_op jit(solution)/shard_map/grsk,kgh->grsh/dot_general | solution.py:52
  68.1 0.0 copy-start.10
  68.1 0.0 copy-done.9
  68.1 0.0 copy-done.11
  68.1 1.1 %fusion.16 = bf16[256,2,2,128]{3,0,2,1:T(8,128)(2,1)} fusion(f32[2,2,256,128]{3,2,1,0:T(8,128)S(1)} %fusion.2, bf16[2,2,256,256]{2,3,1,0:T(8,128)(2,1)S(1)} %copy-done.11, f32[256,2,2]{0,2,1:T(2,128)S(1)} %add_bitcast_fusion, bf16[256,2,128,1]{2,1,0,3:T(2,128)(2,1)S(1)} %bitcast.52), kind=kOutput, calls=%fused_computation.24 | convolution fusion | flops 67502080 | bytes 1445888 | tf_op jit(solution)/shard_map/grsk,kgh->grsh/dot_general | solution.py:52
  69.2 0.0 all-gather.5.cloned.1.call-update
  69.2 0.0 copy-done.10
  69.2 0.0 copy-start.4
  69.2 16.8 %all-gather.5.cloned.1.call-done = bf16[256,16,128]{2,0,1:T(8,128)(2,1)} async-done(((bf16[256,4,128]{2,0,1:T(8,128)(2,1)}), bf16[256,16,128]{2,0,1:T(8,128)(2,1)}) %all-gather.5.cloned.1.call-update) | async-done | bytes 1048592 | tf_op jit(solution)/shard_map/all_gather | solution.py:108
  86.1 0.0 copy-done
  86.1 3.1 %multiply_reduce_fusion = (f32[256]{0:T(256)S(1)}, f32[256,768]{1,0:T(8,128)}) fusion(bf16[256,16,128]{2,0,1:T(8,128)(2,1)} %all-gather.5.cloned.1.call-done, bf16[16,128,768]{2,1,0:T(8,128)(2,1)S(1)} %copy-done), kind=kOutput, calls=%fused_computation.32 | convolution fusion | flops 805699328 | bytes 4981760 | tf_op jit(solution)/shard_map/dot_general | solution.py:111
  89.2 6.0 %psum.7 = f32[256]{0:T(256)S(1)} all-reduce(f32[256]{0:T(256)S(1)} %get-tuple-element.21), channel_id=1, replica_groups=mesh['ctx'=8,'tp'=4] {'tp'}, use_global_device_ids=true, to_apply=%region_3.4 | all-reduce | flops 256 | bytes 2048 | tf_op jit(solution)/shard_map/psum | solution.py:114
  95.3 0.0 copy-done.4
  95.3 2.1 %add_convert_fusion.1 = bf16[256,768]{1,0:T(8,128)(2,1)} fusion(f32[256,768]{1,0:T(8,128)} %get-tuple-element.22, bf16[256,768]{1,0:T(8,128)(2,1)S(1)} %copy-done.4, f32[768]{0:T(1024)S(1)} %convert_element_type.66, f32[256]{0:T(256)S(1)} %add_rsqrt_fusion), kind=kLoop, calls=%fused_computation.31 | loop fusion | flops 983040 | bytes 1576960 | tf_op jit(solution)/shard_map/convert_element_type | solution.py:117
  (11 shorter events, 0.1 us)
Async XLA Ops:
  6.5 79.6 %copy-start = (bf16[16,128,768]{2,1,0:T(8,128)(2,1)S(1)}, bf16[16,128,768]{2,1,0:T(8,128)(2,1)}, u32[]{:S(2)}) copy-start(bf16[16,128,768]{2,1,0:T(8,128)(2,1)} %param.10) | copy-start | bytes 9437188
  6.5 51.9 %all-gather.3.cloned.1.call-start = ((), (), s32[]{:S(2)}) async-start(), calls=%async_computation | async-start | bytes 2359296 | tf_op jit(solution)/shard_map/all_gather | solution.py:75
  9.3 76.8 %all-gather.5.cloned.1.call-start = ((), (), s32[]{:S(2)}) async-start(), calls=%async_computation.1 | async-start | bytes 1310720 | tf_op jit(solution)/shard_map/all_gather | solution.py:108
  13.5 1.8 %copy-start.5 = (bf16[256,4,64]{2,0,1:T(8,128)(2,1)}, bf16[256,4,64]{2,0,1:T(8,128)(2,1)S(1)}, u32[]{:S(2)}) copy-start(bf16[256,4,64]{2,0,1:T(8,128)(2,1)S(1)} %copy.17) | copy-start | bytes 393220
  13.6 3.5 %copy-start.7 = (bf16[256,4,64]{2,0,1:T(8,128)(2,1)}, bf16[256,4,64]{2,0,1:T(8,128)(2,1)S(1)}, u32[]{:S(2)}) copy-start(bf16[256,4,64]{2,0,1:T(8,128)(2,1)S(1)} %copy.16) | copy-start | bytes 393220
  58.5 1.5 %copy-start.1 = (f32[1792,64]{1,0:T(8,128)S(1)}, f32[1792,64]{1,0:T(8,128)}, u32[]{:S(2)}) copy-start(f32[1792,64]{1,0:T(8,128)} %get-tuple-element.13) | copy-start | bytes 1376260
  58.5 1.7 %copy-start.2 = (f32[1792,64]{1,0:T(8,128)S(1)}, f32[1792,64]{1,0:T(8,128)}, u32[]{:S(2)}) copy-start(f32[1792,64]{1,0:T(8,128)} %get-tuple-element.14) | copy-start | bytes 1376260
  60.2 1.0 copy-start.3
  60.2 1.1 %copy-start.6 = (bf16[256,4,64]{2,0,1:T(8,128)(2,1)S(1)}, bf16[256,4,64]{2,0,1:T(8,128)(2,1)}, u32[]{:S(2)}) copy-start(bf16[256,4,64]{2,0,1:T(8,128)(2,1)} %copy-done.5) | copy-start | bytes 393220
  60.2 1.2 %copy-start.8 = (bf16[256,4,64]{2,0,1:T(8,128)(2,1)S(1)}, bf16[256,4,64]{2,0,1:T(8,128)(2,1)}, u32[]{:S(2)}) copy-start(bf16[256,4,64]{2,0,1:T(8,128)(2,1)} %copy-done.7) | copy-start | bytes 393220
  64.1 4.0 %copy-start.9 = (bf16[256,2,128]{2,1,0:T(2,128)(2,1)S(1)}, bf16[256,2,128]{2,1,0:T(2,128)(2,1)}, u32[]{:S(2)}) copy-start(bf16[256,2,128]{2,1,0:T(2,128)(2,1)} %param.8) | copy-start | bytes 393220
  64.1 4.0 %copy-start.11 = (bf16[2,2,256,256]{2,3,1,0:T(8,128)(2,1)S(1)}, bf16[2,2,256,256]{2,3,1,0:T(8,128)(2,1)}, u32[]{:S(2)}) copy-start(bf16[2,2,256,256]{2,3,1,0:T(8,128)(2,1)} %get-tuple-element.18) | copy-start | bytes 1572868
  68.1 1.2 %copy-start.10 = (bf16[768]{0:T(1024)(128)(2,1)S(1)}, bf16[768]{0:T(1024)(128)(2,1)}, u32[]{:S(2)}) copy-start(bf16[768]{0:T(1024)(128)(2,1)} %param.11) | copy-start | bytes 4612
  69.2 26.0 %copy-start.4 = (bf16[256,768]{1,0:T(8,128)(2,1)S(1)}, bf16[256,768]{1,0:T(8,128)(2,1)}, u32[]{:S(2)}) copy-start(bf16[256,768]{1,0:T(8,128)(2,1)} %param.9) | copy-start | bytes 1179652
Sparse Core Ops, SparseCore 0:
  9.5 48.8 all-gather.2
  69.3 16.7 all-gather.4

commit v2 on v0

--- a/solution.py
+++ b/solution.py
@@ -60,6 +60,32 @@
     return (numerators, denominators)
 
 
+def along_lines(state, key_block, value_block, rotary_queries, device_index, cycle_size):
+    kv_heads = key_block.shape[1]
+    outer = cycle_size // 2
+    forward = [(source, source + 2) for source in range(cycle_size - 2)]
+    up = [(source, source + 1) for source in range(0, cycle_size, 2)]
+    down = [(source + 1, source) for source in range(0, cycle_size, 2)]
+    plane = device_index // 2
+    side = device_index % 2
+
+    def attend_stacked(state, stacked, source):
+        return attend_block(
+            state, stacked[:, :kv_heads], stacked[:, kv_heads:], source, rotary_queries, device_index
+        )
+
+    line = jnp.concatenate([key_block, value_block], axis=1)
+    for step in range(1, outer + 1):
+        if step < outer:
+            arrived = lax.ppermute(line, "ctx", forward)
+        crossed = lax.ppermute(line, "ctx", up if step == 1 else up + down)
+        state = attend_stacked(state, crossed, 2 * (plane - step + 1) + 1 - side)
+        if step < outer:
+            state = attend_stacked(state, arrived, device_index - 2 * step)
+            line = arrived
+    return state
+
+
 def local(queries, keys, values, residual, out_weight, post_gain):
     rows = queries.shape[0]
     q_heads = queries.shape[1]
@@ -72,29 +98,32 @@
     rotary_queries = rotate(queries.astype(jnp.float32), positions).astype(jnp.bfloat16)
     rotary_queries = rotary_queries.reshape(rows, kv_heads, heads_per_group, head_size)
     rotary_keys = rotate(keys.astype(jnp.float32), positions).astype(jnp.bfloat16)
-    reach = min(WINDOW_TOKENS // rows, cycle_size - 1)
+    reach = min((WINDOW_TOKENS + rows - 2) // rows, cycle_size - 1)
     state = (
         jnp.zeros((kv_heads, heads_per_group, rows, head_size), jnp.float32),
         jnp.zeros((kv_heads, heads_per_group, rows), jnp.float32),
     )
     state = attend_block(state, rotary_keys, values, device_index, rotary_queries, device_index)
+    if reach == cycle_size - 1 and cycle_size % 2 == 0:
+        state = along_lines(state, rotary_keys, values, rotary_queries, device_index, cycle_size)
+    elif reach > 0:
 
-    def advance(step_index, carried):
-        running, key_block, value_block = carried
-        key_block, value_block = passed_along((key_block, value_block), "ctx", 1)
-        running = attend_block(
-            running,
-            key_block,
-            value_block,
-            device_index - step_index - 1,
-            rotary_queries,
-            device_index,
+        def advance(step_index, carried):
+            running, key_block, value_block = carried
+            key_block, value_block = passed_along((key_block, value_block), "ctx", 1)
+            running = attend_block(
+                running,
+                key_block,
+                value_block,
+                device_index - step_index - 1,
+                rotary_queries,
+                device_index,
+            )
+            return (running, key_block, value_block)
+
+        state, unused_keys, unused_values = lax.fori_loop(
+            0, reach, advance, (state, rotary_keys, values)
         )
-        return (running, key_block, value_block)
-
-    state, unused_keys, unused_values = lax.fori_loop(
-        0, reach, advance, (state, rotary_keys, values)
-    )
     numerators, denominators = state
     attended = (numerators / denominators[..., None]).astype(jnp.bfloat16)
     attended = jnp.transpose(attended, (2, 0, 1, 3)).reshape(rows, q_heads, head_size)
@@ -105,7 +134,8 @@
     projected = jnp.dot(
         piece.reshape(rows, heads_in * head_size), weight_rows, preferred_element_type=jnp.float32
     )
-    square_sums = lax.psum(jnp.sum(projected * projected, axis=1), "tp")
+    partial_sums = jnp.sum(projected * projected, axis=1)
+    square_sums = jnp.sum(lax.all_gather(partial_sums, "tp", axis=0), axis=0)
     normed = projected * lax.rsqrt(square_sums / D + 1e-06)[:, None] * post_gain.astype(jnp.float32)
     mixed = residual.astype(jnp.float32) + normed
     return mixed.astype(jnp.bfloat16)

time: 138 us -> 85.2 us (0.62)
  the two profiles are of different devices: /device:TPU:24 before, /device:TPU:0 now
where the time goes in v2:
time: 85.2 us; the launch traced here: 84.9 us
  waiting for transfers between devices  21.1 us (25%)
  starting transfers between devices  19.9 us (23%)
  matrix products  14.3 us (17%)
  between operations  13.8 us (16%)
  other arithmetic  9.49 us (11%)
  blocking collectives  5.06 us (6%)
  local copies, waits for them, and re-layouts  1.21 us (1%)
    all_gather x1, waiting for transfers between devices, local(): piece = lax.all_gather(attended, 'tp', axis=1, tiled=True)  15.6 us
    ppermute x3, starting transfers between devices, along_lines(): arrived = lax.ppermute(line, 'ctx', forward)  12.6 us
    ppermute x4, starting transfers between devices, along_lines(): crossed = lax.ppermute(line, 'ctx', up if step == 1 else up + down)  7.37 us
    dot_general x8, matrix products, attend_block(): jnp.einsum('sgrh,kgh->grsk', rotary_queries, key_block, preferred_element...  5.82 us
    dot_general x8, matrix products, attend_block(): jnp.einsum('grsk,kgh->grsh', weights.astype(jnp.bfloat16), value_block, p...  5.35 us
    all_gather x1, blocking collectives, local(): square_sums = jnp.sum(lax.all_gather(partial_sums, 'tp', axis=0), axis=0)  5.06 us
    ppermute x4, waiting for transfers between devices, along_lines(): crossed = lax.ppermute(line, 'ctx', up if step == 1 else up + down)  4.56 us
    dot_general x1, matrix products, local(): jnp.dot(piece.reshape(rows, heads_in * head_size), weight_rows, preferred...  3.15 us
  transfers between devices with their start and end apart: 8, of which 4 were waited for; matrix products, arithmetic and copies ran while one was open for 17% of the time, Pallas kernels for 0%

profile of v2, /device:TPU:0, one launch (start us, length us, event | category | flops | bytes accessed | tf_op | source)
XLA Modules:
  0.0 84.9 jit_solution(15954004986510782237)
XLA Ops:
  6.5 0.0 copy-start
  6.5 0.0 all-gather.4.cloned.1.call-start
  6.6 1.1 %copy.25 = bf16[256,2,128]{2,0,1:T(8,128)(2,1)S(1)} copy(bf16[256,2,128]{2,1,0:T(2,128)(2,1)} %param.8) | data formatting | bytes 262144 | tf_op args[2]
  7.6 0.9 %copy_convert_fusion = f32[256,2,128]{2,0,1:T(8,128)S(1)} fusion(bf16[256,2,128]{2,1,0:T(2,128)(2,1)} %param.7), kind=kLoop, calls=%fused_computation.130 | loop fusion | flops 65536 | bytes 393216 | tf_op jit(solution)/shard_map/convert_element_type | solution.py:100
  8.6 0.5 multiply_cosine_fusion
  9.1 0.2 subtract_convert_fusion.1
  9.3 0.0 copy-start.2
  9.3 0.8 pad_maximum_fusion.1
  10.1 0.0 copy-done.2
  10.1 5.6 %collective-permute-start.1 = (bf16[256,4,128]{2,0,1:T(8,128)(2,1)}, bf16[256,4,128]{2,0,1:T(8,128)(2,1)}, u32[]{:S(2)}, u32[]{:S(2)}) collective-permute-start(bf16[256,4,128]{2,0,1:T(8,128)(2,1)} %pad_maximum_fusion.1), channel_id=1, source_target_pairs={{0,8},{4,12},{8,16},{12,20},{16,24},{20,28},{1,9},{5,13},{9,17},{1... | collective-permute-start | bytes 786440 | tf_op jit(solution)/shard_map/ppermute | solution.py:80
  15.7 4.1 %collective-permute-start = (bf16[256,4,128]{2,0,1:T(8,128)(2,1)}, bf16[256,4,128]{2,0,1:T(8,128)(2,1)}, u32[]{:S(2)}, u32[]{:S(2)}) collective-permute-start(bf16[256,4,128]{2,0,1:T(8,128)(2,1)} %pad_maximum_fusion.1), channel_id=1, source_target_pairs={{0,4},{8,12},{16,20},{24,28},{1,5},{9,13},{17,21},{25,29},{2,6},{1... | collective-permute-start | bytes 786440 | tf_op jit(solution)/shard_map/ppermute | solution.py:81
  19.9 0.6 fusion.76
  20.4 0.6 broadcast_compare_fusion.1
  21.0 0.6 iota_add_fusion.2
  21.6 0.6 broadcast_compare_fusion.3
  22.2 0.0 copy-start.10
  22.2 0.0 copy-start.11
  22.2 0.0 copy-start.12
  22.2 0.0 copy-start.3
  22.3 1.0 %convert_element_type.59 = f32[256,4,128]{2,1,0:T(4,128)S(1)} convert(bf16[256,4,128]{2,1,0:T(4,128)(2,1)} %param.6) | non-fusion elementwise | flops 131072 | bytes 786432 | tf_op jit(solution)/shard_map/convert_element_type | solution.py:98
  23.3 0.0 copy-start.1
  23.3 0.5 subtract_convert_fusion
  24.0 0.1 pad_maximum_fusion
  24.1 0.0 copy-done.5
  24.1 0.0 copy-done.7
  24.1 0.0 copy-done.8
  24.2 0.0 copy-done.9
  24.2 0.9 %fusion.71 = (pred[256,256]{0,1:T(8,128)(4,1)S(1)}, pred[256,256]{0,1:T(8,128)(4,1)S(1)}, pred[256,256]{0,1:T(8,128)(4,1)S(1)}, pred[256,256]{0,1:T(8,128)(4,1)S...) fusion(s32[256]{0:T(256)S(1)} %get-tuple-element.39, ...), kind=kLoop, calls=%fused_computation.109 | loop fusion | flops 2621440 | bytes 534528 | tf_op jit(solution)/shard_map/and | solution.py:51
  25.1 0.5 fusion.84
  25.6 0.0 copy-done.1
  25.6 0.4 fusion.54
  26.0 0.0 collective-permute-done.1
  26.0 2.8 %collective-permute-start.3 = (bf16[256,4,128]{2,0,1:T(8,128)(2,1)}, bf16[256,4,128]{2,0,1:T(8,128)(2,1)S(1)}, u32[]{:S(2)}, u32[]{:S(2)}) collective-permute-start(bf16[256,4,128]{2,0,1:T(8,128)(2,1)} %collective-permute-done.1), channel_id=1, source_target_pairs={{0,8},{4,12},{8,16},{12,20},{16,24},{20,28},{1,9},{5,13},{9,17},{1... | collective-permute-start | bytes 786440 | tf_op jit(solution)/shard_map/ppermute | solution.py:80
  28.8 0.1 collective-permute-start.2
  28.9 1.4 %fusion.83 = (f32[2,2,256]{2,1,0:T(2,128)S(1)}, bf16[2,2,256,256]{2,3,1,0:T(8,128)(2,1)S(1)}) fusion(bf16[256,2,2,128]{3,0,2,1:T(8,128)(2,1)S(1)} %pad_maximum_fusion, bf16[256,4,128]{2,0,1:T(8,128)(2,1)} %collective-permute-done.1, pred[256,256]{0,1:T(8,128)(4,1)S(1)} %get-tuple-element.15), kind=kOutput, calls=%fused_computation.157 | convolution fusion | flops 68418560 | bytes 987136 | tf_op jit(solution)/shard_map/sgrh,kgh->grsk/dot_general | solution.py:43
  30.3 0.0 collective-permute-done
  30.3 1.4 %fusion.85 = (f32[2,2,256]{2,1,0:T(2,128)S(1)}, bf16[2,2,256,256]{2,3,1,0:T(8,128)(2,1)S(1)}) fusion(bf16[256,2,2,128]{3,0,2,1:T(8,128)(2,1)S(1)} %pad_maximum_fusion, bf16[256,4,128]{2,0,1:T(8,128)(2,1)} %collective-permute-done, pred[256,256]{0,1:T(8,128)(4,1)S(1)} %get-tuple-element.18), kind=kOutput, calls=%fused_computation.159 | convolution fusion | flops 68418560 | bytes 987136 | tf_op jit(solution)/shard_map/sgrh,kgh->grsk/dot_general | solution.py:43
  31.7 1.3 %convolution_add_fusion.4 = f32[2,2,256,128]{3,2,1,0:T(8,128)S(1)} fusion(f32[2,2,256,128]{3,2,1,0:T(8,128)S(1)} %fusion.54, bf16[2,2,256,256]{2,3,1,0:T(8,128)(2,1)S(1)} %get-tuple-element.34, bf16[256,4,128]{2,0,1:T(8,128)(2,1)} %collective-permute-done), kind=kOutput, calls=%fused_computation.57 | convolution fusion | flops 67239936 | bytes 1703936 | tf_op jit(solution)/shard_map/grsk,kgh->grsh/dot_general | solution.py:54
  33.0 1.3 %convolution_add_fusion.3 = f32[2,2,256,128]{3,2,1,0:T(8,128)S(1)} fusion(f32[2,2,256,128]{3,2,1,0:T(8,128)S(1)} %convolution_add_fusion.4, bf16[2,2,256,256]{2,3,1,0:T(8,128)(2,1)S(1)} %get-tuple-element.30, bf16[256,4,128]{2,0,1:T(8,128)(2,1)} %collective-permute-done.1), kind=kOutput, calls=%fused_computation.56 | convolution fusion | flops 67239936 | bytes 1703936 | tf_op jit(solution)/shard_map/grsk,kgh->grsh/dot_general | solution.py:54
  34.2 0.0 collective-permute-done.3
  34.3 4.1 %collective-permute-start.5 = (bf16[256,4,128]{2,0,1:T(8,128)(2,1)S(1)}, bf16[256,4,128]{2,0,1:T(8,128)(2,1)S(1)}, u32[]{:S(2)}, u32[]{:S(2)}) collective-permute-start(bf16[256,4,128]{2,0,1:T(8,128)(2,1)S(1)} %collective-permute-done.3), channel_id=1, source_target_pairs={{0,8},{4,12},{8,16},{12,20},{16,24},{20,28},{1,9},{5,13},{9,17},{1... | collective-permute-start | bytes 786440 | tf_op jit(solution)/shard_map/ppermute | solution.py:80
  38.4 1.4 %collective-permute-start.4 = (bf16[256,4,128]{2,0,1:T(8,128)(2,1)S(1)}, bf16[256,4,128]{2,0,1:T(8,128)(2,1)S(1)}, u32[]{:S(2)}, u32[]{:S(2)}) collective-permute-start(bf16[256,4,128]{2,0,1:T(8,128)(2,1)S(1)} %collective-permute-done.3), channel_id=1, source_target_pairs={{0,4},{8,12},{16,20},{24,28},{4,0},{12,8},{20,16},{28,24},{1,5},{9... | collective-permute-start | bytes 786440 | tf_op jit(solution)/shard_map/ppermute | solution.py:81
  39.8 0.5 fusion.81
  40.3 0.3 fusion.49
  40.7 0.0 collective-permute-done.2
  40.7 0.5 fusion.82
  41.2 0.3 fusion.43
  41.6 0.9 %collective-permute-done.5 = bf16[256,4,128]{2,0,1:T(8,128)(2,1)S(1)} collective-permute-done((bf16[256,4,128]{2,0,1:T(8,128)(2,1)S(1)}, bf16[256,4,128]{2,0,1:T(8,128)(2,1)S(1)}, u32[]{:S(2)}, u32[]{:S(2)}) %collective-permute-start.5) | collective-permute-done | bytes 262176 | tf_op jit(solution)/shard_map/ppermute | solution.py:80
  42.5 1.7 %collective-permute-start.6 = (bf16[256,4,128]{2,0,1:T(8,128)(2,1)S(1)}, bf16[256,4,128]{2,0,1:T(8,128)(2,1)S(1)}, u32[]{:S(2)}, u32[]{:S(2)}) collective-permute-start(bf16[256,4,128]{2,0,1:T(8,128)(2,1)S(1)} %collective-permute-done.5), channel_id=1, source_target_pairs={{0,4},{8,12},{16,20},{24,28},{4,0},{12,8},{20,16},{28,24},{1,5},{9... | collective-permute-start | bytes 786440 | tf_op jit(solution)/shard_map/ppermute | solution.py:81
  44.2 0.5 fusion.79
  44.7 0.3 fusion.46
  45.0 1.9 %collective-permute-done.4 = bf16[256,4,128]{2,0,1:T(8,128)(2,1)S(1)} collective-permute-done((bf16[256,4,128]{2,0,1:T(8,128)(2,1)S(1)}, bf16[256,4,128]{2,0,1:T(8,128)(2,1)S(1)}, u32[]{:S(2)}, u32[]{:S(2)}) %collective-permute-start.4) | collective-permute-done | bytes 262176 | tf_op jit(solution)/shard_map/ppermute | solution.py:81
  46.9 0.5 fusion.80
  47.4 0.4 fusion.42
  47.7 0.0 copy-start.6
  47.8 2.7 %collective-permute-done.6 = bf16[256,4,128]{2,0,1:T(8,128)(2,1)S(1)} collective-permute-done((bf16[256,4,128]{2,0,1:T(8,128)(2,1)S(1)}, bf16[256,4,128]{2,0,1:T(8,128)(2,1)S(1)}, u32[]{:S(2)}, u32[]{:S(2)}) %collective-permute-start.6) | collective-permute-done | bytes 262176 | tf_op jit(solution)/shard_map/ppermute | solution.py:81
  50.5 0.5 fusion.78
  51.0 1.1 %fusion.44 = bf16[256,2,2,128]{3,0,2,1:T(8,128)(2,1)} fusion(f32[2,2,256,128]{3,2,1,0:T(8,128)S(1)} %fusion.42, bf16[2,2,256,256]{2,3,1,0:T(8,128)(2,1)S(1)} %get-tuple-element.20, f32[256,2,2]{0,2,1:T(2,128)S(1)} %add_bitcast_fusion, bf16[256,4,128]{2,0,1:T(8,128)(2,1)S(1)} %collective-permute-done.6), kind=kOutput, calls=%fused_computation.58 | convolution fusion | flops 67502080 | bytes 1445888 | tf_op jit(solution)/shard_map/grsk,kgh->grsh/dot_general | solution.py:54
  52.1 0.0 all-gather.4.cloned.1.call-update
  52.1 15.6 %all-gather.4.cloned.1.call-done = bf16[256,16,128]{2,0,1:T(8,128)(2,1)} async-done(((bf16[256,4,128]{2,0,1:T(8,128)(2,1)}), bf16[256,16,128]{2,0,1:T(8,128)(2,1)}) %all-gather.4.cloned.1.call-update) | async-done | bytes 1048592 | tf_op jit(solution)/shard_map/all_gather | solution.py:131
  67.7 3.1 %multiply_reduce_fusion = (f32[256]{0:T(256)S(1)}, f32[256,768]{1,0:T(8,128)}) fusion(bf16[256,16,128]{2,0,1:T(8,128)(2,1)} %all-gather.4.cloned.1.call-done, bf16[16,128,768]{2,1,0:T(8,128)(2,1)S(1)} %copy-done), kind=kOutput, calls=%fused_computation.60 | convolution fusion | flops 805699328 | bytes 4981760 | tf_op jit(solution)/shard_map/dot_general | solution.py:134
  70.8 5.1 %all-gather.1 = f32[4,1,256]{2,1,0:T(1,128)S(1)} all-gather(f32[1,1,256]{2,1,0:T(1,128)S(1)} %bitcast.160), channel_id=2, replica_groups=mesh['ctx'=8,'tp'=4] {'tp'}, dimensions={0}, use_global_device_ids=true | all-gather | bytes 5120 | tf_op jit(solution)/shard_map/all_gather | solution.py:138
  75.9 0.0 copy-done.4
  75.9 2.1 %add_convert_fusion = bf16[256,768]{1,0:T(8,128)(2,1)} fusion(f32[256,768]{1,0:T(8,128)} %get-tuple-element.36, bf16[256,768]{1,0:T(8,128)(2,1)S(1)} %copy-done.4, f32[768]{0:T(1024)S(1)} %convert_element_type.69, f32[256]{0:T(256)S(1)} %add_rsqrt_fusion), kind=kLoop, calls=%fused_computation.59 | loop fusion | flops 983040 | bytes 1576960 | tf_op jit(solution)/shard_map/convert_element_type | solution.py:141
  (23 shorter events, 0.2 us)
Async XLA Ops:
  6.5 61.2 %copy-start = (bf16[16,128,768]{2,1,0:T(8,128)(2,1)S(1)}, bf16[16,128,768]{2,1,0:T(8,128)(2,1)}, u32[]{:S(2)}) copy-start(bf16[16,128,768]{2,1,0:T(8,128)(2,1)} %param.10) | copy-start | bytes 9437188
  6.5 61.2 %all-gather.4.cloned.1.call-start = ((), (), s32[]{:S(2)}) async-start(), calls=%async_computation | async-start | bytes 1310720 | tf_op jit(solution)/shard_map/all_gather | solution.py:131
  9.3 0.8 copy-start.2
  10.1 15.9 %collective-permute-start.1 = (bf16[256,4,128]{2,0,1:T(8,128)(2,1)}, bf16[256,4,128]{2,0,1:T(8,128)(2,1)}, u32[]{:S(2)}, u32[]{:S(2)}) collective-permute-start(bf16[256,4,128]{2,0,1:T(8,128)(2,1)} %pad_maximum_fusion.1), channel_id=1, source_target_pairs={{0,8},{4,12},{8,16},{12,20},{16,24},{20,28},{1,9},{5,13},{9,17},{1... | collective-permute-start | bytes 786440 | tf_op jit(solution)/shard_map/ppermute | solution.py:80
  15.7 14.6 %collective-permute-start = (bf16[256,4,128]{2,0,1:T(8,128)(2,1)}, bf16[256,4,128]{2,0,1:T(8,128)(2,1)}, u32[]{:S(2)}, u32[]{:S(2)}) collective-permute-start(bf16[256,4,128]{2,0,1:T(8,128)(2,1)} %pad_maximum_fusion.1), channel_id=1, source_target_pairs={{0,4},{8,12},{16,20},{24,28},{1,5},{9,13},{17,21},{25,29},{2,6},{1... | collective-permute-start | bytes 786440 | tf_op jit(solution)/shard_map/ppermute | solution.py:81
  22.2 1.9 %copy-start.5 = (s32[256]{0:T(256)S(1)}, s32[256]{0:T(256)}, u32[]{:S(2)}) copy-start(s32[256]{0:T(256)} %get-tuple-element.42) | copy-start | bytes 3076
  22.2 2.0 %copy-start.7 = (pred[256]{0:T(512)(128)(4,1)S(1)}, pred[256]{0:T(512)(128)(4,1)}, u32[]{:S(2)}) copy-start(pred[256]{0:T(512)(128)(4,1)} %get-tuple-element.45) | copy-start | bytes 772
  22.2 2.0 %copy-start.8 = (pred[256]{0:T(512)(128)(4,1)S(1)}, pred[256]{0:T(512)(128)(4,1)}, u32[]{:S(2)}) copy-start(pred[256]{0:T(512)(128)(4,1)} %get-tuple-element.46) | copy-start | bytes 772
  22.2 2.0 %copy-start.9 = (pred[256]{0:T(512)(128)(4,1)S(1)}, pred[256]{0:T(512)(128)(4,1)}, u32[]{:S(2)}) copy-start(pred[256]{0:T(512)(128)(4,1)} %get-tuple-element.47) | copy-start | bytes 772
  22.2 2.0 %copy-start.10 = (pred[256]{0:T(512)(128)(4,1)S(1)}, pred[256]{0:T(512)(128)(4,1)}, u32[]{:S(2)}) copy-start(pred[256]{0:T(512)(128)(4,1)} %get-tuple-element.48) | copy-start | bytes 772
  22.2 2.0 %copy-start.11 = (pred[256]{0:T(512)(128)(4,1)S(1)}, pred[256]{0:T(512)(128)(4,1)}, u32[]{:S(2)}) copy-start(pred[256]{0:T(512)(128)(4,1)} %get-tuple-element.49) | copy-start | bytes 772
  22.2 2.0 %copy-start.12 = (pred[256]{0:T(512)(128)(4,1)S(1)}, pred[256]{0:T(512)(128)(4,1)}, u32[]{:S(2)}) copy-start(pred[256]{0:T(512)(128)(4,1)} %get-tuple-element.50) | copy-start | bytes 772
  22.2 2.8 %copy-start.3 = (bf16[256,2,64]{2,0,1:T(8,128)(2,1)S(1)}, bf16[256,2,64]{2,0,1:T(8,128)(2,1)}, u32[]{:S(2)}) copy-start(bf16[256,2,64]{2,0,1:T(8,128)(2,1)} %copy-done.2) | copy-start | bytes 196612
  23.3 2.3 %copy-start.1 = (bf16[256,2,128]{2,1,0:T(2,128)(2,1)S(1)}, bf16[256,2,128]{2,1,0:T(2,128)(2,1)}, u32[]{:S(2)}) copy-start(bf16[256,2,128]{2,1,0:T(2,128)(2,1)} %param.8) | copy-start | bytes 393220
  26.0 8.3 %collective-permute-start.3 = (bf16[256,4,128]{2,0,1:T(8,128)(2,1)}, bf16[256,4,128]{2,0,1:T(8,128)(2,1)S(1)}, u32[]{:S(2)}, u32[]{:S(2)}) collective-permute-start(bf16[256,4,128]{2,0,1:T(8,128)(2,1)} %collective-permute-done.1), channel_id=1, source_target_pairs={{0,8},{4,12},{8,16},{12,20},{16,24},{20,28},{1,9},{5,13},{9,17},{1... | collective-permute-start | bytes 786440 | tf_op jit(solution)/shard_map/ppermute | solution.py:80
  28.8 11.9 %collective-permute-start.2 = (bf16[256,4,128]{2,0,1:T(8,128)(2,1)}, bf16[256,4,128]{2,0,1:T(8,128)(2,1)S(1)}, u32[]{:S(2)}, u32[]{:S(2)}) collective-permute-start(bf16[256,4,128]{2,0,1:T(8,128)(2,1)} %collective-permute-done.1), channel_id=1, source_target_pairs={{0,4},{8,12},{16,20},{24,28},{4,0},{12,8},{20,16},{28,24},{1,5},{9... | collective-permute-start | bytes 786440 | tf_op jit(solution)/shard_map/ppermute | solution.py:81
  34.3 8.2 %collective-permute-start.5 = (bf16[256,4,128]{2,0,1:T(8,128)(2,1)S(1)}, bf16[256,4,128]{2,0,1:T(8,128)(2,1)S(1)}, u32[]{:S(2)}, u32[]{:S(2)}) collective-permute-start(bf16[256,4,128]{2,0,1:T(8,128)(2,1)S(1)} %collective-permute-done.3), channel_id=1, source_target_pairs={{0,8},{4,12},{8,16},{12,20},{16,24},{20,28},{1,9},{5,13},{9,17},{1... | collective-permute-start | bytes 786440 | tf_op jit(solution)/shard_map/ppermute | solution.py:80
  38.4 8.5 %collective-permute-start.4 = (bf16[256,4,128]{2,0,1:T(8,128)(2,1)S(1)}, bf16[256,4,128]{2,0,1:T(8,128)(2,1)S(1)}, u32[]{:S(2)}, u32[]{:S(2)}) collective-permute-start(bf16[256,4,128]{2,0,1:T(8,128)(2,1)S(1)} %collective-permute-done.3), channel_id=1, source_target_pairs={{0,4},{8,12},{16,20},{24,28},{4,0},{12,8},{20,16},{28,24},{1,5},{9... | collective-permute-start | bytes 786440 | tf_op jit(solution)/shard_map/ppermute | solution.py:81
  42.5 8.0 %collective-permute-start.6 = (bf16[256,4,128]{2,0,1:T(8,128)(2,1)S(1)}, bf16[256,4,128]{2,0,1:T(8,128)(2,1)S(1)}, u32[]{:S(2)}, u32[]{:S(2)}) collective-permute-start(bf16[256,4,128]{2,0,1:T(8,128)(2,1)S(1)} %collective-permute-done.5), channel_id=1, source_target_pairs={{0,4},{8,12},{16,20},{24,28},{4,0},{12,8},{20,16},{28,24},{1,5},{9... | collective-permute-start | bytes 786440 | tf_op jit(solution)/shard_map/ppermute | solution.py:81
  47.7 4.4 %copy-start.6 = (bf16[768]{0:T(1024)(128)(2,1)S(1)}, bf16[768]{0:T(1024)(128)(2,1)}, u32[]{:S(2)}) copy-start(bf16[768]{0:T(1024)(128)(2,1)} %param.11) | copy-start | bytes 4612
  52.1 23.9 %copy-start.4 = (bf16[256,768]{1,0:T(8,128)(2,1)S(1)}, bf16[256,768]{1,0:T(8,128)(2,1)}, u32[]{:S(2)}) copy-start(bf16[256,768]{1,0:T(8,128)(2,1)} %param.9) | copy-start | bytes 1179652
Sparse Core Ops, SparseCore 0:
  52.2 15.4 all-gather.3

commit v3 on v2

--- a/solution.py
+++ b/solution.py
@@ -86,6 +86,26 @@
     return state
 
 
+def exchanged(piece, count, index):
+    bit = 1
+    while bit < count:
+        other = lax.ppermute(piece, "tp", [(source, source ^ bit) for source in range(count)])
+        lower = (index & bit) == 0
+        first = jnp.where(lower, piece, other)
+        second = jnp.where(lower, other, piece)
+        piece = jnp.concatenate([first, second], axis=1)
+        bit *= 2
+    return piece
+
+
+def summed(partial, count):
+    bit = 1
+    while bit < count:
+        partial = partial + lax.ppermute(partial, "tp", [(source, source ^ bit) for source in range(count)])
+        bit *= 2
+    return partial
+
+
 def local(queries, keys, values, residual, out_weight, post_gain):
     rows = queries.shape[0]
     q_heads = queries.shape[1]
@@ -128,14 +148,23 @@
     attended = (numerators / denominators[..., None]).astype(jnp.bfloat16)
     attended = jnp.transpose(attended, (2, 0, 1, 3)).reshape(rows, q_heads, head_size)
     local_cols = out_weight.shape[2]
-    piece = lax.all_gather(attended, "tp", axis=1, tiled=True)
+    tp_size = lax.axis_size("tp")
+    tp_index = lax.axis_index("tp")
+    butterfly = tp_size & (tp_size - 1) == 0
+    if butterfly:
+        piece = exchanged(attended, tp_size, tp_index)
+    else:
+        piece = lax.all_gather(attended, "tp", axis=1, tiled=True)
     heads_in = piece.shape[1]
     weight_rows = out_weight.reshape(heads_in * head_size, local_cols)
     projected = jnp.dot(
         piece.reshape(rows, heads_in * head_size), weight_rows, preferred_element_type=jnp.float32
     )
     partial_sums = jnp.sum(projected * projected, axis=1)
-    square_sums = jnp.sum(lax.all_gather(partial_sums, "tp", axis=0), axis=0)
+    if butterfly:
+        square_sums = summed(partial_sums, tp_size)
+    else:
+        square_sums = jnp.sum(lax.all_gather(partial_sums, "tp", axis=0), axis=0)
     normed = projected * lax.rsqrt(square_sums / D + 1e-06)[:, None] * post_gain.astype(jnp.float32)
     mixed = residual.astype(jnp.float32) + normed
     return mixed.astype(jnp.bfloat16)

time: 85.2 us -> 71.8 us (0.84)
  between operations: 13.8 us -> 0.44 us
  blocking collectives: 5.06 us -> 0 us
  starting transfers between devices: 19.9 us -> 23 us
  matrix products: 14.3 us -> 11.5 us
  other arithmetic: 9.49 us -> 11.5 us
  waiting for transfers between devices: 21.1 us -> 22.6 us
  local copies, waits for them, and re-layouts: 1.21 us -> 2.52 us
    ppermute x0 -> x4, waiting for transfers between devices: none -> 17.1 us  [the longest x2 13.9 us: exchanged(): lax.ppermute(piece, 'tp', [(source, source ^ bit) for source in range(cou...]
    all_gather x1 -> x0, waiting for transfers between devices: 15.6 us -> none  [local(): piece = lax.all_gather(attended, 'tp', axis=1, tiled=True)]
    all_gather x1 -> x0, blocking collectives: 5.06 us -> none  [local(): square_sums = jnp.sum(lax.all_gather(partial_sums, 'tp', axis=0), axis=0)]
    ppermute x0 -> x4, starting transfers between devices: none -> 3.07 us  [the longest x2 1.54 us: exchanged(): lax.ppermute(piece, 'tp', [(source, source ^ bit) for source in range(cou...]
    select_n x0 -> x2, other arithmetic: none -> 2.25 us  [exchanged(): first = jnp.where(lower, piece, other)]
    dot_general x1, matrix products: 3.15 us -> 1.06 us  [local(): jnp.dot(piece.reshape(rows, heads_in * head_size), weight_rows, preferred...]
    unnamed x27 -> x31, local copies, waits for them, and re-layouts: 1.13 us -> 2.44 us
    convert_element_type x1, other arithmetic: 2.07 us -> 0.94 us  [local(): return mixed.astype(jnp.bfloat16)]
  transfers between devices with their start and end apart: 8 -> 11, of which waited for: 4 -> 7; matrix products, arithmetic and copies ran while one was open for 17% -> 20% of each run, Pallas kernels for 0% -> 0%
where the time goes in v3:
time: 71.8 us; the launch traced here: 71.5 us
  starting transfers between devices  23 us (32%)
  waiting for transfers between devices  22.6 us (31%)
  other arithmetic  11.5 us (16%)
  matrix products  11.5 us (16%)
  local copies, waits for them, and re-layouts  2.52 us (4%)
    ppermute x2, waiting for transfers between devices, exchanged(): lax.ppermute(piece, 'tp', [(source, source ^ bit) for source in range(cou...  13.9 us
    ppermute x3, starting transfers between devices, along_lines(): arrived = lax.ppermute(line, 'ctx', forward)  12.6 us
    ppermute x4, starting transfers between devices, along_lines(): crossed = lax.ppermute(line, 'ctx', up if step == 1 else up + down)  7.32 us
    dot_general x8, matrix products, attend_block(): jnp.einsum('sgrh,kgh->grsk', rotary_queries, key_block, preferred_element...  5.82 us
    dot_general x8, matrix products, attend_block(): jnp.einsum('grsk,kgh->grsh', weights.astype(jnp.bfloat16), value_block, p...  4.65 us
    ppermute x4, waiting for transfers between devices, along_lines(): crossed = lax.ppermute(line, 'ctx', up if step == 1 else up + down)  4.6 us
    ppermute x2, waiting for transfers between devices, summed(): lax.ppermute(partial, 'tp', [(source, source ^ bit) for source in range(c...  3.22 us
    unnamed x31, local copies, waits for them, and re-layouts  2.44 us
  transfers between devices with their start and end apart: 11, of which 7 were waited for; matrix products, arithmetic and copies ran while one was open for 20% of the time, Pallas kernels for 0%

profile of v3, /device:TPU:0, one launch (start us, length us, event | category | flops | bytes accessed | tf_op | source)
XLA Modules:
  0.0 71.5 jit_solution(18371988602328918467)
XLA Ops:
  0.0 0.0 copy-start
  0.0 1.1 %copy.12 = bf16[256,2,128]{2,0,1:T(8,128)(2,1)S(1)} copy(bf16[256,2,128]{2,1,0:T(2,128)(2,1)} %param.8) | data formatting | bytes 262144 | tf_op args[2]
  1.1 0.9 %copy_convert_fusion = f32[256,2,128]{2,0,1:T(8,128)S(1)} fusion(bf16[256,2,128]{2,1,0:T(2,128)(2,1)} %param.7), kind=kLoop, calls=%fused_computation.138 | loop fusion | flops 65536 | bytes 393216 | tf_op jit(solution)/shard_map/convert_element_type | solution.py:120
  2.0 0.5 multiply_cosine_fusion
  2.6 0.2 subtract_convert_fusion.1
  2.7 0.8 %pad_maximum_fusion.2 = bf16[256,4,128]{2,0,1:T(8,128)(2,1)} fusion(bf16[256,2,128]{2,0,1:T(8,128)(2,1)S(1)} %copy.12, bf16[256,2,64]{2,0,1:T(8,128)(2,1)S(1)} %get-tuple-element.12, bf16[256,2,64]{2,0,1:T(8,128)(2,1)S(1)} %get-tuple-element.11), kind=kLoop, calls=%fused_computation.97 | loop fusion | flops 786432 | bytes 524288 | tf_op jit(solution)/shard_map/concatenate | solution.py:77
  3.6 5.6 %collective-permute-start.1 = (bf16[256,4,128]{2,0,1:T(8,128)(2,1)}, bf16[256,4,128]{2,0,1:T(8,128)(2,1)}, u32[]{:S(2)}, u32[]{:S(2)}) collective-permute-start(bf16[256,4,128]{2,0,1:T(8,128)(2,1)} %pad_maximum_fusion.2), channel_id=1, source_target_pairs={{0,8},{4,12},{8,16},{12,20},{16,24},{20,28},{1,9},{5,13},{9,17},{1... | collective-permute-start | bytes 786440 | tf_op jit(solution)/shard_map/ppermute | solution.py:80
  9.2 4.1 %collective-permute-start = (bf16[256,4,128]{2,0,1:T(8,128)(2,1)}, bf16[256,4,128]{2,0,1:T(8,128)(2,1)}, u32[]{:S(2)}, u32[]{:S(2)}) collective-permute-start(bf16[256,4,128]{2,0,1:T(8,128)(2,1)} %pad_maximum_fusion.2), channel_id=1, source_target_pairs={{0,4},{8,12},{16,20},{24,28},{1,5},{9,13},{17,21},{25,29},{2,6},{1... | collective-permute-start | bytes 786440 | tf_op jit(solution)/shard_map/ppermute | solution.py:81
  13.3 0.6 fusion.79
  13.9 0.6 broadcast_compare_fusion.1
  14.5 0.6 iota_add_fusion.2
  15.1 0.6 broadcast_compare_fusion.3
  15.8 1.0 %convert_element_type.59 = f32[256,4,128]{2,1,0:T(4,128)S(1)} convert(bf16[256,4,128]{2,1,0:T(4,128)(2,1)} %param.6) | non-fusion elementwise | flops 131072 | bytes 786432 | tf_op jit(solution)/shard_map/convert_element_type | solution.py:118
  16.8 0.0 copy-start.2
  16.8 0.5 subtract_convert_fusion
  17.4 0.1 pad_maximum_fusion.1
  17.7 0.9 %fusion.74 = (pred[256,256]{0,1:T(8,128)(4,1)S(1)}, pred[256,256]{0,1:T(8,128)(4,1)S(1)}, pred[256,256]{0,1:T(8,128)(4,1)S(1)}, pred[256,256]{0,1:T(8,128)(4,1)S...) fusion(s32[256]{0:T(256)S(1)} %get-tuple-element.43, ...), kind=kLoop, calls=%fused_computation.115 | loop fusion | flops 2621440 | bytes 534528 | tf_op jit(solution)/shard_map/and | solution.py:51
  18.5 0.5 fusion.88
  19.1 0.3 fusion.57
  19.5 0.0 collective-permute-done.1
  19.5 2.8 %collective-permute-start.3 = (bf16[256,4,128]{2,0,1:T(8,128)(2,1)}, bf16[256,4,128]{2,0,1:T(8,128)(2,1)S(1)}, u32[]{:S(2)}, u32[]{:S(2)}) collective-permute-start(bf16[256,4,128]{2,0,1:T(8,128)(2,1)} %collective-permute-done.1), channel_id=1, source_target_pairs={{0,8},{4,12},{8,16},{12,20},{16,24},{20,28},{1,9},{5,13},{9,17},{1... | collective-permute-start | bytes 786440 | tf_op jit(solution)/shard_map/ppermute | solution.py:80
  22.3 0.1 collective-permute-start.2
  22.4 1.4 %fusion.87 = (f32[2,2,256]{2,1,0:T(2,128)S(1)}, bf16[2,2,256,256]{2,3,1,0:T(8,128)(2,1)S(1)}) fusion(bf16[256,2,2,128]{3,0,2,1:T(8,128)(2,1)S(1)} %pad_maximum_fusion.1, bf16[256,4,128]{2,0,1:T(8,128)(2,1)} %collective-permute-done.1, pred[256,256]{0,1:T(8,128)(4,1)S(1)} %get-tuple-element.19), kind=kOutput, calls=%fused_computation.166 | convolution fusion | flops 68418560 | bytes 987136 | tf_op jit(solution)/shard_map/sgrh,kgh->grsk/dot_general | solution.py:43
  23.8 0.0 collective-permute-done
  23.8 1.4 %fusion.89 = (f32[2,2,256]{2,1,0:T(2,128)S(1)}, bf16[2,2,256,256]{2,3,1,0:T(8,128)(2,1)S(1)}) fusion(bf16[256,2,2,128]{3,0,2,1:T(8,128)(2,1)S(1)} %pad_maximum_fusion.1, bf16[256,4,128]{2,0,1:T(8,128)(2,1)} %collective-permute-done, pred[256,256]{0,1:T(8,128)(4,1)S(1)} %get-tuple-element.22), kind=kOutput, calls=%fused_computation.168 | convolution fusion | flops 68418560 | bytes 987136 | tf_op jit(solution)/shard_map/sgrh,kgh->grsk/dot_general | solution.py:43
  25.2 1.3 %convolution_add_fusion.4 = f32[2,2,256,128]{3,2,1,0:T(8,128)S(1)} fusion(f32[2,2,256,128]{3,2,1,0:T(8,128)S(1)} %fusion.57, bf16[2,2,256,256]{2,3,1,0:T(8,128)(2,1)S(1)} %get-tuple-element.38, bf16[256,4,128]{2,0,1:T(8,128)(2,1)} %collective-permute-done), kind=kOutput, calls=%fused_computation.57 | convolution fusion | flops 67239936 | bytes 1703936 | tf_op jit(solution)/shard_map/grsk,kgh->grsh/dot_general | solution.py:54
  26.5 1.3 %convolution_add_fusion.3 = f32[2,2,256,128]{3,2,1,0:T(8,128)S(1)} fusion(f32[2,2,256,128]{3,2,1,0:T(8,128)S(1)} %convolution_add_fusion.4, bf16[2,2,256,256]{2,3,1,0:T(8,128)(2,1)S(1)} %get-tuple-element.34, bf16[256,4,128]{2,0,1:T(8,128)(2,1)} %collective-permute-done.1), kind=kOutput, calls=%fused_computation.56 | convolution fusion | flops 67239936 | bytes 1703936 | tf_op jit(solution)/shard_map/grsk,kgh->grsh/dot_general | solution.py:54
  27.7 0.0 collective-permute-done.3
  27.7 4.1 %collective-permute-start.5 = (bf16[256,4,128]{2,0,1:T(8,128)(2,1)S(1)}, bf16[256,4,128]{2,0,1:T(8,128)(2,1)S(1)}, u32[]{:S(2)}, u32[]{:S(2)}) collective-permute-start(bf16[256,4,128]{2,0,1:T(8,128)(2,1)S(1)} %collective-permute-done.3), channel_id=1, source_target_pairs={{0,8},{4,12},{8,16},{12,20},{16,24},{20,28},{1,9},{5,13},{9,17},{1... | collective-permute-start | bytes 786440 | tf_op jit(solution)/shard_map/ppermute | solution.py:80
  31.9 1.4 %collective-permute-start.4 = (bf16[256,4,128]{2,0,1:T(8,128)(2,1)S(1)}, bf16[256,4,128]{2,0,1:T(8,128)(2,1)S(1)}, u32[]{:S(2)}, u32[]{:S(2)}) collective-permute-start(bf16[256,4,128]{2,0,1:T(8,128)(2,1)S(1)} %collective-permute-done.3), channel_id=1, source_target_pairs={{0,4},{8,12},{16,20},{24,28},{4,0},{12,8},{20,16},{28,24},{1,5},{9... | collective-permute-start | bytes 786440 | tf_op jit(solution)/shard_map/ppermute | solution.py:81
  33.3 0.5 fusion.85
  33.8 0.3 fusion.52
  34.1 0.0 collective-permute-done.2
  34.2 0.5 fusion.86
  34.7 0.4 fusion.43
  35.0 0.9 %collective-permute-done.5 = bf16[256,4,128]{2,0,1:T(8,128)(2,1)S(1)} collective-permute-done((bf16[256,4,128]{2,0,1:T(8,128)(2,1)S(1)}, bf16[256,4,128]{2,0,1:T(8,128)(2,1)S(1)}, u32[]{:S(2)}, u32[]{:S(2)}) %collective-permute-start.5) | collective-permute-done | bytes 262176 | tf_op jit(solution)/shard_map/ppermute | solution.py:80
  35.9 1.7 %collective-permute-start.6 = (bf16[256,4,128]{2,0,1:T(8,128)(2,1)S(1)}, bf16[256,4,128]{2,0,1:T(8,128)(2,1)S(1)}, u32[]{:S(2)}, u32[]{:S(2)}) collective-permute-start(bf16[256,4,128]{2,0,1:T(8,128)(2,1)S(1)} %collective-permute-done.5), channel_id=1, source_target_pairs={{0,4},{8,12},{16,20},{24,28},{4,0},{12,8},{20,16},{28,24},{1,5},{9... | collective-permute-start | bytes 786440 | tf_op jit(solution)/shard_map/ppermute | solution.py:81
  37.6 0.5 fusion.83
  38.1 0.3 fusion.49
  38.5 1.9 %collective-permute-done.4 = bf16[256,4,128]{2,0,1:T(8,128)(2,1)S(1)} collective-permute-done((bf16[256,4,128]{2,0,1:T(8,128)(2,1)S(1)}, bf16[256,4,128]{2,0,1:T(8,128)(2,1)S(1)}, u32[]{:S(2)}, u32[]{:S(2)}) %collective-permute-start.4) | collective-permute-done | bytes 262176 | tf_op jit(solution)/shard_map/ppermute | solution.py:81
  40.4 0.5 fusion.84
  40.9 0.4 fusion.42
  41.2 2.7 %collective-permute-done.6 = bf16[256,4,128]{2,0,1:T(8,128)(2,1)S(1)} collective-permute-done((bf16[256,4,128]{2,0,1:T(8,128)(2,1)S(1)}, bf16[256,4,128]{2,0,1:T(8,128)(2,1)S(1)}, u32[]{:S(2)}, u32[]{:S(2)}) %collective-permute-start.6) | collective-permute-done | bytes 262176 | tf_op jit(solution)/shard_map/ppermute | solution.py:81
  43.9 0.5 fusion.82
  44.4 0.4 fusion.44
  44.8 0.0 copy-start.6
  44.9 0.1 collective-permute-start.7
  44.9 0.6 copy-done.6
  45.6 1.0 %collective-permute-done.7 = bf16[256,4,128]{2,0,1:T(8,128)(2,1)} collective-permute-done((bf16[256,4,128]{2,0,1:T(8,128)(2,1)S(1)}, bf16[256,4,128]{2,0,1:T(8,128)(2,1)}, u32[]{:S(2)}, u32[]{:S(2)}) %collective-permute-start.7) | collective-permute-done | bytes 262176 | tf_op jit(solution)/shard_map/ppermute | solution.py:92
  46.6 1.1 %broadcast_select_fusion.3 = (bf16[256,4,128]{2,0,1:T(8,128)(2,1)S(1)}, bf16[256,4,128]{2,0,1:T(8,128)(2,1)S(1)}) fusion(bf16[256,4,128]{2,0,1:T(8,128)(2,1)} %collective-permute-done.7, pred[]{:T(512)S(6)} %eq.9, bf16[256,2,2,128]{3,0,2,1:T(8,128)(2,1)} %copy-done.6), kind=kLoop, calls=%fused_computation.117 | loop fusion | flops 262144 | bytes 1048577 | tf_op jit(solution)/shard_map/jit(_where)/select_n | solution.py:94
  47.7 0.0 copy-start.1
  47.7 0.7 copy-done.1
  48.4 0.9 %pad_maximum_fusion = bf16[256,8,128]{2,0,1:T(8,128)(2,1)} fusion(bf16[256,4,128]{2,0,1:T(8,128)(2,1)S(1)} %get-tuple-element.10, bf16[256,4,128]{2,0,1:T(8,128)(2,1)S(1)} %get-tuple-element.9), kind=kLoop, calls=%fused_computation.64 | loop fusion | flops 262144 | bytes 1048576 | tf_op jit(solution)/shard_map/concatenate | solution.py:96
  49.2 1.5 %collective-permute-start.8 = (bf16[256,8,128]{2,0,1:T(8,128)(2,1)}, bf16[256,8,128]{2,0,1:T(8,128)(2,1)}, u32[]{:S(2)}, u32[]{:S(2)}) collective-permute-start(bf16[256,8,128]{2,0,1:T(8,128)(2,1)} %pad_maximum_fusion), channel_id=1, source_target_pairs={{0,2},{1,3},{2,0},{3,1},{4,6},{5,7},{6,4},{7,5},{8,10},{9,11},{10,... | collective-permute-start | bytes 1572872 | tf_op jit(solution)/shard_map/ppermute | solution.py:92
  50.7 12.8 %collective-permute-done.8 = bf16[256,8,128]{2,0,1:T(8,128)(2,1)} collective-permute-done((bf16[256,8,128]{2,0,1:T(8,128)(2,1)}, bf16[256,8,128]{2,0,1:T(8,128)(2,1)}, u32[]{:S(2)}, u32[]{:S(2)}) %collective-permute-start.8) | collective-permute-done | bytes 524320 | tf_op jit(solution)/shard_map/ppermute | solution.py:92
  63.5 1.2 %broadcast_select_fusion.1 = (bf16[256,8,128]{2,0,1:T(8,128)(2,1)S(1)}, bf16[256,8,128]{2,0,1:T(8,128)(2,1)S(1)}) fusion(bf16[256,8,128]{2,0,1:T(8,128)(2,1)} %collective-permute-done.8, pred[]{:T(512)S(6)} %eq.8, bf16[256,4,128]{2,0,1:T(8,128)(2,1)} %copy-done.1, bf16[256,4,128]{2,0,1:T(8,128)(2,1)S(1)} %get-tuple-element.9), kind=kLoop, calls=%fused_computation.79 | loop fusion | flops 786432 | bytes 2097153 | tf_op jit(solution)/shard_map/jit(_where)/select_n | solution.py:94
  64.7 0.0 copy-start.8
  64.7 0.0 copy-start.5
  64.7 1.1 %multiply_reduce_fusion = (f32[256]{0:T(256)S(1)}, f32[256,768]{1,0:T(8,128)S(1)}) fusion(bf16[16,128,768]{2,1,0:T(8,128)(2,1)S(1)} %copy-done, bf16[256,8,128]{2,0,1:T(8,128)(2,1)S(1)} %get-tuple-element.6, bf16[256,8,128]{2,0,1:T(8,128)(2,1)S(1)} %get-tuple-element.5), kind=kOutput, calls=%fused_computation.63 | convolution fusion | flops 806223616 | bytes 4981760 | tf_op jit(solution)/shard_map/dot_general | solution.py:160
  65.8 0.1 collective-permute-start.9
  65.9 1.1 %collective-permute-done.9 = f32[256]{0:T(256)S(1)} collective-permute-done((f32[256]{0:T(256)S(1)}, f32[256]{0:T(256)S(1)}, u32[]{:S(2)}, u32[]{:S(2)}) %collective-permute-start.9) | collective-permute-done | bytes 1056 | tf_op jit(solution)/shard_map/ppermute | solution.py:104
  67.0 1.5 %collective-permute-start.10 = (f32[256]{0:T(256)S(1)}, f32[256]{0:T(256)S(1)}, u32[]{:S(2)}, u32[]{:S(2)}) collective-permute-start(f32[256]{0:T(256)S(1)} %add.332), channel_id=1, source_target_pairs={{0,2},{1,3},{2,0},{3,1},{4,6},{5,7},{6,4},{7,5},{8,10},{9,11},{10,... | collective-permute-start | bytes 3080 | tf_op jit(solution)/shard_map/ppermute | solution.py:104
  68.5 2.1 %collective-permute-done.10 = f32[256]{0:T(256)S(1)} collective-permute-done((f32[256]{0:T(256)S(1)}, f32[256]{0:T(256)S(1)}, u32[]{:S(2)}, u32[]{:S(2)}) %collective-permute-start.10) | collective-permute-done | bytes 1056 | tf_op jit(solution)/shard_map/ppermute | solution.py:104
  70.6 0.9 %add_convert_fusion = bf16[256,768]{1,0:T(8,128)(2,1)} fusion(f32[256,768]{1,0:T(8,128)S(1)} %get-tuple-element.40, bf16[256,768]{1,0:T(8,128)(2,1)S(1)} %copy-done.5, f32[768]{0:T(1024)S(1)} %convert_element_type.69, f32[256]{0:T(256)S(1)} %add_rsqrt_fusion), kind=kLoop, calls=%fused_computation.62 | loop fusion | flops 983040 | bytes 1576960 | tf_op jit(solution)/shard_map/convert_element_type | solution.py:170
  (34 shorter events, 0.2 us)
Async XLA Ops:
  0.0 64.7 %copy-start = (bf16[16,128,768]{2,1,0:T(8,128)(2,1)S(1)}, bf16[16,128,768]{2,1,0:T(8,128)(2,1)}, u32[]{:S(2)}) copy-start(bf16[16,128,768]{2,1,0:T(8,128)(2,1)} %param.10) | copy-start | bytes 9437188
  2.7 0.8 %copy-start.3 = (bf16[256,2,64]{2,0,1:T(8,128)(2,1)}, bf16[256,2,64]{2,0,1:T(8,128)(2,1)S(1)}, u32[]{:S(2)}) copy-start(bf16[256,2,64]{2,0,1:T(8,128)(2,1)S(1)} %get-tuple-element.12) | copy-start | bytes 196612
  3.6 15.9 %collective-permute-start.1 = (bf16[256,4,128]{2,0,1:T(8,128)(2,1)}, bf16[256,4,128]{2,0,1:T(8,128)(2,1)}, u32[]{:S(2)}, u32[]{:S(2)}) collective-permute-start(bf16[256,4,128]{2,0,1:T(8,128)(2,1)} %pad_maximum_fusion.2), channel_id=1, source_target_pairs={{0,8},{4,12},{8,16},{12,20},{16,24},{20,28},{1,9},{5,13},{9,17},{1... | collective-permute-start | bytes 786440 | tf_op jit(solution)/shard_map/ppermute | solution.py:80
  9.2 14.6 %collective-permute-start = (bf16[256,4,128]{2,0,1:T(8,128)(2,1)}, bf16[256,4,128]{2,0,1:T(8,128)(2,1)}, u32[]{:S(2)}, u32[]{:S(2)}) collective-permute-start(bf16[256,4,128]{2,0,1:T(8,128)(2,1)} %pad_maximum_fusion.2), channel_id=1, source_target_pairs={{0,4},{8,12},{16,20},{24,28},{1,5},{9,13},{17,21},{25,29},{2,6},{1... | collective-permute-start | bytes 786440 | tf_op jit(solution)/shard_map/ppermute | solution.py:81
  15.7 1.9 %copy-start.7 = (s32[256]{0:T(256)S(1)}, s32[256]{0:T(256)}, u32[]{:S(2)}) copy-start(s32[256]{0:T(256)} %get-tuple-element.46) | copy-start | bytes 3076
  15.7 1.9 %copy-start.9 = (pred[256]{0:T(512)(128)(4,1)S(1)}, pred[256]{0:T(512)(128)(4,1)}, u32[]{:S(2)}) copy-start(pred[256]{0:T(512)(128)(4,1)} %get-tuple-element.49) | copy-start | bytes 772
  15.7 1.9 %copy-start.10 = (pred[256]{0:T(512)(128)(4,1)S(1)}, pred[256]{0:T(512)(128)(4,1)}, u32[]{:S(2)}) copy-start(pred[256]{0:T(512)(128)(4,1)} %get-tuple-element.50) | copy-start | bytes 772
  15.7 1.9 %copy-start.11 = (pred[256]{0:T(512)(128)(4,1)S(1)}, pred[256]{0:T(512)(128)(4,1)}, u32[]{:S(2)}) copy-start(pred[256]{0:T(512)(128)(4,1)} %get-tuple-element.51) | copy-start | bytes 772
  15.7 1.9 %copy-start.12 = (pred[256]{0:T(512)(128)(4,1)S(1)}, pred[256]{0:T(512)(128)(4,1)}, u32[]{:S(2)}) copy-start(pred[256]{0:T(512)(128)(4,1)} %get-tuple-element.52) | copy-start | bytes 772
  15.7 1.9 %copy-start.13 = (pred[256]{0:T(512)(128)(4,1)S(1)}, pred[256]{0:T(512)(128)(4,1)}, u32[]{:S(2)}) copy-start(pred[256]{0:T(512)(128)(4,1)} %get-tuple-element.53) | copy-start | bytes 772
  15.7 1.9 %copy-start.14 = (pred[256]{0:T(512)(128)(4,1)S(1)}, pred[256]{0:T(512)(128)(4,1)}, u32[]{:S(2)}) copy-start(pred[256]{0:T(512)(128)(4,1)} %get-tuple-element.54) | copy-start | bytes 772
  15.7 2.8 %copy-start.4 = (bf16[256,2,64]{2,0,1:T(8,128)(2,1)S(1)}, bf16[256,2,64]{2,0,1:T(8,128)(2,1)}, u32[]{:S(2)}) copy-start(bf16[256,2,64]{2,0,1:T(8,128)(2,1)} %copy-done.3) | copy-start | bytes 196612
  16.8 2.3 %copy-start.2 = (bf16[256,2,128]{2,1,0:T(2,128)(2,1)S(1)}, bf16[256,2,128]{2,1,0:T(2,128)(2,1)}, u32[]{:S(2)}) copy-start(bf16[256,2,128]{2,1,0:T(2,128)(2,1)} %param.8) | copy-start | bytes 393220
  19.5 8.3 %collective-permute-start.3 = (bf16[256,4,128]{2,0,1:T(8,128)(2,1)}, bf16[256,4,128]{2,0,1:T(8,128)(2,1)S(1)}, u32[]{:S(2)}, u32[]{:S(2)}) collective-permute-start(bf16[256,4,128]{2,0,1:T(8,128)(2,1)} %collective-permute-done.1), channel_id=1, source_target_pairs={{0,8},{4,12},{8,16},{12,20},{16,24},{20,28},{1,9},{5,13},{9,17},{1... | collective-permute-start | bytes 786440 | tf_op jit(solution)/shard_map/ppermute | solution.py:80
  22.3 11.9 %collective-permute-start.2 = (bf16[256,4,128]{2,0,1:T(8,128)(2,1)}, bf16[256,4,128]{2,0,1:T(8,128)(2,1)S(1)}, u32[]{:S(2)}, u32[]{:S(2)}) collective-permute-start(bf16[256,4,128]{2,0,1:T(8,128)(2,1)} %collective-permute-done.1), channel_id=1, source_target_pairs={{0,4},{8,12},{16,20},{24,28},{4,0},{12,8},{20,16},{28,24},{1,5},{9... | collective-permute-start | bytes 786440 | tf_op jit(solution)/shard_map/ppermute | solution.py:81
  27.7 8.2 %collective-permute-start.5 = (bf16[256,4,128]{2,0,1:T(8,128)(2,1)S(1)}, bf16[256,4,128]{2,0,1:T(8,128)(2,1)S(1)}, u32[]{:S(2)}, u32[]{:S(2)}) collective-permute-start(bf16[256,4,128]{2,0,1:T(8,128)(2,1)S(1)} %collective-permute-done.3), channel_id=1, source_target_pairs={{0,8},{4,12},{8,16},{12,20},{16,24},{20,28},{1,9},{5,13},{9,17},{1... | collective-permute-start | bytes 786440 | tf_op jit(solution)/shard_map/ppermute | solution.py:80
  31.9 8.5 %collective-permute-start.4 = (bf16[256,4,128]{2,0,1:T(8,128)(2,1)S(1)}, bf16[256,4,128]{2,0,1:T(8,128)(2,1)S(1)}, u32[]{:S(2)}, u32[]{:S(2)}) collective-permute-start(bf16[256,4,128]{2,0,1:T(8,128)(2,1)S(1)} %collective-permute-done.3), channel_id=1, source_target_pairs={{0,4},{8,12},{16,20},{24,28},{4,0},{12,8},{20,16},{28,24},{1,5},{9... | collective-permute-start | bytes 786440 | tf_op jit(solution)/shard_map/ppermute | solution.py:81
  35.9 8.0 %collective-permute-start.6 = (bf16[256,4,128]{2,0,1:T(8,128)(2,1)S(1)}, bf16[256,4,128]{2,0,1:T(8,128)(2,1)S(1)}, u32[]{:S(2)}, u32[]{:S(2)}) collective-permute-start(bf16[256,4,128]{2,0,1:T(8,128)(2,1)S(1)} %collective-permute-done.5), channel_id=1, source_target_pairs={{0,4},{8,12},{16,20},{24,28},{4,0},{12,8},{20,16},{28,24},{1,5},{9... | collective-permute-start | bytes 786440 | tf_op jit(solution)/shard_map/ppermute | solution.py:81
  44.8 0.7 copy-start.6
  44.9 1.7 %collective-permute-start.7 = (bf16[256,4,128]{2,0,1:T(8,128)(2,1)S(1)}, bf16[256,4,128]{2,0,1:T(8,128)(2,1)}, u32[]{:S(2)}, u32[]{:S(2)}) collective-permute-start(bf16[256,4,128]{2,0,1:T(8,128)(2,1)S(1)} %bitcast.159), channel_id=1, source_target_pairs={{0,1},{1,0},{2,3},{3,2},{4,5},{5,4},{6,7},{7,6},{8,9},{9,8},{10,11... | collective-permute-start | bytes 786440 | tf_op jit(solution)/shard_map/ppermute | solution.py:92
  47.7 0.7 copy-start.1
  49.2 14.3 %collective-permute-start.8 = (bf16[256,8,128]{2,0,1:T(8,128)(2,1)}, bf16[256,8,128]{2,0,1:T(8,128)(2,1)}, u32[]{:S(2)}, u32[]{:S(2)}) collective-permute-start(bf16[256,8,128]{2,0,1:T(8,128)(2,1)} %pad_maximum_fusion), channel_id=1, source_target_pairs={{0,2},{1,3},{2,0},{3,1},{4,6},{5,7},{6,4},{7,5},{8,10},{9,11},{10,... | collective-permute-start | bytes 1572872 | tf_op jit(solution)/shard_map/ppermute | solution.py:92
  64.7 3.8 %copy-start.8 = (bf16[768]{0:T(1024)(128)(2,1)S(1)}, bf16[768]{0:T(1024)(128)(2,1)}, u32[]{:S(2)}) copy-start(bf16[768]{0:T(1024)(128)(2,1)} %param.11) | copy-start | bytes 4612
  64.7 5.9 %copy-start.5 = (bf16[256,768]{1,0:T(8,128)(2,1)S(1)}, bf16[256,768]{1,0:T(8,128)(2,1)}, u32[]{:S(2)}) copy-start(bf16[256,768]{1,0:T(8,128)(2,1)} %param.9) | copy-start | bytes 1179652
  65.8 1.2 %collective-permute-start.9 = (f32[256]{0:T(256)S(1)}, f32[256]{0:T(256)S(1)}, u32[]{:S(2)}, u32[]{:S(2)}) collective-permute-start(f32[256]{0:T(256)S(1)} %get-tuple-element.39), channel_id=1, source_target_pairs={{0,1},{1,0},{2,3},{3,2},{4,5},{5,4},{6,7},{7,6},{8,9},{9,8},{10,11... | collective-permute-start | bytes 3080 | tf_op jit(solution)/shard_map/ppermute | solution.py:104
  67.0 3.6 %collective-permute-start.10 = (f32[256]{0:T(256)S(1)}, f32[256]{0:T(256)S(1)}, u32[]{:S(2)}, u32[]{:S(2)}) collective-permute-start(f32[256]{0:T(256)S(1)} %add.332), channel_id=1, source_target_pairs={{0,2},{1,3},{2,0},{3,1},{4,6},{5,7},{6,4},{7,5},{8,10},{9,11},{10,... | collective-permute-start | bytes 3080 | tf_op jit(solution)/shard_map/ppermute | solution.py:104

commit v4 on v3

--- a/solution.py
+++ b/solution.py
@@ -86,23 +86,26 @@
     return state
 
 
-def exchanged(piece, count, index):
-    bit = 1
-    while bit < count:
-        other = lax.ppermute(piece, "tp", [(source, source ^ bit) for source in range(count)])
-        lower = (index & bit) == 0
-        first = jnp.where(lower, piece, other)
-        second = jnp.where(lower, other, piece)
-        piece = jnp.concatenate([first, second], axis=1)
-        bit *= 2
-    return piece
+def exchanged(piece, count):
+    pieces = [(piece, 0)]
+    bit = count // 2
+    while bit >= 1:
+        sent = jnp.concatenate([held for held, unused in pieces], axis=1)
+        arrived = lax.ppermute(sent, "tp", [(source, source ^ bit) for source in range(count)])
+        width = piece.shape[1]
+        pieces = pieces + [
+            (arrived[:, slot * width : (slot + 1) * width], offset ^ bit)
+            for slot, (unused, offset) in enumerate(pieces)
+        ]
+        bit //= 2
+    return pieces
 
 
 def summed(partial, count):
-    bit = 1
-    while bit < count:
+    bit = count // 2
+    while bit >= 1:
         partial = partial + lax.ppermute(partial, "tp", [(source, source ^ bit) for source in range(count)])
-        bit *= 2
+        bit //= 2
     return partial
 
 
@@ -152,14 +155,23 @@
     tp_index = lax.axis_index("tp")
     butterfly = tp_size & (tp_size - 1) == 0
     if butterfly:
-        piece = exchanged(attended, tp_size, tp_index)
+        projected = None
+        for held, offset in exchanged(attended, tp_size):
+            owner = jnp.bitwise_xor(tp_index, offset)
+            weight_rows = lax.dynamic_slice_in_dim(out_weight, owner * q_heads, q_heads, 0)
+            part = jnp.dot(
+                held.reshape(rows, q_heads * head_size),
+                weight_rows.reshape(q_heads * head_size, local_cols),
+                preferred_element_type=jnp.float32,
+            )
+            projected = part if projected is None else projected + part
     else:
         piece = lax.all_gather(attended, "tp", axis=1, tiled=True)
-    heads_in = piece.shape[1]
-    weight_rows = out_weight.reshape(heads_in * head_size, local_cols)
-    projected = jnp.dot(
-        piece.reshape(rows, heads_in * head_size), weight_rows, preferred_element_type=jnp.float32
-    )
+        heads_in = piece.shape[1]
+        weight_rows = out_weight.reshape(heads_in * head_size, local_cols)
+        projected = jnp.dot(
+            piece.reshape(rows, heads_in * head_size), weight_rows, preferred_element_type=jnp.float32
+        )
     partial_sums = jnp.sum(projected * projected, axis=1)
     if butterfly:
         square_sums = summed(partial_sums, tp_size)

time: 71.8 us -> 66.1 us (0.921)
  waiting for transfers between devices: 22.6 us -> 16.2 us
  matrix products: 11.5 us -> 13.3 us
  other arithmetic: 11.5 us -> 10.1 us
    ppermute x2, waiting for transfers between devices: 13.9 us -> 6.89 us  [exchanged(): lax.ppermute(sent, 'tp', [(source, source ^ bit) for source in range(coun...]
    dot_general x1 -> x4, matrix products: 1.06 us -> 3.56 us  [local(): jnp.dot(held.reshape(rows, q_heads * head_size), weight_rows.reshape(q_he...]
    select_n x2 -> x0, other arithmetic: 2.25 us -> none  [exchanged(): first = jnp.where(lower, piece, other)]
    concatenate x1, other arithmetic: 0.85 us -> 1.79 us  [exchanged(): sent = jnp.concatenate([held for held, unused in pieces], axis=1)]
    reshape x0 -> x1, local copies, waits for them, and re-layouts: none -> 0.84 us  [local(): jnp.transpose(attended, (2, 0, 1, 3)).reshape(rows, q_heads, head_size)]
  transfers between devices with their start and end apart: 11 -> 11, of which waited for: 7 -> 7; matrix products, arithmetic and copies ran while one was open for 20% -> 22% of each run, Pallas kernels for 0% -> 0%
where the time goes in v4:
time: 66.1 us; the launch traced here: 65.7 us
  starting transfers between devices  22.8 us (34%)
  waiting for transfers between devices  16.2 us (25%)
  matrix products  13.3 us (20%)
  other arithmetic  10.1 us (15%)
  local copies, waits for them, and re-layouts  2.82 us (4%)
    ppermute x3, starting transfers between devices, along_lines(): arrived = lax.ppermute(line, 'ctx', forward)  12.7 us
    ppermute x4, starting transfers between devices, along_lines(): crossed = lax.ppermute(line, 'ctx', up if step == 1 else up + down)  7.05 us
    ppermute x2, waiting for transfers between devices, exchanged(): lax.ppermute(sent, 'tp', [(source, source ^ bit) for source in range(coun...  6.89 us
    dot_general x8, matrix products, attend_block(): jnp.einsum('sgrh,kgh->grsk', rotary_queries, key_block, preferred_element...  5.81 us
    ppermute x4, waiting for transfers between devices, along_lines(): crossed = lax.ppermute(line, 'ctx', up if step == 1 else up + down)  4.88 us
    dot_general x8, matrix products, attend_block(): jnp.einsum('grsk,kgh->grsh', weights.astype(jnp.bfloat16), value_block, p...  3.95 us
    dot_general x4, matrix products, local(): jnp.dot(held.reshape(rows, q_heads * head_size), weight_rows.reshape(q_he...  3.56 us
    ppermute x2, waiting for transfers between devices, summed(): lax.ppermute(partial, 'tp', [(source, source ^ bit) for source in range(c...  3.21 us
  transfers between devices with their start and end apart: 11, of which 7 were waited for; matrix products, arithmetic and copies ran while one was open for 22% of the time, Pallas kernels for 0%

profile of v4, /device:TPU:0, one launch (start us, length us, event | category | flops | bytes accessed | tf_op | source)
XLA Modules:
  0.0 65.7 jit_solution(10099210537749127448)
XLA Ops:
  0.0 1.1 %copy.12 = bf16[256,2,128]{2,0,1:T(8,128)(2,1)S(1)} copy(bf16[256,2,128]{2,1,0:T(2,128)(2,1)} %param.8) | data formatting | bytes 262144 | tf_op args[2]
  1.1 0.9 %copy_convert_fusion = f32[256,2,128]{2,0,1:T(8,128)S(1)} fusion(bf16[256,2,128]{2,1,0:T(2,128)(2,1)} %param.7), kind=kLoop, calls=%fused_computation.139 | loop fusion | flops 65536 | bytes 393216 | tf_op jit(solution)/shard_map/convert_element_type | solution.py:123
  2.0 0.5 multiply_cosine_fusion
  2.6 0.2 subtract_convert_fusion.1
  2.7 0.8 %pad_maximum_fusion.2 = bf16[256,4,128]{2,0,1:T(8,128)(2,1)} fusion(bf16[256,2,128]{2,0,1:T(8,128)(2,1)S(1)} %copy.12, bf16[256,2,64]{2,0,1:T(8,128)(2,1)S(1)} %get-tuple-element.8, bf16[256,2,64]{2,0,1:T(8,128)(2,1)S(1)} %get-tuple-element.7), kind=kLoop, calls=%fused_computation.100 | loop fusion | flops 786432 | bytes 524288 | tf_op jit(solution)/shard_map/concatenate | solution.py:77
  3.6 5.6 %collective-permute-start.1 = (bf16[256,4,128]{2,0,1:T(8,128)(2,1)}, bf16[256,4,128]{2,0,1:T(8,128)(2,1)}, u32[]{:S(2)}, u32[]{:S(2)}) collective-permute-start(bf16[256,4,128]{2,0,1:T(8,128)(2,1)} %pad_maximum_fusion.2), channel_id=1, source_target_pairs={{0,8},{4,12},{8,16},{12,20},{16,24},{20,28},{1,9},{5,13},{9,17},{1... | collective-permute-start | bytes 786440 | tf_op jit(solution)/shard_map/ppermute | solution.py:80
  9.2 4.1 %collective-permute-start = (bf16[256,4,128]{2,0,1:T(8,128)(2,1)}, bf16[256,4,128]{2,0,1:T(8,128)(2,1)}, u32[]{:S(2)}, u32[]{:S(2)}) collective-permute-start(bf16[256,4,128]{2,0,1:T(8,128)(2,1)} %pad_maximum_fusion.2), channel_id=1, source_target_pairs={{0,4},{8,12},{16,20},{24,28},{1,5},{9,13},{17,21},{25,29},{2,6},{1... | collective-permute-start | bytes 786440 | tf_op jit(solution)/shard_map/ppermute | solution.py:81
  13.3 0.6 fusion.85
  13.9 0.6 broadcast_compare_fusion.1
  14.5 0.6 iota_add_fusion.2
  15.1 0.6 broadcast_compare_fusion.3
  15.8 1.0 %convert_element_type.59 = f32[256,4,128]{2,1,0:T(4,128)S(1)} convert(bf16[256,4,128]{2,1,0:T(4,128)(2,1)} %param.6) | non-fusion elementwise | flops 131072 | bytes 786432 | tf_op jit(solution)/shard_map/convert_element_type | solution.py:121
  16.8 0.0 copy-start.3
  16.8 0.5 subtract_convert_fusion
  17.4 0.1 pad_maximum_fusion.1
  17.7 0.9 %fusion.77 = (pred[256,256]{0,1:T(8,128)(4,1)S(1)}, pred[256,256]{0,1:T(8,128)(4,1)S(1)}, pred[256,256]{0,1:T(8,128)(4,1)S(1)}, pred[256,256]{0,1:T(8,128)(4,1)S...) fusion(s32[256]{0:T(256)S(1)} %get-tuple-element.47, ...), kind=kLoop, calls=%fused_computation.118 | loop fusion | flops 2621440 | bytes 534528 | tf_op jit(solution)/shard_map/and | solution.py:51
  18.5 0.0 copy-done.5
  18.5 0.5 fusion.93
  19.1 0.3 fusion.60
  19.3 0.0 collective-permute-done.1
  19.4 2.8 %collective-permute-start.3 = (bf16[256,4,128]{2,0,1:T(8,128)(2,1)}, bf16[256,4,128]{2,0,1:T(8,128)(2,1)S(1)}, u32[]{:S(2)}, u32[]{:S(2)}) collective-permute-start(bf16[256,4,128]{2,0,1:T(8,128)(2,1)} %collective-permute-done.1), channel_id=1, source_target_pairs={{0,8},{4,12},{8,16},{12,20},{16,24},{20,28},{1,9},{5,13},{9,17},{1... | collective-permute-start | bytes 786440 | tf_op jit(solution)/shard_map/ppermute | solution.py:80
  22.2 0.1 collective-permute-start.2
  22.3 1.4 %fusion.92 = (f32[2,2,256]{2,1,0:T(2,128)S(1)}, bf16[2,2,256,256]{2,3,1,0:T(8,128)(2,1)S(1)}) fusion(bf16[256,2,2,128]{3,0,2,1:T(8,128)(2,1)S(1)} %pad_maximum_fusion.1, bf16[256,4,128]{2,0,1:T(8,128)(2,1)} %collective-permute-done.1, pred[256,256]{0,1:T(8,128)(4,1)S(1)} %get-tuple-element.15), kind=kOutput, calls=%fused_computation.170 | convolution fusion | flops 68418560 | bytes 987136 | tf_op jit(solution)/shard_map/sgrh,kgh->grsk/dot_general | solution.py:43
  23.7 0.0 collective-permute-done
  23.7 1.4 %fusion.94 = (f32[2,2,256]{2,1,0:T(2,128)S(1)}, bf16[2,2,256,256]{2,3,1,0:T(8,128)(2,1)S(1)}) fusion(bf16[256,2,2,128]{3,0,2,1:T(8,128)(2,1)S(1)} %pad_maximum_fusion.1, bf16[256,4,128]{2,0,1:T(8,128)(2,1)} %collective-permute-done, pred[256,256]{0,1:T(8,128)(4,1)S(1)} %get-tuple-element.18), kind=kOutput, calls=%fused_computation.172 | convolution fusion | flops 68418560 | bytes 987136 | tf_op jit(solution)/shard_map/sgrh,kgh->grsk/dot_general | solution.py:43
  25.1 1.2 %convolution_add_fusion.4 = f32[2,2,256,128]{2,3,1,0:T(8,128)S(1)} fusion(f32[2,2,256,128]{2,3,1,0:T(8,128)S(1)} %fusion.60, bf16[2,2,256,256]{2,3,1,0:T(8,128)(2,1)S(1)} %get-tuple-element.34, bf16[256,4,128]{2,0,1:T(8,128)(2,1)} %collective-permute-done), kind=kOutput, calls=%fused_computation.62 | convolution fusion | flops 67239936 | bytes 1703936 | tf_op jit(solution)/shard_map/grsk,kgh->grsh/dot_general | solution.py:54
  26.3 1.2 %convolution_add_fusion.3 = f32[2,2,256,128]{2,3,1,0:T(8,128)S(1)} fusion(f32[2,2,256,128]{2,3,1,0:T(8,128)S(1)} %convolution_add_fusion.4, bf16[2,2,256,256]{2,3,1,0:T(8,128)(2,1)S(1)} %get-tuple-element.30, bf16[256,4,128]{2,0,1:T(8,128)(2,1)} %collective-permute-done.1), kind=kOutput, calls=%fused_computation.61 | convolution fusion | flops 67239936 | bytes 1703936 | tf_op jit(solution)/shard_map/grsk,kgh->grsh/dot_general | solution.py:54
  27.5 0.0 collective-permute-done.3
  27.5 4.3 %collective-permute-start.5 = (bf16[256,4,128]{2,0,1:T(8,128)(2,1)S(1)}, bf16[256,4,128]{2,0,1:T(8,128)(2,1)S(1)}, u32[]{:S(2)}, u32[]{:S(2)}) collective-permute-start(bf16[256,4,128]{2,0,1:T(8,128)(2,1)S(1)} %collective-permute-done.3), channel_id=1, source_target_pairs={{0,8},{4,12},{8,16},{12,20},{16,24},{20,28},{1,9},{5,13},{9,17},{1... | collective-permute-start | bytes 786440 | tf_op jit(solution)/shard_map/ppermute | solution.py:80
  31.8 1.3 %collective-permute-start.4 = (bf16[256,4,128]{2,0,1:T(8,128)(2,1)S(1)}, bf16[256,4,128]{2,0,1:T(8,128)(2,1)S(1)}, u32[]{:S(2)}, u32[]{:S(2)}) collective-permute-start(bf16[256,4,128]{2,0,1:T(8,128)(2,1)S(1)} %collective-permute-done.3), channel_id=1, source_target_pairs={{0,4},{8,12},{16,20},{24,28},{4,0},{12,8},{20,16},{28,24},{1,5},{9... | collective-permute-start | bytes 786440 | tf_op jit(solution)/shard_map/ppermute | solution.py:81
  33.0 0.5 fusion.90
  33.5 0.3 fusion.55
  33.8 0.0 collective-permute-done.2
  33.8 0.5 fusion.91
  34.3 0.3 fusion.46
  34.6 1.2 %collective-permute-done.5 = bf16[256,4,128]{2,0,1:T(8,128)(2,1)S(1)} collective-permute-done((bf16[256,4,128]{2,0,1:T(8,128)(2,1)S(1)}, bf16[256,4,128]{2,0,1:T(8,128)(2,1)S(1)}, u32[]{:S(2)}, u32[]{:S(2)}) %collective-permute-start.5) | collective-permute-done | bytes 262176 | tf_op jit(solution)/shard_map/ppermute | solution.py:80
  35.8 1.6 %collective-permute-start.6 = (bf16[256,4,128]{2,0,1:T(8,128)(2,1)S(1)}, bf16[256,4,128]{2,0,1:T(8,128)(2,1)S(1)}, u32[]{:S(2)}, u32[]{:S(2)}) collective-permute-start(bf16[256,4,128]{2,0,1:T(8,128)(2,1)S(1)} %collective-permute-done.5), channel_id=1, source_target_pairs={{0,4},{8,12},{16,20},{24,28},{4,0},{12,8},{20,16},{28,24},{1,5},{9... | collective-permute-start | bytes 786440 | tf_op jit(solution)/shard_map/ppermute | solution.py:81
  37.4 0.5 fusion.88
  37.9 0.3 fusion.52
  38.2 2.2 %collective-permute-done.4 = bf16[256,4,128]{2,0,1:T(8,128)(2,1)S(1)} collective-permute-done((bf16[256,4,128]{2,0,1:T(8,128)(2,1)S(1)}, bf16[256,4,128]{2,0,1:T(8,128)(2,1)S(1)}, u32[]{:S(2)}, u32[]{:S(2)}) %collective-permute-start.4) | collective-permute-done | bytes 262176 | tf_op jit(solution)/shard_map/ppermute | solution.py:81
  40.4 0.5 fusion.89
  40.9 0.3 fusion.45
  41.2 2.7 %collective-permute-done.6 = bf16[256,4,128]{2,0,1:T(8,128)(2,1)S(1)} collective-permute-done((bf16[256,4,128]{2,0,1:T(8,128)(2,1)S(1)}, bf16[256,4,128]{2,0,1:T(8,128)(2,1)S(1)}, u32[]{:S(2)}, u32[]{:S(2)}) %collective-permute-start.6) | collective-permute-done | bytes 262176 | tf_op jit(solution)/shard_map/ppermute | solution.py:81
  43.8 0.5 fusion.87
  44.3 0.3 fusion.47
  44.6 0.8 %copy.27 = bf16[256,4,128]{2,0,1:T(8,128)(2,1)} copy(bf16[256,4,128]{0,2,1:T(8,128)(2,1)S(1)} %bitcast.171) | data formatting | bytes 524288 | tf_op jit(solution)/shard_map/reshape | solution.py:152
  45.5 1.5 %collective-permute-start.7 = (bf16[256,4,128]{2,0,1:T(8,128)(2,1)}, bf16[256,4,128]{2,0,1:T(8,128)(2,1)S(1)}, u32[]{:S(2)}, u32[]{:S(2)}) collective-permute-start(bf16[256,4,128]{2,0,1:T(8,128)(2,1)} %copy.27), channel_id=1, source_target_pairs={{0,2},{1,3},{2,0},{3,1},{4,6},{5,7},{6,4},{7,5},{8,10},{9,11},{10,... | collective-permute-start | bytes 786440 | tf_op jit(solution)/shard_map/ppermute | solution.py:94
  46.9 5.1 %collective-permute-done.7 = bf16[256,4,128]{2,0,1:T(8,128)(2,1)S(1)} collective-permute-done((bf16[256,4,128]{2,0,1:T(8,128)(2,1)}, bf16[256,4,128]{2,0,1:T(8,128)(2,1)S(1)}, u32[]{:S(2)}, u32[]{:S(2)}) %collective-permute-start.7) | collective-permute-done | bytes 262176 | tf_op jit(solution)/shard_map/ppermute | solution.py:94
  52.0 0.7 %copy-done.1 = bf16[256,4,128]{2,0,1:T(8,128)(2,1)} copy-done((bf16[256,4,128]{2,0,1:T(8,128)(2,1)}, bf16[256,4,128]{2,0,1:T(8,128)(2,1)S(1)}, u32[]{:S(2)}) %copy-start.1) | copy-done | bytes 262168
  52.8 1.8 %pad_maximum_fusion = bf16[256,8,128]{2,0,1:T(8,128)(2,1)} fusion(bf16[256,4,128]{2,0,1:T(8,128)(2,1)S(1)} %collective-permute-done.7, bf16[256,4,128]{2,0,1:T(8,128)(2,1)} %copy.27), kind=kLoop, calls=%fused_computation.69 | loop fusion | flops 262144 | bytes 1048576 | tf_op jit(solution)/shard_map/concatenate | solution.py:93
  54.6 0.0 collective-permute-start.8
  54.6 0.1 constant_dynamic-slice_fusion
  54.6 0.4 fusion.95
  55.0 1.8 %collective-permute-done.8 = bf16[256,8,128]{2,0,1:T(8,128)(2,1)} collective-permute-done((bf16[256,8,128]{2,0,1:T(8,128)(2,1)}, bf16[256,8,128]{2,0,1:T(8,128)(2,1)}, u32[]{:S(2)}, u32[]{:S(2)}) %collective-permute-start.8) | collective-permute-done | bytes 524320 | tf_op jit(solution)/shard_map/ppermute | solution.py:94
  56.8 1.3 %convolution_bitcast_fusion = f32[256,768]{1,0:T(8,128)S(1)} fusion(bf16[256,8,128]{2,0,1:T(8,128)(2,1)} %collective-permute-done.8, bf16[16,128,768]{2,1,0:T(8,128)(2,1)S(1)} %copy-done, s32[]{:T(128)S(6)} %select_n.61), kind=kOutput, calls=%fused_computation.48 | convolution fusion | flops 201326592 | bytes 2097156 | tf_op jit(solution)/shard_map/dot_general | solution.py:162
  58.1 0.0 copy-start.8
  58.1 0.0 copy-start.6
  58.1 1.4 %convolution_bitcast_fusion.1 = f32[256,768]{1,0:T(8,128)S(1)} fusion(bf16[256,8,128]{2,0,1:T(8,128)(2,1)} %collective-permute-done.8, bf16[16,128,768]{2,1,0:T(8,128)(2,1)S(1)} %copy-done, s32[]{:T(128)S(6)} %select_n.60), kind=kOutput, calls=%fused_computation.49 | convolution fusion | flops 201326592 | bytes 2097156 | tf_op jit(solution)/shard_map/dot_general | solution.py:162
  59.5 0.5 multiply_reduce_fusion
  60.0 1.5 %collective-permute-start.9 = (f32[256]{0:T(256)S(1)}, f32[256]{0:T(256)S(1)}, u32[]{:S(2)}, u32[]{:S(2)}) collective-permute-start(f32[256]{0:T(256)S(1)} %get-tuple-element.35), channel_id=1, source_target_pairs={{0,2},{1,3},{2,0},{3,1},{4,6},{5,7},{6,4},{7,5},{8,10},{9,11},{10,... | collective-permute-start | bytes 3080 | tf_op jit(solution)/shard_map/ppermute | solution.py:107
  61.6 2.1 %collective-permute-done.9 = f32[256]{0:T(256)S(1)} collective-permute-done((f32[256]{0:T(256)S(1)}, f32[256]{0:T(256)S(1)}, u32[]{:S(2)}, u32[]{:S(2)}) %collective-permute-start.9) | collective-permute-done | bytes 1056 | tf_op jit(solution)/shard_map/ppermute | solution.py:107
  63.7 0.0 collective-permute-start.10
  63.7 1.1 %collective-permute-done.10 = f32[256]{0:T(256)S(1)} collective-permute-done((f32[256]{0:T(256)S(1)}, f32[256]{0:T(256)S(1)}, u32[]{:S(2)}, u32[]{:S(2)}) %collective-permute-start.10) | collective-permute-done | bytes 1056 | tf_op jit(solution)/shard_map/ppermute | solution.py:107
  64.8 0.9 %add_convert_fusion = bf16[256,768]{1,0:T(8,128)(2,1)} fusion(f32[256,768]{1,0:T(8,128)S(1)} %get-tuple-element.36, bf16[256,768]{1,0:T(8,128)(2,1)S(1)} %copy-done.6, f32[768]{0:T(1024)S(1)} %convert_element_type.69, f32[256]{0:T(256)S(1)} %add_rsqrt_fusion), kind=kLoop, calls=%fused_computation.64 | loop fusion | flops 983040 | bytes 1576960 | tf_op jit(solution)/shard_map/convert_element_type | solution.py:182
  (37 shorter events, 0.2 us)
Async XLA Ops:
  0.0 54.6 %copy-start = (bf16[16,128,768]{2,1,0:T(8,128)(2,1)S(1)}, bf16[16,128,768]{2,1,0:T(8,128)(2,1)}, u32[]{:S(2)}) copy-start(bf16[16,128,768]{2,1,0:T(8,128)(2,1)} %param.10) | copy-start | bytes 9437188
  2.7 0.8 %copy-start.4 = (bf16[256,2,64]{2,0,1:T(8,128)(2,1)}, bf16[256,2,64]{2,0,1:T(8,128)(2,1)S(1)}, u32[]{:S(2)}) copy-start(bf16[256,2,64]{2,0,1:T(8,128)(2,1)S(1)} %get-tuple-element.8) | copy-start | bytes 196612
  3.6 15.8 %collective-permute-start.1 = (bf16[256,4,128]{2,0,1:T(8,128)(2,1)}, bf16[256,4,128]{2,0,1:T(8,128)(2,1)}, u32[]{:S(2)}, u32[]{:S(2)}) collective-permute-start(bf16[256,4,128]{2,0,1:T(8,128)(2,1)} %pad_maximum_fusion.2), channel_id=1, source_target_pairs={{0,8},{4,12},{8,16},{12,20},{16,24},{20,28},{1,9},{5,13},{9,17},{1... | collective-permute-start | bytes 786440 | tf_op jit(solution)/shard_map/ppermute | solution.py:80
  9.2 14.5 %collective-permute-start = (bf16[256,4,128]{2,0,1:T(8,128)(2,1)}, bf16[256,4,128]{2,0,1:T(8,128)(2,1)}, u32[]{:S(2)}, u32[]{:S(2)}) collective-permute-start(bf16[256,4,128]{2,0,1:T(8,128)(2,1)} %pad_maximum_fusion.2), channel_id=1, source_target_pairs={{0,4},{8,12},{16,20},{24,28},{1,5},{9,13},{17,21},{25,29},{2,6},{1... | collective-permute-start | bytes 786440 | tf_op jit(solution)/shard_map/ppermute | solution.py:81
  15.7 1.9 %copy-start.7 = (s32[256]{0:T(256)S(1)}, s32[256]{0:T(256)}, u32[]{:S(2)}) copy-start(s32[256]{0:T(256)} %get-tuple-element.50) | copy-start | bytes 3076
  15.7 1.9 %copy-start.9 = (pred[256]{0:T(512)(128)(4,1)S(1)}, pred[256]{0:T(512)(128)(4,1)}, u32[]{:S(2)}) copy-start(pred[256]{0:T(512)(128)(4,1)} %get-tuple-element.39) | copy-start | bytes 772
  15.7 1.9 %copy-start.10 = (pred[256]{0:T(512)(128)(4,1)S(1)}, pred[256]{0:T(512)(128)(4,1)}, u32[]{:S(2)}) copy-start(pred[256]{0:T(512)(128)(4,1)} %get-tuple-element.40) | copy-start | bytes 772
  15.7 1.9 %copy-start.11 = (pred[256]{0:T(512)(128)(4,1)S(1)}, pred[256]{0:T(512)(128)(4,1)}, u32[]{:S(2)}) copy-start(pred[256]{0:T(512)(128)(4,1)} %get-tuple-element.41) | copy-start | bytes 772
  15.7 1.9 %copy-start.12 = (pred[256]{0:T(512)(128)(4,1)S(1)}, pred[256]{0:T(512)(128)(4,1)}, u32[]{:S(2)}) copy-start(pred[256]{0:T(512)(128)(4,1)} %get-tuple-element.42) | copy-start | bytes 772
  15.7 1.9 %copy-start.13 = (pred[256]{0:T(512)(128)(4,1)S(1)}, pred[256]{0:T(512)(128)(4,1)}, u32[]{:S(2)}) copy-start(pred[256]{0:T(512)(128)(4,1)} %get-tuple-element.43) | copy-start | bytes 772
  15.7 1.9 %copy-start.14 = (pred[256]{0:T(512)(128)(4,1)S(1)}, pred[256]{0:T(512)(128)(4,1)}, u32[]{:S(2)}) copy-start(pred[256]{0:T(512)(128)(4,1)} %get-tuple-element.44) | copy-start | bytes 772
  15.7 2.8 %copy-start.5 = (bf16[256,2,64]{2,0,1:T(8,128)(2,1)S(1)}, bf16[256,2,64]{2,0,1:T(8,128)(2,1)}, u32[]{:S(2)}) copy-start(bf16[256,2,64]{2,0,1:T(8,128)(2,1)} %copy-done.4) | copy-start | bytes 196612
  16.8 2.3 %copy-start.3 = (bf16[256,2,128]{2,1,0:T(2,128)(2,1)S(1)}, bf16[256,2,128]{2,1,0:T(2,128)(2,1)}, u32[]{:S(2)}) copy-start(bf16[256,2,128]{2,1,0:T(2,128)(2,1)} %param.8) | copy-start | bytes 393220
  19.4 8.1 %collective-permute-start.3 = (bf16[256,4,128]{2,0,1:T(8,128)(2,1)}, bf16[256,4,128]{2,0,1:T(8,128)(2,1)S(1)}, u32[]{:S(2)}, u32[]{:S(2)}) collective-permute-start(bf16[256,4,128]{2,0,1:T(8,128)(2,1)} %collective-permute-done.1), channel_id=1, source_target_pairs={{0,8},{4,12},{8,16},{12,20},{16,24},{20,28},{1,9},{5,13},{9,17},{1... | collective-permute-start | bytes 786440 | tf_op jit(solution)/shard_map/ppermute | solution.py:80
  22.2 11.6 %collective-permute-start.2 = (bf16[256,4,128]{2,0,1:T(8,128)(2,1)}, bf16[256,4,128]{2,0,1:T(8,128)(2,1)S(1)}, u32[]{:S(2)}, u32[]{:S(2)}) collective-permute-start(bf16[256,4,128]{2,0,1:T(8,128)(2,1)} %collective-permute-done.1), channel_id=1, source_target_pairs={{0,4},{8,12},{16,20},{24,28},{4,0},{12,8},{20,16},{28,24},{1,5},{9... | collective-permute-start | bytes 786440 | tf_op jit(solution)/shard_map/ppermute | solution.py:81
  27.5 8.3 %collective-permute-start.5 = (bf16[256,4,128]{2,0,1:T(8,128)(2,1)S(1)}, bf16[256,4,128]{2,0,1:T(8,128)(2,1)S(1)}, u32[]{:S(2)}, u32[]{:S(2)}) collective-permute-start(bf16[256,4,128]{2,0,1:T(8,128)(2,1)S(1)} %collective-permute-done.3), channel_id=1, source_target_pairs={{0,8},{4,12},{8,16},{12,20},{16,24},{20,28},{1,9},{5,13},{9,17},{1... | collective-permute-start | bytes 786440 | tf_op jit(solution)/shard_map/ppermute | solution.py:80
  31.8 8.6 %collective-permute-start.4 = (bf16[256,4,128]{2,0,1:T(8,128)(2,1)S(1)}, bf16[256,4,128]{2,0,1:T(8,128)(2,1)S(1)}, u32[]{:S(2)}, u32[]{:S(2)}) collective-permute-start(bf16[256,4,128]{2,0,1:T(8,128)(2,1)S(1)} %collective-permute-done.3), channel_id=1, source_target_pairs={{0,4},{8,12},{16,20},{24,28},{4,0},{12,8},{20,16},{28,24},{1,5},{9... | collective-permute-start | bytes 786440 | tf_op jit(solution)/shard_map/ppermute | solution.py:81
  35.8 8.0 %collective-permute-start.6 = (bf16[256,4,128]{2,0,1:T(8,128)(2,1)S(1)}, bf16[256,4,128]{2,0,1:T(8,128)(2,1)S(1)}, u32[]{:S(2)}, u32[]{:S(2)}) collective-permute-start(bf16[256,4,128]{2,0,1:T(8,128)(2,1)S(1)} %collective-permute-done.5), channel_id=1, source_target_pairs={{0,4},{8,12},{16,20},{24,28},{4,0},{12,8},{20,16},{28,24},{1,5},{9... | collective-permute-start | bytes 786440 | tf_op jit(solution)/shard_map/ppermute | solution.py:81
  45.5 6.6 %collective-permute-start.7 = (bf16[256,4,128]{2,0,1:T(8,128)(2,1)}, bf16[256,4,128]{2,0,1:T(8,128)(2,1)S(1)}, u32[]{:S(2)}, u32[]{:S(2)}) collective-permute-start(bf16[256,4,128]{2,0,1:T(8,128)(2,1)} %copy.27), channel_id=1, source_target_pairs={{0,2},{1,3},{2,0},{3,1},{4,6},{5,7},{6,4},{7,5},{8,10},{9,11},{10,... | collective-permute-start | bytes 786440 | tf_op jit(solution)/shard_map/ppermute | solution.py:94
  52.0 0.7 %copy-start.1 = (bf16[256,4,128]{2,0,1:T(8,128)(2,1)}, bf16[256,4,128]{2,0,1:T(8,128)(2,1)S(1)}, u32[]{:S(2)}) copy-start(bf16[256,4,128]{2,0,1:T(8,128)(2,1)S(1)} %collective-permute-done.7) | copy-start | bytes 786436
  54.6 2.3 %collective-permute-start.8 = (bf16[256,8,128]{2,0,1:T(8,128)(2,1)}, bf16[256,8,128]{2,0,1:T(8,128)(2,1)}, u32[]{:S(2)}, u32[]{:S(2)}) collective-permute-start(bf16[256,8,128]{2,0,1:T(8,128)(2,1)} %pad_maximum_fusion), channel_id=1, source_target_pairs={{0,1},{1,0},{2,3},{3,2},{4,5},{5,4},{6,7},{7,6},{8,9},{9,8},{10,11... | collective-permute-start | bytes 1572872 | tf_op jit(solution)/shard_map/ppermute | solution.py:94
  54.6 4.9 %copy-start.2 = (bf16[256,4,128]{2,0,1:T(8,128)(2,1)S(1)}, bf16[256,4,128]{2,0,1:T(8,128)(2,1)}, u32[]{:S(2)}) copy-start(bf16[256,4,128]{2,0,1:T(8,128)(2,1)} %copy-done.1) | copy-start | bytes 786436
  58.1 5.5 %copy-start.8 = (bf16[768]{0:T(1024)(128)(2,1)S(1)}, bf16[768]{0:T(1024)(128)(2,1)}, u32[]{:S(2)}) copy-start(bf16[768]{0:T(1024)(128)(2,1)} %param.11) | copy-start | bytes 4612
  58.1 6.7 %copy-start.6 = (bf16[256,768]{1,0:T(8,128)(2,1)S(1)}, bf16[256,768]{1,0:T(8,128)(2,1)}, u32[]{:S(2)}) copy-start(bf16[256,768]{1,0:T(8,128)(2,1)} %param.9) | copy-start | bytes 1179652
  60.0 3.6 %collective-permute-start.9 = (f32[256]{0:T(256)S(1)}, f32[256]{0:T(256)S(1)}, u32[]{:S(2)}, u32[]{:S(2)}) collective-permute-start(f32[256]{0:T(256)S(1)} %get-tuple-element.35), channel_id=1, source_target_pairs={{0,2},{1,3},{2,0},{3,1},{4,6},{5,7},{6,4},{7,5},{8,10},{9,11},{10,... | collective-permute-start | bytes 3080 | tf_op jit(solution)/shard_map/ppermute | solution.py:107
  63.7 1.1 %collective-permute-start.10 = (f32[256]{0:T(256)S(1)}, f32[256]{0:T(256)S(1)}, u32[]{:S(2)}, u32[]{:S(2)}) collective-permute-start(f32[256]{0:T(256)S(1)} %add.360), channel_id=1, source_target_pairs={{0,1},{1,0},{2,3},{3,2},{4,5},{5,4},{6,7},{7,6},{8,9},{9,8},{10,11... | collective-permute-start | bytes 3080 | tf_op jit(solution)/shard_map/ppermute | solution.py:107

commit v5 on v4

--- a/solution.py
+++ b/solution.py
@@ -36,7 +36,7 @@
     )
 
 
-def attend_block(state, key_block, value_block, source, rotary_queries, device_index):
+def attend_block(state, key_block, value_block, source, rotary_queries, device_index, whole=False):
     numerators, denominators = state
     rows = key_block.shape[0]
     scores = (
@@ -44,12 +44,16 @@
         * query_scale
     )
     capped = softcap_value * jnp.tanh(scores / softcap_value)
-    offsets = jnp.arange(rows, dtype=jnp.int32)
-    query_pos = device_index * rows + offsets
-    key_pos = source * rows + offsets
-    distance = query_pos[:, None] - key_pos[None, :]
-    allowed = (distance >= 0) & (distance < WINDOW_TOKENS) & (key_pos[None, :] >= 0)
-    weights = jnp.where(allowed[None, None], jnp.exp(capped), 0.0)
+    if whole:
+        allowed = (source >= 0) & (source < device_index)
+        weights = jnp.where(allowed, jnp.exp(capped), 0.0)
+    else:
+        offsets = jnp.arange(rows, dtype=jnp.int32)
+        query_pos = device_index * rows + offsets
+        key_pos = source * rows + offsets
+        distance = query_pos[:, None] - key_pos[None, :]
+        allowed = (distance >= 0) & (distance < WINDOW_TOKENS) & (key_pos[None, :] >= 0)
+        weights = jnp.where(allowed[None, None], jnp.exp(capped), 0.0)
     denominators = denominators + jnp.sum(weights, axis=-1)
     numerators = numerators + jnp.einsum(
         "grsk,kgh->grsh",
@@ -69,9 +73,12 @@
     plane = device_index // 2
     side = device_index % 2
 
+    rows = key_block.shape[0]
+    whole = cycle_size * rows - 1 < WINDOW_TOKENS
+
     def attend_stacked(state, stacked, source):
         return attend_block(
-            state, stacked[:, :kv_heads], stacked[:, kv_heads:], source, rotary_queries, device_index
+            state, stacked[:, :kv_heads], stacked[:, kv_heads:], source, rotary_queries, device_index, whole
         )
 
     line = jnp.concatenate([key_block, value_block], axis=1)
@@ -90,13 +97,8 @@
     pieces = [(piece, 0)]
     bit = count // 2
     while bit >= 1:
-        sent = jnp.concatenate([held for held, unused in pieces], axis=1)
-        arrived = lax.ppermute(sent, "tp", [(source, source ^ bit) for source in range(count)])
-        width = piece.shape[1]
-        pieces = pieces + [
-            (arrived[:, slot * width : (slot + 1) * width], offset ^ bit)
-            for slot, (unused, offset) in enumerate(pieces)
-        ]
+        pairs = [(source, source ^ bit) for source in range(count)]
+        pieces = pieces + [(lax.ppermute(held, "tp", pairs), offset ^ bit) for held, offset in pieces]
         bit //= 2
     return pieces
 

time: 66.1 us -> 61 us (0.923)
  other arithmetic: 10.1 us -> 5.23 us
    concatenate x1 -> x0, other arithmetic: 1.79 us -> none  [exchanged(): sent = jnp.concatenate([held for held, unused in pieces], axis=1)]
    ge x4 -> x1, other arithmetic: 1.78 us -> 0.01 us  [attend_block(): key_pos[None, :] >= 0]
    dynamic_slice x1, local copies, waits for them, and re-layouts: 0.05 us -> 0.94 us  [local(): lax.dynamic_slice_in_dim(out_weight, owner * q_heads, q_heads, 0)]
    dot_general x4, matrix products: 3.56 us -> 2.72 us  [local(): jnp.dot(held.reshape(rows, q_heads * head_size), weight_rows.reshape(q_he...]
    dot_general x8, matrix products: 3.95 us -> 4.75 us  [attend_block(): jnp.einsum('grsk,kgh->grsh', weights.astype(jnp.bfloat16), value_block, p...]
    unnamed x31 -> x11, local copies, waits for them, and re-layouts: 1.86 us -> 1.1 us
    and x1, other arithmetic: 0.86 us -> 0.14 us  [attend_block(): (distance >= 0) & (distance < WINDOW_TOKENS) & (key_pos[None, :] >= 0)]
    ppermute x2 -> x3, waiting for transfers between devices: 6.89 us -> 6.69 us  [exchanged(): lax.ppermute(held, 'tp', pairs)]
  transfers between devices with their start and end apart: 11 -> 12, of which waited for: 7 -> 8; matrix products, arithmetic and copies ran while one was open for 22% -> 24% of each run, Pallas kernels for 0% -> 0%
where the time goes in v5:
time: 61 us; the launch traced here: 60.7 us
  starting transfers between devices  22.8 us (37%)
  waiting for transfers between devices  16.2 us (27%)
  matrix products  13.2 us (22%)
  other arithmetic  5.23 us (9%)
  local copies, waits for them, and re-layouts  2.96 us (5%)
    ppermute x3, starting transfers between devices, along_lines(): arrived = lax.ppermute(line, 'ctx', forward)  12.8 us
    ppermute x4, starting transfers between devices, along_lines(): crossed = lax.ppermute(line, 'ctx', up if step == 1 else up + down)  6.98 us
    ppermute x3, waiting for transfers between devices, exchanged(): lax.ppermute(held, 'tp', pairs)  6.69 us
    dot_general x8, matrix products, attend_block(): jnp.einsum('sgrh,kgh->grsk', rotary_queries, key_block, preferred_element...  5.72 us
    ppermute x4, waiting for transfers between devices, along_lines(): crossed = lax.ppermute(line, 'ctx', up if step == 1 else up + down)  4.95 us
    dot_general x8, matrix products, attend_block(): jnp.einsum('grsk,kgh->grsh', weights.astype(jnp.bfloat16), value_block, p...  4.75 us
    ppermute x2, waiting for transfers between devices, summed(): lax.ppermute(partial, 'tp', [(source, source ^ bit) for source in range(c...  3.22 us
    dot_general x4, matrix products, local(): jnp.dot(held.reshape(rows, q_heads * head_size), weight_rows.reshape(q_he...  2.72 us
  transfers between devices with their start and end apart: 12, of which 8 were waited for; matrix products, arithmetic and copies ran while one was open for 24% of the time, Pallas kernels for 0%

profile of v5, /device:TPU:0, one launch (start us, length us, event | category | flops | bytes accessed | tf_op | source)
XLA Modules:
  0.0 60.7 jit_solution(9010584870189123267)
XLA Ops:
  0.0 0.0 copy-start
  0.0 1.1 %copy.12 = bf16[256,2,128]{2,0,1:T(8,128)(2,1)S(1)} copy(bf16[256,2,128]{2,1,0:T(2,128)(2,1)} %param.8) | data formatting | bytes 262144 | tf_op args[2]
  1.1 0.9 %copy_convert_fusion = f32[256,2,128]{2,0,1:T(8,128)S(1)} fusion(bf16[256,2,128]{2,1,0:T(2,128)(2,1)} %param.7), kind=kLoop, calls=%fused_computation.110 | loop fusion | flops 65536 | bytes 393216 | tf_op jit(solution)/shard_map/convert_element_type | solution.py:125
  2.0 0.5 multiply_cosine_fusion
  2.6 0.2 subtract_convert_fusion.1
  2.7 0.8 %pad_maximum_fusion.1 = bf16[256,4,128]{2,0,1:T(8,128)(2,1)} fusion(bf16[256,2,128]{2,0,1:T(8,128)(2,1)S(1)} %copy.12, bf16[256,2,64]{2,0,1:T(8,128)(2,1)S(1)} %get-tuple-element.8, bf16[256,2,64]{2,0,1:T(8,128)(2,1)S(1)} %get-tuple-element.7), kind=kLoop, calls=%fused_computation.85 | loop fusion | flops 786432 | bytes 524288 | tf_op jit(solution)/shard_map/concatenate | solution.py:84
  3.6 5.6 %collective-permute-start.1 = (bf16[256,4,128]{2,0,1:T(8,128)(2,1)}, bf16[256,4,128]{2,0,1:T(8,128)(2,1)}, u32[]{:S(2)}, u32[]{:S(2)}) collective-permute-start(bf16[256,4,128]{2,0,1:T(8,128)(2,1)} %pad_maximum_fusion.1), channel_id=1, source_target_pairs={{0,8},{4,12},{8,16},{12,20},{16,24},{20,28},{1,9},{5,13},{9,17},{1... | collective-permute-start | bytes 786440 | tf_op jit(solution)/shard_map/ppermute | solution.py:87
  9.2 4.1 %collective-permute-start = (bf16[256,4,128]{2,0,1:T(8,128)(2,1)}, bf16[256,4,128]{2,0,1:T(8,128)(2,1)}, u32[]{:S(2)}, u32[]{:S(2)}) collective-permute-start(bf16[256,4,128]{2,0,1:T(8,128)(2,1)} %pad_maximum_fusion.1), channel_id=1, source_target_pairs={{0,4},{8,12},{16,20},{24,28},{1,5},{9,13},{17,21},{25,29},{2,6},{1... | collective-permute-start | bytes 786440 | tf_op jit(solution)/shard_map/ppermute | solution.py:88
  13.3 1.0 %convert_element_type.59 = f32[256,4,128]{2,1,0:T(4,128)S(1)} convert(bf16[256,4,128]{2,1,0:T(4,128)(2,1)} %param.6) | non-fusion elementwise | flops 131072 | bytes 786432 | tf_op jit(solution)/shard_map/convert_element_type | solution.py:123
  14.3 0.0 copy-start.2
  14.4 0.5 subtract_convert_fusion
  15.0 0.1 pad_maximum_fusion
  15.1 0.1 fusion.63
  15.3 0.5 fusion.79
  15.8 0.0 copy-done.2
  15.8 1.1 %fusion.60 = f32[2,2,256,128]{2,3,1,0:T(8,128)} fusion(bf16[2,2,256,256]{2,3,1,0:T(8,128)(2,1)S(1)} %get-tuple-element.24, bf16[256,2,128,1]{2,1,0,3:T(2,128)(2,1)S(1)} %bitcast.161), kind=kOutput, calls=%fused_computation.78 | convolution fusion | flops 67108864 | bytes 1179648 | tf_op jit(solution)/shard_map/grsk,kgh->grsh/dot_general | solution.py:58
  16.9 0.0 copy-done
  16.9 0.9 %constant_dynamic-slice_fusion = bf16[4,128,768]{2,1,0:T(8,128)(2,1)} fusion(bf16[16,128,768]{2,1,0:T(8,128)(2,1)S(1)} %copy-done, s32[]{:T(128)S(6)} %select_n.88), kind=kLoop, calls=%fused_computation.116 | loop fusion | bytes 1572868 | tf_op jit(solution)/shard_map/dynamic_slice | solution.py:163
  17.8 0.0 collective-permute-done.1
  17.8 2.9 %collective-permute-start.3 = (bf16[256,4,128]{2,0,1:T(8,128)(2,1)}, bf16[256,4,128]{2,0,1:T(8,128)(2,1)S(1)}, u32[]{:S(2)}, u32[]{:S(2)}) collective-permute-start(bf16[256,4,128]{2,0,1:T(8,128)(2,1)} %collective-permute-done.1), channel_id=1, source_target_pairs={{0,8},{4,12},{8,16},{12,20},{16,24},{20,28},{1,9},{5,13},{9,17},{1... | collective-permute-start | bytes 786440 | tf_op jit(solution)/shard_map/ppermute | solution.py:87
  20.8 0.1 collective-permute-start.2
  20.8 1.4 %fusion.78 = (f32[2,2,256]{2,1,0:T(2,128)S(1)}, bf16[2,2,256,256]{2,3,1,0:T(8,128)(2,1)S(1)}) fusion(bf16[256,2,2,128]{3,0,2,1:T(8,128)(2,1)S(1)} %pad_maximum_fusion, bf16[256,4,128]{2,0,1:T(8,128)(2,1)} %collective-permute-done.1, pred[]{:T(512)S(6)} %and.58), kind=kOutput, calls=%fused_computation.127 | convolution fusion | flops 68418560 | bytes 921601 | tf_op jit(solution)/shard_map/sgrh,kgh->grsk/dot_general | solution.py:43
  22.2 0.0 collective-permute-done
  22.3 1.4 %fusion.80 = (f32[2,2,256]{2,1,0:T(2,128)S(1)}, bf16[2,2,256,256]{2,3,1,0:T(8,128)(2,1)S(1)}) fusion(bf16[256,2,2,128]{3,0,2,1:T(8,128)(2,1)S(1)} %pad_maximum_fusion, bf16[256,4,128]{2,0,1:T(8,128)(2,1)} %collective-permute-done, pred[]{:T(512)S(6)} %and.57), kind=kOutput, calls=%fused_computation.129 | convolution fusion | flops 68418560 | bytes 921601 | tf_op jit(solution)/shard_map/sgrh,kgh->grsk/dot_general | solution.py:43
  23.6 0.0 copy-done.1
  23.7 1.2 %convolution_add_fusion.4 = f32[2,2,256,128]{2,3,1,0:T(8,128)S(1)} fusion(f32[2,2,256,128]{2,3,1,0:T(8,128)S(1)} %copy-done.1, bf16[2,2,256,256]{2,3,1,0:T(8,128)(2,1)S(1)} %get-tuple-element.26, bf16[256,4,128]{2,0,1:T(8,128)(2,1)} %collective-permute-done), kind=kOutput, calls=%fused_computation.62 | convolution fusion | flops 67239936 | bytes 1703936 | tf_op jit(solution)/shard_map/grsk,kgh->grsh/dot_general | solution.py:58
  24.8 1.2 %convolution_add_fusion.3 = f32[2,2,256,128]{2,3,1,0:T(8,128)S(1)} fusion(f32[2,2,256,128]{2,3,1,0:T(8,128)S(1)} %convolution_add_fusion.4, bf16[2,2,256,256]{2,3,1,0:T(8,128)(2,1)S(1)} %get-tuple-element.22, bf16[256,4,128]{2,0,1:T(8,128)(2,1)} %collective-permute-done.1), kind=kOutput, calls=%fused_computation.61 | convolution fusion | flops 67239936 | bytes 1703936 | tf_op jit(solution)/shard_map/grsk,kgh->grsh/dot_general | solution.py:58
  26.0 0.1 collective-permute-done.3
  26.1 4.3 %collective-permute-start.5 = (bf16[256,4,128]{2,0,1:T(8,128)(2,1)S(1)}, bf16[256,4,128]{2,0,1:T(8,128)(2,1)S(1)}, u32[]{:S(2)}, u32[]{:S(2)}) collective-permute-start(bf16[256,4,128]{2,0,1:T(8,128)(2,1)S(1)} %collective-permute-done.3), channel_id=1, source_target_pairs={{0,8},{4,12},{8,16},{12,20},{16,24},{20,28},{1,9},{5,13},{9,17},{1... | collective-permute-start | bytes 786440 | tf_op jit(solution)/shard_map/ppermute | solution.py:87
  30.4 1.2 %collective-permute-start.4 = (bf16[256,4,128]{2,0,1:T(8,128)(2,1)S(1)}, bf16[256,4,128]{2,0,1:T(8,128)(2,1)S(1)}, u32[]{:S(2)}, u32[]{:S(2)}) collective-permute-start(bf16[256,4,128]{2,0,1:T(8,128)(2,1)S(1)} %collective-permute-done.3), channel_id=1, source_target_pairs={{0,4},{8,12},{16,20},{24,28},{4,0},{12,8},{20,16},{28,24},{1,5},{9... | collective-permute-start | bytes 786440 | tf_op jit(solution)/shard_map/ppermute | solution.py:88
  31.6 0.5 fusion.76
  32.1 0.3 fusion.55
  32.4 0.0 collective-permute-done.2
  32.4 0.5 fusion.77
  32.9 0.3 fusion.46
  33.1 1.3 %collective-permute-done.5 = bf16[256,4,128]{2,0,1:T(8,128)(2,1)S(1)} collective-permute-done((bf16[256,4,128]{2,0,1:T(8,128)(2,1)S(1)}, bf16[256,4,128]{2,0,1:T(8,128)(2,1)S(1)}, u32[]{:S(2)}, u32[]{:S(2)}) %collective-permute-start.5) | collective-permute-done | bytes 262176 | tf_op jit(solution)/shard_map/ppermute | solution.py:87
  34.4 1.5 %collective-permute-start.6 = (bf16[256,4,128]{2,0,1:T(8,128)(2,1)S(1)}, bf16[256,4,128]{2,0,1:T(8,128)(2,1)S(1)}, u32[]{:S(2)}, u32[]{:S(2)}) collective-permute-start(bf16[256,4,128]{2,0,1:T(8,128)(2,1)S(1)} %collective-permute-done.5), channel_id=1, source_target_pairs={{0,4},{8,12},{16,20},{24,28},{4,0},{12,8},{20,16},{28,24},{1,5},{9... | collective-permute-start | bytes 786440 | tf_op jit(solution)/shard_map/ppermute | solution.py:88
  36.0 0.5 fusion.74
  36.4 0.3 fusion.52
  36.7 2.3 %collective-permute-done.4 = bf16[256,4,128]{2,0,1:T(8,128)(2,1)S(1)} collective-permute-done((bf16[256,4,128]{2,0,1:T(8,128)(2,1)S(1)}, bf16[256,4,128]{2,0,1:T(8,128)(2,1)S(1)}, u32[]{:S(2)}, u32[]{:S(2)}) %collective-permute-start.4) | collective-permute-done | bytes 262176 | tf_op jit(solution)/shard_map/ppermute | solution.py:88
  39.0 0.5 fusion.75
  39.5 0.3 fusion.45
  39.8 2.6 %collective-permute-done.6 = bf16[256,4,128]{2,0,1:T(8,128)(2,1)S(1)} collective-permute-done((bf16[256,4,128]{2,0,1:T(8,128)(2,1)S(1)}, bf16[256,4,128]{2,0,1:T(8,128)(2,1)S(1)}, u32[]{:S(2)}, u32[]{:S(2)}) %collective-permute-start.6) | collective-permute-done | bytes 262176 | tf_op jit(solution)/shard_map/ppermute | solution.py:88
  42.4 0.5 fusion.73
  42.9 0.3 fusion.47
  43.2 0.8 %copy.27 = bf16[256,4,128]{2,0,1:T(8,128)(2,1)} copy(bf16[256,4,128]{0,2,1:T(8,128)(2,1)S(1)} %bitcast.157) | data formatting | bytes 524288 | tf_op jit(solution)/shard_map/reshape | solution.py:154
  44.0 0.0 collective-permute-start.8
  44.0 1.5 %collective-permute-start.7 = (bf16[256,4,128]{2,0,1:T(8,128)(2,1)}, bf16[256,4,128]{2,0,1:T(8,128)(2,1)S(1)}, u32[]{:S(2)}, u32[]{:S(2)}) collective-permute-start(bf16[256,4,128]{2,0,1:T(8,128)(2,1)} %copy.27), channel_id=1, source_target_pairs={{0,2},{1,3},{2,0},{3,1},{4,6},{5,7},{6,4},{7,5},{8,10},{9,11},{10,... | collective-permute-start | bytes 786440 | tf_op jit(solution)/shard_map/ppermute | solution.py:101
  45.5 1.5 %fusion.81 = f32[256,768]{1,0:T(8,128)S(1)} fusion(bf16[256,512]{0,1:T(8,128)(2,1)S(1)} %bitcast.158, bf16[512,768]{1,0:T(8,128)(2,1)} %bitcast.156), kind=kOutput, calls=%fused_computation.130 | convolution fusion | flops 201326592 | bytes 1835008 | tf_op jit(solution)/shard_map/dot_general | solution.py:164
  47.0 5.9 %collective-permute-done.7 = bf16[256,4,128]{2,0,1:T(8,128)(2,1)S(1)} collective-permute-done((bf16[256,4,128]{2,0,1:T(8,128)(2,1)}, bf16[256,4,128]{2,0,1:T(8,128)(2,1)S(1)}, u32[]{:S(2)}, u32[]{:S(2)}) %collective-permute-start.7) | collective-permute-done | bytes 262176 | tf_op jit(solution)/shard_map/ppermute | solution.py:101
  53.0 0.0 collective-permute-start.9
  53.0 0.0 collective-permute-done.8
  53.0 0.4 convolution_bitcast_fusion.1
  53.4 0.0 copy-start.4
  53.4 0.0 copy-start.3
  53.4 0.4 fusion.41
  53.8 0.7 %collective-permute-done.9 = bf16[256,4,128]{2,0,1:T(8,128)(2,1)S(1)} collective-permute-done((bf16[256,4,128]{2,0,1:T(8,128)(2,1)S(1)}, bf16[256,4,128]{2,0,1:T(8,128)(2,1)S(1)}, u32[]{:S(2)}, u32[]{:S(2)}) %collective-permute-start.9) | collective-permute-done | bytes 262176 | tf_op jit(solution)/shard_map/ppermute | solution.py:101
  54.5 0.5 multiply_reduce_fusion
  55.0 1.5 %collective-permute-start.10 = (f32[256]{0:T(256)S(1)}, f32[256]{0:T(256)S(1)}, u32[]{:S(2)}, u32[]{:S(2)}) collective-permute-start(f32[256]{0:T(256)S(1)} %get-tuple-element.27), channel_id=1, source_target_pairs={{0,2},{1,3},{2,0},{3,1},{4,6},{5,7},{6,4},{7,5},{8,10},{9,11},{10,... | collective-permute-start | bytes 3080 | tf_op jit(solution)/shard_map/ppermute | solution.py:109
  56.5 2.1 %collective-permute-done.10 = f32[256]{0:T(256)S(1)} collective-permute-done((f32[256]{0:T(256)S(1)}, f32[256]{0:T(256)S(1)}, u32[]{:S(2)}, u32[]{:S(2)}) %collective-permute-start.10) | collective-permute-done | bytes 1056 | tf_op jit(solution)/shard_map/ppermute | solution.py:109
  58.6 0.0 collective-permute-start.11
  58.6 1.1 %collective-permute-done.11 = f32[256]{0:T(256)S(1)} collective-permute-done((f32[256]{0:T(256)S(1)}, f32[256]{0:T(256)S(1)}, u32[]{:S(2)}, u32[]{:S(2)}) %collective-permute-start.11) | collective-permute-done | bytes 1056 | tf_op jit(solution)/shard_map/ppermute | solution.py:109
  59.7 0.0 copy-done.3
  59.8 0.9 %add_convert_fusion = bf16[256,768]{1,0:T(8,128)(2,1)} fusion(f32[256,768]{1,0:T(8,128)S(1)} %get-tuple-element.28, bf16[256,768]{1,0:T(8,128)(2,1)S(1)} %copy-done.3, f32[768]{0:T(1024)S(1)} %convert_element_type.69, f32[256]{0:T(256)S(1)} %add_rsqrt_fusion), kind=kLoop, calls=%fused_computation.64 | loop fusion | flops 983040 | bytes 1576960 | tf_op jit(solution)/shard_map/convert_element_type | solution.py:184
  (11 shorter events, 0.1 us)
Async XLA Ops:
  0.0 16.9 %copy-start = (bf16[16,128,768]{2,1,0:T(8,128)(2,1)S(1)}, bf16[16,128,768]{2,1,0:T(8,128)(2,1)}, u32[]{:S(2)}) copy-start(bf16[16,128,768]{2,1,0:T(8,128)(2,1)} %param.10) | copy-start | bytes 9437188
  3.6 14.3 %collective-permute-start.1 = (bf16[256,4,128]{2,0,1:T(8,128)(2,1)}, bf16[256,4,128]{2,0,1:T(8,128)(2,1)}, u32[]{:S(2)}, u32[]{:S(2)}) collective-permute-start(bf16[256,4,128]{2,0,1:T(8,128)(2,1)} %pad_maximum_fusion.1), channel_id=1, source_target_pairs={{0,8},{4,12},{8,16},{12,20},{16,24},{20,28},{1,9},{5,13},{9,17},{1... | collective-permute-start | bytes 786440 | tf_op jit(solution)/shard_map/ppermute | solution.py:87
  9.2 13.1 %collective-permute-start = (bf16[256,4,128]{2,0,1:T(8,128)(2,1)}, bf16[256,4,128]{2,0,1:T(8,128)(2,1)}, u32[]{:S(2)}, u32[]{:S(2)}) collective-permute-start(bf16[256,4,128]{2,0,1:T(8,128)(2,1)} %pad_maximum_fusion.1), channel_id=1, source_target_pairs={{0,4},{8,12},{16,20},{24,28},{1,5},{9,13},{17,21},{25,29},{2,6},{1... | collective-permute-start | bytes 786440 | tf_op jit(solution)/shard_map/ppermute | solution.py:88
  14.3 1.5 %copy-start.2 = (bf16[256,2,128]{2,1,0:T(2,128)(2,1)S(1)}, bf16[256,2,128]{2,1,0:T(2,128)(2,1)}, u32[]{:S(2)}) copy-start(bf16[256,2,128]{2,1,0:T(2,128)(2,1)} %param.8) | copy-start | bytes 393220
  17.8 5.8 %copy-start.1 = (f32[2,2,256,128]{2,3,1,0:T(8,128)S(1)}, f32[2,2,256,128]{2,3,1,0:T(8,128)}, u32[]{:S(2)}) copy-start(f32[2,2,256,128]{2,3,1,0:T(8,128)} %fusion.60) | copy-start | bytes 1572868
  17.8 8.2 %collective-permute-start.3 = (bf16[256,4,128]{2,0,1:T(8,128)(2,1)}, bf16[256,4,128]{2,0,1:T(8,128)(2,1)S(1)}, u32[]{:S(2)}, u32[]{:S(2)}) collective-permute-start(bf16[256,4,128]{2,0,1:T(8,128)(2,1)} %collective-permute-done.1), channel_id=1, source_target_pairs={{0,8},{4,12},{8,16},{12,20},{16,24},{20,28},{1,9},{5,13},{9,17},{1... | collective-permute-start | bytes 786440 | tf_op jit(solution)/shard_map/ppermute | solution.py:87
  20.8 11.6 %collective-permute-start.2 = (bf16[256,4,128]{2,0,1:T(8,128)(2,1)}, bf16[256,4,128]{2,0,1:T(8,128)(2,1)S(1)}, u32[]{:S(2)}, u32[]{:S(2)}) collective-permute-start(bf16[256,4,128]{2,0,1:T(8,128)(2,1)} %collective-permute-done.1), channel_id=1, source_target_pairs={{0,4},{8,12},{16,20},{24,28},{4,0},{12,8},{20,16},{28,24},{1,5},{9... | collective-permute-start | bytes 786440 | tf_op jit(solution)/shard_map/ppermute | solution.py:88
  26.1 8.4 %collective-permute-start.5 = (bf16[256,4,128]{2,0,1:T(8,128)(2,1)S(1)}, bf16[256,4,128]{2,0,1:T(8,128)(2,1)S(1)}, u32[]{:S(2)}, u32[]{:S(2)}) collective-permute-start(bf16[256,4,128]{2,0,1:T(8,128)(2,1)S(1)} %collective-permute-done.3), channel_id=1, source_target_pairs={{0,8},{4,12},{8,16},{12,20},{16,24},{20,28},{1,9},{5,13},{9,17},{1... | collective-permute-start | bytes 786440 | tf_op jit(solution)/shard_map/ppermute | solution.py:87
  30.4 8.7 %collective-permute-start.4 = (bf16[256,4,128]{2,0,1:T(8,128)(2,1)S(1)}, bf16[256,4,128]{2,0,1:T(8,128)(2,1)S(1)}, u32[]{:S(2)}, u32[]{:S(2)}) collective-permute-start(bf16[256,4,128]{2,0,1:T(8,128)(2,1)S(1)} %collective-permute-done.3), channel_id=1, source_target_pairs={{0,4},{8,12},{16,20},{24,28},{4,0},{12,8},{20,16},{28,24},{1,5},{9... | collective-permute-start | bytes 786440 | tf_op jit(solution)/shard_map/ppermute | solution.py:88
  34.4 8.0 %collective-permute-start.6 = (bf16[256,4,128]{2,0,1:T(8,128)(2,1)S(1)}, bf16[256,4,128]{2,0,1:T(8,128)(2,1)S(1)}, u32[]{:S(2)}, u32[]{:S(2)}) collective-permute-start(bf16[256,4,128]{2,0,1:T(8,128)(2,1)S(1)} %collective-permute-done.5), channel_id=1, source_target_pairs={{0,4},{8,12},{16,20},{24,28},{4,0},{12,8},{20,16},{28,24},{1,5},{9... | collective-permute-start | bytes 786440 | tf_op jit(solution)/shard_map/ppermute | solution.py:88
  44.0 8.9 %collective-permute-start.8 = (bf16[256,4,128]{2,0,1:T(8,128)(2,1)}, bf16[256,4,128]{2,0,1:T(8,128)(2,1)S(1)}, u32[]{:S(2)}, u32[]{:S(2)}) collective-permute-start(bf16[256,4,128]{2,0,1:T(8,128)(2,1)} %copy.27), channel_id=1, source_target_pairs={{0,1},{1,0},{2,3},{3,2},{4,5},{5,4},{6,7},{7,6},{8,9},{9,8},{10,11... | collective-permute-start | bytes 786440 | tf_op jit(solution)/shard_map/ppermute | solution.py:101
  44.0 8.9 %collective-permute-start.7 = (bf16[256,4,128]{2,0,1:T(8,128)(2,1)}, bf16[256,4,128]{2,0,1:T(8,128)(2,1)S(1)}, u32[]{:S(2)}, u32[]{:S(2)}) collective-permute-start(bf16[256,4,128]{2,0,1:T(8,128)(2,1)} %copy.27), channel_id=1, source_target_pairs={{0,2},{1,3},{2,0},{3,1},{4,6},{5,7},{6,4},{7,5},{8,10},{9,11},{10,... | collective-permute-start | bytes 786440 | tf_op jit(solution)/shard_map/ppermute | solution.py:101
  53.0 1.5 %collective-permute-start.9 = (bf16[256,4,128]{2,0,1:T(8,128)(2,1)S(1)}, bf16[256,4,128]{2,0,1:T(8,128)(2,1)S(1)}, u32[]{:S(2)}, u32[]{:S(2)}) collective-permute-start(bf16[256,4,128]{2,0,1:T(8,128)(2,1)S(1)} %collective-permute-done.7), channel_id=1, source_target_pairs={{0,1},{1,0},{2,3},{3,2},{4,5},{5,4},{6,7},{7,6},{8,9},{9,8},{10,11... | collective-permute-start | bytes 786440 | tf_op jit(solution)/shard_map/ppermute | solution.py:101
  53.4 5.3 %copy-start.4 = (bf16[768]{0:T(1024)(128)(2,1)S(1)}, bf16[768]{0:T(1024)(128)(2,1)}, u32[]{:S(2)}) copy-start(bf16[768]{0:T(1024)(128)(2,1)} %param.11) | copy-start | bytes 4612
  53.4 6.4 %copy-start.3 = (bf16[256,768]{1,0:T(8,128)(2,1)S(1)}, bf16[256,768]{1,0:T(8,128)(2,1)}, u32[]{:S(2)}) copy-start(bf16[256,768]{1,0:T(8,128)(2,1)} %param.9) | copy-start | bytes 1179652
  55.0 3.6 %collective-permute-start.10 = (f32[256]{0:T(256)S(1)}, f32[256]{0:T(256)S(1)}, u32[]{:S(2)}, u32[]{:S(2)}) collective-permute-start(f32[256]{0:T(256)S(1)} %get-tuple-element.27), channel_id=1, source_target_pairs={{0,2},{1,3},{2,0},{3,1},{4,6},{5,7},{6,4},{7,5},{8,10},{9,11},{10,... | collective-permute-start | bytes 3080 | tf_op jit(solution)/shard_map/ppermute | solution.py:109
  58.6 1.1 %collective-permute-start.11 = (f32[256]{0:T(256)S(1)}, f32[256]{0:T(256)S(1)}, u32[]{:S(2)}, u32[]{:S(2)}) collective-permute-start(f32[256]{0:T(256)S(1)} %add.241), channel_id=1, source_target_pairs={{0,1},{1,0},{2,3},{3,2},{4,5},{5,4},{6,7},{7,6},{8,9},{9,8},{10,11... | collective-permute-start | bytes 3080 | tf_op jit(solution)/shard_map/ppermute | solution.py:109

commit v6 on v5

--- a/solution.py
+++ b/solution.py
@@ -36,32 +36,37 @@
     )
 
 
-def attend_block(state, key_block, value_block, source, rotary_queries, device_index, whole=False):
+def attend_block(state, key_block, value_block, source, queries_by_group, device_index, whole=False):
     numerators, denominators = state
     rows = key_block.shape[0]
-    scores = (
-        jnp.einsum("sgrh,kgh->grsk", rotary_queries, key_block, preferred_element_type=jnp.float32)
-        * query_scale
-    )
-    capped = softcap_value * jnp.tanh(scores / softcap_value)
     if whole:
         allowed = (source >= 0) & (source < device_index)
-        weights = jnp.where(allowed, jnp.exp(capped), 0.0)
     else:
-        offsets = jnp.arange(rows, dtype=jnp.int32)
-        query_pos = device_index * rows + offsets
-        key_pos = source * rows + offsets
+        group_rows = queries_by_group[0].shape[0]
+        query_pos = device_index * rows + jnp.arange(group_rows, dtype=jnp.int32) // (group_rows // rows)
+        key_pos = source * rows + jnp.arange(rows, dtype=jnp.int32)
         distance = query_pos[:, None] - key_pos[None, :]
         allowed = (distance >= 0) & (distance < WINDOW_TOKENS) & (key_pos[None, :] >= 0)
-        weights = jnp.where(allowed[None, None], jnp.exp(capped), 0.0)
-    denominators = denominators + jnp.sum(weights, axis=-1)
-    numerators = numerators + jnp.einsum(
-        "grsk,kgh->grsh",
-        weights.astype(jnp.bfloat16),
-        value_block,
-        preferred_element_type=jnp.float32,
-    )
-    return (numerators, denominators)
+    new_numerators = []
+    new_denominators = []
+    for group, group_queries in enumerate(queries_by_group):
+        scores = (
+            lax.dot_general(
+                group_queries,
+                key_block[:, group],
+                (((1,), (1,)), ((), ())),
+                preferred_element_type=jnp.float32,
+            )
+            * query_scale
+        )
+        capped = softcap_value * jnp.tanh(scores / softcap_value)
+        weights = jnp.where(allowed, jnp.exp(capped), 0.0)
+        new_denominators.append(denominators[group] + jnp.sum(weights, axis=-1))
+        new_numerators.append(
+            numerators[group]
+            + jnp.dot(weights.astype(jnp.bfloat16), value_block[:, group], preferred_element_type=jnp.float32)
+        )
+    return (new_numerators, new_denominators)
 
 
 def along_lines(state, key_block, value_block, rotary_queries, device_index, cycle_size):
@@ -104,11 +109,10 @@
 
 
 def summed(partial, count):
-    bit = count // 2
-    while bit >= 1:
-        partial = partial + lax.ppermute(partial, "tp", [(source, source ^ bit) for source in range(count)])
-        bit //= 2
-    return partial
+    total = partial
+    for offset in range(1, count):
+        total = total + lax.ppermute(partial, "tp", [(source, source ^ offset) for source in range(count)])
+    return total
 
 
 def local(queries, keys, values, residual, out_weight, post_gain):
@@ -122,11 +126,14 @@
     positions = (device_index * rows + jnp.arange(rows, dtype=jnp.int32))[:, None]
     rotary_queries = rotate(queries.astype(jnp.float32), positions).astype(jnp.bfloat16)
     rotary_queries = rotary_queries.reshape(rows, kv_heads, heads_per_group, head_size)
+    rotary_queries = [
+        rotary_queries[:, group].reshape(rows * heads_per_group, head_size) for group in range(kv_heads)
+    ]
     rotary_keys = rotate(keys.astype(jnp.float32), positions).astype(jnp.bfloat16)
     reach = min((WINDOW_TOKENS + rows - 2) // rows, cycle_size - 1)
     state = (
-        jnp.zeros((kv_heads, heads_per_group, rows, head_size), jnp.float32),
-        jnp.zeros((kv_heads, heads_per_group, rows), jnp.float32),
+        [jnp.zeros((rows * heads_per_group, head_size), jnp.float32)] * kv_heads,
+        [jnp.zeros((rows * heads_per_group,), jnp.float32)] * kv_heads,
     )
     state = attend_block(state, rotary_keys, values, device_index, rotary_queries, device_index)
     if reach == cycle_size - 1 and cycle_size % 2 == 0:
@@ -150,8 +157,13 @@
             0, reach, advance, (state, rotary_keys, values)
         )
     numerators, denominators = state
-    attended = (numerators / denominators[..., None]).astype(jnp.bfloat16)
-    attended = jnp.transpose(attended, (2, 0, 1, 3)).reshape(rows, q_heads, head_size)
+    attended = jnp.stack(
+        [
+            (numerator / denominator[:, None]).astype(jnp.bfloat16).reshape(rows, heads_per_group, head_size)
+            for numerator, denominator in zip(numerators, denominators)
+        ],
+        axis=1,
+    ).reshape(rows, q_heads, head_size)
     local_cols = out_weight.shape[2]
     tp_size = lax.axis_size("tp")
     tp_index = lax.axis_index("tp")

time: 61 us -> 75 us (1.23)
  matrix products: 13.2 us -> 26.4 us
  waiting for transfers between devices: 16.2 us -> 12.3 us
  local copies, waits for them, and re-layouts: 2.96 us -> 5.57 us
  other arithmetic: 5.23 us -> 7.28 us
    dot_general x16 -> x32, matrix products: 10.5 us -> 23.7 us  [the longest x16 13 us: attend_block(): lax.dot_general(group_queries, key_block[:, group], (((1,), (1,)), ((), (...]
    another operation x2 -> x3, local copies, waits for them, and re-layouts: 0.07 us -> 3.53 us  [local(): jnp.stack([(numerator / denominator[:, None]).astype(jnp.bfloat16).reshap...]
    ppermute x4, waiting for transfers between devices: 4.95 us -> 2.66 us  [along_lines(): crossed = lax.ppermute(line, 'ctx', up if step == 1 else up + down)]
    ppermute x3, waiting for transfers between devices: 1.35 us -> 0.01 us  [along_lines(): arrived = lax.ppermute(line, 'ctx', forward)]
    another operation x2 -> x3, other arithmetic: 0.68 us -> 1.61 us  [the longest x1 0.93 us: local(): jnp.stack([(numerator / denominator[:, None]).astype(jnp.bfloat16).reshap...]
    ppermute x3, starting transfers between devices: 12.8 us -> 11.9 us  [along_lines(): arrived = lax.ppermute(line, 'ctx', forward)]
    reshape x1 -> x0, local copies, waits for them, and re-layouts: 0.84 us -> none  [local(): jnp.transpose(attended, (2, 0, 1, 3)).reshape(rows, q_heads, head_size)]
    ppermute x2 -> x3, starting transfers between devices: 1.53 us -> 1.92 us  [summed(): lax.ppermute(partial, 'tp', [(source, source ^ offset) for source in rang...]
  transfers between devices with their start and end apart: 12 -> 13, of which waited for: 8 -> 5; matrix products, arithmetic and copies ran while one was open for 24% -> 34% of each run, Pallas kernels for 0% -> 0%
where the time goes in v6:
time: 75 us; the launch traced here: 74.3 us
  matrix products  26.4 us (35%)
  starting transfers between devices  22.4 us (30%)
  waiting for transfers between devices  12.3 us (16%)
  other arithmetic  7.28 us (10%)
  local copies, waits for them, and re-layouts  5.57 us (7%)
    dot_general x16, matrix products, attend_block(): lax.dot_general(group_queries, key_block[:, group], (((1,), (1,)), ((), (...  13 us
    ppermute x3, starting transfers between devices, along_lines(): arrived = lax.ppermute(line, 'ctx', forward)  11.9 us
    dot_general x16, matrix products, attend_block(): jnp.dot(weights.astype(jnp.bfloat16), value_block[:, group], preferred_el...  10.7 us
    ppermute x4, starting transfers between devices, along_lines(): crossed = lax.ppermute(line, 'ctx', up if step == 1 else up + down)  7.02 us
    ppermute x3, waiting for transfers between devices, exchanged(): lax.ppermute(held, 'tp', pairs)  6.66 us
    another operation x3, local copies, waits for them, and re-layouts, local(): jnp.stack([(numerator / denominator[:, None]).astype(jnp.bfloat16).reshap...  3.53 us
    ppermute x3, waiting for transfers between devices, summed(): lax.ppermute(partial, 'tp', [(source, source ^ offset) for source in rang...  2.95 us
    dot_general x4, matrix products, local(): jnp.dot(held.reshape(rows, q_heads * head_size), weight_rows.reshape(q_he...  2.72 us
  transfers between devices with their start and end apart: 13, of which 5 were waited for; matrix products, arithmetic and copies ran while one was open for 34% of the time, Pallas kernels for 0%

profile of v6, /device:TPU:0, one launch (start us, length us, event | category | flops | bytes accessed | tf_op | source)
XLA Modules:
  0.0 74.3 jit_solution(15490057328168321013)
XLA Ops:
  0.0 1.1 %copy.9 = bf16[256,2,128]{2,0,1:T(8,128)(2,1)S(1)} copy(bf16[256,2,128]{2,1,0:T(2,128)(2,1)} %param.8) | data formatting | bytes 262144 | tf_op args[2]
  1.1 0.9 %copy_convert_fusion = f32[256,2,128]{2,0,1:T(8,128)S(1)} fusion(bf16[256,2,128]{2,1,0:T(2,128)(2,1)} %param.7), kind=kLoop, calls=%fused_computation.149 | loop fusion | flops 65536 | bytes 393216 | tf_op jit(solution)/shard_map/convert_element_type | solution.py:132
  2.0 0.5 multiply_cosine_fusion
  2.7 0.8 %pad_maximum_fusion = bf16[256,4,128]{2,0,1:T(8,128)(2,1)} fusion(bf16[256,2,128]{2,0,1:T(8,128)(2,1)S(1)} %copy.9, bf16[256,2,64]{2,0,1:T(8,128)(2,1)S(1)} %get-tuple-element.10, bf16[256,2,64]{2,0,1:T(8,128)(2,1)S(1)} %get-tuple-element.9), kind=kLoop, calls=%fused_computation.117 | loop fusion | flops 786432 | bytes 524288 | tf_op jit(solution)/shard_map/concatenate | solution.py:89
  3.6 5.6 %collective-permute-start.1 = (bf16[256,4,128]{2,0,1:T(8,128)(2,1)}, bf16[256,4,128]{2,0,1:T(8,128)(2,1)}, u32[]{:S(2)}, u32[]{:S(2)}) collective-permute-start(bf16[256,4,128]{2,0,1:T(8,128)(2,1)} %pad_maximum_fusion), channel_id=1, source_target_pairs={{0,8},{4,12},{8,16},{12,20},{16,24},{20,28},{1,9},{5,13},{9,17},{1... | collective-permute-start | bytes 786440 | tf_op jit(solution)/shard_map/ppermute | solution.py:92
  9.2 4.1 %collective-permute-start = (bf16[256,4,128]{2,0,1:T(8,128)(2,1)}, bf16[256,4,128]{2,0,1:T(8,128)(2,1)}, u32[]{:S(2)}, u32[]{:S(2)}) collective-permute-start(bf16[256,4,128]{2,0,1:T(8,128)(2,1)} %pad_maximum_fusion), channel_id=1, source_target_pairs={{0,4},{8,12},{16,20},{24,28},{1,5},{9,13},{17,21},{25,29},{2,6},{1... | collective-permute-start | bytes 786440 | tf_op jit(solution)/shard_map/ppermute | solution.py:93
  13.3 1.0 %convert_element_type.83 = f32[256,4,128]{2,1,0:T(4,128)S(1)} convert(bf16[256,4,128]{2,1,0:T(4,128)(2,1)} %param.6) | non-fusion elementwise | flops 131072 | bytes 786432 | tf_op jit(solution)/shard_map/convert_element_type | solution.py:127
  14.4 0.5 subtract_convert_fusion
  14.9 0.7 fusion.102
  15.6 0.4 fusion.126
  16.1 0.3 fusion.89
  16.4 1.1 %fusion.134 = (f32[512]{0:T(512)S(1)}, bf16[512,256]{0,1:T(8,128)(2,1)}) fusion(bf16[512,128]{1,0:T(8,128)(2,1)S(1)} %bitcast.194, bf16[256,2,64]{2,0,1:T(8,128)(2,1)S(1)} %get-tuple-element.9, bf16[256,2,64]{2,0,1:T(8,128)(2,1)S(1)} %get-tuple-element.10, pred[256]{0:T(512)(128)(4,1)S(1)} %fusion.117, s32[256]{0:T(256)S(1)} %get-tuple-element.47, ...), kind=kOutput, calls=%fused_computation.220 | convolution fusion | flops 34995712 | bytes 529664 | tf_op jit(solution)/shard_map/dot_general | solution.py:54
  17.5 0.9 %constant_dynamic-slice_fusion = bf16[4,128,768]{2,1,0:T(8,128)(2,1)} fusion(bf16[16,128,768]{2,1,0:T(8,128)(2,1)S(1)} %copy-done, s32[]{:T(128)S(6)} %select_n.137), kind=kLoop, calls=%fused_computation.200 | loop fusion | bytes 1572868 | tf_op jit(solution)/shard_map/dynamic_slice | solution.py:175
  18.4 1.2 %fusion.100 = f32[512,128]{1,0:T(8,128)S(1)} fusion(bf16[512,256]{0,1:T(8,128)(2,1)} %get-tuple-element.42, bf16[256,2,128]{2,0,1:T(8,128)(2,1)S(1)} %copy.9), kind=kOutput, calls=%fused_computation.139 | convolution fusion | flops 33554432 | bytes 589824 | tf_op jit(solution)/shard_map/dot_general | solution.py:67
  19.7 2.8 %collective-permute-start.3 = (bf16[256,4,128]{2,0,1:T(8,128)(2,1)}, bf16[256,4,128]{2,0,1:T(8,128)(2,1)S(1)}, u32[]{:S(2)}, u32[]{:S(2)}) collective-permute-start(bf16[256,4,128]{2,0,1:T(8,128)(2,1)} %collective-permute-done.1), channel_id=1, source_target_pairs={{0,8},{4,12},{8,16},{12,20},{16,24},{20,28},{1,9},{5,13},{9,17},{1... | collective-permute-start | bytes 786440 | tf_op jit(solution)/shard_map/ppermute | solution.py:92
  22.6 1.2 %fusion.127 = (f32[512]{0:T(512)S(1)}, bf16[512,256]{0,1:T(8,128)(2,1)S(1)}) fusion(bf16[512,128]{1,0:T(8,128)(2,1)} %bitcast.203, bf16[256,4,128]{2,0,1:T(8,128)(2,1)} %collective-permute-done, pred[]{:T(512)S(6)} %and.63), kind=kOutput, calls=%fused_computation.213 | convolution fusion | flops 34209280 | bytes 460801 | tf_op jit(solution)/shard_map/dot_general | solution.py:54
  23.8 1.3 %fusion.135 = (f32[512]{0:T(512)S(1)}, bf16[512,256]{0,1:T(8,128)(2,1)S(1)}) fusion(bf16[512,128]{1,0:T(8,128)(2,1)} %bitcast.195, bf16[256,4,128]{2,0,1:T(8,128)(2,1)} %collective-permute-done, pred[]{:T(512)S(6)} %and.63), kind=kOutput, calls=%fused_computation.221 | convolution fusion | flops 34209280 | bytes 460801 | tf_op jit(solution)/shard_map/dot_general | solution.py:54
  25.1 1.2 %fusion.125 = (f32[512]{0:T(512)S(1)}, bf16[512,256]{0,1:T(8,128)(2,1)S(1)}) fusion(bf16[512,128]{1,0:T(8,128)(2,1)} %bitcast.204, bf16[256,4,128]{2,0,1:T(8,128)(2,1)} %collective-permute-done.1, pred[]{:T(512)S(6)} %and.64), kind=kOutput, calls=%fused_computation.211 | convolution fusion | flops 34209280 | bytes 460801 | tf_op jit(solution)/shard_map/dot_general | solution.py:54
  26.3 1.1 %convolution_add_fusion.4 = f32[512,128]{1,0:T(8,128)S(1)} fusion(f32[512,128]{1,0:T(8,128)S(1)} %fusion.89, bf16[512,256]{0,1:T(8,128)(2,1)S(1)} %get-tuple-element.28, bf16[256,4,128]{2,0,1:T(8,128)(2,1)} %collective-permute-done), kind=kOutput, calls=%fused_computation.93 | convolution fusion | flops 33619968 | bytes 851968 | tf_op jit(solution)/shard_map/dot_general | solution.py:67
  27.5 1.1 %convolution_add_fusion.3 = f32[512,128]{1,0:T(8,128)S(1)} fusion(f32[512,128]{1,0:T(8,128)S(1)} %convolution_add_fusion.4, bf16[512,256]{0,1:T(8,128)(2,1)S(1)} %get-tuple-element.24, bf16[256,4,128]{2,0,1:T(8,128)(2,1)} %collective-permute-done.1), kind=kOutput, calls=%fused_computation.92 | convolution fusion | flops 33619968 | bytes 851968 | tf_op jit(solution)/shard_map/dot_general | solution.py:67
  28.6 1.1 %convolution_add_fusion.9 = f32[512,128]{1,0:T(8,128)S(1)} fusion(f32[512,128]{1,0:T(8,128)S(1)} %fusion.100, bf16[512,256]{0,1:T(8,128)(2,1)S(1)} %get-tuple-element.44, bf16[256,4,128]{2,0,1:T(8,128)(2,1)} %collective-permute-done), kind=kOutput, calls=%fused_computation.101 | convolution fusion | flops 33619968 | bytes 851968 | tf_op jit(solution)/shard_map/dot_general | solution.py:67
  29.7 1.2 %fusion.133 = (f32[512]{0:T(512)S(1)}, bf16[512,256]{0,1:T(8,128)(2,1)S(1)}) fusion(bf16[512,128]{1,0:T(8,128)(2,1)S(1)} %bitcast.197, bf16[256,4,128]{2,0,1:T(8,128)(2,1)} %collective-permute-done.1, pred[]{:T(512)S(6)} %and.64), kind=kOutput, calls=%fused_computation.219 | convolution fusion | flops 34209280 | bytes 460801 | tf_op jit(solution)/shard_map/dot_general | solution.py:54
  30.9 1.1 %convolution_add_fusion.8 = f32[512,128]{1,0:T(8,128)S(1)} fusion(f32[512,128]{1,0:T(8,128)S(1)} %convolution_add_fusion.9, bf16[512,256]{0,1:T(8,128)(2,1)S(1)} %get-tuple-element.40, bf16[256,4,128]{2,0,1:T(8,128)(2,1)} %collective-permute-done.1), kind=kOutput, calls=%fused_computation.100 | convolution fusion | flops 33619968 | bytes 851968 | tf_op jit(solution)/shard_map/dot_general | solution.py:67
  32.0 3.5 %collective-permute-start.5 = (bf16[256,4,128]{2,0,1:T(8,128)(2,1)S(1)}, bf16[256,4,128]{2,0,1:T(8,128)(2,1)S(1)}, u32[]{:S(2)}, u32[]{:S(2)}) collective-permute-start(bf16[256,4,128]{2,0,1:T(8,128)(2,1)S(1)} %collective-permute-done.3), channel_id=1, source_target_pairs={{0,8},{4,12},{8,16},{12,20},{16,24},{20,28},{1,9},{5,13},{9,17},{1... | collective-permute-start | bytes 786440 | tf_op jit(solution)/shard_map/ppermute | solution.py:92
  35.5 2.1 %collective-permute-start.4 = (bf16[256,4,128]{2,0,1:T(8,128)(2,1)S(1)}, bf16[256,4,128]{2,0,1:T(8,128)(2,1)S(1)}, u32[]{:S(2)}, u32[]{:S(2)}) collective-permute-start(bf16[256,4,128]{2,0,1:T(8,128)(2,1)S(1)} %collective-permute-done.3), channel_id=1, source_target_pairs={{0,4},{8,12},{16,20},{24,28},{4,0},{12,8},{20,16},{28,24},{1,5},{9... | collective-permute-start | bytes 786440 | tf_op jit(solution)/shard_map/ppermute | solution.py:93
  37.5 0.3 fusion.123
  37.9 0.3 fusion.84
  38.1 0.9 %fusion.131 = (f32[512]{0:T(512)}, bf16[512,256]{0,1:T(8,128)(2,1)S(1)}) fusion(bf16[512,128]{1,0:T(8,128)(2,1)S(1)} %bitcast.198, bf16[256,4,128]{2,0,1:T(8,128)(2,1)S(1)} %collective-permute-done.3, pred[]{:T(512)S(6)} %and.66), kind=kOutput, calls=%fused_computation.217 | convolution fusion | flops 34209280 | bytes 460801 | tf_op jit(solution)/shard_map/dot_general | solution.py:54
  39.1 0.3 fusion.95
  39.3 0.3 fusion.124
  39.7 0.3 fusion.69
  39.9 0.9 %fusion.132 = (f32[512]{0:T(512)}, bf16[512,256]{0,1:T(8,128)(2,1)S(1)}) fusion(bf16[512,128]{1,0:T(8,128)(2,1)S(1)} %bitcast.199, bf16[256,4,128]{2,0,1:T(8,128)(2,1)S(1)} %collective-permute-done.2, pred[]{:T(512)S(6)} %and.65), kind=kOutput, calls=%fused_computation.218 | convolution fusion | flops 34209280 | bytes 460801 | tf_op jit(solution)/shard_map/dot_general | solution.py:54
  40.9 0.3 fusion.72
  41.1 0.8 %collective-permute-start.6 = (bf16[256,4,128]{2,0,1:T(8,128)(2,1)S(1)}, bf16[256,4,128]{2,0,1:T(8,128)(2,1)S(1)}, u32[]{:S(2)}, u32[]{:S(2)}) collective-permute-start(bf16[256,4,128]{2,0,1:T(8,128)(2,1)S(1)} %collective-permute-done.5), channel_id=1, source_target_pairs={{0,4},{8,12},{16,20},{24,28},{4,0},{12,8},{20,16},{28,24},{1,5},{9... | collective-permute-start | bytes 786440 | tf_op jit(solution)/shard_map/ppermute | solution.py:93
  41.9 0.3 fusion.121
  42.2 0.3 fusion.81
  42.5 0.9 %fusion.129 = (f32[512]{0:T(512)}, bf16[512,256]{0,1:T(8,128)(2,1)S(1)}) fusion(bf16[512,128]{1,0:T(8,128)(2,1)S(1)} %bitcast.200, bf16[256,4,128]{2,0,1:T(8,128)(2,1)S(1)} %collective-permute-done.5, pred[]{:T(512)S(6)} %and.68), kind=kOutput, calls=%fused_computation.215 | convolution fusion | flops 34209280 | bytes 460801 | tf_op jit(solution)/shard_map/dot_general | solution.py:54
  43.4 0.3 fusion.92
  43.7 0.3 fusion.122
  44.0 0.3 fusion.68
  44.3 0.9 %fusion.130 = (f32[512]{0:T(512)}, bf16[512,256]{0,1:T(8,128)(2,1)S(1)}) fusion(bf16[512,128]{1,0:T(8,128)(2,1)S(1)} %bitcast.201, bf16[256,4,128]{2,0,1:T(8,128)(2,1)S(1)} %collective-permute-done.4, pred[]{:T(512)S(6)} %and.67), kind=kOutput, calls=%fused_computation.216 | convolution fusion | flops 34209280 | bytes 460801 | tf_op jit(solution)/shard_map/dot_general | solution.py:54
  45.2 0.3 fusion.71
  45.4 2.7 %collective-permute-done.6 = bf16[256,4,128]{2,0,1:T(8,128)(2,1)S(1)} collective-permute-done((bf16[256,4,128]{2,0,1:T(8,128)(2,1)S(1)}, bf16[256,4,128]{2,0,1:T(8,128)(2,1)S(1)}, u32[]{:S(2)}, u32[]{:S(2)}) %collective-permute-start.6) | collective-permute-done | bytes 262176 | tf_op jit(solution)/shard_map/ppermute | solution.py:93
  48.1 0.3 fusion.120
  48.4 0.9 %fusion.74 = bf16[512,128]{1,0:T(8,128)(2,1)} fusion(f32[512,128]{1,0:T(8,128)S(1)} %fusion.68, bf16[512,256]{0,1:T(8,128)(2,1)S(1)} %get-tuple-element.14, f32[512]{0:T(512)S(1)} %add_add_fusion, bf16[256,4,128]{2,0,1:T(8,128)(2,1)S(1)} %collective-permute-done.6), kind=kOutput, calls=%fused_computation.103 | convolution fusion | flops 33751040 | bytes 722944 | tf_op jit(solution)/shard_map/dot_general | solution.py:67
  49.4 1.0 %copy.13 = bf16[256,1,2,128]{0,3,2,1:T(8,128)(2,1)S(1)} copy(bf16[256,1,2,128]{3,2,0,1:T(2,128)(2,1)} %bitcast.193) | data formatting | bytes 262144 | tf_op jit(solution)/shard_map/stack;reshape | solution.py:160
  50.4 1.2 %fusion.128 = (f32[512]{0:T(512)S(1)}, bf16[512,256]{0,1:T(8,128)(2,1)S(1)}) fusion(bf16[512,128]{1,0:T(8,128)(2,1)} %bitcast.196, bf16[256,4,128]{2,0,1:T(8,128)(2,1)} %copy-done.7, pred[]{:T(512)S(6)} %and.69), kind=kOutput, calls=%fused_computation.214 | convolution fusion | flops 34209280 | bytes 460801 | tf_op jit(solution)/shard_map/dot_general | solution.py:54
  51.6 0.7 add_add_fusion.1
  52.3 1.8 %fusion.73 = bf16[512,128]{1,0:T(8,128)(2,1)} fusion(f32[512,128]{1,0:T(8,128)S(1)} %fusion.71, bf16[512,256]{0,1:T(8,128)(2,1)S(1)} %get-tuple-element.30, f32[512]{0:T(512)S(1)} %add_add_fusion.1, bf16[256,4,128]{2,0,1:T(8,128)(2,1)} %copy-done.7), kind=kOutput, calls=%fused_computation.102 | convolution fusion | flops 33751040 | bytes 722944 | tf_op jit(solution)/shard_map/dot_general | solution.py:67
  54.1 1.7 %copy.12 = bf16[256,1,2,128]{0,3,2,1:T(8,128)(2,1)} copy(bf16[256,1,2,128]{3,2,0,1:T(2,128)(2,1)} %bitcast.192) | data formatting | bytes 262144 | tf_op jit(solution)/shard_map/stack;reshape | solution.py:160
  55.8 0.9 %pad_maximum_fusion.1 = bf16[256,2,2,128]{0,3,2,1:T(8,128)(2,1)S(1)} fusion(bf16[256,1,2,128]{0,3,2,1:T(8,128)(2,1)S(1)} %copy.13, bf16[256,1,2,128]{0,3,2,1:T(8,128)(2,1)} %copy.12), kind=kLoop, calls=%fused_computation.118 | loop fusion | flops 131072 | bytes 524288 | tf_op jit(solution)/shard_map/stack | solution.py:160
  56.7 0.8 %copy.14 = bf16[256,2,2,128]{3,0,2,1:T(8,128)(2,1)} copy(bf16[256,2,2,128]{0,3,2,1:T(8,128)(2,1)S(1)} %pad_maximum_fusion.1) | data formatting | bytes 524288 | tf_op jit(solution)/shard_map/stack | solution.py:160
  57.5 1.5 %collective-permute-start.7 = (bf16[256,4,128]{2,0,1:T(8,128)(2,1)}, bf16[256,4,128]{2,0,1:T(8,128)(2,1)S(1)}, u32[]{:S(2)}, u32[]{:S(2)}) collective-permute-start(bf16[256,4,128]{2,0,1:T(8,128)(2,1)} %bitcast.191), channel_id=1, source_target_pairs={{0,2},{1,3},{2,0},{3,1},{4,6},{5,7},{6,4},{7,5},{8,10},{9,11},{10,... | collective-permute-start | bytes 786440 | tf_op jit(solution)/shard_map/ppermute | solution.py:106
  59.0 1.5 %fusion.136 = f32[256,768]{1,0:T(8,128)S(1)} fusion(bf16[256,512]{0,1:T(8,128)(2,1)S(1)} %bitcast.187, bf16[512,768]{1,0:T(8,128)(2,1)} %bitcast.186), kind=kOutput, calls=%fused_computation.222 | convolution fusion | flops 201326592 | bytes 1835008 | tf_op jit(solution)/shard_map/dot_general | solution.py:176
  60.6 5.9 %collective-permute-done.7 = bf16[256,4,128]{2,0,1:T(8,128)(2,1)S(1)} collective-permute-done((bf16[256,4,128]{2,0,1:T(8,128)(2,1)}, bf16[256,4,128]{2,0,1:T(8,128)(2,1)S(1)}, u32[]{:S(2)}, u32[]{:S(2)}) %collective-permute-start.7) | collective-permute-done | bytes 262176 | tf_op jit(solution)/shard_map/ppermute | solution.py:106
  66.5 0.4 convolution_bitcast_fusion.1
  66.9 0.4 fusion.1
  67.3 0.7 collective-permute-done.9
  68.0 0.5 multiply_reduce_fusion
  68.5 1.3 %collective-permute-start.12 = (f32[256]{0:T(256)S(1)}, f32[256]{0:T(256)S(1)}, u32[]{:S(2)}, u32[]{:S(2)}) collective-permute-start(f32[256]{0:T(256)S(1)} %get-tuple-element.45), channel_id=1, source_target_pairs={{0,3},{1,2},{2,1},{3,0},{4,7},{5,6},{6,5},{7,4},{8,11},{9,10},{10,... | collective-permute-start | bytes 3080 | tf_op jit(solution)/shard_map/ppermute | solution.py:114
  69.8 0.6 collective-permute-start.11
  70.4 1.1 %collective-permute-done.12 = f32[256]{0:T(256)S(1)} collective-permute-done((f32[256]{0:T(256)S(1)}, f32[256]{0:T(256)S(1)}, u32[]{:S(2)}, u32[]{:S(2)}) %collective-permute-start.12) | collective-permute-done | bytes 1056 | tf_op jit(solution)/shard_map/ppermute | solution.py:114
  71.5 1.8 %collective-permute-done.11 = f32[256]{0:T(256)S(1)} collective-permute-done((f32[256]{0:T(256)S(1)}, f32[256]{0:T(256)S(1)}, u32[]{:S(2)}, u32[]{:S(2)}) %collective-permute-start.11) | collective-permute-done | bytes 1056 | tf_op jit(solution)/shard_map/ppermute | solution.py:114
  73.4 0.9 %add_convert_fusion = bf16[256,768]{1,0:T(8,128)(2,1)} fusion(f32[256,768]{1,0:T(8,128)S(1)} %get-tuple-element.46, bf16[256,768]{1,0:T(8,128)(2,1)S(1)} %copy-done.1, f32[768]{0:T(1024)S(1)} %convert_element_type.104, f32[256]{0:T(256)S(1)} %add_rsqrt_fusion), kind=kLoop, calls=%fused_computation.104 | loop fusion | flops 983040 | bytes 1576960 | tf_op jit(solution)/shard_map/convert_element_type | solution.py:196
  (36 shorter events, 0.4 us)
Async XLA Ops:
  0.0 17.5 %copy-start = (bf16[16,128,768]{2,1,0:T(8,128)(2,1)S(1)}, bf16[16,128,768]{2,1,0:T(8,128)(2,1)}, u32[]{:S(2)}) copy-start(bf16[16,128,768]{2,1,0:T(8,128)(2,1)} %param.10) | copy-start | bytes 9437188
  3.6 16.1 %collective-permute-start.1 = (bf16[256,4,128]{2,0,1:T(8,128)(2,1)}, bf16[256,4,128]{2,0,1:T(8,128)(2,1)}, u32[]{:S(2)}, u32[]{:S(2)}) collective-permute-start(bf16[256,4,128]{2,0,1:T(8,128)(2,1)} %pad_maximum_fusion), channel_id=1, source_target_pairs={{0,8},{4,12},{8,16},{12,20},{16,24},{20,28},{1,9},{5,13},{9,17},{1... | collective-permute-start | bytes 786440 | tf_op jit(solution)/shard_map/ppermute | solution.py:92
  9.2 13.4 %collective-permute-start = (bf16[256,4,128]{2,0,1:T(8,128)(2,1)}, bf16[256,4,128]{2,0,1:T(8,128)(2,1)}, u32[]{:S(2)}, u32[]{:S(2)}) collective-permute-start(bf16[256,4,128]{2,0,1:T(8,128)(2,1)} %pad_maximum_fusion), channel_id=1, source_target_pairs={{0,4},{8,12},{16,20},{24,28},{1,5},{9,13},{17,21},{25,29},{2,6},{1... | collective-permute-start | bytes 786440 | tf_op jit(solution)/shard_map/ppermute | solution.py:93
  15.6 0.7 copy-start.4
  15.6 0.7 copy-start.2
  18.4 11.3 %copy-start.3 = (bf16[256,1,2,128]{3,2,1,0:T(2,128)(2,1)S(1)}, bf16[256,1,2,128]{3,2,1,0:T(2,128)(2,1)}, u32[]{:S(2)}) copy-start(bf16[256,1,2,128]{3,2,1,0:T(2,128)(2,1)} %copy-done.2) | copy-start | bytes 393220
  19.7 12.3 %collective-permute-start.3 = (bf16[256,4,128]{2,0,1:T(8,128)(2,1)}, bf16[256,4,128]{2,0,1:T(8,128)(2,1)S(1)}, u32[]{:S(2)}, u32[]{:S(2)}) collective-permute-start(bf16[256,4,128]{2,0,1:T(8,128)(2,1)} %collective-permute-done.1), channel_id=1, source_target_pairs={{0,8},{4,12},{8,16},{12,20},{16,24},{20,28},{1,9},{5,13},{9,17},{1... | collective-permute-start | bytes 786440 | tf_op jit(solution)/shard_map/ppermute | solution.py:92
  22.5 16.8 %collective-permute-start.2 = (bf16[256,4,128]{2,0,1:T(8,128)(2,1)}, bf16[256,4,128]{2,0,1:T(8,128)(2,1)S(1)}, u32[]{:S(2)}, u32[]{:S(2)}) collective-permute-start(bf16[256,4,128]{2,0,1:T(8,128)(2,1)} %collective-permute-done.1), channel_id=1, source_target_pairs={{0,4},{8,12},{16,20},{24,28},{4,0},{12,8},{20,16},{28,24},{1,5},{9... | collective-permute-start | bytes 786440 | tf_op jit(solution)/shard_map/ppermute | solution.py:93
  23.8 13.7 %copy-start.5 = (bf16[256,1,2,128]{3,2,1,0:T(2,128)(2,1)S(1)}, bf16[256,1,2,128]{3,2,1,0:T(2,128)(2,1)}, u32[]{:S(2)}) copy-start(bf16[256,1,2,128]{3,2,1,0:T(2,128)(2,1)} %copy-done.4) | copy-start | bytes 393220
  32.0 9.1 %collective-permute-start.5 = (bf16[256,4,128]{2,0,1:T(8,128)(2,1)S(1)}, bf16[256,4,128]{2,0,1:T(8,128)(2,1)S(1)}, u32[]{:S(2)}, u32[]{:S(2)}) collective-permute-start(bf16[256,4,128]{2,0,1:T(8,128)(2,1)S(1)} %collective-permute-done.3), channel_id=1, source_target_pairs={{0,8},{4,12},{8,16},{12,20},{16,24},{20,28},{1,9},{5,13},{9,17},{1... | collective-permute-start | bytes 786440 | tf_op jit(solution)/shard_map/ppermute | solution.py:92
  35.5 8.2 %collective-permute-start.4 = (bf16[256,4,128]{2,0,1:T(8,128)(2,1)S(1)}, bf16[256,4,128]{2,0,1:T(8,128)(2,1)S(1)}, u32[]{:S(2)}, u32[]{:S(2)}) collective-permute-start(bf16[256,4,128]{2,0,1:T(8,128)(2,1)S(1)} %collective-permute-done.3), channel_id=1, source_target_pairs={{0,4},{8,12},{16,20},{24,28},{4,0},{12,8},{20,16},{28,24},{1,5},{9... | collective-permute-start | bytes 786440 | tf_op jit(solution)/shard_map/ppermute | solution.py:93
  41.1 7.0 %collective-permute-start.6 = (bf16[256,4,128]{2,0,1:T(8,128)(2,1)S(1)}, bf16[256,4,128]{2,0,1:T(8,128)(2,1)S(1)}, u32[]{:S(2)}, u32[]{:S(2)}) collective-permute-start(bf16[256,4,128]{2,0,1:T(8,128)(2,1)S(1)} %collective-permute-done.5), channel_id=1, source_target_pairs={{0,4},{8,12},{16,20},{24,28},{4,0},{12,8},{20,16},{28,24},{1,5},{9... | collective-permute-start | bytes 786440 | tf_op jit(solution)/shard_map/ppermute | solution.py:93
  48.1 1.3 %copy-start.7 = (bf16[256,4,128]{2,0,1:T(8,128)(2,1)}, bf16[256,4,128]{2,0,1:T(8,128)(2,1)S(1)}, u32[]{:S(2)}) copy-start(bf16[256,4,128]{2,0,1:T(8,128)(2,1)S(1)} %collective-permute-done.6) | copy-start | bytes 786436
  57.5 8.9 %collective-permute-start.8 = (bf16[256,4,128]{2,0,1:T(8,128)(2,1)}, bf16[256,4,128]{2,0,1:T(8,128)(2,1)S(1)}, u32[]{:S(2)}, u32[]{:S(2)}) collective-permute-start(bf16[256,4,128]{2,0,1:T(8,128)(2,1)} %bitcast.190), channel_id=1, source_target_pairs={{0,1},{1,0},{2,3},{3,2},{4,5},{5,4},{6,7},{7,6},{8,9},{9,8},{10,11... | collective-permute-start | bytes 786440 | tf_op jit(solution)/shard_map/ppermute | solution.py:106
  57.5 8.9 %collective-permute-start.7 = (bf16[256,4,128]{2,0,1:T(8,128)(2,1)}, bf16[256,4,128]{2,0,1:T(8,128)(2,1)S(1)}, u32[]{:S(2)}, u32[]{:S(2)}) collective-permute-start(bf16[256,4,128]{2,0,1:T(8,128)(2,1)} %bitcast.191), channel_id=1, source_target_pairs={{0,2},{1,3},{2,0},{3,1},{4,6},{5,7},{6,4},{7,5},{8,10},{9,11},{10,... | collective-permute-start | bytes 786440 | tf_op jit(solution)/shard_map/ppermute | solution.py:106
  66.5 1.5 %collective-permute-start.9 = (bf16[256,4,128]{2,0,1:T(8,128)(2,1)S(1)}, bf16[256,4,128]{2,0,1:T(8,128)(2,1)S(1)}, u32[]{:S(2)}, u32[]{:S(2)}) collective-permute-start(bf16[256,4,128]{2,0,1:T(8,128)(2,1)S(1)} %collective-permute-done.7), channel_id=1, source_target_pairs={{0,1},{1,0},{2,3},{3,2},{4,5},{5,4},{6,7},{7,6},{8,9},{9,8},{10,11... | collective-permute-start | bytes 786440 | tf_op jit(solution)/shard_map/ppermute | solution.py:106
  66.9 3.5 %copy-start.6 = (bf16[768]{0:T(1024)(128)(2,1)S(1)}, bf16[768]{0:T(1024)(128)(2,1)}, u32[]{:S(2)}) copy-start(bf16[768]{0:T(1024)(128)(2,1)} %param.11) | copy-start | bytes 4612
  66.9 6.5 %copy-start.1 = (bf16[256,768]{1,0:T(8,128)(2,1)S(1)}, bf16[256,768]{1,0:T(8,128)(2,1)}, u32[]{:S(2)}) copy-start(bf16[256,768]{1,0:T(8,128)(2,1)} %param.9) | copy-start | bytes 1179652
  68.5 3.1 %collective-permute-start.12 = (f32[256]{0:T(256)S(1)}, f32[256]{0:T(256)S(1)}, u32[]{:S(2)}, u32[]{:S(2)}) collective-permute-start(f32[256]{0:T(256)S(1)} %get-tuple-element.45), channel_id=1, source_target_pairs={{0,3},{1,2},{2,1},{3,0},{4,7},{5,6},{6,5},{7,4},{8,11},{9,10},{10,... | collective-permute-start | bytes 3080 | tf_op jit(solution)/shard_map/ppermute | solution.py:114
  69.8 3.6 %collective-permute-start.11 = (f32[256]{0:T(256)S(1)}, f32[256]{0:T(256)S(1)}, u32[]{:S(2)}, u32[]{:S(2)}) collective-permute-start(f32[256]{0:T(256)S(1)} %get-tuple-element.45), channel_id=1, source_target_pairs={{0,2},{1,3},{2,0},{3,1},{4,6},{5,7},{6,4},{7,5},{8,10},{9,11},{10,... | collective-permute-start | bytes 3080 | tf_op jit(solution)/shard_map/ppermute | solution.py:114
  70.3 3.0 %collective-permute-start.10 = (f32[256]{0:T(256)S(1)}, f32[256]{0:T(256)S(1)}, u32[]{:S(2)}, u32[]{:S(2)}) collective-permute-start(f32[256]{0:T(256)S(1)} %get-tuple-element.45), channel_id=1, source_target_pairs={{0,1},{1,0},{2,3},{3,2},{4,5},{5,4},{6,7},{7,6},{8,9},{9,8},{10,11... | collective-permute-start | bytes 3080 | tf_op jit(solution)/shard_map/ppermute | solution.py:114

commit v7 on v5

--- a/solution.py
+++ b/solution.py
@@ -67,9 +67,14 @@
 def along_lines(state, key_block, value_block, rotary_queries, device_index, cycle_size):
     kv_heads = key_block.shape[1]
     outer = cycle_size // 2
-    forward = [(source, source + 2) for source in range(cycle_size - 2)]
-    up = [(source, source + 1) for source in range(0, cycle_size, 2)]
-    down = [(source + 1, source) for source in range(0, cycle_size, 2)]
+    def forward(step):
+        return [(source, source + 2) for source in range(2 * step - 2, cycle_size - 2)]
+
+    def across(step):
+        pairs = [(2 * level, 2 * level + 1) for level in range(max(step - 1, 0), outer)]
+        if step > 1:
+            pairs = pairs + [(2 * level + 1, 2 * level) for level in range(step - 1, outer)]
+        return pairs
     plane = device_index // 2
     side = device_index % 2
 
@@ -84,8 +89,8 @@
     line = jnp.concatenate([key_block, value_block], axis=1)
     for step in range(1, outer + 1):
         if step < outer:
-            arrived = lax.ppermute(line, "ctx", forward)
-        crossed = lax.ppermute(line, "ctx", up if step == 1 else up + down)
+            arrived = lax.ppermute(line, "ctx", forward(step))
+        crossed = lax.ppermute(line, "ctx", across(step))
         state = attend_stacked(state, crossed, 2 * (plane - step + 1) + 1 - side)
         if step < outer:
             state = attend_stacked(state, arrived, device_index - 2 * step)
@@ -104,11 +109,10 @@
 
 
 def summed(partial, count):
-    bit = count // 2
-    while bit >= 1:
-        partial = partial + lax.ppermute(partial, "tp", [(source, source ^ bit) for source in range(count)])
-        bit //= 2
-    return partial
+    total = partial
+    for offset in range(1, count):
+        total = total + lax.ppermute(partial, "tp", [(source, source ^ offset) for source in range(count)])
+    return total
 
 
 def local(queries, keys, values, residual, out_weight, post_gain):
@@ -151,7 +155,6 @@
         )
     numerators, denominators = state
     attended = (numerators / denominators[..., None]).astype(jnp.bfloat16)
-    attended = jnp.transpose(attended, (2, 0, 1, 3)).reshape(rows, q_heads, head_size)
     local_cols = out_weight.shape[2]
     tp_size = lax.axis_size("tp")
     tp_index = lax.axis_index("tp")
@@ -161,13 +164,15 @@
         for held, offset in exchanged(attended, tp_size):
             owner = jnp.bitwise_xor(tp_index, offset)
             weight_rows = lax.dynamic_slice_in_dim(out_weight, owner * q_heads, q_heads, 0)
-            part = jnp.dot(
-                held.reshape(rows, q_heads * head_size),
-                weight_rows.reshape(q_heads * head_size, local_cols),
+            part = lax.dot_general(
+                held,
+                weight_rows.reshape(kv_heads, heads_per_group, head_size, local_cols),
+                (((0, 1, 3), (0, 1, 2)), ((), ())),
                 preferred_element_type=jnp.float32,
             )
             projected = part if projected is None else projected + part
     else:
+        attended = jnp.transpose(attended, (2, 0, 1, 3)).reshape(rows, q_heads, head_size)
         piece = lax.all_gather(attended, "tp", axis=1, tiled=True)
         heads_in = piece.shape[1]
         weight_rows = out_weight.reshape(heads_in * head_size, local_cols)

time: 61 us -> 56 us (0.918)
  the two profiles are of different devices: /device:TPU:0 before, /device:TPU:24 now
where the time goes in v7:
time: 56 us; the launch traced here: 55.7 us
  starting transfers between devices  21.1 us (38%)
  waiting for transfers between devices  20.1 us (36%)
  matrix products  8.29 us (15%)
  other arithmetic  4.53 us (8%)
  local copies, waits for them, and re-layouts  1.31 us (2%)
    ppermute x4, starting transfers between devices, along_lines(): crossed = lax.ppermute(line, 'ctx', across(step))  13.7 us
    ppermute x3, waiting for transfers between devices, exchanged(): lax.ppermute(held, 'tp', pairs)  7.25 us
    ppermute x3, waiting for transfers between devices, along_lines(): arrived = lax.ppermute(line, 'ctx', forward(step))  6.74 us
    dot_general x8, matrix products, attend_block(): jnp.einsum('sgrh,kgh->grsk', rotary_queries, key_block, preferred_element...  3.91 us
    ppermute x3, starting transfers between devices, along_lines(): arrived = lax.ppermute(line, 'ctx', forward(step))  3.85 us
    ppermute x4, waiting for transfers between devices, along_lines(): crossed = lax.ppermute(line, 'ctx', across(step))  3.14 us
    ppermute x3, waiting for transfers between devices, summed(): lax.ppermute(partial, 'tp', [(source, source ^ offset) for source in rang...  2.95 us
    dot_general x8, matrix products, attend_block(): jnp.einsum('grsk,kgh->grsh', weights.astype(jnp.bfloat16), value_block, p...  2.82 us
  transfers between devices with their start and end apart: 13, of which 8 were waited for; matrix products, arithmetic and copies ran while one was open for 16% of the time, Pallas kernels for 0%

profile of v7, /device:TPU:24, one launch (start us, length us, event | category | flops | bytes accessed | tf_op | source)
XLA Modules:
  0.0 55.7 jit_solution(15562304518588987192)
XLA Ops:
  0.0 0.9 %copy.12 = bf16[256,2,128]{2,0,1:T(8,128)(2,1)S(1)} copy(bf16[256,2,128]{2,1,0:T(2,128)(2,1)} %param.8) | data formatting | bytes 262144 | tf_op args[2]
  1.0 0.9 %copy_convert_fusion = f32[256,2,128]{2,0,1:T(8,128)S(1)} fusion(bf16[256,2,128]{2,1,0:T(2,128)(2,1)} %param.7), kind=kLoop, calls=%fused_computation.107 | loop fusion | flops 65536 | bytes 393216 | tf_op jit(solution)/shard_map/convert_element_type | solution.py:129
  1.9 0.5 multiply_cosine_fusion
  2.4 0.2 subtract_convert_fusion.1
  2.6 0.1 pad_maximum_fusion.1
  2.7 1.3 %collective-permute-start.1 = (bf16[256,4,128]{2,0,1:T(8,128)(2,1)S(1)}, bf16[256,4,128]{2,0,1:T(8,128)(2,1)S(1)}, u32[]{:S(2)}, u32[]{:S(2)}) collective-permute-start(bf16[256,4,128]{2,0,1:T(8,128)(2,1)S(1)} %pad_maximum_fusion.1), channel_id=1, source_target_pairs={{0,8},{4,12},{8,16},{12,20},{16,24},{20,28},{1,9},{5,13},{9,17},{1... | collective-permute-start | bytes 786440 | tf_op jit(solution)/shard_map/ppermute | solution.py:92
  4.0 3.4 %collective-permute-start = (bf16[256,4,128]{2,0,1:T(8,128)(2,1)S(1)}, bf16[256,4,128]{2,0,1:T(8,128)(2,1)S(1)}, u32[]{:S(2)}, u32[]{:S(2)}) collective-permute-start(bf16[256,4,128]{2,0,1:T(8,128)(2,1)S(1)} %pad_maximum_fusion.1), channel_id=1, source_target_pairs={{0,4},{8,12},{16,20},{24,28},{1,5},{9,13},{17,21},{25,29},{2,6},{1... | collective-permute-start | bytes 786440 | tf_op jit(solution)/shard_map/ppermute | solution.py:93
  7.5 1.0 %convert_element_type.58 = f32[256,4,128]{2,1,0:T(4,128)S(1)} convert(bf16[256,4,128]{2,1,0:T(4,128)(2,1)} %param.6) | non-fusion elementwise | flops 131072 | bytes 786432 | tf_op jit(solution)/shard_map/convert_element_type | solution.py:127
  8.5 0.0 copy-start.1
  8.5 0.5 subtract_convert_fusion
  9.1 0.1 pad_maximum_fusion
  9.3 0.1 fusion.59
  9.4 0.5 fusion.72
  10.0 0.0 copy-done.1
  10.0 0.3 fusion.56
  10.4 2.2 %collective-permute-done.1 = bf16[256,4,128]{2,0,1:T(8,128)(2,1)S(1)} collective-permute-done((bf16[256,4,128]{2,0,1:T(8,128)(2,1)S(1)}, bf16[256,4,128]{2,0,1:T(8,128)(2,1)S(1)}, u32[]{:S(2)}, u32[]{:S(2)}) %collective-permute-start.1) | collective-permute-done | bytes 262176 | tf_op jit(solution)/shard_map/ppermute | solution.py:92
  12.6 1.3 %collective-permute-start.3 = (bf16[256,4,128]{2,0,1:T(8,128)(2,1)S(1)}, bf16[256,4,128]{2,0,1:T(8,128)(2,1)S(1)}, u32[]{:S(2)}, u32[]{:S(2)}) collective-permute-start(bf16[256,4,128]{2,0,1:T(8,128)(2,1)S(1)} %collective-permute-done.1), channel_id=1, source_target_pairs={{8,16},{12,20},{16,24},{20,28},{9,17},{13,21},{17,25},{21,29},{10,... | collective-permute-start | bytes 786440 | tf_op jit(solution)/shard_map/ppermute | solution.py:92
  13.9 3.4 %collective-permute-start.2 = (bf16[256,4,128]{2,0,1:T(8,128)(2,1)S(1)}, bf16[256,4,128]{2,0,1:T(8,128)(2,1)S(1)}, u32[]{:S(2)}, u32[]{:S(2)}) collective-permute-start(bf16[256,4,128]{2,0,1:T(8,128)(2,1)S(1)} %collective-permute-done.1), channel_id=1, source_target_pairs={{8,12},{16,20},{24,28},{12,8},{20,16},{28,24},{9,13},{17,21},{25,2... | collective-permute-start | bytes 786440 | tf_op jit(solution)/shard_map/ppermute | solution.py:93
  17.4 0.5 fusion.71
  17.8 0.0 collective-permute-done
  17.9 0.5 fusion.73
  18.3 0.3 convolution_add_fusion.4
  18.7 0.3 convolution_add_fusion.3
  19.0 2.6 %collective-permute-done.3 = bf16[256,4,128]{2,0,1:T(8,128)(2,1)S(1)} collective-permute-done((bf16[256,4,128]{2,0,1:T(8,128)(2,1)S(1)}, bf16[256,4,128]{2,0,1:T(8,128)(2,1)S(1)}, u32[]{:S(2)}, u32[]{:S(2)}) %collective-permute-start.3) | collective-permute-done | bytes 262176 | tf_op jit(solution)/shard_map/ppermute | solution.py:92
  21.7 1.3 %collective-permute-start.5 = (bf16[256,4,128]{2,0,1:T(8,128)(2,1)S(1)}, bf16[256,4,128]{2,0,1:T(8,128)(2,1)S(1)}, u32[]{:S(2)}, u32[]{:S(2)}) collective-permute-start(bf16[256,4,128]{2,0,1:T(8,128)(2,1)S(1)} %collective-permute-done.3), channel_id=1, source_target_pairs={{16,24},{20,28},{17,25},{21,29},{18,26},{22,30},{19,27},{23,31}} | collective-permute-start | bytes 786440 | tf_op jit(solution)/shard_map/ppermute | solution.py:92
  23.0 3.4 %collective-permute-start.4 = (bf16[256,4,128]{2,0,1:T(8,128)(2,1)S(1)}, bf16[256,4,128]{2,0,1:T(8,128)(2,1)S(1)}, u32[]{:S(2)}, u32[]{:S(2)}) collective-permute-start(bf16[256,4,128]{2,0,1:T(8,128)(2,1)S(1)} %collective-permute-done.3), channel_id=1, source_target_pairs={{16,20},{24,28},{20,16},{28,24},{17,21},{25,29},{21,17},{29,25},{1... | collective-permute-start | bytes 786440 | tf_op jit(solution)/shard_map/ppermute | solution.py:93
  26.4 0.5 fusion.69
  26.9 0.3 fusion.51
  27.3 0.0 collective-permute-done.2
  27.3 0.5 fusion.70
  27.7 0.3 fusion.45
  28.1 1.9 %collective-permute-done.5 = bf16[256,4,128]{2,0,1:T(8,128)(2,1)S(1)} collective-permute-done((bf16[256,4,128]{2,0,1:T(8,128)(2,1)S(1)}, bf16[256,4,128]{2,0,1:T(8,128)(2,1)S(1)}, u32[]{:S(2)}, u32[]{:S(2)}) %collective-permute-start.5) | collective-permute-done | bytes 262176 | tf_op jit(solution)/shard_map/ppermute | solution.py:92
  30.0 3.4 %collective-permute-start.6 = (bf16[256,4,128]{2,0,1:T(8,128)(2,1)S(1)}, bf16[256,4,128]{2,0,1:T(8,128)(2,1)S(1)}, u32[]{:S(2)}, u32[]{:S(2)}) collective-permute-start(bf16[256,4,128]{2,0,1:T(8,128)(2,1)S(1)} %collective-permute-done.5), channel_id=1, source_target_pairs={{24,28},{28,24},{25,29},{29,25},{26,30},{30,26},{27,31},{31,27}} | collective-permute-start | bytes 786440 | tf_op jit(solution)/shard_map/ppermute | solution.py:93
  33.4 0.5 fusion.67
  33.9 0.3 fusion.48
  34.2 0.0 collective-permute-done.4
  34.2 0.5 fusion.68
  34.7 0.0 copy-start
  34.7 0.4 fusion.44
  35.1 3.1 %collective-permute-done.6 = bf16[256,4,128]{2,0,1:T(8,128)(2,1)S(1)} collective-permute-done((bf16[256,4,128]{2,0,1:T(8,128)(2,1)S(1)}, bf16[256,4,128]{2,0,1:T(8,128)(2,1)S(1)}, u32[]{:S(2)}, u32[]{:S(2)}) %collective-permute-start.6) | collective-permute-done | bytes 262176 | tf_op jit(solution)/shard_map/ppermute | solution.py:93
  38.2 0.5 fusion.66
  38.7 0.4 fusion.46
  39.1 0.1 collective-permute-start.8
  39.2 1.6 %collective-permute-start.7 = (bf16[2,2,256,128]{3,2,1,0:T(8,128)(2,1)S(1)}, bf16[2,2,256,128]{3,2,1,0:T(8,128)(2,1)S(1)}, u32[]{:S(2)}, u32[]{:S(2)}) collective-permute-start(bf16[2,2,256,128]{3,2,1,0:T(8,128)(2,1)S(1)} %fusion.46), channel_id=1, source_target_pairs={{0,2},{1,3},{2,0},{3,1},{4,6},{5,7},{6,4},{7,5},{8,10},{9,11},{10,... | collective-permute-start | bytes 786440 | tf_op jit(solution)/shard_map/ppermute | solution.py:106
  40.7 0.3 constant_dynamic-slice_fusion
  41.0 0.4 convolution_bitcast_fusion.3
  41.4 6.5 %collective-permute-done.7 = bf16[2,2,256,128]{3,2,1,0:T(8,128)(2,1)S(1)} collective-permute-done((bf16[2,2,256,128]{3,2,1,0:T(8,128)(2,1)S(1)}, bf16[2,2,256,128]{3,2,1,0:T(8,128)(2,1)S(1)}, u32[]{:S(2)}, u32[]{:S(2)}) %collective-permute-start.7) | collective-permute-done | bytes 262176 | tf_op jit(solution)/shard_map/ppermute | solution.py:106
  47.9 0.0 collective-permute-start.9
  47.9 0.0 collective-permute-done.8
  47.9 0.4 convolution_bitcast_fusion.1
  48.3 0.0 copy-start.3
  48.3 0.0 copy-start.2
  48.3 0.4 fusion.41
  48.7 0.8 %collective-permute-done.9 = bf16[2,2,256,128]{3,2,1,0:T(8,128)(2,1)S(1)} collective-permute-done((bf16[2,2,256,128]{3,2,1,0:T(8,128)(2,1)S(1)}, bf16[2,2,256,128]{3,2,1,0:T(8,128)(2,1)S(1)}, u32[]{:S(2)}, u32[]{:S(2)}) %collective-permute-start.9) | collective-permute-done | bytes 262176 | tf_op jit(solution)/shard_map/ppermute | solution.py:106
  49.5 0.5 multiply_reduce_fusion
  49.9 1.3 %collective-permute-start.12 = (f32[256]{0:T(256)S(1)}, f32[256]{0:T(256)S(1)}, u32[]{:S(2)}, u32[]{:S(2)}) collective-permute-start(f32[256]{0:T(256)S(1)} %get-tuple-element.31), channel_id=1, source_target_pairs={{0,3},{1,2},{2,1},{3,0},{4,7},{5,6},{6,5},{7,4},{8,11},{9,10},{10,... | collective-permute-start | bytes 3080 | tf_op jit(solution)/shard_map/ppermute | solution.py:114
  51.2 0.6 collective-permute-start.11
  51.7 0.1 collective-permute-start.10
  51.8 0.0 copy-done.3
  51.8 1.1 %collective-permute-done.12 = f32[256]{0:T(256)S(1)} collective-permute-done((f32[256]{0:T(256)S(1)}, f32[256]{0:T(256)S(1)}, u32[]{:S(2)}, u32[]{:S(2)}) %collective-permute-start.12) | collective-permute-done | bytes 1056 | tf_op jit(solution)/shard_map/ppermute | solution.py:114
  53.0 1.8 %collective-permute-done.11 = f32[256]{0:T(256)S(1)} collective-permute-done((f32[256]{0:T(256)S(1)}, f32[256]{0:T(256)S(1)}, u32[]{:S(2)}, u32[]{:S(2)}) %collective-permute-start.11) | collective-permute-done | bytes 1056 | tf_op jit(solution)/shard_map/ppermute | solution.py:114
  54.8 0.0 collective-permute-done.10
  54.8 0.0 copy-done.2
  54.8 0.9 %add_convert_fusion = bf16[256,768]{1,0:T(8,128)(2,1)} fusion(f32[256,768]{1,0:T(8,128)S(1)} %get-tuple-element.32, bf16[256,768]{1,0:T(8,128)(2,1)S(1)} %copy-done.2, f32[768]{0:T(1024)S(1)} %convert_element_type.68, f32[256]{0:T(256)S(1)} %add_rsqrt_fusion), kind=kLoop, calls=%fused_computation.64 | loop fusion | flops 983040 | bytes 1576960 | tf_op jit(solution)/shard_map/convert_element_type | solution.py:189
  (9 shorter events, 0.1 us)
Async XLA Ops:
  2.7 9.9 %collective-permute-start.1 = (bf16[256,4,128]{2,0,1:T(8,128)(2,1)S(1)}, bf16[256,4,128]{2,0,1:T(8,128)(2,1)S(1)}, u32[]{:S(2)}, u32[]{:S(2)}) collective-permute-start(bf16[256,4,128]{2,0,1:T(8,128)(2,1)S(1)} %pad_maximum_fusion.1), channel_id=1, source_target_pairs={{0,8},{4,12},{8,16},{12,20},{16,24},{20,28},{1,9},{5,13},{9,17},{1... | collective-permute-start | bytes 786440 | tf_op jit(solution)/shard_map/ppermute | solution.py:92
  4.0 13.8 %collective-permute-start = (bf16[256,4,128]{2,0,1:T(8,128)(2,1)S(1)}, bf16[256,4,128]{2,0,1:T(8,128)(2,1)S(1)}, u32[]{:S(2)}, u32[]{:S(2)}) collective-permute-start(bf16[256,4,128]{2,0,1:T(8,128)(2,1)S(1)} %pad_maximum_fusion.1), channel_id=1, source_target_pairs={{0,4},{8,12},{16,20},{24,28},{1,5},{9,13},{17,21},{25,29},{2,6},{1... | collective-permute-start | bytes 786440 | tf_op jit(solution)/shard_map/ppermute | solution.py:93
  8.5 1.5 %copy-start.1 = (bf16[256,2,128]{2,1,0:T(2,128)(2,1)S(1)}, bf16[256,2,128]{2,1,0:T(2,128)(2,1)}, u32[]{:S(2)}) copy-start(bf16[256,2,128]{2,1,0:T(2,128)(2,1)} %param.8) | copy-start | bytes 393220
  12.6 9.1 %collective-permute-start.3 = (bf16[256,4,128]{2,0,1:T(8,128)(2,1)S(1)}, bf16[256,4,128]{2,0,1:T(8,128)(2,1)S(1)}, u32[]{:S(2)}, u32[]{:S(2)}) collective-permute-start(bf16[256,4,128]{2,0,1:T(8,128)(2,1)S(1)} %collective-permute-done.1), channel_id=1, source_target_pairs={{8,16},{12,20},{16,24},{20,28},{9,17},{13,21},{17,25},{21,29},{10,... | collective-permute-start | bytes 786440 | tf_op jit(solution)/shard_map/ppermute | solution.py:92
  13.9 13.3 %collective-permute-start.2 = (bf16[256,4,128]{2,0,1:T(8,128)(2,1)S(1)}, bf16[256,4,128]{2,0,1:T(8,128)(2,1)S(1)}, u32[]{:S(2)}, u32[]{:S(2)}) collective-permute-start(bf16[256,4,128]{2,0,1:T(8,128)(2,1)S(1)} %collective-permute-done.1), channel_id=1, source_target_pairs={{8,12},{16,20},{24,28},{12,8},{20,16},{28,24},{9,13},{17,21},{25,2... | collective-permute-start | bytes 786440 | tf_op jit(solution)/shard_map/ppermute | solution.py:93
  21.7 8.3 %collective-permute-start.5 = (bf16[256,4,128]{2,0,1:T(8,128)(2,1)S(1)}, bf16[256,4,128]{2,0,1:T(8,128)(2,1)S(1)}, u32[]{:S(2)}, u32[]{:S(2)}) collective-permute-start(bf16[256,4,128]{2,0,1:T(8,128)(2,1)S(1)} %collective-permute-done.3), channel_id=1, source_target_pairs={{16,24},{20,28},{17,25},{21,29},{18,26},{22,30},{19,27},{23,31}} | collective-permute-start | bytes 786440 | tf_op jit(solution)/shard_map/ppermute | solution.py:92
  23.0 11.2 %collective-permute-start.4 = (bf16[256,4,128]{2,0,1:T(8,128)(2,1)S(1)}, bf16[256,4,128]{2,0,1:T(8,128)(2,1)S(1)}, u32[]{:S(2)}, u32[]{:S(2)}) collective-permute-start(bf16[256,4,128]{2,0,1:T(8,128)(2,1)S(1)} %collective-permute-done.3), channel_id=1, source_target_pairs={{16,20},{24,28},{20,16},{28,24},{17,21},{25,29},{21,17},{29,25},{1... | collective-permute-start | bytes 786440 | tf_op jit(solution)/shard_map/ppermute | solution.py:93
  30.0 8.3 %collective-permute-start.6 = (bf16[256,4,128]{2,0,1:T(8,128)(2,1)S(1)}, bf16[256,4,128]{2,0,1:T(8,128)(2,1)S(1)}, u32[]{:S(2)}, u32[]{:S(2)}) collective-permute-start(bf16[256,4,128]{2,0,1:T(8,128)(2,1)S(1)} %collective-permute-done.5), channel_id=1, source_target_pairs={{24,28},{28,24},{25,29},{29,25},{26,30},{30,26},{27,31},{31,27}} | collective-permute-start | bytes 786440 | tf_op jit(solution)/shard_map/ppermute | solution.py:93
  34.7 6.0 %copy-start = (bf16[16,128,768]{2,1,0:T(8,128)(2,1)S(1)}, bf16[16,128,768]{2,1,0:T(8,128)(2,1)}, u32[]{:S(2)}) copy-start(bf16[16,128,768]{2,1,0:T(8,128)(2,1)} %param.10) | copy-start | bytes 9437188
  39.1 8.8 %collective-permute-start.8 = (bf16[2,2,256,128]{3,2,1,0:T(8,128)(2,1)S(1)}, bf16[2,2,256,128]{3,2,1,0:T(8,128)(2,1)S(1)}, u32[]{:S(2)}, u32[]{:S(2)}) collective-permute-start(bf16[2,2,256,128]{3,2,1,0:T(8,128)(2,1)S(1)} %fusion.46), channel_id=1, source_target_pairs={{0,1},{1,0},{2,3},{3,2},{4,5},{5,4},{6,7},{7,6},{8,9},{9,8},{10,11... | collective-permute-start | bytes 786440 | tf_op jit(solution)/shard_map/ppermute | solution.py:106
  39.2 8.7 %collective-permute-start.7 = (bf16[2,2,256,128]{3,2,1,0:T(8,128)(2,1)S(1)}, bf16[2,2,256,128]{3,2,1,0:T(8,128)(2,1)S(1)}, u32[]{:S(2)}, u32[]{:S(2)}) collective-permute-start(bf16[2,2,256,128]{3,2,1,0:T(8,128)(2,1)S(1)} %fusion.46), channel_id=1, source_target_pairs={{0,2},{1,3},{2,0},{3,1},{4,6},{5,7},{6,4},{7,5},{8,10},{9,11},{10,... | collective-permute-start | bytes 786440 | tf_op jit(solution)/shard_map/ppermute | solution.py:106
  47.9 1.5 %collective-permute-start.9 = (bf16[2,2,256,128]{3,2,1,0:T(8,128)(2,1)S(1)}, bf16[2,2,256,128]{3,2,1,0:T(8,128)(2,1)S(1)}, u32[]{:S(2)}, u32[]{:S(2)}) collective-permute-start(bf16[2,2,256,128]{3,2,1,0:T(8,128)(2,1)S(1)} %collective-permute-done.7), channel_id=1, source_target_pairs={{0,1},{1,0},{2,3},{3,2},{4,5},{5,4},{6,7},{7,6},{8,9},{9,8},{10,11... | collective-permute-start | bytes 786440 | tf_op jit(solution)/shard_map/ppermute | solution.py:106
  48.3 3.5 %copy-start.3 = (bf16[768]{0:T(1024)(128)(2,1)S(1)}, bf16[768]{0:T(1024)(128)(2,1)}, u32[]{:S(2)}) copy-start(bf16[768]{0:T(1024)(128)(2,1)} %param.11) | copy-start | bytes 4612
  48.3 6.5 %copy-start.2 = (bf16[256,768]{1,0:T(8,128)(2,1)S(1)}, bf16[256,768]{1,0:T(8,128)(2,1)}, u32[]{:S(2)}) copy-start(bf16[256,768]{1,0:T(8,128)(2,1)} %param.9) | copy-start | bytes 1179652
  49.9 3.1 %collective-permute-start.12 = (f32[256]{0:T(256)S(1)}, f32[256]{0:T(256)S(1)}, u32[]{:S(2)}, u32[]{:S(2)}) collective-permute-start(f32[256]{0:T(256)S(1)} %get-tuple-element.31), channel_id=1, source_target_pairs={{0,3},{1,2},{2,1},{3,0},{4,7},{5,6},{6,5},{7,4},{8,11},{9,10},{10,... | collective-permute-start | bytes 3080 | tf_op jit(solution)/shard_map/ppermute | solution.py:114
  51.2 3.6 %collective-permute-start.11 = (f32[256]{0:T(256)S(1)}, f32[256]{0:T(256)S(1)}, u32[]{:S(2)}, u32[]{:S(2)}) collective-permute-start(f32[256]{0:T(256)S(1)} %get-tuple-element.31), channel_id=1, source_target_pairs={{0,2},{1,3},{2,0},{3,1},{4,6},{5,7},{6,4},{7,5},{8,10},{9,11},{10,... | collective-permute-start | bytes 3080 | tf_op jit(solution)/shard_map/ppermute | solution.py:114
  51.7 3.0 %collective-permute-start.10 = (f32[256]{0:T(256)S(1)}, f32[256]{0:T(256)S(1)}, u32[]{:S(2)}, u32[]{:S(2)}) collective-permute-start(f32[256]{0:T(256)S(1)} %get-tuple-element.31), channel_id=1, source_target_pairs={{0,1},{1,0},{2,3},{3,2},{4,5},{5,4},{6,7},{7,6},{8,9},{9,8},{10,11... | collective-permute-start | bytes 3080 | tf_op jit(solution)/shard_map/ppermute | solution.py:114

commit v8 on v7

--- a/solution.py
+++ b/solution.py
@@ -88,13 +88,24 @@
 
     line = jnp.concatenate([key_block, value_block], axis=1)
     for step in range(1, outer + 1):
+        last_forward = step == outer - 1
+        if step == outer and outer >= 2:
+            break
         if step < outer:
             arrived = lax.ppermute(line, "ctx", forward(step))
         crossed = lax.ppermute(line, "ctx", across(step))
+        if last_forward:
+            diagonal = lax.ppermute(
+                line,
+                "ctx",
+                [(source, 2 * (source // 2) + 3 - source % 2) for source, unused in forward(step)],
+            )
         state = attend_stacked(state, crossed, 2 * (plane - step + 1) + 1 - side)
         if step < outer:
             state = attend_stacked(state, arrived, device_index - 2 * step)
             line = arrived
+        if last_forward:
+            state = attend_stacked(state, diagonal, 2 * (plane - step) + 1 - side)
     return state
 
 

time: 56 us -> 55.5 us (level)
  starting transfers between devices: 21.1 us -> 19 us
  waiting for transfers between devices: 20.1 us -> 21.6 us
    ppermute x0 -> x1, waiting for transfers between devices: none -> 4.14 us  [along_lines(): lax.ppermute(line, 'ctx', [(source, 2 * (source // 2) + 3 - source % 2) f...]
    ppermute x4 -> x3, starting transfers between devices: 13.7 us -> 10.3 us  [along_lines(): crossed = lax.ppermute(line, 'ctx', across(step))]
    ppermute x4 -> x3, waiting for transfers between devices: 3.14 us -> 0.01 us  [along_lines(): crossed = lax.ppermute(line, 'ctx', across(step))]
    ppermute x0 -> x1, starting transfers between devices: none -> 1.28 us  [along_lines(): lax.ppermute(line, 'ctx', [(source, 2 * (source // 2) + 3 - source % 2) f...]
  transfers between devices with their start and end apart: 13 -> 13, of which waited for: 8 -> 8; matrix products, arithmetic and copies ran while one was open for 16% -> 15% of each run, Pallas kernels for 0% -> 0%
where the time goes in v8:
time: 55.5 us; the launch traced here: 55.1 us
  waiting for transfers between devices  21.6 us (39%)
  starting transfers between devices  19 us (34%)
  matrix products  8.3 us (15%)
  other arithmetic  4.53 us (8%)
  local copies, waits for them, and re-layouts  1.31 us (2%)
    ppermute x3, starting transfers between devices, along_lines(): crossed = lax.ppermute(line, 'ctx', across(step))  10.3 us
    ppermute x3, waiting for transfers between devices, exchanged(): lax.ppermute(held, 'tp', pairs)  7.26 us
    ppermute x3, waiting for transfers between devices, along_lines(): arrived = lax.ppermute(line, 'ctx', forward(step))  7.26 us
    ppermute x1, waiting for transfers between devices, along_lines(): lax.ppermute(line, 'ctx', [(source, 2 * (source // 2) + 3 - source % 2) f...  4.14 us
    dot_general x8, matrix products, attend_block(): jnp.einsum('sgrh,kgh->grsk', rotary_queries, key_block, preferred_element...  3.91 us
    ppermute x3, starting transfers between devices, along_lines(): arrived = lax.ppermute(line, 'ctx', forward(step))  3.86 us
    ppermute x3, waiting for transfers between devices, summed(): lax.ppermute(partial, 'tp', [(source, source ^ offset) for source in rang...  2.94 us
    dot_general x8, matrix products, attend_block(): jnp.einsum('grsk,kgh->grsh', weights.astype(jnp.bfloat16), value_block, p...  2.84 us
  transfers between devices with their start and end apart: 13, of which 8 were waited for; matrix products, arithmetic and copies ran while one was open for 15% of the time, Pallas kernels for 0%

profile of v8, /device:TPU:24, one launch (start us, length us, event | category | flops | bytes accessed | tf_op | source)
XLA Modules:
  0.0 55.1 jit_solution(3865936587561855816)
XLA Ops:
  0.0 0.9 %copy.12 = bf16[256,2,128]{2,0,1:T(8,128)(2,1)S(1)} copy(bf16[256,2,128]{2,1,0:T(2,128)(2,1)} %param.8) | data formatting | bytes 262144 | tf_op args[2]
  1.0 0.9 %copy_convert_fusion = f32[256,2,128]{2,0,1:T(8,128)S(1)} fusion(bf16[256,2,128]{2,1,0:T(2,128)(2,1)} %param.7), kind=kLoop, calls=%fused_computation.108 | loop fusion | flops 65536 | bytes 393216 | tf_op jit(solution)/shard_map/convert_element_type | solution.py:140
  1.9 0.5 multiply_cosine_fusion
  2.4 0.2 subtract_convert_fusion.1
  2.6 0.1 pad_maximum_fusion.1
  2.7 1.3 %collective-permute-start.1 = (bf16[256,4,128]{2,0,1:T(8,128)(2,1)S(1)}, bf16[256,4,128]{2,0,1:T(8,128)(2,1)S(1)}, u32[]{:S(2)}, u32[]{:S(2)}) collective-permute-start(bf16[256,4,128]{2,0,1:T(8,128)(2,1)S(1)} %pad_maximum_fusion.1), channel_id=1, source_target_pairs={{0,8},{4,12},{8,16},{12,20},{16,24},{20,28},{1,9},{5,13},{9,17},{1... | collective-permute-start | bytes 786440 | tf_op jit(solution)/shard_map/ppermute | solution.py:95
  4.0 3.4 %collective-permute-start = (bf16[256,4,128]{2,0,1:T(8,128)(2,1)S(1)}, bf16[256,4,128]{2,0,1:T(8,128)(2,1)S(1)}, u32[]{:S(2)}, u32[]{:S(2)}) collective-permute-start(bf16[256,4,128]{2,0,1:T(8,128)(2,1)S(1)} %pad_maximum_fusion.1), channel_id=1, source_target_pairs={{0,4},{8,12},{16,20},{24,28},{1,5},{9,13},{17,21},{25,29},{2,6},{1... | collective-permute-start | bytes 786440 | tf_op jit(solution)/shard_map/ppermute | solution.py:96
  7.5 1.0 %convert_element_type.58 = f32[256,4,128]{2,1,0:T(4,128)S(1)} convert(bf16[256,4,128]{2,1,0:T(4,128)(2,1)} %param.6) | non-fusion elementwise | flops 131072 | bytes 786432 | tf_op jit(solution)/shard_map/convert_element_type | solution.py:138
  8.5 0.0 copy-start.1
  8.5 0.5 subtract_convert_fusion
  9.1 0.1 pad_maximum_fusion
  9.3 0.1 fusion.61
  9.4 0.5 fusion.74
  10.0 0.0 copy-done.1
  10.0 0.3 fusion.58
  10.4 2.2 %collective-permute-done.1 = bf16[256,4,128]{2,0,1:T(8,128)(2,1)S(1)} collective-permute-done((bf16[256,4,128]{2,0,1:T(8,128)(2,1)S(1)}, bf16[256,4,128]{2,0,1:T(8,128)(2,1)S(1)}, u32[]{:S(2)}, u32[]{:S(2)}) %collective-permute-start.1) | collective-permute-done | bytes 262176 | tf_op jit(solution)/shard_map/ppermute | solution.py:95
  12.6 1.3 %collective-permute-start.3 = (bf16[256,4,128]{2,0,1:T(8,128)(2,1)S(1)}, bf16[256,4,128]{2,0,1:T(8,128)(2,1)S(1)}, u32[]{:S(2)}, u32[]{:S(2)}) collective-permute-start(bf16[256,4,128]{2,0,1:T(8,128)(2,1)S(1)} %collective-permute-done.1), channel_id=1, source_target_pairs={{8,16},{12,20},{16,24},{20,28},{9,17},{13,21},{17,25},{21,29},{10,... | collective-permute-start | bytes 786440 | tf_op jit(solution)/shard_map/ppermute | solution.py:95
  13.9 3.4 %collective-permute-start.2 = (bf16[256,4,128]{2,0,1:T(8,128)(2,1)S(1)}, bf16[256,4,128]{2,0,1:T(8,128)(2,1)S(1)}, u32[]{:S(2)}, u32[]{:S(2)}) collective-permute-start(bf16[256,4,128]{2,0,1:T(8,128)(2,1)S(1)} %collective-permute-done.1), channel_id=1, source_target_pairs={{8,12},{16,20},{24,28},{12,8},{20,16},{28,24},{9,13},{17,21},{25,2... | collective-permute-start | bytes 786440 | tf_op jit(solution)/shard_map/ppermute | solution.py:96
  17.4 0.5 fusion.73
  17.8 0.0 collective-permute-done
  17.9 0.5 fusion.75
  18.3 0.3 convolution_add_fusion.3
  18.7 0.3 convolution_add_fusion.2
  19.0 2.6 %collective-permute-done.3 = bf16[256,4,128]{2,0,1:T(8,128)(2,1)S(1)} collective-permute-done((bf16[256,4,128]{2,0,1:T(8,128)(2,1)S(1)}, bf16[256,4,128]{2,0,1:T(8,128)(2,1)S(1)}, u32[]{:S(2)}, u32[]{:S(2)}) %collective-permute-start.3) | collective-permute-done | bytes 262176 | tf_op jit(solution)/shard_map/ppermute | solution.py:95
  21.7 1.3 %collective-permute-start.6 = (bf16[256,4,128]{2,0,1:T(8,128)(2,1)S(1)}, bf16[256,4,128]{2,0,1:T(8,128)(2,1)S(1)}, u32[]{:S(2)}, u32[]{:S(2)}) collective-permute-start(bf16[256,4,128]{2,0,1:T(8,128)(2,1)S(1)} %collective-permute-done.3), channel_id=1, source_target_pairs={{16,28},{20,24},{17,29},{21,25},{18,30},{22,26},{19,31},{23,27}} | collective-permute-start | bytes 786440 | tf_op jit(solution)/shard_map/ppermute | solution.py:98
  23.0 1.3 %collective-permute-start.5 = (bf16[256,4,128]{2,0,1:T(8,128)(2,1)S(1)}, bf16[256,4,128]{2,0,1:T(8,128)(2,1)S(1)}, u32[]{:S(2)}, u32[]{:S(2)}) collective-permute-start(bf16[256,4,128]{2,0,1:T(8,128)(2,1)S(1)} %collective-permute-done.3), channel_id=1, source_target_pairs={{16,24},{20,28},{17,25},{21,29},{18,26},{22,30},{19,27},{23,31}} | collective-permute-start | bytes 786440 | tf_op jit(solution)/shard_map/ppermute | solution.py:95
  24.3 3.4 %collective-permute-start.4 = (bf16[256,4,128]{2,0,1:T(8,128)(2,1)S(1)}, bf16[256,4,128]{2,0,1:T(8,128)(2,1)S(1)}, u32[]{:S(2)}, u32[]{:S(2)}) collective-permute-start(bf16[256,4,128]{2,0,1:T(8,128)(2,1)S(1)} %collective-permute-done.3), channel_id=1, source_target_pairs={{16,20},{24,28},{20,16},{28,24},{17,21},{25,29},{21,17},{29,25},{1... | collective-permute-start | bytes 786440 | tf_op jit(solution)/shard_map/ppermute | solution.py:96
  27.7 0.5 fusion.71
  28.2 0.4 fusion.53
  28.6 0.0 collective-permute-done.2
  28.6 0.5 fusion.72
  29.1 0.4 fusion.46
  29.4 4.1 %collective-permute-done.6 = bf16[256,4,128]{2,0,1:T(8,128)(2,1)S(1)} collective-permute-done((bf16[256,4,128]{2,0,1:T(8,128)(2,1)S(1)}, bf16[256,4,128]{2,0,1:T(8,128)(2,1)S(1)}, u32[]{:S(2)}, u32[]{:S(2)}) %collective-permute-start.6) | collective-permute-done | bytes 262176 | tf_op jit(solution)/shard_map/ppermute | solution.py:98
  33.6 0.5 fusion.68
  34.0 2.4 %collective-permute-done.5 = bf16[256,4,128]{2,0,1:T(8,128)(2,1)S(1)} collective-permute-done((bf16[256,4,128]{2,0,1:T(8,128)(2,1)S(1)}, bf16[256,4,128]{2,0,1:T(8,128)(2,1)S(1)}, u32[]{:S(2)}, u32[]{:S(2)}) %collective-permute-start.5) | collective-permute-done | bytes 262176 | tf_op jit(solution)/shard_map/ppermute | solution.py:95
  36.4 0.5 fusion.69
  36.9 0.0 collective-permute-done.4
  36.9 0.5 fusion.70
  37.4 0.0 copy-start
  37.4 0.4 fusion.48
  37.8 0.3 fusion.50
  38.1 0.4 fusion.47
  38.5 0.1 collective-permute-start.8
  38.6 1.5 %collective-permute-start.7 = (bf16[2,2,256,128]{3,2,1,0:T(8,128)(2,1)S(1)}, bf16[2,2,256,128]{3,2,1,0:T(8,128)(2,1)S(1)}, u32[]{:S(2)}, u32[]{:S(2)}) collective-permute-start(bf16[2,2,256,128]{3,2,1,0:T(8,128)(2,1)S(1)} %fusion.47), channel_id=1, source_target_pairs={{0,2},{1,3},{2,0},{3,1},{4,6},{5,7},{6,4},{7,5},{8,10},{9,11},{10,... | collective-permute-start | bytes 786440 | tf_op jit(solution)/shard_map/ppermute | solution.py:117
  40.2 0.0 copy-done
  40.2 0.3 constant_dynamic-slice_fusion
  40.4 0.4 convolution_bitcast_fusion.3
  40.8 6.5 %collective-permute-done.7 = bf16[2,2,256,128]{3,2,1,0:T(8,128)(2,1)S(1)} collective-permute-done((bf16[2,2,256,128]{3,2,1,0:T(8,128)(2,1)S(1)}, bf16[2,2,256,128]{3,2,1,0:T(8,128)(2,1)S(1)}, u32[]{:S(2)}, u32[]{:S(2)}) %collective-permute-start.7) | collective-permute-done | bytes 262176 | tf_op jit(solution)/shard_map/ppermute | solution.py:117
  47.3 0.0 collective-permute-start.9
  47.3 0.0 collective-permute-done.8
  47.3 0.4 convolution_bitcast_fusion.1
  47.7 0.0 copy-start.3
  47.7 0.0 copy-start.2
  47.7 0.4 fusion.41
  48.1 0.7 %collective-permute-done.9 = bf16[2,2,256,128]{3,2,1,0:T(8,128)(2,1)S(1)} collective-permute-done((bf16[2,2,256,128]{3,2,1,0:T(8,128)(2,1)S(1)}, bf16[2,2,256,128]{3,2,1,0:T(8,128)(2,1)S(1)}, u32[]{:S(2)}, u32[]{:S(2)}) %collective-permute-start.9) | collective-permute-done | bytes 262176 | tf_op jit(solution)/shard_map/ppermute | solution.py:117
  48.9 0.5 multiply_reduce_fusion
  49.3 1.3 %collective-permute-start.12 = (f32[256]{0:T(256)S(1)}, f32[256]{0:T(256)S(1)}, u32[]{:S(2)}, u32[]{:S(2)}) collective-permute-start(f32[256]{0:T(256)S(1)} %get-tuple-element.31), channel_id=1, source_target_pairs={{0,3},{1,2},{2,1},{3,0},{4,7},{5,6},{6,5},{7,4},{8,11},{9,10},{10,... | collective-permute-start | bytes 3080 | tf_op jit(solution)/shard_map/ppermute | solution.py:125
  50.6 0.6 %collective-permute-start.11 = (f32[256]{0:T(256)S(1)}, f32[256]{0:T(256)S(1)}, u32[]{:S(2)}, u32[]{:S(2)}) collective-permute-start(f32[256]{0:T(256)S(1)} %get-tuple-element.31), channel_id=1, source_target_pairs={{0,2},{1,3},{2,0},{3,1},{4,6},{5,7},{6,4},{7,5},{8,10},{9,11},{10,... | collective-permute-start | bytes 3080 | tf_op jit(solution)/shard_map/ppermute | solution.py:125
  51.2 0.1 collective-permute-start.10
  51.2 0.0 copy-done.3
  51.2 1.1 %collective-permute-done.12 = f32[256]{0:T(256)S(1)} collective-permute-done((f32[256]{0:T(256)S(1)}, f32[256]{0:T(256)S(1)}, u32[]{:S(2)}, u32[]{:S(2)}) %collective-permute-start.12) | collective-permute-done | bytes 1056 | tf_op jit(solution)/shard_map/ppermute | solution.py:125
  52.4 1.8 %collective-permute-done.11 = f32[256]{0:T(256)S(1)} collective-permute-done((f32[256]{0:T(256)S(1)}, f32[256]{0:T(256)S(1)}, u32[]{:S(2)}, u32[]{:S(2)}) %collective-permute-start.11) | collective-permute-done | bytes 1056 | tf_op jit(solution)/shard_map/ppermute | solution.py:125
  54.2 0.0 collective-permute-done.10
  54.2 0.9 %add_convert_fusion = bf16[256,768]{1,0:T(8,128)(2,1)} fusion(f32[256,768]{1,0:T(8,128)S(1)} %get-tuple-element.32, bf16[256,768]{1,0:T(8,128)(2,1)S(1)} %copy-done.2, f32[768]{0:T(1024)S(1)} %convert_element_type.68, f32[256]{0:T(256)S(1)} %add_rsqrt_fusion), kind=kLoop, calls=%fused_computation.64 | loop fusion | flops 983040 | bytes 1576960 | tf_op jit(solution)/shard_map/convert_element_type | solution.py:200
  (9 shorter events, 0.1 us)
Async XLA Ops:
  2.7 9.9 %collective-permute-start.1 = (bf16[256,4,128]{2,0,1:T(8,128)(2,1)S(1)}, bf16[256,4,128]{2,0,1:T(8,128)(2,1)S(1)}, u32[]{:S(2)}, u32[]{:S(2)}) collective-permute-start(bf16[256,4,128]{2,0,1:T(8,128)(2,1)S(1)} %pad_maximum_fusion.1), channel_id=1, source_target_pairs={{0,8},{4,12},{8,16},{12,20},{16,24},{20,28},{1,9},{5,13},{9,17},{1... | collective-permute-start | bytes 786440 | tf_op jit(solution)/shard_map/ppermute | solution.py:95
  4.0 13.8 %collective-permute-start = (bf16[256,4,128]{2,0,1:T(8,128)(2,1)S(1)}, bf16[256,4,128]{2,0,1:T(8,128)(2,1)S(1)}, u32[]{:S(2)}, u32[]{:S(2)}) collective-permute-start(bf16[256,4,128]{2,0,1:T(8,128)(2,1)S(1)} %pad_maximum_fusion.1), channel_id=1, source_target_pairs={{0,4},{8,12},{16,20},{24,28},{1,5},{9,13},{17,21},{25,29},{2,6},{1... | collective-permute-start | bytes 786440 | tf_op jit(solution)/shard_map/ppermute | solution.py:96
  8.5 1.5 %copy-start.1 = (bf16[256,2,128]{2,1,0:T(2,128)(2,1)S(1)}, bf16[256,2,128]{2,1,0:T(2,128)(2,1)}, u32[]{:S(2)}) copy-start(bf16[256,2,128]{2,1,0:T(2,128)(2,1)} %param.8) | copy-start | bytes 393220
  12.6 9.1 %collective-permute-start.3 = (bf16[256,4,128]{2,0,1:T(8,128)(2,1)S(1)}, bf16[256,4,128]{2,0,1:T(8,128)(2,1)S(1)}, u32[]{:S(2)}, u32[]{:S(2)}) collective-permute-start(bf16[256,4,128]{2,0,1:T(8,128)(2,1)S(1)} %collective-permute-done.1), channel_id=1, source_target_pairs={{8,16},{12,20},{16,24},{20,28},{9,17},{13,21},{17,25},{21,29},{10,... | collective-permute-start | bytes 786440 | tf_op jit(solution)/shard_map/ppermute | solution.py:95
  13.9 14.6 %collective-permute-start.2 = (bf16[256,4,128]{2,0,1:T(8,128)(2,1)S(1)}, bf16[256,4,128]{2,0,1:T(8,128)(2,1)S(1)}, u32[]{:S(2)}, u32[]{:S(2)}) collective-permute-start(bf16[256,4,128]{2,0,1:T(8,128)(2,1)S(1)} %collective-permute-done.1), channel_id=1, source_target_pairs={{8,12},{16,20},{24,28},{12,8},{20,16},{28,24},{9,13},{17,21},{25,2... | collective-permute-start | bytes 786440 | tf_op jit(solution)/shard_map/ppermute | solution.py:96
  21.7 11.9 %collective-permute-start.6 = (bf16[256,4,128]{2,0,1:T(8,128)(2,1)S(1)}, bf16[256,4,128]{2,0,1:T(8,128)(2,1)S(1)}, u32[]{:S(2)}, u32[]{:S(2)}) collective-permute-start(bf16[256,4,128]{2,0,1:T(8,128)(2,1)S(1)} %collective-permute-done.3), channel_id=1, source_target_pairs={{16,28},{20,24},{17,29},{21,25},{18,30},{22,26},{19,31},{23,27}} | collective-permute-start | bytes 786440 | tf_op jit(solution)/shard_map/ppermute | solution.py:98
  23.0 13.4 %collective-permute-start.5 = (bf16[256,4,128]{2,0,1:T(8,128)(2,1)S(1)}, bf16[256,4,128]{2,0,1:T(8,128)(2,1)S(1)}, u32[]{:S(2)}, u32[]{:S(2)}) collective-permute-start(bf16[256,4,128]{2,0,1:T(8,128)(2,1)S(1)} %collective-permute-done.3), channel_id=1, source_target_pairs={{16,24},{20,28},{17,25},{21,29},{18,26},{22,30},{19,27},{23,31}} | collective-permute-start | bytes 786440 | tf_op jit(solution)/shard_map/ppermute | solution.py:95
  24.3 12.6 %collective-permute-start.4 = (bf16[256,4,128]{2,0,1:T(8,128)(2,1)S(1)}, bf16[256,4,128]{2,0,1:T(8,128)(2,1)S(1)}, u32[]{:S(2)}, u32[]{:S(2)}) collective-permute-start(bf16[256,4,128]{2,0,1:T(8,128)(2,1)S(1)} %collective-permute-done.3), channel_id=1, source_target_pairs={{16,20},{24,28},{20,16},{28,24},{17,21},{25,29},{21,17},{29,25},{1... | collective-permute-start | bytes 786440 | tf_op jit(solution)/shard_map/ppermute | solution.py:96
  37.4 2.8 %copy-start = (bf16[16,128,768]{2,1,0:T(8,128)(2,1)S(1)}, bf16[16,128,768]{2,1,0:T(8,128)(2,1)}, u32[]{:S(2)}) copy-start(bf16[16,128,768]{2,1,0:T(8,128)(2,1)} %param.10) | copy-start | bytes 9437188
  38.5 8.8 %collective-permute-start.8 = (bf16[2,2,256,128]{3,2,1,0:T(8,128)(2,1)S(1)}, bf16[2,2,256,128]{3,2,1,0:T(8,128)(2,1)S(1)}, u32[]{:S(2)}, u32[]{:S(2)}) collective-permute-start(bf16[2,2,256,128]{3,2,1,0:T(8,128)(2,1)S(1)} %fusion.47), channel_id=1, source_target_pairs={{0,1},{1,0},{2,3},{3,2},{4,5},{5,4},{6,7},{7,6},{8,9},{9,8},{10,11... | collective-permute-start | bytes 786440 | tf_op jit(solution)/shard_map/ppermute | solution.py:117
  38.6 8.7 %collective-permute-start.7 = (bf16[2,2,256,128]{3,2,1,0:T(8,128)(2,1)S(1)}, bf16[2,2,256,128]{3,2,1,0:T(8,128)(2,1)S(1)}, u32[]{:S(2)}, u32[]{:S(2)}) collective-permute-start(bf16[2,2,256,128]{3,2,1,0:T(8,128)(2,1)S(1)} %fusion.47), channel_id=1, source_target_pairs={{0,2},{1,3},{2,0},{3,1},{4,6},{5,7},{6,4},{7,5},{8,10},{9,11},{10,... | collective-permute-start | bytes 786440 | tf_op jit(solution)/shard_map/ppermute | solution.py:117
  47.3 1.5 %collective-permute-start.9 = (bf16[2,2,256,128]{3,2,1,0:T(8,128)(2,1)S(1)}, bf16[2,2,256,128]{3,2,1,0:T(8,128)(2,1)S(1)}, u32[]{:S(2)}, u32[]{:S(2)}) collective-permute-start(bf16[2,2,256,128]{3,2,1,0:T(8,128)(2,1)S(1)} %collective-permute-done.7), channel_id=1, source_target_pairs={{0,1},{1,0},{2,3},{3,2},{4,5},{5,4},{6,7},{7,6},{8,9},{9,8},{10,11... | collective-permute-start | bytes 786440 | tf_op jit(solution)/shard_map/ppermute | solution.py:117
  47.7 3.5 %copy-start.3 = (bf16[768]{0:T(1024)(128)(2,1)S(1)}, bf16[768]{0:T(1024)(128)(2,1)}, u32[]{:S(2)}) copy-start(bf16[768]{0:T(1024)(128)(2,1)} %param.11) | copy-start | bytes 4612
  47.7 6.5 %copy-start.2 = (bf16[256,768]{1,0:T(8,128)(2,1)S(1)}, bf16[256,768]{1,0:T(8,128)(2,1)}, u32[]{:S(2)}) copy-start(bf16[256,768]{1,0:T(8,128)(2,1)} %param.9) | copy-start | bytes 1179652
  49.3 3.1 %collective-permute-start.12 = (f32[256]{0:T(256)S(1)}, f32[256]{0:T(256)S(1)}, u32[]{:S(2)}, u32[]{:S(2)}) collective-permute-start(f32[256]{0:T(256)S(1)} %get-tuple-element.31), channel_id=1, source_target_pairs={{0,3},{1,2},{2,1},{3,0},{4,7},{5,6},{6,5},{7,4},{8,11},{9,10},{10,... | collective-permute-start | bytes 3080 | tf_op jit(solution)/shard_map/ppermute | solution.py:125
  50.6 3.6 %collective-permute-start.11 = (f32[256]{0:T(256)S(1)}, f32[256]{0:T(256)S(1)}, u32[]{:S(2)}, u32[]{:S(2)}) collective-permute-start(f32[256]{0:T(256)S(1)} %get-tuple-element.31), channel_id=1, source_target_pairs={{0,2},{1,3},{2,0},{3,1},{4,6},{5,7},{6,4},{7,5},{8,10},{9,11},{10,... | collective-permute-start | bytes 3080 | tf_op jit(solution)/shard_map/ppermute | solution.py:125
  51.2 3.0 %collective-permute-start.10 = (f32[256]{0:T(256)S(1)}, f32[256]{0:T(256)S(1)}, u32[]{:S(2)}, u32[]{:S(2)}) collective-permute-start(f32[256]{0:T(256)S(1)} %get-tuple-element.31), channel_id=1, source_target_pairs={{0,1},{1,0},{2,3},{3,2},{4,5},{5,4},{6,7},{7,6},{8,9},{9,8},{10,11... | collective-permute-start | bytes 3080 | tf_op jit(solution)/shard_map/ppermute | solution.py:125

commit v9 on v8

--- a/solution.py
+++ b/solution.py
@@ -2,6 +2,7 @@
 import jax.numpy as jnp
 from jax import lax
 from jax.sharding import PartitionSpec as P
+from jax.experimental import pallas as pl
 
 WINDOW_TOKENS = 4096
 D = 3072
@@ -64,8 +65,8 @@
     return (numerators, denominators)
 
 
-def along_lines(state, key_block, value_block, rotary_queries, device_index, cycle_size):
-    kv_heads = key_block.shape[1]
+def along_lines(state, line, rotary_queries, device_index, cycle_size):
+    kv_heads = line.shape[1] // 2
     outer = cycle_size // 2
     def forward(step):
         return [(source, source + 2) for source in range(2 * step - 2, cycle_size - 2)]
@@ -78,7 +79,7 @@
     plane = device_index // 2
     side = device_index % 2
 
-    rows = key_block.shape[0]
+    rows = line.shape[0]
     whole = cycle_size * rows - 1 < WINDOW_TOKENS
 
     def attend_stacked(state, stacked, source):
@@ -86,7 +87,6 @@
             state, stacked[:, :kv_heads], stacked[:, kv_heads:], source, rotary_queries, device_index, whole
         )
 
-    line = jnp.concatenate([key_block, value_block], axis=1)
     for step in range(1, outer + 1):
         last_forward = step == outer - 1
         if step == outer and outer >= 2:
@@ -126,6 +126,33 @@
     return total
 
 
+def key_value_line(keys, values, positions):
+    rows, kv_heads, head_size = keys.shape
+    half_width = head_size // 2
+    steps_half = jnp.arange(half_width, dtype=jnp.float32)
+    inverse = rope_base ** (-2.0 * steps_half / head_size)
+    angles = positions.astype(jnp.float32)[..., None] * inverse
+    cosine = jnp.cos(angles)
+    sine_part = jnp.sin(angles)
+
+    def kernel(key_ref, value_ref, cosine_ref, sine_ref, out_ref):
+        cos_block = cosine_ref[...]
+        sin_block = sine_ref[...]
+        for head in range(kv_heads):
+            entries = key_ref[head].astype(jnp.float32)
+            first_half = entries[:, :half_width]
+            second_half = entries[:, half_width:]
+            out_ref[head, :, :half_width] = (first_half * cos_block - second_half * sin_block).astype(out_ref.dtype)
+            out_ref[head, :, half_width:] = (second_half * cos_block + first_half * sin_block).astype(out_ref.dtype)
+            out_ref[kv_heads + head] = value_ref[head]
+
+    head_major = pl.pallas_call(
+        kernel,
+        out_shape=jax.ShapeDtypeStruct((2 * kv_heads, rows, head_size), keys.dtype),
+    )(jnp.transpose(keys, (1, 0, 2)), jnp.transpose(values, (1, 0, 2)), cosine, sine_part)
+    return jnp.transpose(head_major, (1, 0, 2))
+
+
 def local(queries, keys, values, residual, out_weight, post_gain):
     rows = queries.shape[0]
     q_heads = queries.shape[1]
@@ -137,15 +164,20 @@
     positions = (device_index * rows + jnp.arange(rows, dtype=jnp.int32))[:, None]
     rotary_queries = rotate(queries.astype(jnp.float32), positions).astype(jnp.bfloat16)
     rotary_queries = rotary_queries.reshape(rows, kv_heads, heads_per_group, head_size)
-    rotary_keys = rotate(keys.astype(jnp.float32), positions).astype(jnp.bfloat16)
     reach = min((WINDOW_TOKENS + rows - 2) // rows, cycle_size - 1)
+    lines = reach == cycle_size - 1 and cycle_size % 2 == 0
+    if lines:
+        line = key_value_line(keys, values, positions[:, 0])
+        rotary_keys = line[:, :kv_heads]
+    else:
+        rotary_keys = rotate(keys.astype(jnp.float32), positions).astype(jnp.bfloat16)
     state = (
         jnp.zeros((kv_heads, heads_per_group, rows, head_size), jnp.float32),
         jnp.zeros((kv_heads, heads_per_group, rows), jnp.float32),
     )
     state = attend_block(state, rotary_keys, values, device_index, rotary_queries, device_index)
-    if reach == cycle_size - 1 and cycle_size % 2 == 0:
-        state = along_lines(state, rotary_keys, values, rotary_queries, device_index, cycle_size)
+    if lines:
+        state = along_lines(state, line, rotary_queries, device_index, cycle_size)
     elif reach > 0:
 
         def advance(step_index, carried):

time: 55.5 us -> 58.2 us (1.049)
  Pallas kernels: 0 us -> 2.1 us
  local copies, waits for them, and re-layouts: 1.31 us -> 2.08 us
  waiting for transfers between devices: 21.6 us -> 20.9 us
    pallas_call x0 -> x1, Pallas kernels: none -> 2.1 us  [key_value_line(): pl.pallas_call(kernel, out_shape=jax.ShapeDtypeStruct((2 * kv_heads, rows...]
    transpose x0 -> x1, local copies, waits for them, and re-layouts: none -> 1.7 us  [key_value_line(): jnp.transpose(values, (1, 0, 2))]
    convert_element_type x1 -> x0, other arithmetic: 0.93 us -> none  [local(): keys.astype(jnp.float32)]
    unnamed x9 -> x10, local copies, waits for them, and re-layouts: 0.95 us -> 0.03 us
    another operation x2 -> x1, other arithmetic: 0.68 us -> 1.51 us
    ppermute x3, waiting for transfers between devices: 7.26 us -> 6.51 us  [along_lines(): arrived = lax.ppermute(line, 'ctx', forward(step))]
    cos x1, other arithmetic: 0.53 us -> 1.24 us  [key_value_line(): cosine = jnp.cos(angles)]
  transfers between devices with their start and end apart: 13 -> 13, of which waited for: 8 -> 8; matrix products, arithmetic and copies ran while one was open for 15% -> 16% of each run, Pallas kernels for 0% -> 0%
where the time goes in v9:
time: 58.2 us; the launch traced here: 57.8 us
  waiting for transfers between devices  20.9 us (36%)
  starting transfers between devices  19.1 us (33%)
  matrix products  8.24 us (14%)
  other arithmetic  5.03 us (9%)
  Pallas kernels  2.1 us (4%)
  local copies, waits for them, and re-layouts  2.08 us (4%)
    ppermute x3, starting transfers between devices, along_lines(): crossed = lax.ppermute(line, 'ctx', across(step))  10.3 us
    ppermute x3, waiting for transfers between devices, exchanged(): lax.ppermute(held, 'tp', pairs)  7.24 us
    ppermute x3, waiting for transfers between devices, along_lines(): arrived = lax.ppermute(line, 'ctx', forward(step))  6.51 us
    ppermute x1, waiting for transfers between devices, along_lines(): lax.ppermute(line, 'ctx', [(source, 2 * (source // 2) + 3 - source % 2) f...  4.14 us
    ppermute x3, starting transfers between devices, along_lines(): arrived = lax.ppermute(line, 'ctx', forward(step))  3.98 us
    dot_general x8, matrix products, attend_block(): jnp.einsum('sgrh,kgh->grsk', rotary_queries, key_block, preferred_element...  3.85 us
    ppermute x3, waiting for transfers between devices, summed(): lax.ppermute(partial, 'tp', [(source, source ^ offset) for source in rang...  2.96 us
    dot_general x8, matrix products, attend_block(): jnp.einsum('grsk,kgh->grsh', weights.astype(jnp.bfloat16), value_block, p...  2.83 us
  transfers between devices with their start and end apart: 13, of which 8 were waited for; matrix products, arithmetic and copies ran while one was open for 16% of the time, Pallas kernels for 0%

profile of v9, /device:TPU:24, one launch (start us, length us, event | category | flops | bytes accessed | tf_op | source)
XLA Modules:
  0.0 57.8 jit_solution(6639191030697273139)
XLA Ops:
  0.0 1.2 %multiply_cosine_fusion = (f32[256,64]{1,0:T(8,128)}, f32[256,64]{1,0:T(8,128)}) fusion(f32[64]{0:T(128)S(1)} %multiply_power_fusion, f32[256]{0:T(256)S(1)} %get-tuple-element.32), kind=kLoop, calls=%fused_computation.86 | loop fusion | flops 16384 | bytes 132352 | tf_op jit(solution)/shard_map/cos | solution.py:135
  1.3 1.7 %copy_bitcast_fusion = (bf16[2,256,128]{2,1,0:T(8,128)(2,1)}, bf16[2,256,128]{2,1,0:T(8,128)(2,1)}) fusion(bf16[256,2,128]{2,1,0:T(2,128)(2,1)} %param.8, bf16[256,2,128]{2,1,0:T(2,128)(2,1)} %param.7), kind=kLoop, calls=%fused_computation.103 | loop fusion | bytes 524288 | tf_op jit(solution)/shard_map/transpose | solution.py:152
  3.0 2.1 %shard_map.64 = bf16[4,256,128]{2,1,0:T(8,128)(2,1)} custom-call(bf16[2,256,128]{2,1,0:T(8,128)(2,1)} %get-tuple-element.34.key_ref, bf16[2,256,128]{2,1,0:T(8,128)(2,1)} %get-tuple-element.33.value_ref, f32[256,64]{1,0:T(8,128)} %get-tuple-element.11.cosine_ref, f32[256,64]{1,0:T(8,128)} %get-tuple-element.12.sine_ref), custom_call_target="tpu_custom_call" | custom-call | tf_op jit(solution)/shard_map/pallas_call | solution.py:149
  5.1 1.4 %collective-permute-start.1 = (bf16[256,4,128]{2,0,1:T(8,128)(2,1)}, bf16[256,4,128]{2,0,1:T(8,128)(2,1)S(1)}, u32[]{:S(2)}, u32[]{:S(2)}) collective-permute-start(bf16[256,4,128]{2,0,1:T(8,128)(2,1)} %bitcast.174), channel_id=1, source_target_pairs={{0,8},{4,12},{8,16},{12,20},{16,24},{20,28},{1,9},{5,13},{9,17},{1... | collective-permute-start | bytes 786440 | tf_op jit(solution)/shard_map/ppermute | solution.py:95
  6.5 3.4 %collective-permute-start = (bf16[256,4,128]{2,0,1:T(8,128)(2,1)}, bf16[256,4,128]{2,0,1:T(8,128)(2,1)S(1)}, u32[]{:S(2)}, u32[]{:S(2)}) collective-permute-start(bf16[256,4,128]{2,0,1:T(8,128)(2,1)} %bitcast.175), channel_id=1, source_target_pairs={{0,4},{8,12},{16,20},{24,28},{1,5},{9,13},{17,21},{25,29},{2,6},{1... | collective-permute-start | bytes 786440 | tf_op jit(solution)/shard_map/ppermute | solution.py:96
  9.9 1.0 %convert_element_type.57 = f32[256,4,128]{2,1,0:T(4,128)S(1)} convert(bf16[256,4,128]{2,1,0:T(4,128)(2,1)} %param.6) | non-fusion elementwise | flops 131072 | bytes 786432 | tf_op jit(solution)/shard_map/convert_element_type | solution.py:165
  11.0 0.0 copy-start.1
  11.0 1.5 %subtract_convert_fusion = (bf16[256,4,64]{2,1,0:T(4,128)(2,1)S(1)}, bf16[256,4,64]{2,1,0:T(4,128)(2,1)S(1)}) fusion(f32[256,4,128]{2,1,0:T(4,128)S(1)} %convert_element_type.57, f32[256,64]{1,0:T(8,128)} %get-tuple-element.12.sine_ref, f32[256,64]{1,0:T(8,128)} %get-tuple-element.11.cosine_ref), kind=kLoop, calls=%fused_computation.79 | loop fusion | flops 524288 | bytes 917504 | tf_op jit(solution)/shard_map/convert.3
  12.6 0.1 pad_maximum_fusion
  12.7 0.1 fusion.61
  12.9 0.0 copy-done.3
  12.9 0.5 fusion.71
  13.4 0.0 copy-done.1
  13.4 0.3 fusion.58
  13.8 1.5 %collective-permute-done.1 = bf16[256,4,128]{2,0,1:T(8,128)(2,1)S(1)} collective-permute-done((bf16[256,4,128]{2,0,1:T(8,128)(2,1)}, bf16[256,4,128]{2,0,1:T(8,128)(2,1)S(1)}, u32[]{:S(2)}, u32[]{:S(2)}) %collective-permute-start.1) | collective-permute-done | bytes 262176 | tf_op jit(solution)/shard_map/ppermute | solution.py:95
  15.3 1.3 %collective-permute-start.3 = (bf16[256,4,128]{2,0,1:T(8,128)(2,1)S(1)}, bf16[256,4,128]{2,0,1:T(8,128)(2,1)S(1)}, u32[]{:S(2)}, u32[]{:S(2)}) collective-permute-start(bf16[256,4,128]{2,0,1:T(8,128)(2,1)S(1)} %collective-permute-done.1), channel_id=1, source_target_pairs={{8,16},{12,20},{16,24},{20,28},{9,17},{13,21},{17,25},{21,29},{10,... | collective-permute-start | bytes 786440 | tf_op jit(solution)/shard_map/ppermute | solution.py:95
  16.6 3.4 %collective-permute-start.2 = (bf16[256,4,128]{2,0,1:T(8,128)(2,1)S(1)}, bf16[256,4,128]{2,0,1:T(8,128)(2,1)S(1)}, u32[]{:S(2)}, u32[]{:S(2)}) collective-permute-start(bf16[256,4,128]{2,0,1:T(8,128)(2,1)S(1)} %collective-permute-done.1), channel_id=1, source_target_pairs={{8,12},{16,20},{24,28},{12,8},{20,16},{28,24},{9,13},{17,21},{25,2... | collective-permute-start | bytes 786440 | tf_op jit(solution)/shard_map/ppermute | solution.py:96
  20.1 0.5 fusion.70
  20.5 0.0 collective-permute-done
  20.5 0.5 fusion.72
  21.0 0.3 convolution_add_fusion.3
  21.4 0.3 convolution_add_fusion.2
  21.7 2.6 %collective-permute-done.3 = bf16[256,4,128]{2,0,1:T(8,128)(2,1)S(1)} collective-permute-done((bf16[256,4,128]{2,0,1:T(8,128)(2,1)S(1)}, bf16[256,4,128]{2,0,1:T(8,128)(2,1)S(1)}, u32[]{:S(2)}, u32[]{:S(2)}) %collective-permute-start.3) | collective-permute-done | bytes 262176 | tf_op jit(solution)/shard_map/ppermute | solution.py:95
  24.4 1.3 %collective-permute-start.6 = (bf16[256,4,128]{2,0,1:T(8,128)(2,1)S(1)}, bf16[256,4,128]{2,0,1:T(8,128)(2,1)S(1)}, u32[]{:S(2)}, u32[]{:S(2)}) collective-permute-start(bf16[256,4,128]{2,0,1:T(8,128)(2,1)S(1)} %collective-permute-done.3), channel_id=1, source_target_pairs={{16,28},{20,24},{17,29},{21,25},{18,30},{22,26},{19,31},{23,27}} | collective-permute-start | bytes 786440 | tf_op jit(solution)/shard_map/ppermute | solution.py:98
  25.7 1.3 %collective-permute-start.5 = (bf16[256,4,128]{2,0,1:T(8,128)(2,1)S(1)}, bf16[256,4,128]{2,0,1:T(8,128)(2,1)S(1)}, u32[]{:S(2)}, u32[]{:S(2)}) collective-permute-start(bf16[256,4,128]{2,0,1:T(8,128)(2,1)S(1)} %collective-permute-done.3), channel_id=1, source_target_pairs={{16,24},{20,28},{17,25},{21,29},{18,26},{22,30},{19,27},{23,31}} | collective-permute-start | bytes 786440 | tf_op jit(solution)/shard_map/ppermute | solution.py:95
  27.0 3.4 %collective-permute-start.4 = (bf16[256,4,128]{2,0,1:T(8,128)(2,1)S(1)}, bf16[256,4,128]{2,0,1:T(8,128)(2,1)S(1)}, u32[]{:S(2)}, u32[]{:S(2)}) collective-permute-start(bf16[256,4,128]{2,0,1:T(8,128)(2,1)S(1)} %collective-permute-done.3), channel_id=1, source_target_pairs={{16,20},{24,28},{20,16},{28,24},{17,21},{25,29},{21,17},{29,25},{1... | collective-permute-start | bytes 786440 | tf_op jit(solution)/shard_map/ppermute | solution.py:96
  30.4 0.5 fusion.68
  30.9 0.4 fusion.53
  31.3 0.0 collective-permute-done.2
  31.3 0.5 fusion.69
  31.7 0.4 fusion.46
  32.1 4.1 %collective-permute-done.6 = bf16[256,4,128]{2,0,1:T(8,128)(2,1)S(1)} collective-permute-done((bf16[256,4,128]{2,0,1:T(8,128)(2,1)S(1)}, bf16[256,4,128]{2,0,1:T(8,128)(2,1)S(1)}, u32[]{:S(2)}, u32[]{:S(2)}) %collective-permute-start.6) | collective-permute-done | bytes 262176 | tf_op jit(solution)/shard_map/ppermute | solution.py:98
  36.2 0.5 fusion.65
  36.7 2.4 %collective-permute-done.5 = bf16[256,4,128]{2,0,1:T(8,128)(2,1)S(1)} collective-permute-done((bf16[256,4,128]{2,0,1:T(8,128)(2,1)S(1)}, bf16[256,4,128]{2,0,1:T(8,128)(2,1)S(1)}, u32[]{:S(2)}, u32[]{:S(2)}) %collective-permute-start.5) | collective-permute-done | bytes 262176 | tf_op jit(solution)/shard_map/ppermute | solution.py:95
  39.1 0.5 fusion.66
  39.6 0.0 collective-permute-done.4
  39.6 0.5 fusion.67
  40.1 0.0 copy-start
  40.1 0.3 fusion.48
  40.5 0.3 fusion.50
  40.8 0.4 fusion.47
  41.2 0.1 collective-permute-start.8
  41.3 1.6 %collective-permute-start.7 = (bf16[2,2,256,128]{3,2,1,0:T(8,128)(2,1)S(1)}, bf16[2,2,256,128]{3,2,1,0:T(8,128)(2,1)S(1)}, u32[]{:S(2)}, u32[]{:S(2)}) collective-permute-start(bf16[2,2,256,128]{3,2,1,0:T(8,128)(2,1)S(1)} %fusion.47), channel_id=1, source_target_pairs={{0,2},{1,3},{2,0},{3,1},{4,6},{5,7},{6,4},{7,5},{8,10},{9,11},{10,... | collective-permute-start | bytes 786440 | tf_op jit(solution)/shard_map/ppermute | solution.py:117
  42.9 0.0 copy-done
  42.9 0.3 constant_dynamic-slice_fusion
  43.1 0.4 convolution_bitcast_fusion.3
  43.5 6.5 %collective-permute-done.7 = bf16[2,2,256,128]{3,2,1,0:T(8,128)(2,1)S(1)} collective-permute-done((bf16[2,2,256,128]{3,2,1,0:T(8,128)(2,1)S(1)}, bf16[2,2,256,128]{3,2,1,0:T(8,128)(2,1)S(1)}, u32[]{:S(2)}, u32[]{:S(2)}) %collective-permute-start.7) | collective-permute-done | bytes 262176 | tf_op jit(solution)/shard_map/ppermute | solution.py:117
  50.0 0.0 collective-permute-start.9
  50.0 0.0 collective-permute-done.8
  50.0 0.4 convolution_bitcast_fusion.1
  50.4 0.0 copy-start.4
  50.4 0.0 copy-start.2
  50.4 0.4 fusion.41
  50.8 0.7 %collective-permute-done.9 = bf16[2,2,256,128]{3,2,1,0:T(8,128)(2,1)S(1)} collective-permute-done((bf16[2,2,256,128]{3,2,1,0:T(8,128)(2,1)S(1)}, bf16[2,2,256,128]{3,2,1,0:T(8,128)(2,1)S(1)}, u32[]{:S(2)}, u32[]{:S(2)}) %collective-permute-start.9) | collective-permute-done | bytes 262176 | tf_op jit(solution)/shard_map/ppermute | solution.py:117
  51.5 0.5 multiply_reduce_fusion
  52.0 1.3 %collective-permute-start.12 = (f32[256]{0:T(256)S(1)}, f32[256]{0:T(256)S(1)}, u32[]{:S(2)}, u32[]{:S(2)}) collective-permute-start(f32[256]{0:T(256)S(1)} %get-tuple-element.29), channel_id=1, source_target_pairs={{0,3},{1,2},{2,1},{3,0},{4,7},{5,6},{6,5},{7,4},{8,11},{9,10},{10,... | collective-permute-start | bytes 3080 | tf_op jit(solution)/shard_map/ppermute | solution.py:125
  53.3 0.5 collective-permute-start.11
  53.8 0.1 collective-permute-start.10
  53.9 0.0 copy-done.4
  53.9 1.1 %collective-permute-done.12 = f32[256]{0:T(256)S(1)} collective-permute-done((f32[256]{0:T(256)S(1)}, f32[256]{0:T(256)S(1)}, u32[]{:S(2)}, u32[]{:S(2)}) %collective-permute-start.12) | collective-permute-done | bytes 1056 | tf_op jit(solution)/shard_map/ppermute | solution.py:125
  55.1 1.8 %collective-permute-done.11 = f32[256]{0:T(256)S(1)} collective-permute-done((f32[256]{0:T(256)S(1)}, f32[256]{0:T(256)S(1)}, u32[]{:S(2)}, u32[]{:S(2)}) %collective-permute-start.11) | collective-permute-done | bytes 1056 | tf_op jit(solution)/shard_map/ppermute | solution.py:125
  56.9 0.0 collective-permute-done.10
  56.9 0.0 copy-done.2
  56.9 0.9 %add_convert_fusion = bf16[256,768]{1,0:T(8,128)(2,1)} fusion(f32[256,768]{1,0:T(8,128)S(1)} %get-tuple-element.30, bf16[256,768]{1,0:T(8,128)(2,1)S(1)} %copy-done.2, f32[768]{0:T(1024)S(1)} %convert_element_type.67, f32[256]{0:T(256)S(1)} %add_rsqrt_fusion), kind=kLoop, calls=%fused_computation.64 | loop fusion | flops 983040 | bytes 1576960 | tf_op jit(solution)/shard_map/convert_element_type | solution.py:232
  (9 shorter events, 0.1 us)
Async XLA Ops:
  5.1 7.8 %copy-start.3 = (bf16[4,256,128]{2,1,0:T(8,128)(2,1)S(1)}, bf16[4,256,128]{2,1,0:T(8,128)(2,1)}, u32[]{:S(2)}) copy-start(bf16[4,256,128]{2,1,0:T(8,128)(2,1)} %shard_map.64) | copy-start | bytes 786436
  5.1 10.3 %collective-permute-start.1 = (bf16[256,4,128]{2,0,1:T(8,128)(2,1)}, bf16[256,4,128]{2,0,1:T(8,128)(2,1)S(1)}, u32[]{:S(2)}, u32[]{:S(2)}) collective-permute-start(bf16[256,4,128]{2,0,1:T(8,128)(2,1)} %bitcast.174), channel_id=1, source_target_pairs={{0,8},{4,12},{8,16},{12,20},{16,24},{20,28},{1,9},{5,13},{9,17},{1... | collective-permute-start | bytes 786440 | tf_op jit(solution)/shard_map/ppermute | solution.py:95
  6.5 14.1 %collective-permute-start = (bf16[256,4,128]{2,0,1:T(8,128)(2,1)}, bf16[256,4,128]{2,0,1:T(8,128)(2,1)S(1)}, u32[]{:S(2)}, u32[]{:S(2)}) collective-permute-start(bf16[256,4,128]{2,0,1:T(8,128)(2,1)} %bitcast.175), channel_id=1, source_target_pairs={{0,4},{8,12},{16,20},{24,28},{1,5},{9,13},{17,21},{25,29},{2,6},{1... | collective-permute-start | bytes 786440 | tf_op jit(solution)/shard_map/ppermute | solution.py:96
  11.0 2.4 %copy-start.1 = (bf16[256,2,128]{2,1,0:T(2,128)(2,1)S(1)}, bf16[256,2,128]{2,1,0:T(2,128)(2,1)}, u32[]{:S(2)}) copy-start(bf16[256,2,128]{2,1,0:T(2,128)(2,1)} %param.8) | copy-start | bytes 393220
  15.3 9.1 %collective-permute-start.3 = (bf16[256,4,128]{2,0,1:T(8,128)(2,1)S(1)}, bf16[256,4,128]{2,0,1:T(8,128)(2,1)S(1)}, u32[]{:S(2)}, u32[]{:S(2)}) collective-permute-start(bf16[256,4,128]{2,0,1:T(8,128)(2,1)S(1)} %collective-permute-done.1), channel_id=1, source_target_pairs={{8,16},{12,20},{16,24},{20,28},{9,17},{13,21},{17,25},{21,29},{10,... | collective-permute-start | bytes 786440 | tf_op jit(solution)/shard_map/ppermute | solution.py:95
  16.6 14.6 %collective-permute-start.2 = (bf16[256,4,128]{2,0,1:T(8,128)(2,1)S(1)}, bf16[256,4,128]{2,0,1:T(8,128)(2,1)S(1)}, u32[]{:S(2)}, u32[]{:S(2)}) collective-permute-start(bf16[256,4,128]{2,0,1:T(8,128)(2,1)S(1)} %collective-permute-done.1), channel_id=1, source_target_pairs={{8,12},{16,20},{24,28},{12,8},{20,16},{28,24},{9,13},{17,21},{25,2... | collective-permute-start | bytes 786440 | tf_op jit(solution)/shard_map/ppermute | solution.py:96
  24.4 11.9 %collective-permute-start.6 = (bf16[256,4,128]{2,0,1:T(8,128)(2,1)S(1)}, bf16[256,4,128]{2,0,1:T(8,128)(2,1)S(1)}, u32[]{:S(2)}, u32[]{:S(2)}) collective-permute-start(bf16[256,4,128]{2,0,1:T(8,128)(2,1)S(1)} %collective-permute-done.3), channel_id=1, source_target_pairs={{16,28},{20,24},{17,29},{21,25},{18,30},{22,26},{19,31},{23,27}} | collective-permute-start | bytes 786440 | tf_op jit(solution)/shard_map/ppermute | solution.py:98
  25.7 13.4 %collective-permute-start.5 = (bf16[256,4,128]{2,0,1:T(8,128)(2,1)S(1)}, bf16[256,4,128]{2,0,1:T(8,128)(2,1)S(1)}, u32[]{:S(2)}, u32[]{:S(2)}) collective-permute-start(bf16[256,4,128]{2,0,1:T(8,128)(2,1)S(1)} %collective-permute-done.3), channel_id=1, source_target_pairs={{16,24},{20,28},{17,25},{21,29},{18,26},{22,30},{19,27},{23,31}} | collective-permute-start | bytes 786440 | tf_op jit(solution)/shard_map/ppermute | solution.py:95
  27.0 12.6 %collective-permute-start.4 = (bf16[256,4,128]{2,0,1:T(8,128)(2,1)S(1)}, bf16[256,4,128]{2,0,1:T(8,128)(2,1)S(1)}, u32[]{:S(2)}, u32[]{:S(2)}) collective-permute-start(bf16[256,4,128]{2,0,1:T(8,128)(2,1)S(1)} %collective-permute-done.3), channel_id=1, source_target_pairs={{16,20},{24,28},{20,16},{28,24},{17,21},{25,29},{21,17},{29,25},{1... | collective-permute-start | bytes 786440 | tf_op jit(solution)/shard_map/ppermute | solution.py:96
  40.1 2.8 %copy-start = (bf16[16,128,768]{2,1,0:T(8,128)(2,1)S(1)}, bf16[16,128,768]{2,1,0:T(8,128)(2,1)}, u32[]{:S(2)}) copy-start(bf16[16,128,768]{2,1,0:T(8,128)(2,1)} %param.10) | copy-start | bytes 9437188
  41.2 8.8 %collective-permute-start.8 = (bf16[2,2,256,128]{3,2,1,0:T(8,128)(2,1)S(1)}, bf16[2,2,256,128]{3,2,1,0:T(8,128)(2,1)S(1)}, u32[]{:S(2)}, u32[]{:S(2)}) collective-permute-start(bf16[2,2,256,128]{3,2,1,0:T(8,128)(2,1)S(1)} %fusion.47), channel_id=1, source_target_pairs={{0,1},{1,0},{2,3},{3,2},{4,5},{5,4},{6,7},{7,6},{8,9},{9,8},{10,11... | collective-permute-start | bytes 786440 | tf_op jit(solution)/shard_map/ppermute | solution.py:117
  41.3 8.7 %collective-permute-start.7 = (bf16[2,2,256,128]{3,2,1,0:T(8,128)(2,1)S(1)}, bf16[2,2,256,128]{3,2,1,0:T(8,128)(2,1)S(1)}, u32[]{:S(2)}, u32[]{:S(2)}) collective-permute-start(bf16[2,2,256,128]{3,2,1,0:T(8,128)(2,1)S(1)} %fusion.47), channel_id=1, source_target_pairs={{0,2},{1,3},{2,0},{3,1},{4,6},{5,7},{6,4},{7,5},{8,10},{9,11},{10,... | collective-permute-start | bytes 786440 | tf_op jit(solution)/shard_map/ppermute | solution.py:117
  50.0 1.5 %collective-permute-start.9 = (bf16[2,2,256,128]{3,2,1,0:T(8,128)(2,1)S(1)}, bf16[2,2,256,128]{3,2,1,0:T(8,128)(2,1)S(1)}, u32[]{:S(2)}, u32[]{:S(2)}) collective-permute-start(bf16[2,2,256,128]{3,2,1,0:T(8,128)(2,1)S(1)} %collective-permute-done.7), channel_id=1, source_target_pairs={{0,1},{1,0},{2,3},{3,2},{4,5},{5,4},{6,7},{7,6},{8,9},{9,8},{10,11... | collective-permute-start | bytes 786440 | tf_op jit(solution)/shard_map/ppermute | solution.py:117
  50.4 3.5 %copy-start.4 = (bf16[768]{0:T(1024)(128)(2,1)S(1)}, bf16[768]{0:T(1024)(128)(2,1)}, u32[]{:S(2)}) copy-start(bf16[768]{0:T(1024)(128)(2,1)} %param.11) | copy-start | bytes 4612
  50.4 6.5 %copy-start.2 = (bf16[256,768]{1,0:T(8,128)(2,1)S(1)}, bf16[256,768]{1,0:T(8,128)(2,1)}, u32[]{:S(2)}) copy-start(bf16[256,768]{1,0:T(8,128)(2,1)} %param.9) | copy-start | bytes 1179652
  52.0 3.1 %collective-permute-start.12 = (f32[256]{0:T(256)S(1)}, f32[256]{0:T(256)S(1)}, u32[]{:S(2)}, u32[]{:S(2)}) collective-permute-start(f32[256]{0:T(256)S(1)} %get-tuple-element.29), channel_id=1, source_target_pairs={{0,3},{1,2},{2,1},{3,0},{4,7},{5,6},{6,5},{7,4},{8,11},{9,10},{10,... | collective-permute-start | bytes 3080 | tf_op jit(solution)/shard_map/ppermute | solution.py:125
  53.3 3.6 %collective-permute-start.11 = (f32[256]{0:T(256)S(1)}, f32[256]{0:T(256)S(1)}, u32[]{:S(2)}, u32[]{:S(2)}) collective-permute-start(f32[256]{0:T(256)S(1)} %get-tuple-element.29), channel_id=1, source_target_pairs={{0,2},{1,3},{2,0},{3,1},{4,6},{5,7},{6,4},{7,5},{8,10},{9,11},{10,... | collective-permute-start | bytes 3080 | tf_op jit(solution)/shard_map/ppermute | solution.py:125
  53.8 3.0 %collective-permute-start.10 = (f32[256]{0:T(256)S(1)}, f32[256]{0:T(256)S(1)}, u32[]{:S(2)}, u32[]{:S(2)}) collective-permute-start(f32[256]{0:T(256)S(1)} %get-tuple-element.29), channel_id=1, source_target_pairs={{0,1},{1,0},{2,3},{3,2},{4,5},{5,4},{6,7},{7,6},{8,9},{9,8},{10,11... | collective-permute-start | bytes 3080 | tf_op jit(solution)/shard_map/ppermute | solution.py:125

commit v10 on v8

--- a/solution.py
+++ b/solution.py
@@ -126,6 +126,55 @@
     return total
 
 
+def with_helpers(state, line, rotary_queries, device_index, cycle_size):
+    kv_heads = line.shape[1] // 2
+    rows = line.shape[0]
+    whole = cycle_size * rows - 1 < WINDOW_TOKENS
+    plane = device_index // 2
+    side = device_index % 2
+    back = cycle_size // 2
+
+    def attend_stacked(state, stacked, source, queries, owner):
+        return attend_block(
+            state, stacked[:, :kv_heads], stacked[:, kv_heads:], source, queries, owner, whole
+        )
+
+    foreign = lax.ppermute(rotary_queries, "ctx", [(source, source - back) for source in range(back, cycle_size)])
+    ahead = lax.ppermute(line, "ctx", [(source, source + 2) for source in range(cycle_size - 2)])
+    slanted = lax.ppermute(
+        line, "ctx", [(source, 2 * (source // 2) + 3 - source % 2) for source in range(cycle_size - 2)]
+    )
+    across = [(2 * level, 2 * level + 1) for level in range(back)]
+    across = across + [(2 * level + 1, 2 * level) for level in range(back // 2)]
+    crossed = lax.ppermute(line, "ctx", across)
+    sources = (
+        (crossed, 2 * plane + 1 - side),
+        (ahead, device_index - 2),
+        (slanted, 2 * (plane - 1) + 1 - side),
+    )
+    for stacked, source in sources:
+        state = attend_stacked(state, stacked, source, rotary_queries, device_index)
+
+    numerators, denominators = state
+    owner = device_index + back
+
+    def help_later():
+        partial = (jnp.zeros_like(numerators), jnp.zeros_like(denominators))
+        partial = attend_stacked(partial, line, device_index, foreign, owner)
+        for stacked, source in sources:
+            partial = attend_stacked(partial, stacked, source, foreign, owner)
+        return partial
+
+    def no_help():
+        return (jnp.zeros_like(numerators), jnp.zeros_like(denominators))
+
+    partial_numerators, partial_denominators = lax.cond(device_index < back, help_later, no_help)
+    returned = [(source, source + back) for source in range(back)]
+    far_numerators = lax.ppermute(partial_numerators.astype(jnp.bfloat16), "ctx", returned)
+    far_denominators = lax.ppermute(partial_denominators, "ctx", returned)
+    return (numerators + far_numerators.astype(jnp.float32), denominators + far_denominators)
+
+
 def local(queries, keys, values, residual, out_weight, post_gain):
     rows = queries.shape[0]
     q_heads = queries.shape[1]
@@ -144,7 +193,10 @@
         jnp.zeros((kv_heads, heads_per_group, rows), jnp.float32),
     )
     state = attend_block(state, rotary_keys, values, device_index, rotary_queries, device_index)
-    if reach == cycle_size - 1 and cycle_size % 2 == 0:
+    if reach == cycle_size - 1 and cycle_size == 8 and cycle_size * rows - 1 < WINDOW_TOKENS:
+        line = jnp.concatenate([rotary_keys, values], axis=1)
+        state = with_helpers(state, line, rotary_queries, device_index, cycle_size)
+    elif reach == cycle_size - 1 and cycle_size % 2 == 0:
         state = along_lines(state, rotary_keys, values, rotary_queries, device_index, cycle_size)
     elif reach > 0:
 

time: 55.5 us -> 64.7 us (1.17)
  the two profiles are of different devices: /device:TPU:24 before, /device:TPU:0 now
where the time goes in v10:
time: 64.7 us; the launch traced here: 64.4 us
  waiting for transfers between devices  21.7 us (34%)
  starting transfers between devices  20.2 us (31%)
  matrix products  16.2 us (25%)
  other arithmetic  4.64 us (7%)
  local copies, waits for them, and re-layouts  1.25 us (2%)
    ppermute x1, waiting for transfers between devices, with_helpers(): lax.ppermute(rotary_queries, 'ctx', [(source, source - back) for source i...  12.3 us
    dot_general x8, matrix products, attend_block(): jnp.einsum('grsk,kgh->grsh', weights.astype(jnp.bfloat16), value_block, p...  7.89 us
    ppermute x1, starting transfers between devices, with_helpers(): lax.ppermute(line, 'ctx', [(source, 2 * (source // 2) + 3 - source % 2) f...  5.91 us
    ppermute x3, waiting for transfers between devices, exchanged(): lax.ppermute(held, 'tp', pairs)  5.85 us
    dot_general x8, matrix products, attend_block(): jnp.einsum('sgrh,kgh->grsk', rotary_queries, key_block, preferred_element...  5.68 us
    ppermute x1, starting transfers between devices, with_helpers(): lax.ppermute(line, 'ctx', [(source, source + 2) for source in range(cycle...  4.18 us
    ppermute x3, waiting for transfers between devices, summed(): lax.ppermute(partial, 'tp', [(source, source ^ offset) for source in rang...  3.02 us
    dot_general x4, matrix products, local(): lax.dot_general(held, weight_rows.reshape(kv_heads, heads_per_group, head...  2.58 us
  transfers between devices with their start and end apart: 12, of which 5 were waited for; matrix products, arithmetic and copies ran while one was open for 16% of the time, Pallas kernels for 0%

profile of v10, /device:TPU:0, one launch (start us, length us, event | category | flops | bytes accessed | tf_op | source)
XLA Modules:
  0.0 64.4 jit_solution(11396752579031763562)
XLA Ops:
  0.0 0.9 %copy.16 = bf16[256,2,128]{2,0,1:T(8,128)(2,1)S(1)} copy(bf16[256,2,128]{2,1,0:T(2,128)(2,1)} %param.10) | data formatting | bytes 262144 | tf_op args[2]
  0.9 0.9 %copy_convert_fusion = f32[256,2,128]{2,0,1:T(8,128)S(1)} fusion(bf16[256,2,128]{2,1,0:T(2,128)(2,1)} %param.9), kind=kLoop, calls=%fused_computation.113 | loop fusion | flops 65536 | bytes 393216 | tf_op jit(solution)/shard_map/convert_element_type | solution.py:189
  1.9 0.5 multiply_cosine_fusion
  2.4 0.2 subtract_convert_fusion.1
  2.6 0.1 pad_maximum_fusion.1
  2.7 5.9 %collective-permute-start.2 = (bf16[256,4,128]{2,0,1:T(8,128)(2,1)S(1)}, bf16[256,4,128]{2,0,1:T(8,128)(2,1)S(1)}, u32[]{:S(2)}, u32[]{:S(2)}) collective-permute-start(bf16[256,4,128]{2,0,1:T(8,128)(2,1)S(1)} %pad_maximum_fusion.1), channel_id=1, source_target_pairs={{0,12},{4,8},{8,20},{12,16},{16,28},{20,24},{1,13},{5,9},{9,21},{1... | collective-permute-start | bytes 786440 | tf_op jit(solution)/shard_map/ppermute | solution.py:144
  8.6 2.4 %collective-permute-start = (bf16[256,4,128]{2,0,1:T(8,128)(2,1)S(1)}, bf16[256,4,128]{2,0,1:T(8,128)(2,1)S(1)}, u32[]{:S(2)}, u32[]{:S(2)}) collective-permute-start(bf16[256,4,128]{2,0,1:T(8,128)(2,1)S(1)} %pad_maximum_fusion.1), channel_id=1, source_target_pairs={{0,4},{8,12},{16,20},{24,28},{4,0},{12,8},{1,5},{9,13},{17,21},{25... | collective-permute-start | bytes 786440 | tf_op jit(solution)/shard_map/ppermute | solution.py:149
  11.0 4.2 %collective-permute-start.1 = (bf16[256,4,128]{2,0,1:T(8,128)(2,1)S(1)}, bf16[256,4,128]{2,0,1:T(8,128)(2,1)}, u32[]{:S(2)}, u32[]{:S(2)}) collective-permute-start(bf16[256,4,128]{2,0,1:T(8,128)(2,1)S(1)} %pad_maximum_fusion.1), channel_id=1, source_target_pairs={{0,8},{4,12},{8,16},{12,20},{16,24},{20,28},{1,9},{5,13},{9,17},{1... | collective-permute-start | bytes 786440 | tf_op jit(solution)/shard_map/ppermute | solution.py:143
  15.2 1.0 %convert_element_type.67 = f32[256,4,128]{2,1,0:T(4,128)S(1)} convert(bf16[256,4,128]{2,1,0:T(4,128)(2,1)} %param.8) | non-fusion elementwise | flops 131072 | bytes 786432 | tf_op jit(solution)/shard_map/convert_element_type | solution.py:187
  16.2 0.0 copy-start.2
  16.2 0.5 subtract_convert_fusion
  16.8 0.1 pad_maximum_fusion
  17.0 1.3 %collective-permute-start.3 = (bf16[256,2,2,128]{3,0,2,1:T(8,128)(2,1)S(1)}, bf16[256,2,2,128]{3,0,2,1:T(8,128)(2,1)S(1)}, u32[]{:S(2)}, u32[]{:S(2)}) collective-permute-start(bf16[256,2,2,128]{3,0,2,1:T(8,128)(2,1)S(1)} %pad_maximum_fusion), channel_id=1, source_target_pairs={{16,0},{20,4},{24,8},{28,12},{17,1},{21,5},{25,9},{29,13},{18,2},{... | collective-permute-start | bytes 786440 | tf_op jit(solution)/shard_map/ppermute | solution.py:142
  18.3 0.1 pad_maximum_fusion.2
  18.4 0.1 fusion.73
  18.6 0.5 fusion.84
  19.1 1.1 %fusion.70 = f32[2,2,256,128]{3,2,1,0:T(8,128)} fusion(bf16[2,2,256,256]{2,3,1,0:T(8,128)(2,1)S(1)} %get-tuple-element.75, bf16[256,2,128,1]{2,1,0,3:T(2,128)(2,1)S(1)} %bitcast.162), kind=kOutput, calls=%fused_computation.90 | convolution fusion | flops 67108864 | bytes 1179648 | tf_op jit(solution)/shard_map/grsk,kgh->grsh/dot_general | solution.py:58
  20.3 0.0 collective-permute-done.2
  20.3 0.0 collective-permute-done
  20.3 12.3 %collective-permute-done.3 = bf16[256,2,2,128]{3,0,2,1:T(8,128)(2,1)S(1)} collective-permute-done((bf16[256,2,2,128]{3,0,2,1:T(8,128)(2,1)S(1)}, bf16[256,2,2,128]{3,0,2,1:T(8,128)(2,1)S(1)}, u32[]{:S(2)}, u32[]{:S(2)}) %collective-permute-start.3) | collective-permute-done | bytes 262176 | tf_op jit(solution)/shard_map/ppermute | solution.py:142
  32.6 0.0 collective-permute-done.1
  32.6 5.9 %conditional.1 = (bf16[2,2,256,128]{3,2,1,0:T(8,128)(2,1)}, f32[2,2,256]{2,1,0:T(2,128)S(1)}) conditional(s32[]{:T(128)} %convert_element_type.72, () %tuple.13, (s32[]{:T(128)}, bf16[256,2,128]{2,0,1:T(8,128)(2,1)S(1)}, bf16[256,2,2,128]{3,0,2,1:T(8,128)(2,1)S(1)}, bf16[256,2,128]{2,1,0:T(2,128)(2,1)S(1)}, s32[]{:T(128)}, ...), branch_computations={%region_0.1_spmd, %region_1.6_spmd} | conditional | flops 542637056 | bytes 9736308 | solution.py:171
  32.6 0.5 fusion.80
  33.1 0.3 fusion.23
  33.5 0.5 fusion.81
  34.0 0.3 convolution_add_fusion.2
  34.3 1.4 %fusion.79 = (f32[2,2,256]{2,1,0:T(2,128)S(1)}, bf16[2,2,256,256]{2,3,1,0:T(8,128)(2,1)S(1)}) fusion(bf16[256,2,2,128]{3,0,2,1:T(8,128)(2,1)S(1)} %get-tuple-element.30, bf16[256,4,128]{2,0,1:T(8,128)(2,1)} %get-tuple-element.35, pred[]{:T(512)S(6)} %and.42), kind=kOutput, calls=%fused_computation.125 | convolution fusion | flops 68418560 | bytes 921601 | tf_op jit(solution)/shard_map/cond/branch_1_fun/sgrh,kgh->grsk/dot_general | solution.py:43
  35.7 1.3 %convolution_add_fusion.1 = f32[2,2,256,128]{3,2,1,0:T(8,128)S(1)} fusion(f32[2,2,256,128]{3,2,1,0:T(8,128)S(1)} %convolution_add_fusion.2, bf16[2,2,256,256]{2,3,1,0:T(8,128)(2,1)S(1)} %get-tuple-element.55, bf16[256,4,128]{2,0,1:T(8,128)(2,1)} %get-tuple-element.35), kind=kOutput, calls=%fused_computation.25 | convolution fusion | flops 67239936 | bytes 1703936 | tf_op jit(solution)/shard_map/cond/branch_1_fun/grsk,kgh->grsh/dot_general | solution.py:58
  37.0 0.5 fusion.78
  37.5 1.0 %convolution_add_fusion = bf16[2,2,256,128]{3,2,1,0:T(8,128)(2,1)} fusion(f32[2,2,256,128]{3,2,1,0:T(8,128)S(1)} %convolution_add_fusion.1, bf16[2,2,256,256]{2,3,1,0:T(8,128)(2,1)S(1)} %get-tuple-element.53, bf16[256,4,128]{2,0,1:T(8,128)(2,1)S(1)} %get-tuple-element.37), kind=kOutput, calls=%fused_computation.24 | convolution fusion | flops 67371008 | bytes 1441792 | tf_op jit(solution)/shard_map/cond/branch_1_fun/grsk,kgh->grsh/dot_general | solution.py:58
  38.5 1.4 %collective-permute-start.4 = (bf16[2,2,256,128]{3,2,1,0:T(8,128)(2,1)}, bf16[2,2,256,128]{3,2,1,0:T(8,128)(2,1)S(1)}, u32[]{:S(2)}, u32[]{:S(2)}) collective-permute-start(bf16[2,2,256,128]{3,2,1,0:T(8,128)(2,1)} %get-tuple-element.40), channel_id=1, source_target_pairs={{0,16},{4,20},{8,24},{12,28},{1,17},{5,21},{9,25},{13,29},{2,18},{... | collective-permute-start | bytes 786440 | tf_op jit(solution)/shard_map/ppermute | solution.py:173
  40.0 1.3 %collective-permute-start.5 = (f32[2,2,256]{2,1,0:T(2,128)S(1)}, f32[2,2,256]{2,1,0:T(2,128)S(1)}, u32[]{:S(2)}, u32[]{:S(2)}) collective-permute-start(f32[2,2,256]{2,1,0:T(2,128)S(1)} %get-tuple-element.41), channel_id=1, source_target_pairs={{0,16},{4,20},{8,24},{12,28},{1,17},{5,21},{9,25},{13,29},{2,18},{... | collective-permute-start | bytes 12296 | tf_op jit(solution)/shard_map/ppermute | solution.py:174
  41.3 0.5 fusion.82
  41.8 0.3 fusion.66
  42.1 0.5 fusion.85
  42.6 0.0 copy-done.4
  42.6 0.0 copy-done.1
  42.6 0.0 copy-start
  42.6 1.4 %convolution_add_fusion.4 = f32[2,2,256,128]{3,2,1,0:T(8,128)S(1)} fusion(f32[2,2,256,128]{3,2,1,0:T(8,128)S(1)} %copy-done.1, bf16[2,2,256,256]{2,3,1,0:T(8,128)(2,1)S(1)} %get-tuple-element.77, bf16[256,4,128]{2,0,1:T(8,128)(2,1)} %copy-done.4), kind=kOutput, calls=%fused_computation.82 | convolution fusion | flops 67239936 | bytes 1703936 | tf_op jit(solution)/shard_map/grsk,kgh->grsh/dot_general | solution.py:58
  44.0 1.4 %fusion.83 = (f32[2,2,256]{2,1,0:T(2,128)S(1)}, bf16[2,2,256,256]{2,3,1,0:T(8,128)(2,1)S(1)}) fusion(bf16[256,2,2,128]{3,0,2,1:T(8,128)(2,1)S(1)} %pad_maximum_fusion, bf16[256,4,128]{2,0,1:T(8,128)(2,1)} %collective-permute-done.1, pred[]{:T(512)S(6)} %and.58), kind=kOutput, calls=%fused_computation.129 | convolution fusion | flops 68418560 | bytes 921601 | tf_op jit(solution)/shard_map/sgrh,kgh->grsk/dot_general | solution.py:43
  45.4 0.5 collective-permute-done.5
  45.9 0.0 collective-permute-done.4
  45.9 2.0 %fusion.65 = bf16[2,2,256,128]{3,2,1,0:T(8,128)(2,1)} fusion(f32[2,2,256,128]{3,2,1,0:T(8,128)S(1)} %fusion.66, f32[2,2,256,128]{3,2,1,0:T(8,128)S(1)} %convolution_add_fusion.4, bf16[2,2,256,128]{3,2,1,0:T(8,128)(2,1)S(1)} %collective-permute-done.4, bf16[2,2,256,256]{2,3,1,0:T(8,128)(2,1)S(1)} %get-tuple-element.73, f32[2,2,256]{2,1,0:T(2,128)S(1)} %add_add_fusion.1, ...), kind=kOutput, calls=%fused_computation.83 | convolution fusion | flops 67895296 | bytes 2232320 | tf_op jit(solution)/shard_map/grsk,kgh->grsh/dot_general | solution.py:58
  48.0 1.5 %collective-permute-start.6 = (bf16[2,2,256,128]{3,2,1,0:T(8,128)(2,1)}, bf16[2,2,256,128]{3,2,1,0:T(8,128)(2,1)S(1)}, u32[]{:S(2)}, u32[]{:S(2)}) collective-permute-start(bf16[2,2,256,128]{3,2,1,0:T(8,128)(2,1)} %fusion.65), channel_id=1, source_target_pairs={{0,2},{1,3},{2,0},{3,1},{4,6},{5,7},{6,4},{7,5},{8,10},{9,11},{10,... | collective-permute-start | bytes 786440 | tf_op jit(solution)/shard_map/ppermute | solution.py:117
  49.4 0.0 collective-permute-start.7
  49.5 0.2 constant_dynamic-slice_fusion
  49.7 5.8 %collective-permute-done.6 = bf16[2,2,256,128]{3,2,1,0:T(8,128)(2,1)S(1)} collective-permute-done((bf16[2,2,256,128]{3,2,1,0:T(8,128)(2,1)}, bf16[2,2,256,128]{3,2,1,0:T(8,128)(2,1)S(1)}, u32[]{:S(2)}, u32[]{:S(2)}) %collective-permute-start.6) | collective-permute-done | bytes 262176 | tf_op jit(solution)/shard_map/ppermute | solution.py:117
  55.5 0.0 collective-permute-start.8
  55.5 0.4 convolution_bitcast_fusion.2
  55.9 0.0 collective-permute-done.7
  55.9 0.4 convolution_bitcast_fusion.1
  56.3 0.0 copy-start.5
  56.3 0.0 copy-start.3
  56.3 1.4 %fusion.60 = f32[256,768]{1,0:T(8,128)S(1)} fusion(f32[256,768]{1,0:T(8,128)S(1)} %convolution_bitcast_fusion.1, f32[256,768]{1,0:T(8,128)S(1)} %convolution_bitcast_fusion.2, bf16[2,2,256,128]{3,2,1,0:T(8,128)(2,1)} %fusion.65, bf16[2,2,128,768]{3,2,1,0:T(8,128)(2,1)S(1)} %bitcast.161), kind=kOutput, calls=%fused_computation.76 | convolution fusion | flops 201719808 | bytes 3407872 | tf_op jit(solution)/shard_map/dot_general | solution.py:230
  57.7 0.0 collective-permute-done.8
  57.7 0.5 multiply_reduce_fusion
  58.2 1.7 %collective-permute-start.11 = (f32[256]{0:T(256)S(1)}, f32[256]{0:T(256)S(1)}, u32[]{:S(2)}, u32[]{:S(2)}) collective-permute-start(f32[256]{0:T(256)S(1)} %get-tuple-element.78), channel_id=1, source_target_pairs={{0,3},{1,2},{2,1},{3,0},{4,7},{5,6},{6,5},{7,4},{8,11},{9,10},{10,... | collective-permute-start | bytes 3080 | tf_op jit(solution)/shard_map/ppermute | solution.py:125
  59.8 0.5 collective-permute-start.10
  60.4 0.0 collective-permute-start.9
  60.4 0.9 %collective-permute-done.11 = f32[256]{0:T(256)S(1)} collective-permute-done((f32[256]{0:T(256)S(1)}, f32[256]{0:T(256)S(1)}, u32[]{:S(2)}, u32[]{:S(2)}) %collective-permute-start.11) | collective-permute-done | bytes 1056 | tf_op jit(solution)/shard_map/ppermute | solution.py:125
  61.2 2.2 %collective-permute-done.10 = f32[256]{0:T(256)S(1)} collective-permute-done((f32[256]{0:T(256)S(1)}, f32[256]{0:T(256)S(1)}, u32[]{:S(2)}, u32[]{:S(2)}) %collective-permute-start.10) | collective-permute-done | bytes 1056 | tf_op jit(solution)/shard_map/ppermute | solution.py:125
  63.4 0.0 collective-permute-done.9
  63.4 0.0 copy-done.3
  63.4 0.9 %add_convert_fusion = bf16[256,768]{1,0:T(8,128)(2,1)} fusion(f32[256,768]{1,0:T(8,128)S(1)} %get-tuple-element.79, bf16[256,768]{1,0:T(8,128)(2,1)S(1)} %copy-done.3, f32[768]{0:T(1024)S(1)} %convert_element_type.76, f32[256]{0:T(256)S(1)} %add_rsqrt_fusion), kind=kLoop, calls=%fused_computation.84 | loop fusion | flops 983040 | bytes 1576960 | tf_op jit(solution)/shard_map/convert_element_type | solution.py:252
  (15 shorter events, 0.1 us)
Async XLA Ops:
  2.7 17.6 %collective-permute-start.2 = (bf16[256,4,128]{2,0,1:T(8,128)(2,1)S(1)}, bf16[256,4,128]{2,0,1:T(8,128)(2,1)S(1)}, u32[]{:S(2)}, u32[]{:S(2)}) collective-permute-start(bf16[256,4,128]{2,0,1:T(8,128)(2,1)S(1)} %pad_maximum_fusion.1), channel_id=1, source_target_pairs={{0,12},{4,8},{8,20},{12,16},{16,28},{20,24},{1,13},{5,9},{9,21},{1... | collective-permute-start | bytes 786440 | tf_op jit(solution)/shard_map/ppermute | solution.py:144
  8.6 11.7 %collective-permute-start = (bf16[256,4,128]{2,0,1:T(8,128)(2,1)S(1)}, bf16[256,4,128]{2,0,1:T(8,128)(2,1)S(1)}, u32[]{:S(2)}, u32[]{:S(2)}) collective-permute-start(bf16[256,4,128]{2,0,1:T(8,128)(2,1)S(1)} %pad_maximum_fusion.1), channel_id=1, source_target_pairs={{0,4},{8,12},{16,20},{24,28},{4,0},{12,8},{1,5},{9,13},{17,21},{25... | collective-permute-start | bytes 786440 | tf_op jit(solution)/shard_map/ppermute | solution.py:149
  11.0 21.6 %collective-permute-start.1 = (bf16[256,4,128]{2,0,1:T(8,128)(2,1)S(1)}, bf16[256,4,128]{2,0,1:T(8,128)(2,1)}, u32[]{:S(2)}, u32[]{:S(2)}) collective-permute-start(bf16[256,4,128]{2,0,1:T(8,128)(2,1)S(1)} %pad_maximum_fusion.1), channel_id=1, source_target_pairs={{0,8},{4,12},{8,16},{12,20},{16,24},{20,28},{1,9},{5,13},{9,17},{1... | collective-permute-start | bytes 786440 | tf_op jit(solution)/shard_map/ppermute | solution.py:143
  16.2 2.9 %copy-start.2 = (bf16[256,2,128]{2,1,0:T(2,128)(2,1)S(1)}, bf16[256,2,128]{2,1,0:T(2,128)(2,1)}, u32[]{:S(2)}) copy-start(bf16[256,2,128]{2,1,0:T(2,128)(2,1)} %param.10) | copy-start | bytes 393220
  17.0 15.6 %collective-permute-start.3 = (bf16[256,2,2,128]{3,0,2,1:T(8,128)(2,1)S(1)}, bf16[256,2,2,128]{3,0,2,1:T(8,128)(2,1)S(1)}, u32[]{:S(2)}, u32[]{:S(2)}) collective-permute-start(bf16[256,2,2,128]{3,0,2,1:T(8,128)(2,1)S(1)} %pad_maximum_fusion), channel_id=1, source_target_pairs={{16,0},{20,4},{24,8},{28,12},{17,1},{21,5},{25,9},{29,13},{18,2},{... | collective-permute-start | bytes 786440 | tf_op jit(solution)/shard_map/ppermute | solution.py:142
  20.3 22.3 %copy-start.4 = (bf16[256,4,128]{2,0,1:T(8,128)(2,1)}, bf16[256,4,128]{2,0,1:T(8,128)(2,1)S(1)}, u32[]{:S(2)}) copy-start(bf16[256,4,128]{2,0,1:T(8,128)(2,1)S(1)} %collective-permute-done) | copy-start | bytes 786436
  38.5 4.1 %copy-start.1 = (f32[2,2,256,128]{3,2,1,0:T(8,128)S(1)}, f32[2,2,256,128]{3,2,1,0:T(8,128)}, u32[]{:S(2)}) copy-start(f32[2,2,256,128]{3,2,1,0:T(8,128)} %fusion.70) | copy-start | bytes 1572868
  38.5 7.4 %collective-permute-start.4 = (bf16[2,2,256,128]{3,2,1,0:T(8,128)(2,1)}, bf16[2,2,256,128]{3,2,1,0:T(8,128)(2,1)S(1)}, u32[]{:S(2)}, u32[]{:S(2)}) collective-permute-start(bf16[2,2,256,128]{3,2,1,0:T(8,128)(2,1)} %get-tuple-element.40), channel_id=1, source_target_pairs={{0,16},{4,20},{8,24},{12,28},{1,17},{5,21},{9,25},{13,29},{2,18},{... | collective-permute-start | bytes 786440 | tf_op jit(solution)/shard_map/ppermute | solution.py:173
  40.0 6.0 %collective-permute-start.5 = (f32[2,2,256]{2,1,0:T(2,128)S(1)}, f32[2,2,256]{2,1,0:T(2,128)S(1)}, u32[]{:S(2)}, u32[]{:S(2)}) collective-permute-start(f32[2,2,256]{2,1,0:T(2,128)S(1)} %get-tuple-element.41), channel_id=1, source_target_pairs={{0,16},{4,20},{8,24},{12,28},{1,17},{5,21},{9,25},{13,29},{2,18},{... | collective-permute-start | bytes 12296 | tf_op jit(solution)/shard_map/ppermute | solution.py:174
  42.6 6.8 %copy-start = (bf16[16,128,768]{2,1,0:T(8,128)(2,1)S(1)}, bf16[16,128,768]{2,1,0:T(8,128)(2,1)}, u32[]{:S(2)}) copy-start(bf16[16,128,768]{2,1,0:T(8,128)(2,1)} %param.12) | copy-start | bytes 9437188
  48.0 7.6 %collective-permute-start.6 = (bf16[2,2,256,128]{3,2,1,0:T(8,128)(2,1)}, bf16[2,2,256,128]{3,2,1,0:T(8,128)(2,1)S(1)}, u32[]{:S(2)}, u32[]{:S(2)}) collective-permute-start(bf16[2,2,256,128]{3,2,1,0:T(8,128)(2,1)} %fusion.65), channel_id=1, source_target_pairs={{0,2},{1,3},{2,0},{3,1},{4,6},{5,7},{6,4},{7,5},{8,10},{9,11},{10,... | collective-permute-start | bytes 786440 | tf_op jit(solution)/shard_map/ppermute | solution.py:117
  49.4 6.5 %collective-permute-start.7 = (bf16[2,2,256,128]{3,2,1,0:T(8,128)(2,1)}, bf16[2,2,256,128]{3,2,1,0:T(8,128)(2,1)S(1)}, u32[]{:S(2)}, u32[]{:S(2)}) collective-permute-start(bf16[2,2,256,128]{3,2,1,0:T(8,128)(2,1)} %fusion.65), channel_id=1, source_target_pairs={{0,1},{1,0},{2,3},{3,2},{4,5},{5,4},{6,7},{7,6},{8,9},{9,8},{10,11... | collective-permute-start | bytes 786440 | tf_op jit(solution)/shard_map/ppermute | solution.py:117
  55.5 2.2 %collective-permute-start.8 = (bf16[2,2,256,128]{3,2,1,0:T(8,128)(2,1)S(1)}, bf16[2,2,256,128]{3,2,1,0:T(8,128)(2,1)S(1)}, u32[]{:S(2)}, u32[]{:S(2)}) collective-permute-start(bf16[2,2,256,128]{3,2,1,0:T(8,128)(2,1)S(1)} %collective-permute-done.6), channel_id=1, source_target_pairs={{0,1},{1,0},{2,3},{3,2},{4,5},{5,4},{6,7},{7,6},{8,9},{9,8},{10,11... | collective-permute-start | bytes 786440 | tf_op jit(solution)/shard_map/ppermute | solution.py:117
  56.3 4.1 %copy-start.5 = (bf16[768]{0:T(1024)(128)(2,1)S(1)}, bf16[768]{0:T(1024)(128)(2,1)}, u32[]{:S(2)}) copy-start(bf16[768]{0:T(1024)(128)(2,1)} %param.13) | copy-start | bytes 4612
  56.3 7.1 %copy-start.3 = (bf16[256,768]{1,0:T(8,128)(2,1)S(1)}, bf16[256,768]{1,0:T(8,128)(2,1)}, u32[]{:S(2)}) copy-start(bf16[256,768]{1,0:T(8,128)(2,1)} %param.11) | copy-start | bytes 1179652
  58.2 3.1 %collective-permute-start.11 = (f32[256]{0:T(256)S(1)}, f32[256]{0:T(256)S(1)}, u32[]{:S(2)}, u32[]{:S(2)}) collective-permute-start(f32[256]{0:T(256)S(1)} %get-tuple-element.78), channel_id=1, source_target_pairs={{0,3},{1,2},{2,1},{3,0},{4,7},{5,6},{6,5},{7,4},{8,11},{9,10},{10,... | collective-permute-start | bytes 3080 | tf_op jit(solution)/shard_map/ppermute | solution.py:125
  59.8 3.6 %collective-permute-start.10 = (f32[256]{0:T(256)S(1)}, f32[256]{0:T(256)S(1)}, u32[]{:S(2)}, u32[]{:S(2)}) collective-permute-start(f32[256]{0:T(256)S(1)} %get-tuple-element.78), channel_id=1, source_target_pairs={{0,2},{1,3},{2,0},{3,1},{4,6},{5,7},{6,4},{7,5},{8,10},{9,11},{10,... | collective-permute-start | bytes 3080 | tf_op jit(solution)/shard_map/ppermute | solution.py:125
  60.4 3.0 %collective-permute-start.9 = (f32[256]{0:T(256)S(1)}, f32[256]{0:T(256)S(1)}, u32[]{:S(2)}, u32[]{:S(2)}) collective-permute-start(f32[256]{0:T(256)S(1)} %get-tuple-element.78), channel_id=1, source_target_pairs={{0,1},{1,0},{2,3},{3,2},{4,5},{5,4},{6,7},{7,6},{8,9},{9,8},{10,11... | collective-permute-start | bytes 3080 | tf_op jit(solution)/shard_map/ppermute | solution.py:125

commit v11 on v8

--- a/solution.py
+++ b/solution.py
@@ -81,9 +81,13 @@
     rows = key_block.shape[0]
     whole = cycle_size * rows - 1 < WINDOW_TOKENS
 
+    offsets = jnp.arange(rows, dtype=jnp.int32)
+
     def attend_stacked(state, stacked, source):
+        positions = (source * rows + offsets)[:, None]
+        rotary_block = rotate(stacked[:, :kv_heads].astype(jnp.float32), positions).astype(jnp.bfloat16)
         return attend_block(
-            state, stacked[:, :kv_heads], stacked[:, kv_heads:], source, rotary_queries, device_index, whole
+            state, rotary_block, stacked[:, kv_heads:], source, rotary_queries, device_index, whole
         )
 
     line = jnp.concatenate([key_block, value_block], axis=1)
@@ -145,7 +149,7 @@
     )
     state = attend_block(state, rotary_keys, values, device_index, rotary_queries, device_index)
     if reach == cycle_size - 1 and cycle_size % 2 == 0:
-        state = along_lines(state, rotary_keys, values, rotary_queries, device_index, cycle_size)
+        state = along_lines(state, keys, values, rotary_queries, device_index, cycle_size)
     elif reach > 0:
 
         def advance(step_index, carried):

time: 55.5 us -> 62.3 us (1.12)
  other arithmetic: 4.53 us -> 9.53 us
  waiting for transfers between devices: 21.6 us -> 23.2 us
  starting transfers between devices: 19 us -> 18 us
  local copies, waits for them, and re-layouts: 1.31 us -> 1.96 us
    cos x1, other arithmetic: 0.53 us -> 3.69 us  [rotate(): cosine = jnp.cos(angles)]
    ppermute x1, waiting for transfers between devices: 4.14 us -> 6.04 us  [along_lines(): lax.ppermute(line, 'ctx', [(source, 2 * (source // 2) + 3 - source % 2) f...]
    concatenate x0 -> x1, local copies, waits for them, and re-layouts: none -> 1.58 us  [along_lines(): line = jnp.concatenate([key_block, value_block], axis=1)]
    another operation x2 -> x9, other arithmetic: 0.68 us -> 1.8 us
    ppermute x3, starting transfers between devices: 10.3 us -> 9.3 us  [along_lines(): crossed = lax.ppermute(line, 'ctx', across(step))]
    unnamed x9 -> x8, local copies, waits for them, and re-layouts: 0.95 us -> 0.03 us
    convert_element_type x1, other arithmetic: 0.93 us -> 1.59 us  [local(): keys.astype(jnp.float32)]
  transfers between devices with their start and end apart: 13 -> 13, of which waited for: 8 -> 7; matrix products, arithmetic and copies ran while one was open for 15% -> 20% of each run, Pallas kernels for 0% -> 0%
where the time goes in v11:
time: 62.3 us; the launch traced here: 62 us
  waiting for transfers between devices  23.2 us (37%)
  starting transfers between devices  18 us (29%)
  other arithmetic  9.53 us (15%)
  matrix products  8.67 us (14%)
  local copies, waits for them, and re-layouts  1.96 us (3%)
    ppermute x3, starting transfers between devices, along_lines(): crossed = lax.ppermute(line, 'ctx', across(step))  9.3 us
    ppermute x3, waiting for transfers between devices, exchanged(): lax.ppermute(held, 'tp', pairs)  7.23 us
    ppermute x3, waiting for transfers between devices, along_lines(): arrived = lax.ppermute(line, 'ctx', forward(step))  7 us
    ppermute x1, waiting for transfers between devices, along_lines(): lax.ppermute(line, 'ctx', [(source, 2 * (source // 2) + 3 - source % 2) f...  6.04 us
    dot_general x8, matrix products, attend_block(): jnp.einsum('sgrh,kgh->grsk', rotary_queries, key_block, preferred_element...  4.28 us
    ppermute x3, starting transfers between devices, along_lines(): arrived = lax.ppermute(line, 'ctx', forward(step))  3.86 us
    cos x1, other arithmetic, rotate(): cosine = jnp.cos(angles)  3.69 us
    ppermute x3, waiting for transfers between devices, summed(): lax.ppermute(partial, 'tp', [(source, source ^ offset) for source in rang...  2.97 us
  transfers between devices with their start and end apart: 13, of which 7 were waited for; matrix products, arithmetic and copies ran while one was open for 20% of the time, Pallas kernels for 0%

profile of v11, /device:TPU:24, one launch (start us, length us, event | category | flops | bytes accessed | tf_op | source)
XLA Modules:
  0.0 62.0 jit_solution(12654994523582978585)
XLA Ops:
  0.0 1.6 %copy_convert_fusion = (f32[256,2,128]{2,0,1:T(8,128)S(1)}, bf16[256,4,128]{2,0,1:T(8,128)(2,1)}) fusion(bf16[256,2,128]{2,1,0:T(2,128)(2,1)} %param.7), kind=kLoop, calls=%fused_computation.158 | loop fusion | flops 65535 | bytes 524288 | tf_op jit(solution)/shard_map/convert_element_type | solution.py:144
  1.6 1.6 %copy_dynamic-update-slice_fusion = bf16[256,4,128]{2,0,1:T(8,128)(2,1)} fusion(bf16[256,4,128]{2,0,1:T(8,128)(2,1)} %get-tuple-element.28, bf16[256,2,128]{2,1,0:T(2,128)(2,1)} %param.8), kind=kLoop, calls=%fused_computation.156 | loop fusion | bytes 262144 | tf_op jit(solution)/shard_map/concatenate | solution.py:93
  3.2 1.3 %collective-permute-start.1 = (bf16[256,4,128]{2,0,1:T(8,128)(2,1)}, bf16[256,4,128]{2,0,1:T(8,128)(2,1)S(1)}, u32[]{:S(2)}, u32[]{:S(2)}) collective-permute-start(bf16[256,4,128]{2,0,1:T(8,128)(2,1)} %copy_dynamic-update-slice_fusion), channel_id=1, source_target_pairs={{0,8},{4,12},{8,16},{12,20},{16,24},{20,28},{1,9},{5,13},{9,17},{1... | collective-permute-start | bytes 786440 | tf_op jit(solution)/shard_map/ppermute | solution.py:99
  4.5 3.4 %collective-permute-start = (bf16[256,4,128]{2,0,1:T(8,128)(2,1)}, bf16[256,4,128]{2,0,1:T(8,128)(2,1)S(1)}, u32[]{:S(2)}, u32[]{:S(2)}) collective-permute-start(bf16[256,4,128]{2,0,1:T(8,128)(2,1)} %copy_dynamic-update-slice_fusion), channel_id=1, source_target_pairs={{0,4},{8,12},{16,20},{24,28},{1,5},{9,13},{17,21},{25,29},{2,6},{1... | collective-permute-start | bytes 786440 | tf_op jit(solution)/shard_map/ppermute | solution.py:100
  8.0 1.0 %convert_element_type.149 = f32[256,4,128]{2,1,0:T(4,128)S(1)} convert(bf16[256,4,128]{2,1,0:T(4,128)(2,1)} %param.6) | non-fusion elementwise | flops 131072 | bytes 786432 | tf_op jit(solution)/shard_map/convert_element_type | solution.py:142
  9.1 3.7 %multiply_cosine_fusion.2 = (f32[256,64]{1,0:T(8,128)S(1)}, f32[256,64]{1,0:T(8,128)S(1)}, f32[256,64]{1,0:T(8,128)S(1)}, f32[256,64]{1,0:T(8,128)S(1)}, f32[256...) fusion(f32[256]{0:T(256)S(1)} %get-tuple-element.81, ...), kind=kLoop, calls=%fused_computation.106 | loop fusion | flops 131072 | bytes 1057024 | tf_op jit(solution)/shard_map/cos | solution.py:26
  12.8 0.5 subtract_convert_fusion
  13.3 0.0 copy-start.1
  13.4 0.2 subtract_convert_fusion.8
  13.6 0.1 pad_maximum_fusion
  13.7 0.1 fusion.61
  13.9 0.5 fusion.95
  14.5 0.3 fusion.58
  14.9 0.0 collective-permute-done
  14.9 0.2 subtract_convert_fusion.7
  15.1 0.5 fusion.96
  15.6 0.0 collective-permute-done.1
  15.6 0.2 subtract_convert_fusion.6
  15.8 0.5 fusion.94
  16.3 1.3 %collective-permute-start.3 = (bf16[256,4,128]{2,0,1:T(8,128)(2,1)S(1)}, bf16[256,4,128]{2,0,1:T(8,128)(2,1)S(1)}, u32[]{:S(2)}, u32[]{:S(2)}) collective-permute-start(bf16[256,4,128]{2,0,1:T(8,128)(2,1)S(1)} %collective-permute-done.1), channel_id=1, source_target_pairs={{8,16},{12,20},{16,24},{20,28},{9,17},{13,21},{17,25},{21,29},{10,... | collective-permute-start | bytes 786440 | tf_op jit(solution)/shard_map/ppermute | solution.py:99
  17.6 3.2 %collective-permute-start.2 = (bf16[256,4,128]{2,0,1:T(8,128)(2,1)S(1)}, bf16[256,4,128]{2,0,1:T(8,128)(2,1)S(1)}, u32[]{:S(2)}, u32[]{:S(2)}) collective-permute-start(bf16[256,4,128]{2,0,1:T(8,128)(2,1)S(1)} %collective-permute-done.1), channel_id=1, source_target_pairs={{8,12},{16,20},{24,28},{12,8},{20,16},{28,24},{9,13},{17,21},{25,2... | collective-permute-start | bytes 786440 | tf_op jit(solution)/shard_map/ppermute | solution.py:100
  20.8 0.3 convolution_add_fusion.3
  21.2 0.3 convolution_add_fusion.2
  21.5 5.1 %collective-permute-done.3 = bf16[256,4,128]{2,0,1:T(8,128)(2,1)S(1)} collective-permute-done((bf16[256,4,128]{2,0,1:T(8,128)(2,1)S(1)}, bf16[256,4,128]{2,0,1:T(8,128)(2,1)S(1)}, u32[]{:S(2)}, u32[]{:S(2)}) %collective-permute-start.3) | collective-permute-done | bytes 262176 | tf_op jit(solution)/shard_map/ppermute | solution.py:99
  26.7 0.2 subtract_convert_fusion.4
  26.8 0.5 fusion.92
  27.4 0.2 subtract_convert_fusion.5
  27.6 0.5 fusion.93
  28.1 1.3 %collective-permute-start.6 = (bf16[256,4,128]{2,0,1:T(8,128)(2,1)S(1)}, bf16[256,4,128]{2,0,1:T(8,128)(2,1)S(1)}, u32[]{:S(2)}, u32[]{:S(2)}) collective-permute-start(bf16[256,4,128]{2,0,1:T(8,128)(2,1)S(1)} %collective-permute-done.3), channel_id=1, source_target_pairs={{16,28},{20,24},{17,29},{21,25},{18,30},{22,26},{19,31},{23,27}} | collective-permute-start | bytes 786440 | tf_op jit(solution)/shard_map/ppermute | solution.py:102
  29.4 1.3 %collective-permute-start.5 = (bf16[256,4,128]{2,0,1:T(8,128)(2,1)S(1)}, bf16[256,4,128]{2,0,1:T(8,128)(2,1)S(1)}, u32[]{:S(2)}, u32[]{:S(2)}) collective-permute-start(bf16[256,4,128]{2,0,1:T(8,128)(2,1)S(1)} %collective-permute-done.3), channel_id=1, source_target_pairs={{16,24},{20,28},{17,25},{21,29},{18,26},{22,30},{19,27},{23,31}} | collective-permute-start | bytes 786440 | tf_op jit(solution)/shard_map/ppermute | solution.py:99
  30.7 2.7 %collective-permute-start.4 = (bf16[256,4,128]{2,0,1:T(8,128)(2,1)S(1)}, bf16[256,4,128]{2,0,1:T(8,128)(2,1)S(1)}, u32[]{:S(2)}, u32[]{:S(2)}) collective-permute-start(bf16[256,4,128]{2,0,1:T(8,128)(2,1)S(1)} %collective-permute-done.3), channel_id=1, source_target_pairs={{16,20},{24,28},{20,16},{28,24},{17,21},{25,29},{21,17},{29,25},{1... | collective-permute-start | bytes 786440 | tf_op jit(solution)/shard_map/ppermute | solution.py:100
  33.4 0.4 fusion.53
  33.7 0.4 fusion.46
  34.1 6.0 %collective-permute-done.6 = bf16[256,4,128]{2,0,1:T(8,128)(2,1)S(1)} collective-permute-done((bf16[256,4,128]{2,0,1:T(8,128)(2,1)S(1)}, bf16[256,4,128]{2,0,1:T(8,128)(2,1)S(1)}, u32[]{:S(2)}, u32[]{:S(2)}) %collective-permute-start.6) | collective-permute-done | bytes 262176 | tf_op jit(solution)/shard_map/ppermute | solution.py:102
  40.2 0.2 subtract_convert_fusion.1
  40.3 0.5 fusion.89
  40.9 1.9 %collective-permute-done.5 = bf16[256,4,128]{2,0,1:T(8,128)(2,1)S(1)} collective-permute-done((bf16[256,4,128]{2,0,1:T(8,128)(2,1)S(1)}, bf16[256,4,128]{2,0,1:T(8,128)(2,1)S(1)}, u32[]{:S(2)}, u32[]{:S(2)}) %collective-permute-start.5) | collective-permute-done | bytes 262176 | tf_op jit(solution)/shard_map/ppermute | solution.py:99
  42.8 0.2 subtract_convert_fusion.2
  42.9 0.5 fusion.90
  43.5 0.0 collective-permute-done.4
  43.5 0.2 subtract_convert_fusion.3
  43.7 0.5 fusion.91
  44.2 0.0 copy-start
  44.3 0.3 fusion.48
  44.6 0.3 fusion.50
  45.0 0.4 fusion.47
  45.4 0.1 collective-permute-start.8
  45.4 1.6 %collective-permute-start.7 = (bf16[2,2,256,128]{3,2,1,0:T(8,128)(2,1)S(1)}, bf16[2,2,256,128]{3,2,1,0:T(8,128)(2,1)S(1)}, u32[]{:S(2)}, u32[]{:S(2)}) collective-permute-start(bf16[2,2,256,128]{3,2,1,0:T(8,128)(2,1)S(1)} %fusion.47), channel_id=1, source_target_pairs={{0,2},{1,3},{2,0},{3,1},{4,6},{5,7},{6,4},{7,5},{8,10},{9,11},{10,... | collective-permute-start | bytes 786440 | tf_op jit(solution)/shard_map/ppermute | solution.py:121
  47.0 0.3 constant_dynamic-slice_fusion
  47.3 0.4 convolution_bitcast_fusion.3
  47.7 6.5 %collective-permute-done.7 = bf16[2,2,256,128]{3,2,1,0:T(8,128)(2,1)S(1)} collective-permute-done((bf16[2,2,256,128]{3,2,1,0:T(8,128)(2,1)S(1)}, bf16[2,2,256,128]{3,2,1,0:T(8,128)(2,1)S(1)}, u32[]{:S(2)}, u32[]{:S(2)}) %collective-permute-start.7) | collective-permute-done | bytes 262176 | tf_op jit(solution)/shard_map/ppermute | solution.py:121
  54.2 0.0 collective-permute-start.9
  54.2 0.4 convolution_bitcast_fusion.1
  54.5 0.0 copy-start.3
  54.6 0.0 copy-start.2
  54.6 0.4 fusion.41
  55.0 0.7 %collective-permute-done.9 = bf16[2,2,256,128]{3,2,1,0:T(8,128)(2,1)S(1)} collective-permute-done((bf16[2,2,256,128]{3,2,1,0:T(8,128)(2,1)S(1)}, bf16[2,2,256,128]{3,2,1,0:T(8,128)(2,1)S(1)}, u32[]{:S(2)}, u32[]{:S(2)}) %collective-permute-start.9) | collective-permute-done | bytes 262176 | tf_op jit(solution)/shard_map/ppermute | solution.py:121
  55.7 0.5 multiply_reduce_fusion
  56.2 1.3 %collective-permute-start.12 = (f32[256]{0:T(256)S(1)}, f32[256]{0:T(256)S(1)}, u32[]{:S(2)}, u32[]{:S(2)}) collective-permute-start(f32[256]{0:T(256)S(1)} %get-tuple-element.75), channel_id=1, source_target_pairs={{0,3},{1,2},{2,1},{3,0},{4,7},{5,6},{6,5},{7,4},{8,11},{9,10},{10,... | collective-permute-start | bytes 3080 | tf_op jit(solution)/shard_map/ppermute | solution.py:129
  57.5 0.5 collective-permute-start.11
  58.0 0.1 collective-permute-start.10
  58.1 1.1 %collective-permute-done.12 = f32[256]{0:T(256)S(1)} collective-permute-done((f32[256]{0:T(256)S(1)}, f32[256]{0:T(256)S(1)}, u32[]{:S(2)}, u32[]{:S(2)}) %collective-permute-start.12) | collective-permute-done | bytes 1056 | tf_op jit(solution)/shard_map/ppermute | solution.py:129
  59.2 1.8 %collective-permute-done.11 = f32[256]{0:T(256)S(1)} collective-permute-done((f32[256]{0:T(256)S(1)}, f32[256]{0:T(256)S(1)}, u32[]{:S(2)}, u32[]{:S(2)}) %collective-permute-start.11) | collective-permute-done | bytes 1056 | tf_op jit(solution)/shard_map/ppermute | solution.py:129
  61.1 0.9 %add_convert_fusion = bf16[256,768]{1,0:T(8,128)(2,1)} fusion(f32[256,768]{1,0:T(8,128)S(1)} %get-tuple-element.76, bf16[256,768]{1,0:T(8,128)(2,1)S(1)} %copy-done.2, f32[768]{0:T(1024)S(1)} %convert_element_type.173, f32[256]{0:T(256)S(1)} %add_rsqrt_fusion), kind=kLoop, calls=%fused_computation.64 | loop fusion | flops 983040 | bytes 1576960 | tf_op jit(solution)/shard_map/convert_element_type | solution.py:204
  (26 shorter events, 0.3 us)
Async XLA Ops:
  3.2 12.4 %collective-permute-start.1 = (bf16[256,4,128]{2,0,1:T(8,128)(2,1)}, bf16[256,4,128]{2,0,1:T(8,128)(2,1)S(1)}, u32[]{:S(2)}, u32[]{:S(2)}) collective-permute-start(bf16[256,4,128]{2,0,1:T(8,128)(2,1)} %copy_dynamic-update-slice_fusion), channel_id=1, source_target_pairs={{0,8},{4,12},{8,16},{12,20},{16,24},{20,28},{1,9},{5,13},{9,17},{1... | collective-permute-start | bytes 786440 | tf_op jit(solution)/shard_map/ppermute | solution.py:99
  4.5 10.4 %collective-permute-start = (bf16[256,4,128]{2,0,1:T(8,128)(2,1)}, bf16[256,4,128]{2,0,1:T(8,128)(2,1)S(1)}, u32[]{:S(2)}, u32[]{:S(2)}) collective-permute-start(bf16[256,4,128]{2,0,1:T(8,128)(2,1)} %copy_dynamic-update-slice_fusion), channel_id=1, source_target_pairs={{0,4},{8,12},{16,20},{24,28},{1,5},{9,13},{17,21},{25,29},{2,6},{1... | collective-permute-start | bytes 786440 | tf_op jit(solution)/shard_map/ppermute | solution.py:100
  13.3 1.2 %copy-start.1 = (bf16[256,2,128]{2,1,0:T(2,128)(2,1)S(1)}, bf16[256,2,128]{2,1,0:T(2,128)(2,1)}, u32[]{:S(2)}) copy-start(bf16[256,2,128]{2,1,0:T(2,128)(2,1)} %param.8) | copy-start | bytes 393220
  16.3 10.3 %collective-permute-start.3 = (bf16[256,4,128]{2,0,1:T(8,128)(2,1)S(1)}, bf16[256,4,128]{2,0,1:T(8,128)(2,1)S(1)}, u32[]{:S(2)}, u32[]{:S(2)}) collective-permute-start(bf16[256,4,128]{2,0,1:T(8,128)(2,1)S(1)} %collective-permute-done.1), channel_id=1, source_target_pairs={{8,16},{12,20},{16,24},{20,28},{9,17},{13,21},{17,25},{21,29},{10,... | collective-permute-start | bytes 786440 | tf_op jit(solution)/shard_map/ppermute | solution.py:99
  17.6 9.7 %collective-permute-start.2 = (bf16[256,4,128]{2,0,1:T(8,128)(2,1)S(1)}, bf16[256,4,128]{2,0,1:T(8,128)(2,1)S(1)}, u32[]{:S(2)}, u32[]{:S(2)}) collective-permute-start(bf16[256,4,128]{2,0,1:T(8,128)(2,1)S(1)} %collective-permute-done.1), channel_id=1, source_target_pairs={{8,12},{16,20},{24,28},{12,8},{20,16},{28,24},{9,13},{17,21},{25,2... | collective-permute-start | bytes 786440 | tf_op jit(solution)/shard_map/ppermute | solution.py:100
  28.1 12.0 %collective-permute-start.6 = (bf16[256,4,128]{2,0,1:T(8,128)(2,1)S(1)}, bf16[256,4,128]{2,0,1:T(8,128)(2,1)S(1)}, u32[]{:S(2)}, u32[]{:S(2)}) collective-permute-start(bf16[256,4,128]{2,0,1:T(8,128)(2,1)S(1)} %collective-permute-done.3), channel_id=1, source_target_pairs={{16,28},{20,24},{17,29},{21,25},{18,30},{22,26},{19,31},{23,27}} | collective-permute-start | bytes 786440 | tf_op jit(solution)/shard_map/ppermute | solution.py:102
  29.4 13.4 %collective-permute-start.5 = (bf16[256,4,128]{2,0,1:T(8,128)(2,1)S(1)}, bf16[256,4,128]{2,0,1:T(8,128)(2,1)S(1)}, u32[]{:S(2)}, u32[]{:S(2)}) collective-permute-start(bf16[256,4,128]{2,0,1:T(8,128)(2,1)S(1)} %collective-permute-done.3), channel_id=1, source_target_pairs={{16,24},{20,28},{17,25},{21,29},{18,26},{22,30},{19,27},{23,31}} | collective-permute-start | bytes 786440 | tf_op jit(solution)/shard_map/ppermute | solution.py:99
  30.7 12.8 %collective-permute-start.4 = (bf16[256,4,128]{2,0,1:T(8,128)(2,1)S(1)}, bf16[256,4,128]{2,0,1:T(8,128)(2,1)S(1)}, u32[]{:S(2)}, u32[]{:S(2)}) collective-permute-start(bf16[256,4,128]{2,0,1:T(8,128)(2,1)S(1)} %collective-permute-done.3), channel_id=1, source_target_pairs={{16,20},{24,28},{20,16},{28,24},{17,21},{25,29},{21,17},{29,25},{1... | collective-permute-start | bytes 786440 | tf_op jit(solution)/shard_map/ppermute | solution.py:100
  44.2 2.8 %copy-start = (bf16[16,128,768]{2,1,0:T(8,128)(2,1)S(1)}, bf16[16,128,768]{2,1,0:T(8,128)(2,1)}, u32[]{:S(2)}) copy-start(bf16[16,128,768]{2,1,0:T(8,128)(2,1)} %param.10) | copy-start | bytes 9437188
  45.4 8.8 %collective-permute-start.8 = (bf16[2,2,256,128]{3,2,1,0:T(8,128)(2,1)S(1)}, bf16[2,2,256,128]{3,2,1,0:T(8,128)(2,1)S(1)}, u32[]{:S(2)}, u32[]{:S(2)}) collective-permute-start(bf16[2,2,256,128]{3,2,1,0:T(8,128)(2,1)S(1)} %fusion.47), channel_id=1, source_target_pairs={{0,1},{1,0},{2,3},{3,2},{4,5},{5,4},{6,7},{7,6},{8,9},{9,8},{10,11... | collective-permute-start | bytes 786440 | tf_op jit(solution)/shard_map/ppermute | solution.py:121
  45.4 8.7 %collective-permute-start.7 = (bf16[2,2,256,128]{3,2,1,0:T(8,128)(2,1)S(1)}, bf16[2,2,256,128]{3,2,1,0:T(8,128)(2,1)S(1)}, u32[]{:S(2)}, u32[]{:S(2)}) collective-permute-start(bf16[2,2,256,128]{3,2,1,0:T(8,128)(2,1)S(1)} %fusion.47), channel_id=1, source_target_pairs={{0,2},{1,3},{2,0},{3,1},{4,6},{5,7},{6,4},{7,5},{8,10},{9,11},{10,... | collective-permute-start | bytes 786440 | tf_op jit(solution)/shard_map/ppermute | solution.py:121
  54.2 1.5 %collective-permute-start.9 = (bf16[2,2,256,128]{3,2,1,0:T(8,128)(2,1)S(1)}, bf16[2,2,256,128]{3,2,1,0:T(8,128)(2,1)S(1)}, u32[]{:S(2)}, u32[]{:S(2)}) collective-permute-start(bf16[2,2,256,128]{3,2,1,0:T(8,128)(2,1)S(1)} %collective-permute-done.7), channel_id=1, source_target_pairs={{0,1},{1,0},{2,3},{3,2},{4,5},{5,4},{6,7},{7,6},{8,9},{9,8},{10,11... | collective-permute-start | bytes 786440 | tf_op jit(solution)/shard_map/ppermute | solution.py:121
  54.5 3.5 %copy-start.3 = (bf16[768]{0:T(1024)(128)(2,1)S(1)}, bf16[768]{0:T(1024)(128)(2,1)}, u32[]{:S(2)}) copy-start(bf16[768]{0:T(1024)(128)(2,1)} %param.11) | copy-start | bytes 4612
  54.6 6.5 %copy-start.2 = (bf16[256,768]{1,0:T(8,128)(2,1)S(1)}, bf16[256,768]{1,0:T(8,128)(2,1)}, u32[]{:S(2)}) copy-start(bf16[256,768]{1,0:T(8,128)(2,1)} %param.9) | copy-start | bytes 1179652
  56.2 3.1 %collective-permute-start.12 = (f32[256]{0:T(256)S(1)}, f32[256]{0:T(256)S(1)}, u32[]{:S(2)}, u32[]{:S(2)}) collective-permute-start(f32[256]{0:T(256)S(1)} %get-tuple-element.75), channel_id=1, source_target_pairs={{0,3},{1,2},{2,1},{3,0},{4,7},{5,6},{6,5},{7,4},{8,11},{9,10},{10,... | collective-permute-start | bytes 3080 | tf_op jit(solution)/shard_map/ppermute | solution.py:129
  57.5 3.6 %collective-permute-start.11 = (f32[256]{0:T(256)S(1)}, f32[256]{0:T(256)S(1)}, u32[]{:S(2)}, u32[]{:S(2)}) collective-permute-start(f32[256]{0:T(256)S(1)} %get-tuple-element.75), channel_id=1, source_target_pairs={{0,2},{1,3},{2,0},{3,1},{4,6},{5,7},{6,4},{7,5},{8,10},{9,11},{10,... | collective-permute-start | bytes 3080 | tf_op jit(solution)/shard_map/ppermute | solution.py:129
  58.0 3.1 %collective-permute-start.10 = (f32[256]{0:T(256)S(1)}, f32[256]{0:T(256)S(1)}, u32[]{:S(2)}, u32[]{:S(2)}) collective-permute-start(f32[256]{0:T(256)S(1)} %get-tuple-element.75), channel_id=1, source_target_pairs={{0,1},{1,0},{2,3},{3,2},{4,5},{5,4},{6,7},{7,6},{8,9},{9,8},{10,11... | collective-permute-start | bytes 3080 | tf_op jit(solution)/shard_map/ppermute | solution.py:129

commit v12 on v8

--- a/solution.py
+++ b/solution.py
@@ -170,32 +170,38 @@
     tp_size = lax.axis_size("tp")
     tp_index = lax.axis_index("tp")
     butterfly = tp_size & (tp_size - 1) == 0
-    if butterfly:
-        projected = None
-        for held, offset in exchanged(attended, tp_size):
-            owner = jnp.bitwise_xor(tp_index, offset)
-            weight_rows = lax.dynamic_slice_in_dim(out_weight, owner * q_heads, q_heads, 0)
-            part = lax.dot_general(
-                held,
-                weight_rows.reshape(kv_heads, heads_per_group, head_size, local_cols),
-                (((0, 1, 3), (0, 1, 2)), ((), ())),
-                preferred_element_type=jnp.float32,
-            )
-            projected = part if projected is None else projected + part
-    else:
-        attended = jnp.transpose(attended, (2, 0, 1, 3)).reshape(rows, q_heads, head_size)
-        piece = lax.all_gather(attended, "tp", axis=1, tiled=True)
-        heads_in = piece.shape[1]
-        weight_rows = out_weight.reshape(heads_in * head_size, local_cols)
-        projected = jnp.dot(
-            piece.reshape(rows, heads_in * head_size), weight_rows, preferred_element_type=jnp.float32
-        )
+    gain = post_gain.astype(jnp.float32)
+    if butterfly and rows % 16 == 0:
+        halves = []
+        half_rows = rows // 2
+        for part_index in range(2):
+            block = attended[:, :, part_index * half_rows : (part_index + 1) * half_rows]
+            projected = None
+            for held, offset in exchanged(block, tp_size):
+                owner = jnp.bitwise_xor(tp_index, offset)
+                weight_rows = lax.dynamic_slice_in_dim(out_weight, owner * q_heads, q_heads, 0)
+                part = lax.dot_general(
+                    held,
+                    weight_rows.reshape(kv_heads, heads_per_group, head_size, local_cols),
+                    (((0, 1, 3), (0, 1, 2)), ((), ())),
+                    preferred_element_type=jnp.float32,
+                )
+                projected = part if projected is None else projected + part
+            square_sums = summed(jnp.sum(projected * projected, axis=1), tp_size)
+            normed = projected * lax.rsqrt(square_sums / D + 1e-06)[:, None] * gain
+            rows_in = residual[part_index * half_rows : (part_index + 1) * half_rows]
+            halves.append((rows_in.astype(jnp.float32) + normed).astype(jnp.bfloat16))
+        return jnp.concatenate(halves, axis=0)
+    attended = jnp.transpose(attended, (2, 0, 1, 3)).reshape(rows, q_heads, head_size)
+    piece = lax.all_gather(attended, "tp", axis=1, tiled=True)
+    heads_in = piece.shape[1]
+    weight_rows = out_weight.reshape(heads_in * head_size, local_cols)
+    projected = jnp.dot(
+        piece.reshape(rows, heads_in * head_size), weight_rows, preferred_element_type=jnp.float32
+    )
     partial_sums = jnp.sum(projected * projected, axis=1)
-    if butterfly:
-        square_sums = summed(partial_sums, tp_size)
-    else:
-        square_sums = jnp.sum(lax.all_gather(partial_sums, "tp", axis=0), axis=0)
-    normed = projected * lax.rsqrt(square_sums / D + 1e-06)[:, None] * post_gain.astype(jnp.float32)
+    square_sums = jnp.sum(lax.all_gather(partial_sums, "tp", axis=0), axis=0)
+    normed = projected * lax.rsqrt(square_sums / D + 1e-06)[:, None] * gain
     mixed = residual.astype(jnp.float32) + normed
     return mixed.astype(jnp.bfloat16)
 

time: 55.5 us -> 61.1 us (1.10)
  matrix products: 8.3 us -> 13.5 us
  waiting for transfers between devices: 21.6 us -> 18 us
  local copies, waits for them, and re-layouts: 1.31 us -> 3.9 us
  starting transfers between devices: 19 us -> 20.3 us
    ppermute x3, waiting for transfers between devices: 7.26 us -> 3.72 us  [along_lines(): arrived = lax.ppermute(line, 'ctx', forward(step))]
    dot_general x8, matrix products: 2.84 us -> 5.44 us  [attend_block(): jnp.einsum('grsk,kgh->grsh', weights.astype(jnp.bfloat16), value_block, p...]
    ppermute x3 -> x6, starting transfers between devices: 1.92 us -> 4.41 us  [summed(): lax.ppermute(partial, 'tp', [(source, source ^ offset) for source in rang...]
    ppermute x3, starting transfers between devices: 10.3 us -> 8.32 us  [along_lines(): crossed = lax.ppermute(line, 'ctx', across(step))]
    ppermute x3 -> x6, waiting for transfers between devices: 7.26 us -> 5.34 us  [exchanged(): lax.ppermute(held, 'tp', pairs)]
    dynamic_slice x1, local copies, waits for them, and re-layouts: 0.28 us -> 2.12 us  [local(): lax.dynamic_slice_in_dim(out_weight, owner * q_heads, q_heads, 0)]
    dot_general x8, matrix products: 3.91 us -> 5.73 us  [attend_block(): jnp.einsum('sgrh,kgh->grsk', rotary_queries, key_block, preferred_element...]
    ppermute x1, waiting for transfers between devices: 4.14 us -> 5.75 us  [along_lines(): lax.ppermute(line, 'ctx', [(source, 2 * (source // 2) + 3 - source % 2) f...]
  transfers between devices with their start and end apart: 13 -> 19, of which waited for: 8 -> 9; matrix products, arithmetic and copies ran while one was open for 15% -> 26% of each run, Pallas kernels for 0% -> 0%
where the time goes in v12:
time: 61.1 us; the launch traced here: 60.8 us
  starting transfers between devices  20.3 us (33%)
  waiting for transfers between devices  18 us (29%)
  matrix products  13.5 us (22%)
  other arithmetic  4.45 us (7%)
  local copies, waits for them, and re-layouts  3.9 us (6%)
    ppermute x3, starting transfers between devices, along_lines(): crossed = lax.ppermute(line, 'ctx', across(step))  8.32 us
    ppermute x1, waiting for transfers between devices, along_lines(): lax.ppermute(line, 'ctx', [(source, 2 * (source // 2) + 3 - source % 2) f...  5.75 us
    dot_general x8, matrix products, attend_block(): jnp.einsum('sgrh,kgh->grsk', rotary_queries, key_block, preferred_element...  5.73 us
    dot_general x8, matrix products, attend_block(): jnp.einsum('grsk,kgh->grsh', weights.astype(jnp.bfloat16), value_block, p...  5.44 us
    ppermute x6, waiting for transfers between devices, exchanged(): lax.ppermute(held, 'tp', pairs)  5.34 us
    ppermute x6, starting transfers between devices, summed(): lax.ppermute(partial, 'tp', [(source, source ^ offset) for source in rang...  4.41 us
    ppermute x3, starting transfers between devices, along_lines(): arrived = lax.ppermute(line, 'ctx', forward(step))  4 us
    ppermute x3, waiting for transfers between devices, along_lines(): arrived = lax.ppermute(line, 'ctx', forward(step))  3.72 us
  transfers between devices with their start and end apart: 19, of which 9 were waited for; matrix products, arithmetic and copies ran while one was open for 26% of the time, Pallas kernels for 0%

profile of v12, /device:TPU:24, one launch (start us, length us, event | category | flops | bytes accessed | tf_op | source)
XLA Modules:
  0.0 60.8 jit_solution(4161702257569795212)
XLA Ops:
  0.0 0.9 %copy.12 = bf16[256,2,128]{2,0,1:T(8,128)(2,1)S(1)} copy(bf16[256,2,128]{2,1,0:T(2,128)(2,1)} %param.8) | data formatting | bytes 262144 | tf_op args[2]
  1.0 0.9 %copy_convert_fusion = f32[256,2,128]{2,0,1:T(8,128)S(1)} fusion(bf16[256,2,128]{2,1,0:T(2,128)(2,1)} %param.7), kind=kLoop, calls=%fused_computation.118 | loop fusion | flops 65536 | bytes 393216 | tf_op jit(solution)/shard_map/convert_element_type | solution.py:140
  1.9 0.5 multiply_cosine_fusion
  2.4 0.2 subtract_convert_fusion.1
  2.6 0.8 %pad_maximum_fusion.2 = bf16[256,4,128]{2,0,1:T(8,128)(2,1)} fusion(bf16[256,2,128]{2,0,1:T(8,128)(2,1)S(1)} %copy.12, bf16[256,2,64]{2,0,1:T(8,128)(2,1)S(1)} %get-tuple-element.12, bf16[256,2,64]{2,0,1:T(8,128)(2,1)S(1)} %get-tuple-element.11), kind=kLoop, calls=%fused_computation.93 | loop fusion | flops 786432 | bytes 524288 | tf_op jit(solution)/shard_map/concatenate | solution.py:89
  3.4 1.3 %collective-permute-start.1 = (bf16[256,4,128]{2,0,1:T(8,128)(2,1)}, bf16[256,4,128]{2,0,1:T(8,128)(2,1)}, u32[]{:S(2)}, u32[]{:S(2)}) collective-permute-start(bf16[256,4,128]{2,0,1:T(8,128)(2,1)} %pad_maximum_fusion.2), channel_id=1, source_target_pairs={{0,8},{4,12},{8,16},{12,20},{16,24},{20,28},{1,9},{5,13},{9,17},{1... | collective-permute-start | bytes 786440 | tf_op jit(solution)/shard_map/ppermute | solution.py:95
  4.7 4.2 %collective-permute-start = (bf16[256,4,128]{2,0,1:T(8,128)(2,1)}, bf16[256,4,128]{2,0,1:T(8,128)(2,1)}, u32[]{:S(2)}, u32[]{:S(2)}) collective-permute-start(bf16[256,4,128]{2,0,1:T(8,128)(2,1)} %pad_maximum_fusion.2), channel_id=1, source_target_pairs={{0,4},{8,12},{16,20},{24,28},{1,5},{9,13},{17,21},{25,29},{2,6},{1... | collective-permute-start | bytes 786440 | tf_op jit(solution)/shard_map/ppermute | solution.py:96
  8.9 1.0 %convert_element_type.64 = f32[256,4,128]{2,1,0:T(4,128)S(1)} convert(bf16[256,4,128]{2,1,0:T(4,128)(2,1)} %param.6) | non-fusion elementwise | flops 131072 | bytes 786432 | tf_op jit(solution)/shard_map/convert_element_type | solution.py:138
  9.9 0.0 copy-start.1
  9.9 0.5 subtract_convert_fusion
  10.4 0.1 pad_maximum_fusion.1
  10.6 0.1 fusion.64
  10.8 0.6 fusion.80
  11.3 1.2 %fusion.61 = f32[2,2,256,128]{3,2,1,0:T(8,128)} fusion(bf16[2,2,256,256]{2,3,1,0:T(8,128)(2,1)S(1)} %get-tuple-element.32, bf16[256,2,128,1]{2,1,0,3:T(2,128)(2,1)S(1)} %bitcast.200), kind=kOutput, calls=%fused_computation.81 | convolution fusion | flops 67108864 | bytes 1179648 | tf_op jit(solution)/shard_map/grsk,kgh->grsh/dot_general | solution.py:58
  12.5 2.1 %constant_dynamic-slice_fusion = (bf16[4,128,768]{2,1,0:T(8,128)(2,1)S(1)}, bf16[4,128,768]{2,1,0:T(8,128)(2,1)S(1)}, bf16[4,128,768]{2,1,0:T(8,128)(2,1)S(1)}, bf16[4,128,768]{2,1,0:T(8,128)(2,1)S(1)}) fusion(bf16[16,128,768]{2,1,0:T(8,128)(2,1)} %param.10, s32[]{:T(128)S(6)} %select_n.95, s32[]{:T(128)S(6)} %select_n.93, s32[]{:T(128)S(6)} %select_n.92, ...), kind=kLoop, calls=%fused_computation.120 | loop fusion | bytes 6291472 | tf_op jit(solution)/shard_map/dynamic_slice | solution.py:182
  14.8 1.4 %collective-permute-start.3 = (bf16[256,4,128]{2,0,1:T(8,128)(2,1)}, bf16[256,4,128]{2,0,1:T(8,128)(2,1)S(1)}, u32[]{:S(2)}, u32[]{:S(2)}) collective-permute-start(bf16[256,4,128]{2,0,1:T(8,128)(2,1)} %collective-permute-done.1), channel_id=1, source_target_pairs={{8,16},{12,20},{16,24},{20,28},{9,17},{13,21},{17,25},{21,29},{10,... | collective-permute-start | bytes 786440 | tf_op jit(solution)/shard_map/ppermute | solution.py:95
  16.2 2.2 %collective-permute-start.2 = (bf16[256,4,128]{2,0,1:T(8,128)(2,1)}, bf16[256,4,128]{2,0,1:T(8,128)(2,1)S(1)}, u32[]{:S(2)}, u32[]{:S(2)}) collective-permute-start(bf16[256,4,128]{2,0,1:T(8,128)(2,1)} %collective-permute-done.1), channel_id=1, source_target_pairs={{8,12},{16,20},{24,28},{12,8},{20,16},{28,24},{9,13},{17,21},{25,2... | collective-permute-start | bytes 786440 | tf_op jit(solution)/shard_map/ppermute | solution.py:96
  18.4 1.4 %fusion.79 = (f32[2,2,256]{2,1,0:T(2,128)S(1)}, bf16[2,2,256,256]{2,3,1,0:T(8,128)(2,1)S(1)}) fusion(bf16[256,2,2,128]{3,0,2,1:T(8,128)(2,1)S(1)} %pad_maximum_fusion.1, bf16[256,4,128]{2,0,1:T(8,128)(2,1)} %collective-permute-done.1, pred[]{:T(512)S(6)} %and.58), kind=kOutput, calls=%fused_computation.139 | convolution fusion | flops 68418560 | bytes 921601 | tf_op jit(solution)/shard_map/sgrh,kgh->grsk/dot_general | solution.py:43
  19.8 1.4 %fusion.81 = (f32[2,2,256]{2,1,0:T(2,128)S(1)}, bf16[2,2,256,256]{2,3,1,0:T(8,128)(2,1)S(1)}) fusion(bf16[256,2,2,128]{3,0,2,1:T(8,128)(2,1)S(1)} %pad_maximum_fusion.1, bf16[256,4,128]{2,0,1:T(8,128)(2,1)} %collective-permute-done, pred[]{:T(512)S(6)} %and.57), kind=kOutput, calls=%fused_computation.141 | convolution fusion | flops 68418560 | bytes 921601 | tf_op jit(solution)/shard_map/sgrh,kgh->grsk/dot_general | solution.py:43
  21.2 1.2 %convolution_add_fusion.3 = f32[2,2,256,128]{3,2,1,0:T(8,128)S(1)} fusion(f32[2,2,256,128]{3,2,1,0:T(8,128)S(1)} %copy-done, bf16[2,2,256,256]{2,3,1,0:T(8,128)(2,1)S(1)} %get-tuple-element.34, bf16[256,4,128]{2,0,1:T(8,128)(2,1)} %collective-permute-done), kind=kOutput, calls=%fused_computation.55 | convolution fusion | flops 67239936 | bytes 1703936 | tf_op jit(solution)/shard_map/grsk,kgh->grsh/dot_general | solution.py:58
  22.4 1.2 %convolution_add_fusion.2 = f32[2,2,256,128]{3,2,1,0:T(8,128)S(1)} fusion(f32[2,2,256,128]{3,2,1,0:T(8,128)S(1)} %convolution_add_fusion.3, bf16[2,2,256,256]{2,3,1,0:T(8,128)(2,1)S(1)} %get-tuple-element.30, bf16[256,4,128]{2,0,1:T(8,128)(2,1)} %collective-permute-done.1), kind=kOutput, calls=%fused_computation.54 | convolution fusion | flops 67239936 | bytes 1703936 | tf_op jit(solution)/shard_map/grsk,kgh->grsh/dot_general | solution.py:58
  23.7 1.7 %collective-permute-done.3 = bf16[256,4,128]{2,0,1:T(8,128)(2,1)S(1)} collective-permute-done((bf16[256,4,128]{2,0,1:T(8,128)(2,1)}, bf16[256,4,128]{2,0,1:T(8,128)(2,1)S(1)}, u32[]{:S(2)}, u32[]{:S(2)}) %collective-permute-start.3) | collective-permute-done | bytes 262176 | tf_op jit(solution)/shard_map/ppermute | solution.py:95
  25.4 1.3 %collective-permute-start.6 = (bf16[256,4,128]{2,0,1:T(8,128)(2,1)S(1)}, bf16[256,4,128]{2,0,1:T(8,128)(2,1)S(1)}, u32[]{:S(2)}, u32[]{:S(2)}) collective-permute-start(bf16[256,4,128]{2,0,1:T(8,128)(2,1)S(1)} %collective-permute-done.3), channel_id=1, source_target_pairs={{16,28},{20,24},{17,29},{21,25},{18,30},{22,26},{19,31},{23,27}} | collective-permute-start | bytes 786440 | tf_op jit(solution)/shard_map/ppermute | solution.py:98
  26.7 1.3 %collective-permute-start.5 = (bf16[256,4,128]{2,0,1:T(8,128)(2,1)S(1)}, bf16[256,4,128]{2,0,1:T(8,128)(2,1)S(1)}, u32[]{:S(2)}, u32[]{:S(2)}) collective-permute-start(bf16[256,4,128]{2,0,1:T(8,128)(2,1)S(1)} %collective-permute-done.3), channel_id=1, source_target_pairs={{16,24},{20,28},{17,25},{21,29},{18,26},{22,30},{19,27},{23,31}} | collective-permute-start | bytes 786440 | tf_op jit(solution)/shard_map/ppermute | solution.py:95
  28.0 2.0 %collective-permute-start.4 = (bf16[256,4,128]{2,0,1:T(8,128)(2,1)S(1)}, bf16[256,4,128]{2,0,1:T(8,128)(2,1)S(1)}, u32[]{:S(2)}, u32[]{:S(2)}) collective-permute-start(bf16[256,4,128]{2,0,1:T(8,128)(2,1)S(1)} %collective-permute-done.3), channel_id=1, source_target_pairs={{16,20},{24,28},{20,16},{28,24},{17,21},{25,29},{21,17},{29,25},{1... | collective-permute-start | bytes 786440 | tf_op jit(solution)/shard_map/ppermute | solution.py:96
  30.0 0.5 fusion.77
  30.5 0.4 fusion.56
  30.8 0.5 fusion.78
  31.3 0.3 fusion.43
  31.7 5.8 %collective-permute-done.6 = bf16[256,4,128]{2,0,1:T(8,128)(2,1)S(1)} collective-permute-done((bf16[256,4,128]{2,0,1:T(8,128)(2,1)S(1)}, bf16[256,4,128]{2,0,1:T(8,128)(2,1)S(1)}, u32[]{:S(2)}, u32[]{:S(2)}) %collective-permute-start.6) | collective-permute-done | bytes 262176 | tf_op jit(solution)/shard_map/ppermute | solution.py:98
  37.4 0.5 fusion.74
  37.9 2.0 %collective-permute-done.5 = bf16[256,4,128]{2,0,1:T(8,128)(2,1)S(1)} collective-permute-done((bf16[256,4,128]{2,0,1:T(8,128)(2,1)S(1)}, bf16[256,4,128]{2,0,1:T(8,128)(2,1)S(1)}, u32[]{:S(2)}, u32[]{:S(2)}) %collective-permute-start.5) | collective-permute-done | bytes 262176 | tf_op jit(solution)/shard_map/ppermute | solution.py:95
  39.9 0.5 fusion.75
  40.4 0.3 collective-permute-done.4
  40.7 0.5 fusion.76
  41.2 0.4 fusion.51
  41.5 0.3 fusion.53
  41.9 0.4 fusion.44
  42.3 0.1 collective-permute-start.8
  42.4 1.5 %collective-permute-start.7 = (bf16[2,2,128,128]{3,2,1,0:T(8,128)(2,1)S(1)}, bf16[2,2,128,128]{3,2,1,0:T(8,128)(2,1)S(1)}, u32[]{:S(2)}, u32[]{:S(2)}) collective-permute-start(bf16[2,2,128,128]{3,2,1,0:T(8,128)(2,1)S(1)} %get-tuple-element.15), channel_id=1, source_target_pairs={{0,2},{1,3},{2,0},{3,1},{4,6},{5,7},{6,4},{7,5},{8,10},{9,11},{10,... | collective-permute-start | bytes 393224 | tf_op jit(solution)/shard_map/ppermute | solution.py:117
  43.9 0.2 collective-permute-start.14
  44.0 0.6 collective-permute-start.13
  44.6 0.3 convolution_bitcast_fusion.7
  44.9 0.3 convolution_bitcast_fusion.3
  45.2 3.5 %collective-permute-done.7 = bf16[2,2,128,128]{3,2,1,0:T(8,128)(2,1)S(1)} collective-permute-done((bf16[2,2,128,128]{3,2,1,0:T(8,128)(2,1)S(1)}, bf16[2,2,128,128]{3,2,1,0:T(8,128)(2,1)S(1)}, u32[]{:S(2)}, u32[]{:S(2)}) %collective-permute-start.7) | collective-permute-done | bytes 131104 | tf_op jit(solution)/shard_map/ppermute | solution.py:117
  48.7 0.3 convolution_bitcast_fusion.5
  49.0 0.3 convolution_bitcast_fusion.1
  49.3 1.8 %collective-permute-done.13 = bf16[2,2,128,128]{3,2,1,0:T(8,128)(2,1)S(1)} collective-permute-done((bf16[2,2,128,128]{3,2,1,0:T(8,128)(2,1)S(1)}, bf16[2,2,128,128]{3,2,1,0:T(8,128)(2,1)S(1)}, u32[]{:S(2)}, u32[]{:S(2)}) %collective-permute-start.13) | collective-permute-done | bytes 131104 | tf_op jit(solution)/shard_map/ppermute | solution.py:117
  51.1 0.3 fusion.46
  51.4 0.0 copy-start.2
  51.4 0.0 copy-start.4
  51.4 0.3 fusion.49
  51.7 0.4 multiply_reduce_fusion.1
  52.1 1.6 %collective-permute-start.12 = (f32[128]{0:T(128)S(1)}, f32[128]{0:T(128)S(1)}, u32[]{:S(2)}, u32[]{:S(2)}) collective-permute-start(f32[128]{0:T(128)S(1)} %get-tuple-element.35), channel_id=1, source_target_pairs={{0,3},{1,2},{2,1},{3,0},{4,7},{5,6},{6,5},{7,4},{8,11},{9,10},{10,... | collective-permute-start | bytes 1544 | tf_op jit(solution)/shard_map/ppermute | solution.py:125
  53.7 0.6 collective-permute-start.11
  54.3 0.4 multiply_reduce_fusion
  54.6 1.6 %collective-permute-start.18 = (f32[128]{0:T(128)S(1)}, f32[128]{0:T(128)S(1)}, u32[]{:S(2)}, u32[]{:S(2)}) collective-permute-start(f32[128]{0:T(128)S(1)} %get-tuple-element.37), channel_id=1, source_target_pairs={{0,3},{1,2},{2,1},{3,0},{4,7},{5,6},{6,5},{7,4},{8,11},{9,10},{10,... | collective-permute-start | bytes 1544 | tf_op jit(solution)/shard_map/ppermute | solution.py:125
  56.2 0.6 collective-permute-start.17
  56.8 0.4 collective-permute-done.11
  57.2 0.4 collective-permute-done.18
  57.7 2.1 %collective-permute-done.17 = f32[128]{0:T(128)S(1)} collective-permute-done((f32[128]{0:T(128)S(1)}, f32[128]{0:T(128)S(1)}, u32[]{:S(2)}, u32[]{:S(2)}) %collective-permute-start.17) | collective-permute-done | bytes 544 | tf_op jit(solution)/shard_map/ppermute | solution.py:125
  59.8 0.2 add_convert_fusion.2
  60.0 0.0 copy-start.5
  60.0 0.7 %copy-done.5 = bf16[256,768]{1,0:T(8,128)(2,1)} copy-done((bf16[256,768]{1,0:T(8,128)(2,1)}, bf16[256,768]{1,0:T(8,128)(2,1)S(1)}, u32[]{:S(2)}) %copy-start.5) | copy-done | bytes 393240
  (32 shorter events, 0.2 us)
Async XLA Ops:
  3.4 11.3 %collective-permute-start.1 = (bf16[256,4,128]{2,0,1:T(8,128)(2,1)}, bf16[256,4,128]{2,0,1:T(8,128)(2,1)}, u32[]{:S(2)}, u32[]{:S(2)}) collective-permute-start(bf16[256,4,128]{2,0,1:T(8,128)(2,1)} %pad_maximum_fusion.2), channel_id=1, source_target_pairs={{0,8},{4,12},{8,16},{12,20},{16,24},{20,28},{1,9},{5,13},{9,17},{1... | collective-permute-start | bytes 786440 | tf_op jit(solution)/shard_map/ppermute | solution.py:95
  4.7 15.1 %collective-permute-start = (bf16[256,4,128]{2,0,1:T(8,128)(2,1)}, bf16[256,4,128]{2,0,1:T(8,128)(2,1)}, u32[]{:S(2)}, u32[]{:S(2)}) collective-permute-start(bf16[256,4,128]{2,0,1:T(8,128)(2,1)} %pad_maximum_fusion.2), channel_id=1, source_target_pairs={{0,4},{8,12},{16,20},{24,28},{1,5},{9,13},{17,21},{25,29},{2,6},{1... | collective-permute-start | bytes 786440 | tf_op jit(solution)/shard_map/ppermute | solution.py:96
  9.9 1.5 %copy-start.1 = (bf16[256,2,128]{2,1,0:T(2,128)(2,1)S(1)}, bf16[256,2,128]{2,1,0:T(2,128)(2,1)}, u32[]{:S(2)}) copy-start(bf16[256,2,128]{2,1,0:T(2,128)(2,1)} %param.8) | copy-start | bytes 393220
  12.5 2.2 %copy-start.3 = (bf16[768]{0:T(1024)(128)(2,1)S(1)}, bf16[768]{0:T(1024)(128)(2,1)}, u32[]{:S(2)}) copy-start(bf16[768]{0:T(1024)(128)(2,1)} %param.11) | copy-start | bytes 4612
  14.7 6.4 %copy-start = (f32[2,2,256,128]{3,2,1,0:T(8,128)S(1)}, f32[2,2,256,128]{3,2,1,0:T(8,128)}, u32[]{:S(2)}) copy-start(f32[2,2,256,128]{3,2,1,0:T(8,128)} %fusion.61) | copy-start | bytes 1572868
  14.8 10.6 %collective-permute-start.3 = (bf16[256,4,128]{2,0,1:T(8,128)(2,1)}, bf16[256,4,128]{2,0,1:T(8,128)(2,1)S(1)}, u32[]{:S(2)}, u32[]{:S(2)}) collective-permute-start(bf16[256,4,128]{2,0,1:T(8,128)(2,1)} %collective-permute-done.1), channel_id=1, source_target_pairs={{8,16},{12,20},{16,24},{20,28},{9,17},{13,21},{17,25},{21,29},{10,... | collective-permute-start | bytes 786440 | tf_op jit(solution)/shard_map/ppermute | solution.py:95
  16.2 14.6 %collective-permute-start.2 = (bf16[256,4,128]{2,0,1:T(8,128)(2,1)}, bf16[256,4,128]{2,0,1:T(8,128)(2,1)S(1)}, u32[]{:S(2)}, u32[]{:S(2)}) collective-permute-start(bf16[256,4,128]{2,0,1:T(8,128)(2,1)} %collective-permute-done.1), channel_id=1, source_target_pairs={{8,12},{16,20},{24,28},{12,8},{20,16},{28,24},{9,13},{17,21},{25,2... | collective-permute-start | bytes 786440 | tf_op jit(solution)/shard_map/ppermute | solution.py:96
  25.4 12.0 %collective-permute-start.6 = (bf16[256,4,128]{2,0,1:T(8,128)(2,1)S(1)}, bf16[256,4,128]{2,0,1:T(8,128)(2,1)S(1)}, u32[]{:S(2)}, u32[]{:S(2)}) collective-permute-start(bf16[256,4,128]{2,0,1:T(8,128)(2,1)S(1)} %collective-permute-done.3), channel_id=1, source_target_pairs={{16,28},{20,24},{17,29},{21,25},{18,30},{22,26},{19,31},{23,27}} | collective-permute-start | bytes 786440 | tf_op jit(solution)/shard_map/ppermute | solution.py:98
  26.7 13.2 %collective-permute-start.5 = (bf16[256,4,128]{2,0,1:T(8,128)(2,1)S(1)}, bf16[256,4,128]{2,0,1:T(8,128)(2,1)S(1)}, u32[]{:S(2)}, u32[]{:S(2)}) collective-permute-start(bf16[256,4,128]{2,0,1:T(8,128)(2,1)S(1)} %collective-permute-done.3), channel_id=1, source_target_pairs={{16,24},{20,28},{17,25},{21,29},{18,26},{22,30},{19,27},{23,31}} | collective-permute-start | bytes 786440 | tf_op jit(solution)/shard_map/ppermute | solution.py:95
  28.0 12.7 %collective-permute-start.4 = (bf16[256,4,128]{2,0,1:T(8,128)(2,1)S(1)}, bf16[256,4,128]{2,0,1:T(8,128)(2,1)S(1)}, u32[]{:S(2)}, u32[]{:S(2)}) collective-permute-start(bf16[256,4,128]{2,0,1:T(8,128)(2,1)S(1)} %collective-permute-done.3), channel_id=1, source_target_pairs={{16,20},{24,28},{20,16},{28,24},{17,21},{25,29},{21,17},{29,25},{1... | collective-permute-start | bytes 786440 | tf_op jit(solution)/shard_map/ppermute | solution.py:96
  42.3 6.4 %collective-permute-start.8 = (bf16[2,2,128,128]{3,2,1,0:T(8,128)(2,1)S(1)}, bf16[2,2,128,128]{3,2,1,0:T(8,128)(2,1)S(1)}, u32[]{:S(2)}, u32[]{:S(2)}) collective-permute-start(bf16[2,2,128,128]{3,2,1,0:T(8,128)(2,1)S(1)} %get-tuple-element.15), channel_id=1, source_target_pairs={{0,1},{1,0},{2,3},{3,2},{4,5},{5,4},{6,7},{7,6},{8,9},{9,8},{10,11... | collective-permute-start | bytes 393224 | tf_op jit(solution)/shard_map/ppermute | solution.py:117
  42.4 6.4 %collective-permute-start.7 = (bf16[2,2,128,128]{3,2,1,0:T(8,128)(2,1)S(1)}, bf16[2,2,128,128]{3,2,1,0:T(8,128)(2,1)S(1)}, u32[]{:S(2)}, u32[]{:S(2)}) collective-permute-start(bf16[2,2,128,128]{3,2,1,0:T(8,128)(2,1)S(1)} %get-tuple-element.15), channel_id=1, source_target_pairs={{0,2},{1,3},{2,0},{3,1},{4,6},{5,7},{6,4},{7,5},{8,10},{9,11},{10,... | collective-permute-start | bytes 393224 | tf_op jit(solution)/shard_map/ppermute | solution.py:117
  43.9 5.2 %collective-permute-start.14 = (bf16[2,2,128,128]{3,2,1,0:T(8,128)(2,1)S(1)}, bf16[2,2,128,128]{3,2,1,0:T(8,128)(2,1)S(1)}, u32[]{:S(2)}, u32[]{:S(2)}) collective-permute-start(bf16[2,2,128,128]{3,2,1,0:T(8,128)(2,1)S(1)} %get-tuple-element.16), channel_id=1, source_target_pairs={{0,1},{1,0},{2,3},{3,2},{4,5},{5,4},{6,7},{7,6},{8,9},{9,8},{10,11... | collective-permute-start | bytes 393224 | tf_op jit(solution)/shard_map/ppermute | solution.py:117
  44.0 7.1 %collective-permute-start.13 = (bf16[2,2,128,128]{3,2,1,0:T(8,128)(2,1)S(1)}, bf16[2,2,128,128]{3,2,1,0:T(8,128)(2,1)S(1)}, u32[]{:S(2)}, u32[]{:S(2)}) collective-permute-start(bf16[2,2,128,128]{3,2,1,0:T(8,128)(2,1)S(1)} %get-tuple-element.16), channel_id=1, source_target_pairs={{0,2},{1,3},{2,0},{3,1},{4,6},{5,7},{6,4},{7,5},{8,10},{9,11},{10,... | collective-permute-start | bytes 393224 | tf_op jit(solution)/shard_map/ppermute | solution.py:117
  48.7 3.0 %collective-permute-start.9 = (bf16[2,2,128,128]{3,2,1,0:T(8,128)(2,1)S(1)}, bf16[2,2,128,128]{3,2,1,0:T(8,128)(2,1)S(1)}, u32[]{:S(2)}, u32[]{:S(2)}) collective-permute-start(bf16[2,2,128,128]{3,2,1,0:T(8,128)(2,1)S(1)} %collective-permute-done.7), channel_id=1, source_target_pairs={{0,1},{1,0},{2,3},{3,2},{4,5},{5,4},{6,7},{7,6},{8,9},{9,8},{10,11... | collective-permute-start | bytes 393224 | tf_op jit(solution)/shard_map/ppermute | solution.py:117
  51.1 3.2 %collective-permute-start.15 = (bf16[2,2,128,128]{3,2,1,0:T(8,128)(2,1)S(1)}, bf16[2,2,128,128]{3,2,1,0:T(8,128)(2,1)S(1)}, u32[]{:S(2)}, u32[]{:S(2)}) collective-permute-start(bf16[2,2,128,128]{3,2,1,0:T(8,128)(2,1)S(1)} %collective-permute-done.13), channel_id=1, source_target_pairs={{0,1},{1,0},{2,3},{3,2},{4,5},{5,4},{6,7},{7,6},{8,9},{9,8},{10,11... | collective-permute-start | bytes 393224 | tf_op jit(solution)/shard_map/ppermute | solution.py:117
  51.4 8.4 %copy-start.2 = (bf16[256,768]{1,0:T(8,128)(2,1)S(1)}, bf16[256,768]{1,0:T(8,128)(2,1)}, u32[]{:S(2)}) copy-start(bf16[256,768]{1,0:T(8,128)(2,1)} %param.9) | copy-start | bytes 1179652
  51.4 8.4 %copy-start.4 = (bf16[256,768]{1,0:T(8,128)(2,1)S(1)}, bf16[256,768]{1,0:T(8,128)(2,1)}, u32[]{:S(2)}) copy-start(bf16[256,768]{1,0:T(8,128)(2,1)} %custom-call) | copy-start | bytes 1179652
  52.1 4.8 %collective-permute-start.12 = (f32[128]{0:T(128)S(1)}, f32[128]{0:T(128)S(1)}, u32[]{:S(2)}, u32[]{:S(2)}) collective-permute-start(f32[128]{0:T(128)S(1)} %get-tuple-element.35), channel_id=1, source_target_pairs={{0,3},{1,2},{2,1},{3,0},{4,7},{5,6},{6,5},{7,4},{8,11},{9,10},{10,... | collective-permute-start | bytes 1544 | tf_op jit(solution)/shard_map/ppermute | solution.py:125
  53.7 3.5 %collective-permute-start.11 = (f32[128]{0:T(128)S(1)}, f32[128]{0:T(128)S(1)}, u32[]{:S(2)}, u32[]{:S(2)}) collective-permute-start(f32[128]{0:T(128)S(1)} %get-tuple-element.35), channel_id=1, source_target_pairs={{0,2},{1,3},{2,0},{3,1},{4,6},{5,7},{6,4},{7,5},{8,10},{9,11},{10,... | collective-permute-start | bytes 1544 | tf_op jit(solution)/shard_map/ppermute | solution.py:125
  54.3 2.9 %collective-permute-start.10 = (f32[128]{0:T(128)S(1)}, f32[128]{0:T(128)S(1)}, u32[]{:S(2)}, u32[]{:S(2)}) collective-permute-start(f32[128]{0:T(128)S(1)} %get-tuple-element.35), channel_id=1, source_target_pairs={{0,1},{1,0},{2,3},{3,2},{4,5},{5,4},{6,7},{7,6},{8,9},{9,8},{10,11... | collective-permute-start | bytes 1544 | tf_op jit(solution)/shard_map/ppermute | solution.py:125
  54.6 3.0 %collective-permute-start.18 = (f32[128]{0:T(128)S(1)}, f32[128]{0:T(128)S(1)}, u32[]{:S(2)}, u32[]{:S(2)}) collective-permute-start(f32[128]{0:T(128)S(1)} %get-tuple-element.37), channel_id=1, source_target_pairs={{0,3},{1,2},{2,1},{3,0},{4,7},{5,6},{6,5},{7,4},{8,11},{9,10},{10,... | collective-permute-start | bytes 1544 | tf_op jit(solution)/shard_map/ppermute | solution.py:125
  56.2 3.5 %collective-permute-start.17 = (f32[128]{0:T(128)S(1)}, f32[128]{0:T(128)S(1)}, u32[]{:S(2)}, u32[]{:S(2)}) collective-permute-start(f32[128]{0:T(128)S(1)} %get-tuple-element.37), channel_id=1, source_target_pairs={{0,2},{1,3},{2,0},{3,1},{4,6},{5,7},{6,4},{7,5},{8,10},{9,11},{10,... | collective-permute-start | bytes 1544 | tf_op jit(solution)/shard_map/ppermute | solution.py:125
  56.8 2.9 %collective-permute-start.16 = (f32[128]{0:T(128)S(1)}, f32[128]{0:T(128)S(1)}, u32[]{:S(2)}, u32[]{:S(2)}) collective-permute-start(f32[128]{0:T(128)S(1)} %get-tuple-element.37), channel_id=1, source_target_pairs={{0,1},{1,0},{2,3},{3,2},{4,5},{5,4},{6,7},{7,6},{8,9},{9,8},{10,11... | collective-permute-start | bytes 1544 | tf_op jit(solution)/shard_map/ppermute | solution.py:125
  60.0 0.7 %copy-start.5 = (bf16[256,768]{1,0:T(8,128)(2,1)}, bf16[256,768]{1,0:T(8,128)(2,1)S(1)}, u32[]{:S(2)}) copy-start(bf16[256,768]{1,0:T(8,128)(2,1)S(1)} %get-tuple-element.89) | copy-start | bytes 1179652

commit v13 on v8

--- a/solution.py
+++ b/solution.py
@@ -120,10 +120,11 @@
 
 
 def summed(partial, count):
-    total = partial
-    for offset in range(1, count):
-        total = total + lax.ppermute(partial, "tp", [(source, source ^ offset) for source in range(count)])
-    return total
+    bit = 1
+    while bit < count:
+        partial = partial + lax.ppermute(partial, "tp", [(source, source ^ bit) for source in range(count)])
+        bit *= 2
+    return partial
 
 
 def local(queries, keys, values, residual, out_weight, post_gain):

time: 55.5 us -> 55.4 us (level)
    ppermute x3 -> x2, starting transfers between devices: 1.92 us -> 1.68 us  [summed(): lax.ppermute(partial, 'tp', [(source, source ^ bit) for source in range(c...]
    ppermute x3 -> x2, waiting for transfers between devices: 2.94 us -> 3.08 us  [summed(): lax.ppermute(partial, 'tp', [(source, source ^ bit) for source in range(c...]
  transfers between devices with their start and end apart: 13 -> 12, of which waited for: 8 -> 8; matrix products, arithmetic and copies ran while one was open for 15% -> 15% of each run, Pallas kernels for 0% -> 0%
where the time goes in v13:
time: 55.4 us; the launch traced here: 55 us
  waiting for transfers between devices  21.7 us (39%)
  starting transfers between devices  18.7 us (34%)
  matrix products  8.3 us (15%)
  other arithmetic  4.53 us (8%)
  local copies, waits for them, and re-layouts  1.31 us (2%)
    ppermute x3, starting transfers between devices, along_lines(): crossed = lax.ppermute(line, 'ctx', across(step))  10.3 us
    ppermute x3, waiting for transfers between devices, exchanged(): lax.ppermute(held, 'tp', pairs)  7.26 us
    ppermute x3, waiting for transfers between devices, along_lines(): arrived = lax.ppermute(line, 'ctx', forward(step))  7.26 us
    ppermute x1, waiting for transfers between devices, along_lines(): lax.ppermute(line, 'ctx', [(source, 2 * (source // 2) + 3 - source % 2) f...  4.14 us
    dot_general x8, matrix products, attend_block(): jnp.einsum('sgrh,kgh->grsk', rotary_queries, key_block, preferred_element...  3.91 us
    ppermute x3, starting transfers between devices, along_lines(): arrived = lax.ppermute(line, 'ctx', forward(step))  3.86 us
    ppermute x2, waiting for transfers between devices, summed(): lax.ppermute(partial, 'tp', [(source, source ^ bit) for source in range(c...  3.08 us
    dot_general x8, matrix products, attend_block(): jnp.einsum('grsk,kgh->grsh', weights.astype(jnp.bfloat16), value_block, p...  2.84 us
  transfers between devices with their start and end apart: 12, of which 8 were waited for; matrix products, arithmetic and copies ran while one was open for 15% of the time, Pallas kernels for 0%

profile of v13, /device:TPU:24, one launch (start us, length us, event | category | flops | bytes accessed | tf_op | source)
XLA Modules:
  0.0 55.0 jit_solution(7167079228975189640)
XLA Ops:
  0.0 0.9 %copy.12 = bf16[256,2,128]{2,0,1:T(8,128)(2,1)S(1)} copy(bf16[256,2,128]{2,1,0:T(2,128)(2,1)} %param.8) | data formatting | bytes 262144 | tf_op args[2]
  1.0 0.9 %copy_convert_fusion = f32[256,2,128]{2,0,1:T(8,128)S(1)} fusion(bf16[256,2,128]{2,1,0:T(2,128)(2,1)} %param.7), kind=kLoop, calls=%fused_computation.108 | loop fusion | flops 65536 | bytes 393216 | tf_op jit(solution)/shard_map/convert_element_type | solution.py:141
  1.9 0.5 multiply_cosine_fusion
  2.4 0.2 subtract_convert_fusion.1
  2.6 0.1 pad_maximum_fusion.1
  2.7 1.3 %collective-permute-start.1 = (bf16[256,4,128]{2,0,1:T(8,128)(2,1)S(1)}, bf16[256,4,128]{2,0,1:T(8,128)(2,1)S(1)}, u32[]{:S(2)}, u32[]{:S(2)}) collective-permute-start(bf16[256,4,128]{2,0,1:T(8,128)(2,1)S(1)} %pad_maximum_fusion.1), channel_id=1, source_target_pairs={{0,8},{4,12},{8,16},{12,20},{16,24},{20,28},{1,9},{5,13},{9,17},{1... | collective-permute-start | bytes 786440 | tf_op jit(solution)/shard_map/ppermute | solution.py:95
  4.0 3.4 %collective-permute-start = (bf16[256,4,128]{2,0,1:T(8,128)(2,1)S(1)}, bf16[256,4,128]{2,0,1:T(8,128)(2,1)S(1)}, u32[]{:S(2)}, u32[]{:S(2)}) collective-permute-start(bf16[256,4,128]{2,0,1:T(8,128)(2,1)S(1)} %pad_maximum_fusion.1), channel_id=1, source_target_pairs={{0,4},{8,12},{16,20},{24,28},{1,5},{9,13},{17,21},{25,29},{2,6},{1... | collective-permute-start | bytes 786440 | tf_op jit(solution)/shard_map/ppermute | solution.py:96
  7.5 1.0 %convert_element_type.58 = f32[256,4,128]{2,1,0:T(4,128)S(1)} convert(bf16[256,4,128]{2,1,0:T(4,128)(2,1)} %param.6) | non-fusion elementwise | flops 131072 | bytes 786432 | tf_op jit(solution)/shard_map/convert_element_type | solution.py:139
  8.5 0.0 copy-start.1
  8.5 0.5 subtract_convert_fusion
  9.1 0.1 pad_maximum_fusion
  9.3 0.1 fusion.61
  9.4 0.5 fusion.74
  10.0 0.0 copy-done.1
  10.0 0.3 fusion.58
  10.4 2.2 %collective-permute-done.1 = bf16[256,4,128]{2,0,1:T(8,128)(2,1)S(1)} collective-permute-done((bf16[256,4,128]{2,0,1:T(8,128)(2,1)S(1)}, bf16[256,4,128]{2,0,1:T(8,128)(2,1)S(1)}, u32[]{:S(2)}, u32[]{:S(2)}) %collective-permute-start.1) | collective-permute-done | bytes 262176 | tf_op jit(solution)/shard_map/ppermute | solution.py:95
  12.6 1.3 %collective-permute-start.3 = (bf16[256,4,128]{2,0,1:T(8,128)(2,1)S(1)}, bf16[256,4,128]{2,0,1:T(8,128)(2,1)S(1)}, u32[]{:S(2)}, u32[]{:S(2)}) collective-permute-start(bf16[256,4,128]{2,0,1:T(8,128)(2,1)S(1)} %collective-permute-done.1), channel_id=1, source_target_pairs={{8,16},{12,20},{16,24},{20,28},{9,17},{13,21},{17,25},{21,29},{10,... | collective-permute-start | bytes 786440 | tf_op jit(solution)/shard_map/ppermute | solution.py:95
  13.9 3.4 %collective-permute-start.2 = (bf16[256,4,128]{2,0,1:T(8,128)(2,1)S(1)}, bf16[256,4,128]{2,0,1:T(8,128)(2,1)S(1)}, u32[]{:S(2)}, u32[]{:S(2)}) collective-permute-start(bf16[256,4,128]{2,0,1:T(8,128)(2,1)S(1)} %collective-permute-done.1), channel_id=1, source_target_pairs={{8,12},{16,20},{24,28},{12,8},{20,16},{28,24},{9,13},{17,21},{25,2... | collective-permute-start | bytes 786440 | tf_op jit(solution)/shard_map/ppermute | solution.py:96
  17.4 0.5 fusion.73
  17.8 0.0 collective-permute-done
  17.9 0.5 fusion.75
  18.3 0.3 convolution_add_fusion.3
  18.7 0.3 convolution_add_fusion.2
  19.0 2.6 %collective-permute-done.3 = bf16[256,4,128]{2,0,1:T(8,128)(2,1)S(1)} collective-permute-done((bf16[256,4,128]{2,0,1:T(8,128)(2,1)S(1)}, bf16[256,4,128]{2,0,1:T(8,128)(2,1)S(1)}, u32[]{:S(2)}, u32[]{:S(2)}) %collective-permute-start.3) | collective-permute-done | bytes 262176 | tf_op jit(solution)/shard_map/ppermute | solution.py:95
  21.7 1.3 %collective-permute-start.6 = (bf16[256,4,128]{2,0,1:T(8,128)(2,1)S(1)}, bf16[256,4,128]{2,0,1:T(8,128)(2,1)S(1)}, u32[]{:S(2)}, u32[]{:S(2)}) collective-permute-start(bf16[256,4,128]{2,0,1:T(8,128)(2,1)S(1)} %collective-permute-done.3), channel_id=1, source_target_pairs={{16,28},{20,24},{17,29},{21,25},{18,30},{22,26},{19,31},{23,27}} | collective-permute-start | bytes 786440 | tf_op jit(solution)/shard_map/ppermute | solution.py:98
  23.0 1.3 %collective-permute-start.5 = (bf16[256,4,128]{2,0,1:T(8,128)(2,1)S(1)}, bf16[256,4,128]{2,0,1:T(8,128)(2,1)S(1)}, u32[]{:S(2)}, u32[]{:S(2)}) collective-permute-start(bf16[256,4,128]{2,0,1:T(8,128)(2,1)S(1)} %collective-permute-done.3), channel_id=1, source_target_pairs={{16,24},{20,28},{17,25},{21,29},{18,26},{22,30},{19,27},{23,31}} | collective-permute-start | bytes 786440 | tf_op jit(solution)/shard_map/ppermute | solution.py:95
  24.3 3.4 %collective-permute-start.4 = (bf16[256,4,128]{2,0,1:T(8,128)(2,1)S(1)}, bf16[256,4,128]{2,0,1:T(8,128)(2,1)S(1)}, u32[]{:S(2)}, u32[]{:S(2)}) collective-permute-start(bf16[256,4,128]{2,0,1:T(8,128)(2,1)S(1)} %collective-permute-done.3), channel_id=1, source_target_pairs={{16,20},{24,28},{20,16},{28,24},{17,21},{25,29},{21,17},{29,25},{1... | collective-permute-start | bytes 786440 | tf_op jit(solution)/shard_map/ppermute | solution.py:96
  27.7 0.5 fusion.71
  28.2 0.4 fusion.53
  28.6 0.0 collective-permute-done.2
  28.6 0.5 fusion.72
  29.1 0.4 fusion.46
  29.4 4.1 %collective-permute-done.6 = bf16[256,4,128]{2,0,1:T(8,128)(2,1)S(1)} collective-permute-done((bf16[256,4,128]{2,0,1:T(8,128)(2,1)S(1)}, bf16[256,4,128]{2,0,1:T(8,128)(2,1)S(1)}, u32[]{:S(2)}, u32[]{:S(2)}) %collective-permute-start.6) | collective-permute-done | bytes 262176 | tf_op jit(solution)/shard_map/ppermute | solution.py:98
  33.6 0.5 fusion.68
  34.0 2.4 %collective-permute-done.5 = bf16[256,4,128]{2,0,1:T(8,128)(2,1)S(1)} collective-permute-done((bf16[256,4,128]{2,0,1:T(8,128)(2,1)S(1)}, bf16[256,4,128]{2,0,1:T(8,128)(2,1)S(1)}, u32[]{:S(2)}, u32[]{:S(2)}) %collective-permute-start.5) | collective-permute-done | bytes 262176 | tf_op jit(solution)/shard_map/ppermute | solution.py:95
  36.4 0.5 fusion.69
  36.9 0.0 collective-permute-done.4
  36.9 0.5 fusion.70
  37.4 0.0 copy-start
  37.4 0.4 fusion.48
  37.8 0.3 fusion.50
  38.1 0.4 fusion.47
  38.5 0.1 collective-permute-start.8
  38.6 1.5 %collective-permute-start.7 = (bf16[2,2,256,128]{3,2,1,0:T(8,128)(2,1)S(1)}, bf16[2,2,256,128]{3,2,1,0:T(8,128)(2,1)S(1)}, u32[]{:S(2)}, u32[]{:S(2)}) collective-permute-start(bf16[2,2,256,128]{3,2,1,0:T(8,128)(2,1)S(1)} %fusion.47), channel_id=1, source_target_pairs={{0,2},{1,3},{2,0},{3,1},{4,6},{5,7},{6,4},{7,5},{8,10},{9,11},{10,... | collective-permute-start | bytes 786440 | tf_op jit(solution)/shard_map/ppermute | solution.py:117
  40.2 0.0 copy-done
  40.2 0.3 constant_dynamic-slice_fusion
  40.4 0.4 convolution_bitcast_fusion.3
  40.8 6.5 %collective-permute-done.7 = bf16[2,2,256,128]{3,2,1,0:T(8,128)(2,1)S(1)} collective-permute-done((bf16[2,2,256,128]{3,2,1,0:T(8,128)(2,1)S(1)}, bf16[2,2,256,128]{3,2,1,0:T(8,128)(2,1)S(1)}, u32[]{:S(2)}, u32[]{:S(2)}) %collective-permute-start.7) | collective-permute-done | bytes 262176 | tf_op jit(solution)/shard_map/ppermute | solution.py:117
  47.3 0.0 collective-permute-start.9
  47.3 0.0 collective-permute-done.8
  47.3 0.4 convolution_bitcast_fusion.1
  47.7 0.0 copy-start.3
  47.7 0.0 copy-start.2
  47.7 0.4 fusion.41
  48.1 0.7 %collective-permute-done.9 = bf16[2,2,256,128]{3,2,1,0:T(8,128)(2,1)S(1)} collective-permute-done((bf16[2,2,256,128]{3,2,1,0:T(8,128)(2,1)S(1)}, bf16[2,2,256,128]{3,2,1,0:T(8,128)(2,1)S(1)}, u32[]{:S(2)}, u32[]{:S(2)}) %collective-permute-start.9) | collective-permute-done | bytes 262176 | tf_op jit(solution)/shard_map/ppermute | solution.py:117
  48.9 0.5 multiply_reduce_fusion
  49.3 0.2 collective-permute-start.10
  49.5 1.0 %collective-permute-done.10 = f32[256]{0:T(256)S(1)} collective-permute-done((f32[256]{0:T(256)S(1)}, f32[256]{0:T(256)S(1)}, u32[]{:S(2)}, u32[]{:S(2)}) %collective-permute-start.10) | collective-permute-done | bytes 1056 | tf_op jit(solution)/shard_map/ppermute | solution.py:125
  50.5 1.5 %collective-permute-start.11 = (f32[256]{0:T(256)S(1)}, f32[256]{0:T(256)S(1)}, u32[]{:S(2)}, u32[]{:S(2)}) collective-permute-start(f32[256]{0:T(256)S(1)} %add.206), channel_id=1, source_target_pairs={{0,2},{1,3},{2,0},{3,1},{4,6},{5,7},{6,4},{7,5},{8,10},{9,11},{10,... | collective-permute-start | bytes 3080 | tf_op jit(solution)/shard_map/ppermute | solution.py:125
  52.0 0.0 copy-done.3
  52.0 2.1 %collective-permute-done.11 = f32[256]{0:T(256)S(1)} collective-permute-done((f32[256]{0:T(256)S(1)}, f32[256]{0:T(256)S(1)}, u32[]{:S(2)}, u32[]{:S(2)}) %collective-permute-start.11) | collective-permute-done | bytes 1056 | tf_op jit(solution)/shard_map/ppermute | solution.py:125
  54.1 0.0 copy-done.2
  54.1 0.9 %add_convert_fusion = bf16[256,768]{1,0:T(8,128)(2,1)} fusion(f32[256,768]{1,0:T(8,128)S(1)} %get-tuple-element.32, bf16[256,768]{1,0:T(8,128)(2,1)S(1)} %copy-done.2, f32[768]{0:T(1024)S(1)} %convert_element_type.68, f32[256]{0:T(256)S(1)} %add_rsqrt_fusion), kind=kLoop, calls=%fused_computation.64 | loop fusion | flops 983040 | bytes 1576960 | tf_op jit(solution)/shard_map/convert_element_type | solution.py:201
  (9 shorter events, 0.1 us)
Async XLA Ops:
  2.7 9.9 %collective-permute-start.1 = (bf16[256,4,128]{2,0,1:T(8,128)(2,1)S(1)}, bf16[256,4,128]{2,0,1:T(8,128)(2,1)S(1)}, u32[]{:S(2)}, u32[]{:S(2)}) collective-permute-start(bf16[256,4,128]{2,0,1:T(8,128)(2,1)S(1)} %pad_maximum_fusion.1), channel_id=1, source_target_pairs={{0,8},{4,12},{8,16},{12,20},{16,24},{20,28},{1,9},{5,13},{9,17},{1... | collective-permute-start | bytes 786440 | tf_op jit(solution)/shard_map/ppermute | solution.py:95
  4.0 13.8 %collective-permute-start = (bf16[256,4,128]{2,0,1:T(8,128)(2,1)S(1)}, bf16[256,4,128]{2,0,1:T(8,128)(2,1)S(1)}, u32[]{:S(2)}, u32[]{:S(2)}) collective-permute-start(bf16[256,4,128]{2,0,1:T(8,128)(2,1)S(1)} %pad_maximum_fusion.1), channel_id=1, source_target_pairs={{0,4},{8,12},{16,20},{24,28},{1,5},{9,13},{17,21},{25,29},{2,6},{1... | collective-permute-start | bytes 786440 | tf_op jit(solution)/shard_map/ppermute | solution.py:96
  8.5 1.5 %copy-start.1 = (bf16[256,2,128]{2,1,0:T(2,128)(2,1)S(1)}, bf16[256,2,128]{2,1,0:T(2,128)(2,1)}, u32[]{:S(2)}) copy-start(bf16[256,2,128]{2,1,0:T(2,128)(2,1)} %param.8) | copy-start | bytes 393220
  12.6 9.1 %collective-permute-start.3 = (bf16[256,4,128]{2,0,1:T(8,128)(2,1)S(1)}, bf16[256,4,128]{2,0,1:T(8,128)(2,1)S(1)}, u32[]{:S(2)}, u32[]{:S(2)}) collective-permute-start(bf16[256,4,128]{2,0,1:T(8,128)(2,1)S(1)} %collective-permute-done.1), channel_id=1, source_target_pairs={{8,16},{12,20},{16,24},{20,28},{9,17},{13,21},{17,25},{21,29},{10,... | collective-permute-start | bytes 786440 | tf_op jit(solution)/shard_map/ppermute | solution.py:95
  13.9 14.6 %collective-permute-start.2 = (bf16[256,4,128]{2,0,1:T(8,128)(2,1)S(1)}, bf16[256,4,128]{2,0,1:T(8,128)(2,1)S(1)}, u32[]{:S(2)}, u32[]{:S(2)}) collective-permute-start(bf16[256,4,128]{2,0,1:T(8,128)(2,1)S(1)} %collective-permute-done.1), channel_id=1, source_target_pairs={{8,12},{16,20},{24,28},{12,8},{20,16},{28,24},{9,13},{17,21},{25,2... | collective-permute-start | bytes 786440 | tf_op jit(solution)/shard_map/ppermute | solution.py:96
  21.7 11.9 %collective-permute-start.6 = (bf16[256,4,128]{2,0,1:T(8,128)(2,1)S(1)}, bf16[256,4,128]{2,0,1:T(8,128)(2,1)S(1)}, u32[]{:S(2)}, u32[]{:S(2)}) collective-permute-start(bf16[256,4,128]{2,0,1:T(8,128)(2,1)S(1)} %collective-permute-done.3), channel_id=1, source_target_pairs={{16,28},{20,24},{17,29},{21,25},{18,30},{22,26},{19,31},{23,27}} | collective-permute-start | bytes 786440 | tf_op jit(solution)/shard_map/ppermute | solution.py:98
  23.0 13.4 %collective-permute-start.5 = (bf16[256,4,128]{2,0,1:T(8,128)(2,1)S(1)}, bf16[256,4,128]{2,0,1:T(8,128)(2,1)S(1)}, u32[]{:S(2)}, u32[]{:S(2)}) collective-permute-start(bf16[256,4,128]{2,0,1:T(8,128)(2,1)S(1)} %collective-permute-done.3), channel_id=1, source_target_pairs={{16,24},{20,28},{17,25},{21,29},{18,26},{22,30},{19,27},{23,31}} | collective-permute-start | bytes 786440 | tf_op jit(solution)/shard_map/ppermute | solution.py:95
  24.3 12.6 %collective-permute-start.4 = (bf16[256,4,128]{2,0,1:T(8,128)(2,1)S(1)}, bf16[256,4,128]{2,0,1:T(8,128)(2,1)S(1)}, u32[]{:S(2)}, u32[]{:S(2)}) collective-permute-start(bf16[256,4,128]{2,0,1:T(8,128)(2,1)S(1)} %collective-permute-done.3), channel_id=1, source_target_pairs={{16,20},{24,28},{20,16},{28,24},{17,21},{25,29},{21,17},{29,25},{1... | collective-permute-start | bytes 786440 | tf_op jit(solution)/shard_map/ppermute | solution.py:96
  37.4 2.8 %copy-start = (bf16[16,128,768]{2,1,0:T(8,128)(2,1)S(1)}, bf16[16,128,768]{2,1,0:T(8,128)(2,1)}, u32[]{:S(2)}) copy-start(bf16[16,128,768]{2,1,0:T(8,128)(2,1)} %param.10) | copy-start | bytes 9437188
  38.5 8.8 %collective-permute-start.8 = (bf16[2,2,256,128]{3,2,1,0:T(8,128)(2,1)S(1)}, bf16[2,2,256,128]{3,2,1,0:T(8,128)(2,1)S(1)}, u32[]{:S(2)}, u32[]{:S(2)}) collective-permute-start(bf16[2,2,256,128]{3,2,1,0:T(8,128)(2,1)S(1)} %fusion.47), channel_id=1, source_target_pairs={{0,1},{1,0},{2,3},{3,2},{4,5},{5,4},{6,7},{7,6},{8,9},{9,8},{10,11... | collective-permute-start | bytes 786440 | tf_op jit(solution)/shard_map/ppermute | solution.py:117
  38.6 8.7 %collective-permute-start.7 = (bf16[2,2,256,128]{3,2,1,0:T(8,128)(2,1)S(1)}, bf16[2,2,256,128]{3,2,1,0:T(8,128)(2,1)S(1)}, u32[]{:S(2)}, u32[]{:S(2)}) collective-permute-start(bf16[2,2,256,128]{3,2,1,0:T(8,128)(2,1)S(1)} %fusion.47), channel_id=1, source_target_pairs={{0,2},{1,3},{2,0},{3,1},{4,6},{5,7},{6,4},{7,5},{8,10},{9,11},{10,... | collective-permute-start | bytes 786440 | tf_op jit(solution)/shard_map/ppermute | solution.py:117
  47.3 1.5 %collective-permute-start.9 = (bf16[2,2,256,128]{3,2,1,0:T(8,128)(2,1)S(1)}, bf16[2,2,256,128]{3,2,1,0:T(8,128)(2,1)S(1)}, u32[]{:S(2)}, u32[]{:S(2)}) collective-permute-start(bf16[2,2,256,128]{3,2,1,0:T(8,128)(2,1)S(1)} %collective-permute-done.7), channel_id=1, source_target_pairs={{0,1},{1,0},{2,3},{3,2},{4,5},{5,4},{6,7},{7,6},{8,9},{9,8},{10,11... | collective-permute-start | bytes 786440 | tf_op jit(solution)/shard_map/ppermute | solution.py:117
  47.7 4.3 %copy-start.3 = (bf16[768]{0:T(1024)(128)(2,1)S(1)}, bf16[768]{0:T(1024)(128)(2,1)}, u32[]{:S(2)}) copy-start(bf16[768]{0:T(1024)(128)(2,1)} %param.11) | copy-start | bytes 4612
  47.7 6.4 %copy-start.2 = (bf16[256,768]{1,0:T(8,128)(2,1)S(1)}, bf16[256,768]{1,0:T(8,128)(2,1)}, u32[]{:S(2)}) copy-start(bf16[256,768]{1,0:T(8,128)(2,1)} %param.9) | copy-start | bytes 1179652
  49.3 1.2 %collective-permute-start.10 = (f32[256]{0:T(256)S(1)}, f32[256]{0:T(256)S(1)}, u32[]{:S(2)}, u32[]{:S(2)}) collective-permute-start(f32[256]{0:T(256)S(1)} %get-tuple-element.31), channel_id=1, source_target_pairs={{0,1},{1,0},{2,3},{3,2},{4,5},{5,4},{6,7},{7,6},{8,9},{9,8},{10,11... | collective-permute-start | bytes 3080 | tf_op jit(solution)/shard_map/ppermute | solution.py:125
  50.5 3.6 %collective-permute-start.11 = (f32[256]{0:T(256)S(1)}, f32[256]{0:T(256)S(1)}, u32[]{:S(2)}, u32[]{:S(2)}) collective-permute-start(f32[256]{0:T(256)S(1)} %add.206), channel_id=1, source_target_pairs={{0,2},{1,3},{2,0},{3,1},{4,6},{5,7},{6,4},{7,5},{8,10},{9,11},{10,... | collective-permute-start | bytes 3080 | tf_op jit(solution)/shard_map/ppermute | solution.py:125

commit v14 on v8

--- a/solution.py
+++ b/solution.py
@@ -171,17 +171,24 @@
     tp_index = lax.axis_index("tp")
     butterfly = tp_size & (tp_size - 1) == 0
     if butterfly:
-        projected = None
+        weight_sets = [out_weight]
+        if tp_size >= 2:
+            weight_sets.append(
+                lax.ppermute(out_weight, "tp", [(source, source ^ 1) for source in range(tp_size)])
+            )
+        projections = [None] * len(weight_sets)
         for held, offset in exchanged(attended, tp_size):
             owner = jnp.bitwise_xor(tp_index, offset)
-            weight_rows = lax.dynamic_slice_in_dim(out_weight, owner * q_heads, q_heads, 0)
-            part = lax.dot_general(
-                held,
-                weight_rows.reshape(kv_heads, heads_per_group, head_size, local_cols),
-                (((0, 1, 3), (0, 1, 2)), ((), ())),
-                preferred_element_type=jnp.float32,
-            )
-            projected = part if projected is None else projected + part
+            for slot, weights in enumerate(weight_sets):
+                weight_rows = lax.dynamic_slice_in_dim(weights, owner * q_heads, q_heads, 0)
+                part = lax.dot_general(
+                    held,
+                    weight_rows.reshape(kv_heads, heads_per_group, head_size, local_cols),
+                    (((0, 1, 3), (0, 1, 2)), ((), ())),
+                    preferred_element_type=jnp.float32,
+                )
+                projections[slot] = part if projections[slot] is None else projections[slot] + part
+        projected = projections[0]
     else:
         attended = jnp.transpose(attended, (2, 0, 1, 3)).reshape(rows, q_heads, head_size)
         piece = lax.all_gather(attended, "tp", axis=1, tiled=True)
@@ -192,7 +199,15 @@
         )
     partial_sums = jnp.sum(projected * projected, axis=1)
     if butterfly:
-        square_sums = summed(partial_sums, tp_size)
+        square_sums = partial_sums
+        for extra in projections[1:]:
+            square_sums = square_sums + jnp.sum(extra * extra, axis=1)
+        bit = 2
+        while bit < tp_size:
+            square_sums = square_sums + lax.ppermute(
+                square_sums, "tp", [(source, source ^ bit) for source in range(tp_size)]
+            )
+            bit *= 2
     else:
         square_sums = jnp.sum(lax.all_gather(partial_sums, "tp", axis=0), axis=0)
     normed = projected * lax.rsqrt(square_sums / D + 1e-06)[:, None] * post_gain.astype(jnp.float32)

time: 55.5 us -> 62 us (1.12)
  matrix products: 8.3 us -> 14.3 us
  starting transfers between devices: 19 us -> 18 us
  other arithmetic: 4.53 us -> 5.24 us
    ppermute x3, waiting for transfers between devices: 0.01 us -> 3.4 us  [along_lines(): crossed = lax.ppermute(line, 'ctx', across(step))]
    dot_general x8, matrix products: 2.84 us -> 5.43 us  [attend_block(): jnp.einsum('grsk,kgh->grsh', weights.astype(jnp.bfloat16), value_block, p...]
    ppermute x3, waiting for transfers between devices: 7.26 us -> 4.76 us  [along_lines(): arrived = lax.ppermute(line, 'ctx', forward(step))]
    dot_general x8, matrix products: 3.91 us -> 5.72 us  [attend_block(): jnp.einsum('sgrh,kgh->grsk', rotary_queries, key_block, preferred_element...]
    dot_general x4 -> x8, matrix products: 1.56 us -> 3.11 us  [local(): lax.dot_general(held, weight_rows.reshape(kv_heads, heads_per_group, head...]
    ppermute x3 -> x2, waiting for transfers between devices: 2.94 us -> 2.03 us  [the longest x1 2.03 us: local(): lax.ppermute(square_sums, 'tp', [(source, source ^ bit) for source in ran...]
    ppermute x3, starting transfers between devices: 10.3 us -> 9.55 us  [along_lines(): crossed = lax.ppermute(line, 'ctx', across(step))]
    concatenate x1, other arithmetic: 0.11 us -> 0.81 us  [along_lines(): line = jnp.concatenate([key_block, value_block], axis=1)]
  transfers between devices with their start and end apart: 13 -> 12, of which waited for: 8 -> 8; matrix products, arithmetic and copies ran while one was open for 15% -> 24% of each run, Pallas kernels for 0% -> 0%
where the time goes in v14:
time: 62 us; the launch traced here: 61.6 us
  waiting for transfers between devices  22.2 us (36%)
  starting transfers between devices  18 us (29%)
  matrix products  14.3 us (23%)
  other arithmetic  5.24 us (8%)
  local copies, waits for them, and re-layouts  1.53 us (2%)
    ppermute x3, starting transfers between devices, along_lines(): crossed = lax.ppermute(line, 'ctx', across(step))  9.55 us
    ppermute x3, waiting for transfers between devices, exchanged(): lax.ppermute(held, 'tp', pairs)  7.23 us
    dot_general x8, matrix products, attend_block(): jnp.einsum('sgrh,kgh->grsk', rotary_queries, key_block, preferred_element...  5.72 us
    dot_general x8, matrix products, attend_block(): jnp.einsum('grsk,kgh->grsh', weights.astype(jnp.bfloat16), value_block, p...  5.43 us
    ppermute x1, waiting for transfers between devices, along_lines(): lax.ppermute(line, 'ctx', [(source, 2 * (source // 2) + 3 - source % 2) f...  4.81 us
    ppermute x3, waiting for transfers between devices, along_lines(): arrived = lax.ppermute(line, 'ctx', forward(step))  4.76 us
    ppermute x3, starting transfers between devices, along_lines(): arrived = lax.ppermute(line, 'ctx', forward(step))  3.85 us
    ppermute x3, waiting for transfers between devices, along_lines(): crossed = lax.ppermute(line, 'ctx', across(step))  3.4 us
  transfers between devices with their start and end apart: 12, of which 8 were waited for; matrix products, arithmetic and copies ran while one was open for 24% of the time, Pallas kernels for 0%

profile of v14, /device:TPU:24, one launch (start us, length us, event | category | flops | bytes accessed | tf_op | source)
XLA Modules:
  0.0 61.6 jit_solution(16894771528009990232)
XLA Ops:
  0.0 0.9 %copy_convert_fusion = f32[256,2,128]{2,0,1:T(8,128)S(1)} fusion(bf16[256,2,128]{2,1,0:T(2,128)(2,1)} %param.7), kind=kLoop, calls=%fused_computation.117 | loop fusion | flops 65536 | bytes 393216 | tf_op jit(solution)/shard_map/convert_element_type | solution.py:140
  1.0 0.9 %copy.12 = bf16[256,2,128]{2,0,1:T(8,128)(2,1)S(1)} copy(bf16[256,2,128]{2,1,0:T(2,128)(2,1)} %param.8) | data formatting | bytes 262144 | tf_op args[2]
  1.9 0.5 multiply_cosine_fusion
  2.4 0.2 subtract_convert_fusion.1
  2.6 0.8 %pad_maximum_fusion.1 = bf16[256,4,128]{2,0,1:T(8,128)(2,1)} fusion(bf16[256,2,128]{2,0,1:T(8,128)(2,1)S(1)} %copy.12, bf16[256,2,64]{2,0,1:T(8,128)(2,1)S(1)} %get-tuple-element.16, bf16[256,2,64]{2,0,1:T(8,128)(2,1)S(1)} %get-tuple-element.15), kind=kLoop, calls=%fused_computation.92 | loop fusion | flops 786432 | bytes 524288 | tf_op jit(solution)/shard_map/concatenate | solution.py:89
  3.4 1.3 %collective-permute-start.1 = (bf16[256,4,128]{2,0,1:T(8,128)(2,1)}, bf16[256,4,128]{2,0,1:T(8,128)(2,1)}, u32[]{:S(2)}, u32[]{:S(2)}) collective-permute-start(bf16[256,4,128]{2,0,1:T(8,128)(2,1)} %pad_maximum_fusion.1), channel_id=1, source_target_pairs={{0,8},{4,12},{8,16},{12,20},{16,24},{20,28},{1,9},{5,13},{9,17},{1... | collective-permute-start | bytes 786440 | tf_op jit(solution)/shard_map/ppermute | solution.py:95
  4.7 4.1 %collective-permute-start = (bf16[256,4,128]{2,0,1:T(8,128)(2,1)}, bf16[256,4,128]{2,0,1:T(8,128)(2,1)}, u32[]{:S(2)}, u32[]{:S(2)}) collective-permute-start(bf16[256,4,128]{2,0,1:T(8,128)(2,1)} %pad_maximum_fusion.1), channel_id=1, source_target_pairs={{0,4},{8,12},{16,20},{24,28},{1,5},{9,13},{17,21},{25,29},{2,6},{1... | collective-permute-start | bytes 786440 | tf_op jit(solution)/shard_map/ppermute | solution.py:96
  8.8 0.0 collective-permute-start.10
  8.8 1.0 %convert_element_type.58 = f32[256,4,128]{2,1,0:T(4,128)S(1)} convert(bf16[256,4,128]{2,1,0:T(4,128)(2,1)} %param.6) | non-fusion elementwise | flops 131072 | bytes 786432 | tf_op jit(solution)/shard_map/convert_element_type | solution.py:138
  9.8 0.0 copy-start.2
  9.9 0.5 subtract_convert_fusion
  10.5 0.1 pad_maximum_fusion
  10.6 0.1 fusion.66
  10.8 0.6 fusion.79
  11.3 1.1 %fusion.63 = f32[2,2,256,128]{3,2,1,0:T(8,128)} fusion(bf16[2,2,256,256]{2,3,1,0:T(8,128)(2,1)S(1)} %get-tuple-element.32, bf16[256,2,128,1]{2,1,0,3:T(2,128)(2,1)S(1)} %bitcast.210), kind=kOutput, calls=%fused_computation.85 | convolution fusion | flops 67108864 | bytes 1179648 | tf_op jit(solution)/shard_map/grsk,kgh->grsh/dot_general | solution.py:58
  12.5 1.2 %collective-permute-done.1 = bf16[256,4,128]{2,0,1:T(8,128)(2,1)} collective-permute-done((bf16[256,4,128]{2,0,1:T(8,128)(2,1)}, bf16[256,4,128]{2,0,1:T(8,128)(2,1)}, u32[]{:S(2)}, u32[]{:S(2)}) %collective-permute-start.1) | collective-permute-done | bytes 262176 | tf_op jit(solution)/shard_map/ppermute | solution.py:95
  13.6 1.3 %collective-permute-start.3 = (bf16[256,4,128]{2,0,1:T(8,128)(2,1)}, bf16[256,4,128]{2,0,1:T(8,128)(2,1)S(1)}, u32[]{:S(2)}, u32[]{:S(2)}) collective-permute-start(bf16[256,4,128]{2,0,1:T(8,128)(2,1)} %collective-permute-done.1), channel_id=1, source_target_pairs={{8,16},{12,20},{16,24},{20,28},{9,17},{13,21},{17,25},{21,29},{10,... | collective-permute-start | bytes 786440 | tf_op jit(solution)/shard_map/ppermute | solution.py:95
  14.9 3.4 %collective-permute-start.2 = (bf16[256,4,128]{2,0,1:T(8,128)(2,1)}, bf16[256,4,128]{2,0,1:T(8,128)(2,1)S(1)}, u32[]{:S(2)}, u32[]{:S(2)}) collective-permute-start(bf16[256,4,128]{2,0,1:T(8,128)(2,1)} %collective-permute-done.1), channel_id=1, source_target_pairs={{8,12},{16,20},{24,28},{12,8},{20,16},{28,24},{9,13},{17,21},{25,2... | collective-permute-start | bytes 786440 | tf_op jit(solution)/shard_map/ppermute | solution.py:96
  18.4 1.4 %fusion.78 = (f32[2,2,256]{2,1,0:T(2,128)S(1)}, bf16[2,2,256,256]{2,3,1,0:T(8,128)(2,1)S(1)}) fusion(bf16[256,2,2,128]{3,0,2,1:T(8,128)(2,1)S(1)} %pad_maximum_fusion, bf16[256,4,128]{2,0,1:T(8,128)(2,1)} %collective-permute-done.1, pred[]{:T(512)S(6)} %and.58), kind=kOutput, calls=%fused_computation.138 | convolution fusion | flops 68418560 | bytes 921601 | tf_op jit(solution)/shard_map/sgrh,kgh->grsk/dot_general | solution.py:43
  19.8 0.0 collective-permute-done
  19.8 1.4 %fusion.80 = (f32[2,2,256]{2,1,0:T(2,128)S(1)}, bf16[2,2,256,256]{2,3,1,0:T(8,128)(2,1)S(1)}) fusion(bf16[256,2,2,128]{3,0,2,1:T(8,128)(2,1)S(1)} %pad_maximum_fusion, bf16[256,4,128]{2,0,1:T(8,128)(2,1)} %collective-permute-done, pred[]{:T(512)S(6)} %and.57), kind=kOutput, calls=%fused_computation.140 | convolution fusion | flops 68418560 | bytes 921601 | tf_op jit(solution)/shard_map/sgrh,kgh->grsk/dot_general | solution.py:43
  21.2 1.2 %convolution_add_fusion.3 = f32[2,2,256,128]{3,2,1,0:T(8,128)S(1)} fusion(f32[2,2,256,128]{3,2,1,0:T(8,128)S(1)} %copy-done.1, bf16[2,2,256,256]{2,3,1,0:T(8,128)(2,1)S(1)} %get-tuple-element.34, bf16[256,4,128]{2,0,1:T(8,128)(2,1)} %collective-permute-done), kind=kOutput, calls=%fused_computation.70 | convolution fusion | flops 67239936 | bytes 1703936 | tf_op jit(solution)/shard_map/grsk,kgh->grsh/dot_general | solution.py:58
  22.4 1.2 %convolution_add_fusion.2 = f32[2,2,256,128]{3,2,1,0:T(8,128)S(1)} fusion(f32[2,2,256,128]{3,2,1,0:T(8,128)S(1)} %convolution_add_fusion.3, bf16[2,2,256,256]{2,3,1,0:T(8,128)(2,1)S(1)} %get-tuple-element.30, bf16[256,4,128]{2,0,1:T(8,128)(2,1)} %collective-permute-done.1), kind=kOutput, calls=%fused_computation.69 | convolution fusion | flops 67239936 | bytes 1703936 | tf_op jit(solution)/shard_map/grsk,kgh->grsh/dot_general | solution.py:58
  23.7 0.7 %collective-permute-done.3 = bf16[256,4,128]{2,0,1:T(8,128)(2,1)S(1)} collective-permute-done((bf16[256,4,128]{2,0,1:T(8,128)(2,1)}, bf16[256,4,128]{2,0,1:T(8,128)(2,1)S(1)}, u32[]{:S(2)}, u32[]{:S(2)}) %collective-permute-start.3) | collective-permute-done | bytes 262176 | tf_op jit(solution)/shard_map/ppermute | solution.py:95
  24.3 2.0 %collective-permute-start.4 = (bf16[256,4,128]{2,0,1:T(8,128)(2,1)S(1)}, bf16[256,4,128]{2,0,1:T(8,128)(2,1)S(1)}, u32[]{:S(2)}, u32[]{:S(2)}) collective-permute-start(bf16[256,4,128]{2,0,1:T(8,128)(2,1)S(1)} %collective-permute-done.3), channel_id=1, source_target_pairs={{16,20},{24,28},{20,16},{28,24},{17,21},{25,29},{21,17},{29,25},{1... | collective-permute-start | bytes 786440 | tf_op jit(solution)/shard_map/ppermute | solution.py:96
  26.3 1.3 %collective-permute-start.5 = (bf16[256,4,128]{2,0,1:T(8,128)(2,1)S(1)}, bf16[256,4,128]{2,0,1:T(8,128)(2,1)S(1)}, u32[]{:S(2)}, u32[]{:S(2)}) collective-permute-start(bf16[256,4,128]{2,0,1:T(8,128)(2,1)S(1)} %collective-permute-done.3), channel_id=1, source_target_pairs={{16,24},{20,28},{17,25},{21,29},{18,26},{22,30},{19,27},{23,31}} | collective-permute-start | bytes 786440 | tf_op jit(solution)/shard_map/ppermute | solution.py:95
  27.6 1.3 %collective-permute-start.6 = (bf16[256,4,128]{2,0,1:T(8,128)(2,1)S(1)}, bf16[256,4,128]{2,0,1:T(8,128)(2,1)S(1)}, u32[]{:S(2)}, u32[]{:S(2)}) collective-permute-start(bf16[256,4,128]{2,0,1:T(8,128)(2,1)S(1)} %collective-permute-done.3), channel_id=1, source_target_pairs={{16,28},{20,24},{17,29},{21,25},{18,30},{22,26},{19,31},{23,27}} | collective-permute-start | bytes 786440 | tf_op jit(solution)/shard_map/ppermute | solution.py:98
  28.9 0.5 fusion.76
  29.4 0.4 fusion.58
  29.8 0.0 collective-permute-done.2
  29.8 0.5 fusion.77
  30.3 0.4 fusion.50
  30.6 3.4 %collective-permute-done.4 = bf16[256,4,128]{2,0,1:T(8,128)(2,1)S(1)} collective-permute-done((bf16[256,4,128]{2,0,1:T(8,128)(2,1)S(1)}, bf16[256,4,128]{2,0,1:T(8,128)(2,1)S(1)}, u32[]{:S(2)}, u32[]{:S(2)}) %collective-permute-start.4) | collective-permute-done | bytes 262176 | tf_op jit(solution)/shard_map/ppermute | solution.py:96
  34.0 0.5 fusion.75
  34.5 2.9 %collective-permute-done.5 = bf16[256,4,128]{2,0,1:T(8,128)(2,1)S(1)} collective-permute-done((bf16[256,4,128]{2,0,1:T(8,128)(2,1)S(1)}, bf16[256,4,128]{2,0,1:T(8,128)(2,1)S(1)}, u32[]{:S(2)}, u32[]{:S(2)}) %collective-permute-start.5) | collective-permute-done | bytes 262176 | tf_op jit(solution)/shard_map/ppermute | solution.py:95
  37.4 0.5 fusion.74
  37.9 4.8 %collective-permute-done.6 = bf16[256,4,128]{2,0,1:T(8,128)(2,1)S(1)} collective-permute-done((bf16[256,4,128]{2,0,1:T(8,128)(2,1)S(1)}, bf16[256,4,128]{2,0,1:T(8,128)(2,1)S(1)}, u32[]{:S(2)}, u32[]{:S(2)}) %collective-permute-start.6) | collective-permute-done | bytes 262176 | tf_op jit(solution)/shard_map/ppermute | solution.py:98
  42.7 0.5 fusion.73
  43.2 0.0 copy-start
  43.3 0.3 fusion.55
  43.6 0.3 fusion.53
  44.0 0.4 fusion.52
  44.4 0.1 collective-permute-start.8
  44.4 1.6 %collective-permute-start.7 = (bf16[2,2,256,128]{3,2,1,0:T(8,128)(2,1)S(1)}, bf16[2,2,256,128]{3,2,1,0:T(8,128)(2,1)S(1)}, u32[]{:S(2)}, u32[]{:S(2)}) collective-permute-start(bf16[2,2,256,128]{3,2,1,0:T(8,128)(2,1)S(1)} %fusion.52), channel_id=1, source_target_pairs={{0,2},{1,3},{2,0},{3,1},{4,6},{5,7},{6,4},{7,5},{8,10},{9,11},{10,... | collective-permute-start | bytes 786440 | tf_op jit(solution)/shard_map/ppermute | solution.py:117
  46.0 0.3 constant_dynamic-slice_fusion.4
  46.3 0.4 convolution_bitcast_fusion.7
  46.7 6.5 %collective-permute-done.7 = bf16[2,2,256,128]{3,2,1,0:T(8,128)(2,1)S(1)} collective-permute-done((bf16[2,2,256,128]{3,2,1,0:T(8,128)(2,1)S(1)}, bf16[2,2,256,128]{3,2,1,0:T(8,128)(2,1)S(1)}, u32[]{:S(2)}, u32[]{:S(2)}) %collective-permute-start.7) | collective-permute-done | bytes 262176 | tf_op jit(solution)/shard_map/ppermute | solution.py:117
  53.2 0.0 collective-permute-start.9
  53.2 0.0 collective-permute-done.8
  53.2 0.4 convolution_bitcast_fusion.5
  53.5 0.4 fusion.41
  53.9 0.8 %collective-permute-done.9 = bf16[2,2,256,128]{3,2,1,0:T(8,128)(2,1)S(1)} collective-permute-done((bf16[2,2,256,128]{3,2,1,0:T(8,128)(2,1)S(1)}, bf16[2,2,256,128]{3,2,1,0:T(8,128)(2,1)S(1)}, u32[]{:S(2)}, u32[]{:S(2)}) %collective-permute-start.9) | collective-permute-done | bytes 262176 | tf_op jit(solution)/shard_map/ppermute | solution.py:117
  54.7 0.5 multiply_reduce_fusion
  55.1 0.0 collective-permute-done.10
  55.2 0.2 constant_dynamic-slice_fusion
  55.4 0.4 convolution_bitcast_fusion.1
  55.8 0.0 copy-start.4
  55.8 0.0 copy-start.3
  55.8 0.4 convolution_bitcast_fusion.2
  56.2 0.4 fusion.44
  56.5 0.5 fusion.51
  57.0 1.6 %collective-permute-start.11 = (f32[256]{0:T(256)S(1)}, f32[256]{0:T(256)S(1)}, u32[]{:S(2)}, u32[]{:S(2)}) collective-permute-start(f32[256]{0:T(256)S(1)} %add.222), channel_id=1, source_target_pairs={{0,2},{1,3},{2,0},{3,1},{4,6},{5,7},{6,4},{7,5},{8,10},{9,11},{10,... | collective-permute-start | bytes 3080 | tf_op jit(solution)/shard_map/ppermute | solution.py:207
  58.6 2.0 %collective-permute-done.11 = f32[256]{0:T(256)S(1)} collective-permute-done((f32[256]{0:T(256)S(1)}, f32[256]{0:T(256)S(1)}, u32[]{:S(2)}, u32[]{:S(2)}) %collective-permute-start.11) | collective-permute-done | bytes 1056 | tf_op jit(solution)/shard_map/ppermute | solution.py:207
  60.6 0.9 %add_convert_fusion = bf16[256,768]{1,0:T(8,128)(2,1)} fusion(f32[256,768]{1,0:T(8,128)S(1)} %get-tuple-element.36, bf16[256,768]{1,0:T(8,128)(2,1)S(1)} %copy-done.3, f32[768]{0:T(1024)S(1)} %convert_element_type.68, f32[256]{0:T(256)S(1)} %add_rsqrt_fusion), kind=kLoop, calls=%fused_computation.73 | loop fusion | flops 983040 | bytes 1576960 | tf_op jit(solution)/shard_map/convert_element_type | solution.py:215
  (15 shorter events, 0.1 us)
Async XLA Ops:
  3.4 10.2 %collective-permute-start.1 = (bf16[256,4,128]{2,0,1:T(8,128)(2,1)}, bf16[256,4,128]{2,0,1:T(8,128)(2,1)}, u32[]{:S(2)}, u32[]{:S(2)}) collective-permute-start(bf16[256,4,128]{2,0,1:T(8,128)(2,1)} %pad_maximum_fusion.1), channel_id=1, source_target_pairs={{0,8},{4,12},{8,16},{12,20},{16,24},{20,28},{1,9},{5,13},{9,17},{1... | collective-permute-start | bytes 786440 | tf_op jit(solution)/shard_map/ppermute | solution.py:95
  4.7 15.1 %collective-permute-start = (bf16[256,4,128]{2,0,1:T(8,128)(2,1)}, bf16[256,4,128]{2,0,1:T(8,128)(2,1)}, u32[]{:S(2)}, u32[]{:S(2)}) collective-permute-start(bf16[256,4,128]{2,0,1:T(8,128)(2,1)} %pad_maximum_fusion.1), channel_id=1, source_target_pairs={{0,4},{8,12},{16,20},{24,28},{1,5},{9,13},{17,21},{25,29},{2,6},{1... | collective-permute-start | bytes 786440 | tf_op jit(solution)/shard_map/ppermute | solution.py:96
  8.8 46.3 %collective-permute-start.10 = (bf16[16,128,768]{2,1,0:T(8,128)(2,1)}, bf16[16,128,768]{2,1,0:T(8,128)(2,1)S(1)}, u32[]{:S(2)}, u32[]{:S(2)}) collective-permute-start(bf16[16,128,768]{2,1,0:T(8,128)(2,1)} %param.10), channel_id=1, source_target_pairs={{0,1},{1,0},{2,3},{3,2},{4,5},{5,4},{6,7},{7,6},{8,9},{9,8},{10,11... | collective-permute-start | bytes 9437192 | tf_op jit(solution)/shard_map/ppermute | solution.py:177
  9.8 1.5 %copy-start.2 = (bf16[256,2,128]{2,1,0:T(2,128)(2,1)S(1)}, bf16[256,2,128]{2,1,0:T(2,128)(2,1)}, u32[]{:S(2)}) copy-start(bf16[256,2,128]{2,1,0:T(2,128)(2,1)} %param.8) | copy-start | bytes 393220
  12.5 8.7 %copy-start.1 = (f32[2,2,256,128]{3,2,1,0:T(8,128)S(1)}, f32[2,2,256,128]{3,2,1,0:T(8,128)}, u32[]{:S(2)}) copy-start(f32[2,2,256,128]{3,2,1,0:T(8,128)} %fusion.63) | copy-start | bytes 1572868
  13.6 10.7 %collective-permute-start.3 = (bf16[256,4,128]{2,0,1:T(8,128)(2,1)}, bf16[256,4,128]{2,0,1:T(8,128)(2,1)S(1)}, u32[]{:S(2)}, u32[]{:S(2)}) collective-permute-start(bf16[256,4,128]{2,0,1:T(8,128)(2,1)} %collective-permute-done.1), channel_id=1, source_target_pairs={{8,16},{12,20},{16,24},{20,28},{9,17},{13,21},{17,25},{21,29},{10,... | collective-permute-start | bytes 786440 | tf_op jit(solution)/shard_map/ppermute | solution.py:95
  14.9 14.8 %collective-permute-start.2 = (bf16[256,4,128]{2,0,1:T(8,128)(2,1)}, bf16[256,4,128]{2,0,1:T(8,128)(2,1)S(1)}, u32[]{:S(2)}, u32[]{:S(2)}) collective-permute-start(bf16[256,4,128]{2,0,1:T(8,128)(2,1)} %collective-permute-done.1), channel_id=1, source_target_pairs={{8,12},{16,20},{24,28},{12,8},{20,16},{28,24},{9,13},{17,21},{25,2... | collective-permute-start | bytes 786440 | tf_op jit(solution)/shard_map/ppermute | solution.py:96
  24.3 9.7 %collective-permute-start.4 = (bf16[256,4,128]{2,0,1:T(8,128)(2,1)S(1)}, bf16[256,4,128]{2,0,1:T(8,128)(2,1)S(1)}, u32[]{:S(2)}, u32[]{:S(2)}) collective-permute-start(bf16[256,4,128]{2,0,1:T(8,128)(2,1)S(1)} %collective-permute-done.3), channel_id=1, source_target_pairs={{16,20},{24,28},{20,16},{28,24},{17,21},{25,29},{21,17},{29,25},{1... | collective-permute-start | bytes 786440 | tf_op jit(solution)/shard_map/ppermute | solution.py:96
  26.3 11.1 %collective-permute-start.5 = (bf16[256,4,128]{2,0,1:T(8,128)(2,1)S(1)}, bf16[256,4,128]{2,0,1:T(8,128)(2,1)S(1)}, u32[]{:S(2)}, u32[]{:S(2)}) collective-permute-start(bf16[256,4,128]{2,0,1:T(8,128)(2,1)S(1)} %collective-permute-done.3), channel_id=1, source_target_pairs={{16,24},{20,28},{17,25},{21,29},{18,26},{22,30},{19,27},{23,31}} | collective-permute-start | bytes 786440 | tf_op jit(solution)/shard_map/ppermute | solution.py:95
  27.6 15.1 %collective-permute-start.6 = (bf16[256,4,128]{2,0,1:T(8,128)(2,1)S(1)}, bf16[256,4,128]{2,0,1:T(8,128)(2,1)S(1)}, u32[]{:S(2)}, u32[]{:S(2)}) collective-permute-start(bf16[256,4,128]{2,0,1:T(8,128)(2,1)S(1)} %collective-permute-done.3), channel_id=1, source_target_pairs={{16,28},{20,24},{17,29},{21,25},{18,30},{22,26},{19,31},{23,27}} | collective-permute-start | bytes 786440 | tf_op jit(solution)/shard_map/ppermute | solution.py:98
  43.2 2.8 %copy-start = (bf16[16,128,768]{2,1,0:T(8,128)(2,1)S(1)}, bf16[16,128,768]{2,1,0:T(8,128)(2,1)}, u32[]{:S(2)}) copy-start(bf16[16,128,768]{2,1,0:T(8,128)(2,1)} %param.10) | copy-start | bytes 9437188
  44.4 8.8 %collective-permute-start.8 = (bf16[2,2,256,128]{3,2,1,0:T(8,128)(2,1)S(1)}, bf16[2,2,256,128]{3,2,1,0:T(8,128)(2,1)S(1)}, u32[]{:S(2)}, u32[]{:S(2)}) collective-permute-start(bf16[2,2,256,128]{3,2,1,0:T(8,128)(2,1)S(1)} %fusion.52), channel_id=1, source_target_pairs={{0,1},{1,0},{2,3},{3,2},{4,5},{5,4},{6,7},{7,6},{8,9},{9,8},{10,11... | collective-permute-start | bytes 786440 | tf_op jit(solution)/shard_map/ppermute | solution.py:117
  44.4 8.7 %collective-permute-start.7 = (bf16[2,2,256,128]{3,2,1,0:T(8,128)(2,1)S(1)}, bf16[2,2,256,128]{3,2,1,0:T(8,128)(2,1)S(1)}, u32[]{:S(2)}, u32[]{:S(2)}) collective-permute-start(bf16[2,2,256,128]{3,2,1,0:T(8,128)(2,1)S(1)} %fusion.52), channel_id=1, source_target_pairs={{0,2},{1,3},{2,0},{3,1},{4,6},{5,7},{6,4},{7,5},{8,10},{9,11},{10,... | collective-permute-start | bytes 786440 | tf_op jit(solution)/shard_map/ppermute | solution.py:117
  53.2 1.5 %collective-permute-start.9 = (bf16[2,2,256,128]{3,2,1,0:T(8,128)(2,1)S(1)}, bf16[2,2,256,128]{3,2,1,0:T(8,128)(2,1)S(1)}, u32[]{:S(2)}, u32[]{:S(2)}) collective-permute-start(bf16[2,2,256,128]{3,2,1,0:T(8,128)(2,1)S(1)} %collective-permute-done.7), channel_id=1, source_target_pairs={{0,1},{1,0},{2,3},{3,2},{4,5},{5,4},{6,7},{7,6},{8,9},{9,8},{10,11... | collective-permute-start | bytes 786440 | tf_op jit(solution)/shard_map/ppermute | solution.py:117
  55.8 2.8 %copy-start.4 = (bf16[768]{0:T(1024)(128)(2,1)S(1)}, bf16[768]{0:T(1024)(128)(2,1)}, u32[]{:S(2)}) copy-start(bf16[768]{0:T(1024)(128)(2,1)} %param.11) | copy-start | bytes 4612
  55.8 4.9 %copy-start.3 = (bf16[256,768]{1,0:T(8,128)(2,1)S(1)}, bf16[256,768]{1,0:T(8,128)(2,1)}, u32[]{:S(2)}) copy-start(bf16[256,768]{1,0:T(8,128)(2,1)} %param.9) | copy-start | bytes 1179652
  57.0 3.6 %collective-permute-start.11 = (f32[256]{0:T(256)S(1)}, f32[256]{0:T(256)S(1)}, u32[]{:S(2)}, u32[]{:S(2)}) collective-permute-start(f32[256]{0:T(256)S(1)} %add.222), channel_id=1, source_target_pairs={{0,2},{1,3},{2,0},{3,1},{4,6},{5,7},{6,4},{7,5},{8,10},{9,11},{10,... | collective-permute-start | bytes 3080 | tf_op jit(solution)/shard_map/ppermute | solution.py:207

commit v15 on v8

--- a/solution.py
+++ b/solution.py
@@ -100,12 +100,12 @@
                 "ctx",
                 [(source, 2 * (source // 2) + 3 - source % 2) for source, unused in forward(step)],
             )
-        state = attend_stacked(state, crossed, 2 * (plane - step + 1) + 1 - side)
         if step < outer:
             state = attend_stacked(state, arrived, device_index - 2 * step)
             line = arrived
         if last_forward:
             state = attend_stacked(state, diagonal, 2 * (plane - step) + 1 - side)
+        state = attend_stacked(state, crossed, 2 * (plane - step + 1) + 1 - side)
     return state
 
 

time: 55.5 us -> 57.2 us (1.031)
  waiting for transfers between devices: 21.6 us -> 23.3 us
    ppermute x3, waiting for transfers between devices: 0.01 us -> 4.57 us  [along_lines(): crossed = lax.ppermute(line, 'ctx', across(step))]
    ppermute x1, waiting for transfers between devices: 4.14 us -> 2.29 us  [along_lines(): lax.ppermute(line, 'ctx', [(source, 2 * (source // 2) + 3 - source % 2) f...]
    ppermute x3, waiting for transfers between devices: 7.26 us -> 6.26 us  [along_lines(): arrived = lax.ppermute(line, 'ctx', forward(step))]
  transfers between devices with their start and end apart: 13 -> 13, of which waited for: 8 -> 9; matrix products, arithmetic and copies ran while one was open for 15% -> 15% of each run, Pallas kernels for 0% -> 0%
where the time goes in v15:
time: 57.2 us; the launch traced here: 56.8 us
  waiting for transfers between devices  23.3 us (41%)
  starting transfers between devices  19 us (33%)
  matrix products  8.29 us (14%)
  other arithmetic  4.53 us (8%)
  local copies, waits for them, and re-layouts  1.31 us (2%)
    ppermute x3, starting transfers between devices, along_lines(): crossed = lax.ppermute(line, 'ctx', across(step))  10.3 us
    ppermute x3, waiting for transfers between devices, exchanged(): lax.ppermute(held, 'tp', pairs)  7.25 us
    ppermute x3, waiting for transfers between devices, along_lines(): arrived = lax.ppermute(line, 'ctx', forward(step))  6.26 us
    ppermute x3, waiting for transfers between devices, along_lines(): crossed = lax.ppermute(line, 'ctx', across(step))  4.57 us
    dot_general x8, matrix products, attend_block(): jnp.einsum('sgrh,kgh->grsk', rotary_queries, key_block, preferred_element...  3.9 us
    ppermute x3, starting transfers between devices, along_lines(): arrived = lax.ppermute(line, 'ctx', forward(step))  3.86 us
    ppermute x3, waiting for transfers between devices, summed(): lax.ppermute(partial, 'tp', [(source, source ^ offset) for source in rang...  2.95 us
    dot_general x8, matrix products, attend_block(): jnp.einsum('grsk,kgh->grsh', weights.astype(jnp.bfloat16), value_block, p...  2.84 us
  transfers between devices with their start and end apart: 13, of which 9 were waited for; matrix products, arithmetic and copies ran while one was open for 15% of the time, Pallas kernels for 0%

profile of v15, /device:TPU:24, one launch (start us, length us, event | category | flops | bytes accessed | tf_op | source)
XLA Modules:
  0.0 56.8 jit_solution(12336818379570482189)
XLA Ops:
  0.0 0.9 %copy.12 = bf16[256,2,128]{2,0,1:T(8,128)(2,1)S(1)} copy(bf16[256,2,128]{2,1,0:T(2,128)(2,1)} %param.8) | data formatting | bytes 262144 | tf_op args[2]
  1.0 0.9 %copy_convert_fusion = f32[256,2,128]{2,0,1:T(8,128)S(1)} fusion(bf16[256,2,128]{2,1,0:T(2,128)(2,1)} %param.7), kind=kLoop, calls=%fused_computation.108 | loop fusion | flops 65536 | bytes 393216 | tf_op jit(solution)/shard_map/convert_element_type | solution.py:140
  1.9 0.5 multiply_cosine_fusion
  2.4 0.2 subtract_convert_fusion.1
  2.6 0.1 pad_maximum_fusion.1
  2.7 1.3 %collective-permute-start = (bf16[256,4,128]{2,0,1:T(8,128)(2,1)S(1)}, bf16[256,4,128]{2,0,1:T(8,128)(2,1)S(1)}, u32[]{:S(2)}, u32[]{:S(2)}) collective-permute-start(bf16[256,4,128]{2,0,1:T(8,128)(2,1)S(1)} %pad_maximum_fusion.1), channel_id=1, source_target_pairs={{0,8},{4,12},{8,16},{12,20},{16,24},{20,28},{1,9},{5,13},{9,17},{1... | collective-permute-start | bytes 786440 | tf_op jit(solution)/shard_map/ppermute | solution.py:95
  4.0 3.4 %collective-permute-start.1 = (bf16[256,4,128]{2,0,1:T(8,128)(2,1)S(1)}, bf16[256,4,128]{2,0,1:T(8,128)(2,1)S(1)}, u32[]{:S(2)}, u32[]{:S(2)}) collective-permute-start(bf16[256,4,128]{2,0,1:T(8,128)(2,1)S(1)} %pad_maximum_fusion.1), channel_id=1, source_target_pairs={{0,4},{8,12},{16,20},{24,28},{1,5},{9,13},{17,21},{25,29},{2,6},{1... | collective-permute-start | bytes 786440 | tf_op jit(solution)/shard_map/ppermute | solution.py:96
  7.5 1.0 %convert_element_type.58 = f32[256,4,128]{2,1,0:T(4,128)S(1)} convert(bf16[256,4,128]{2,1,0:T(4,128)(2,1)} %param.6) | non-fusion elementwise | flops 131072 | bytes 786432 | tf_op jit(solution)/shard_map/convert_element_type | solution.py:138
  8.5 0.0 copy-start.1
  8.5 0.5 subtract_convert_fusion
  9.1 0.1 pad_maximum_fusion
  9.3 0.1 fusion.61
  9.4 0.5 fusion.74
  10.0 0.0 copy-done.1
  10.0 0.3 fusion.58
  10.4 2.2 %collective-permute-done = bf16[256,4,128]{2,0,1:T(8,128)(2,1)S(1)} collective-permute-done((bf16[256,4,128]{2,0,1:T(8,128)(2,1)S(1)}, bf16[256,4,128]{2,0,1:T(8,128)(2,1)S(1)}, u32[]{:S(2)}, u32[]{:S(2)}) %collective-permute-start) | collective-permute-done | bytes 262176 | tf_op jit(solution)/shard_map/ppermute | solution.py:95
  12.6 1.3 %collective-permute-start.2 = (bf16[256,4,128]{2,0,1:T(8,128)(2,1)S(1)}, bf16[256,4,128]{2,0,1:T(8,128)(2,1)S(1)}, u32[]{:S(2)}, u32[]{:S(2)}) collective-permute-start(bf16[256,4,128]{2,0,1:T(8,128)(2,1)S(1)} %collective-permute-done), channel_id=1, source_target_pairs={{8,16},{12,20},{16,24},{20,28},{9,17},{13,21},{17,25},{21,29},{10,... | collective-permute-start | bytes 786440 | tf_op jit(solution)/shard_map/ppermute | solution.py:95
  13.9 3.4 %collective-permute-start.3 = (bf16[256,4,128]{2,0,1:T(8,128)(2,1)S(1)}, bf16[256,4,128]{2,0,1:T(8,128)(2,1)S(1)}, u32[]{:S(2)}, u32[]{:S(2)}) collective-permute-start(bf16[256,4,128]{2,0,1:T(8,128)(2,1)S(1)} %collective-permute-done), channel_id=1, source_target_pairs={{8,12},{16,20},{24,28},{12,8},{20,16},{28,24},{9,13},{17,21},{25,2... | collective-permute-start | bytes 786440 | tf_op jit(solution)/shard_map/ppermute | solution.py:96
  17.4 0.5 fusion.75
  17.8 0.3 convolution_add_fusion.3
  18.2 0.0 collective-permute-done.1
  18.2 0.5 fusion.73
  18.7 0.3 convolution_add_fusion.2
  19.0 2.6 %collective-permute-done.2 = bf16[256,4,128]{2,0,1:T(8,128)(2,1)S(1)} collective-permute-done((bf16[256,4,128]{2,0,1:T(8,128)(2,1)S(1)}, bf16[256,4,128]{2,0,1:T(8,128)(2,1)S(1)}, u32[]{:S(2)}, u32[]{:S(2)}) %collective-permute-start.2) | collective-permute-done | bytes 262176 | tf_op jit(solution)/shard_map/ppermute | solution.py:95
  21.7 3.4 %collective-permute-start.6 = (bf16[256,4,128]{2,0,1:T(8,128)(2,1)S(1)}, bf16[256,4,128]{2,0,1:T(8,128)(2,1)S(1)}, u32[]{:S(2)}, u32[]{:S(2)}) collective-permute-start(bf16[256,4,128]{2,0,1:T(8,128)(2,1)S(1)} %collective-permute-done.2), channel_id=1, source_target_pairs={{16,20},{24,28},{20,16},{28,24},{17,21},{25,29},{21,17},{29,25},{1... | collective-permute-start | bytes 786440 | tf_op jit(solution)/shard_map/ppermute | solution.py:96
  25.1 1.3 %collective-permute-start.5 = (bf16[256,4,128]{2,0,1:T(8,128)(2,1)S(1)}, bf16[256,4,128]{2,0,1:T(8,128)(2,1)S(1)}, u32[]{:S(2)}, u32[]{:S(2)}) collective-permute-start(bf16[256,4,128]{2,0,1:T(8,128)(2,1)S(1)} %collective-permute-done.2), channel_id=1, source_target_pairs={{16,28},{20,24},{17,29},{21,25},{18,30},{22,26},{19,31},{23,27}} | collective-permute-start | bytes 786440 | tf_op jit(solution)/shard_map/ppermute | solution.py:98
  26.4 1.3 %collective-permute-start.4 = (bf16[256,4,128]{2,0,1:T(8,128)(2,1)S(1)}, bf16[256,4,128]{2,0,1:T(8,128)(2,1)S(1)}, u32[]{:S(2)}, u32[]{:S(2)}) collective-permute-start(bf16[256,4,128]{2,0,1:T(8,128)(2,1)S(1)} %collective-permute-done.2), channel_id=1, source_target_pairs={{16,24},{20,28},{17,25},{21,29},{18,26},{22,30},{19,27},{23,31}} | collective-permute-start | bytes 786440 | tf_op jit(solution)/shard_map/ppermute | solution.py:95
  27.7 0.0 collective-permute-done.3
  27.7 0.5 fusion.71
  28.2 0.3 fusion.53
  28.6 0.5 fusion.72
  29.0 0.4 fusion.46
  29.4 4.6 %collective-permute-done.6 = bf16[256,4,128]{2,0,1:T(8,128)(2,1)S(1)} collective-permute-done((bf16[256,4,128]{2,0,1:T(8,128)(2,1)S(1)}, bf16[256,4,128]{2,0,1:T(8,128)(2,1)S(1)}, u32[]{:S(2)}, u32[]{:S(2)}) %collective-permute-start.6) | collective-permute-done | bytes 262176 | tf_op jit(solution)/shard_map/ppermute | solution.py:96
  34.0 0.5 fusion.68
  34.5 2.3 %collective-permute-done.5 = bf16[256,4,128]{2,0,1:T(8,128)(2,1)S(1)} collective-permute-done((bf16[256,4,128]{2,0,1:T(8,128)(2,1)S(1)}, bf16[256,4,128]{2,0,1:T(8,128)(2,1)S(1)}, u32[]{:S(2)}, u32[]{:S(2)}) %collective-permute-start.5) | collective-permute-done | bytes 262176 | tf_op jit(solution)/shard_map/ppermute | solution.py:98
  36.7 0.5 fusion.69
  37.2 1.4 %collective-permute-done.4 = bf16[256,4,128]{2,0,1:T(8,128)(2,1)S(1)} collective-permute-done((bf16[256,4,128]{2,0,1:T(8,128)(2,1)S(1)}, bf16[256,4,128]{2,0,1:T(8,128)(2,1)S(1)}, u32[]{:S(2)}, u32[]{:S(2)}) %collective-permute-start.4) | collective-permute-done | bytes 262176 | tf_op jit(solution)/shard_map/ppermute | solution.py:95
  38.6 0.5 fusion.70
  39.1 0.0 copy-start
  39.1 0.4 fusion.48
  39.5 0.4 fusion.50
  39.8 0.4 fusion.47
  40.2 0.1 collective-permute-start.8
  40.3 1.6 %collective-permute-start.7 = (bf16[2,2,256,128]{3,2,1,0:T(8,128)(2,1)S(1)}, bf16[2,2,256,128]{3,2,1,0:T(8,128)(2,1)S(1)}, u32[]{:S(2)}, u32[]{:S(2)}) collective-permute-start(bf16[2,2,256,128]{3,2,1,0:T(8,128)(2,1)S(1)} %fusion.47), channel_id=1, source_target_pairs={{0,2},{1,3},{2,0},{3,1},{4,6},{5,7},{6,4},{7,5},{8,10},{9,11},{10,... | collective-permute-start | bytes 786440 | tf_op jit(solution)/shard_map/ppermute | solution.py:117
  41.9 0.0 copy-done
  41.9 0.3 constant_dynamic-slice_fusion
  42.1 0.4 convolution_bitcast_fusion.3
  42.5 6.5 %collective-permute-done.7 = bf16[2,2,256,128]{3,2,1,0:T(8,128)(2,1)S(1)} collective-permute-done((bf16[2,2,256,128]{3,2,1,0:T(8,128)(2,1)S(1)}, bf16[2,2,256,128]{3,2,1,0:T(8,128)(2,1)S(1)}, u32[]{:S(2)}, u32[]{:S(2)}) %collective-permute-start.7) | collective-permute-done | bytes 262176 | tf_op jit(solution)/shard_map/ppermute | solution.py:117
  49.0 0.0 collective-permute-start.9
  49.0 0.0 collective-permute-done.8
  49.0 0.4 convolution_bitcast_fusion.1
  49.4 0.0 copy-start.3
  49.4 0.0 copy-start.2
  49.4 0.4 fusion.41
  49.8 0.7 %collective-permute-done.9 = bf16[2,2,256,128]{3,2,1,0:T(8,128)(2,1)S(1)} collective-permute-done((bf16[2,2,256,128]{3,2,1,0:T(8,128)(2,1)S(1)}, bf16[2,2,256,128]{3,2,1,0:T(8,128)(2,1)S(1)}, u32[]{:S(2)}, u32[]{:S(2)}) %collective-permute-start.9) | collective-permute-done | bytes 262176 | tf_op jit(solution)/shard_map/ppermute | solution.py:117
  50.6 0.5 multiply_reduce_fusion
  51.0 1.3 %collective-permute-start.12 = (f32[256]{0:T(256)S(1)}, f32[256]{0:T(256)S(1)}, u32[]{:S(2)}, u32[]{:S(2)}) collective-permute-start(f32[256]{0:T(256)S(1)} %get-tuple-element.31), channel_id=1, source_target_pairs={{0,3},{1,2},{2,1},{3,0},{4,7},{5,6},{6,5},{7,4},{8,11},{9,10},{10,... | collective-permute-start | bytes 3080 | tf_op jit(solution)/shard_map/ppermute | solution.py:125
  52.3 0.6 collective-permute-start.11
  52.9 0.1 collective-permute-start.10
  52.9 0.0 copy-done.3
  52.9 1.1 %collective-permute-done.12 = f32[256]{0:T(256)S(1)} collective-permute-done((f32[256]{0:T(256)S(1)}, f32[256]{0:T(256)S(1)}, u32[]{:S(2)}, u32[]{:S(2)}) %collective-permute-start.12) | collective-permute-done | bytes 1056 | tf_op jit(solution)/shard_map/ppermute | solution.py:125
  54.1 1.8 %collective-permute-done.11 = f32[256]{0:T(256)S(1)} collective-permute-done((f32[256]{0:T(256)S(1)}, f32[256]{0:T(256)S(1)}, u32[]{:S(2)}, u32[]{:S(2)}) %collective-permute-start.11) | collective-permute-done | bytes 1056 | tf_op jit(solution)/shard_map/ppermute | solution.py:125
  55.9 0.0 collective-permute-done.10
  55.9 0.9 %add_convert_fusion = bf16[256,768]{1,0:T(8,128)(2,1)} fusion(f32[256,768]{1,0:T(8,128)S(1)} %get-tuple-element.32, bf16[256,768]{1,0:T(8,128)(2,1)S(1)} %copy-done.2, f32[768]{0:T(1024)S(1)} %convert_element_type.68, f32[256]{0:T(256)S(1)} %add_rsqrt_fusion), kind=kLoop, calls=%fused_computation.64 | loop fusion | flops 983040 | bytes 1576960 | tf_op jit(solution)/shard_map/convert_element_type | solution.py:200
  (9 shorter events, 0.1 us)
Async XLA Ops:
  2.7 9.9 %collective-permute-start = (bf16[256,4,128]{2,0,1:T(8,128)(2,1)S(1)}, bf16[256,4,128]{2,0,1:T(8,128)(2,1)S(1)}, u32[]{:S(2)}, u32[]{:S(2)}) collective-permute-start(bf16[256,4,128]{2,0,1:T(8,128)(2,1)S(1)} %pad_maximum_fusion.1), channel_id=1, source_target_pairs={{0,8},{4,12},{8,16},{12,20},{16,24},{20,28},{1,9},{5,13},{9,17},{1... | collective-permute-start | bytes 786440 | tf_op jit(solution)/shard_map/ppermute | solution.py:95
  4.0 14.2 %collective-permute-start.1 = (bf16[256,4,128]{2,0,1:T(8,128)(2,1)S(1)}, bf16[256,4,128]{2,0,1:T(8,128)(2,1)S(1)}, u32[]{:S(2)}, u32[]{:S(2)}) collective-permute-start(bf16[256,4,128]{2,0,1:T(8,128)(2,1)S(1)} %pad_maximum_fusion.1), channel_id=1, source_target_pairs={{0,4},{8,12},{16,20},{24,28},{1,5},{9,13},{17,21},{25,29},{2,6},{1... | collective-permute-start | bytes 786440 | tf_op jit(solution)/shard_map/ppermute | solution.py:96
  8.5 1.6 %copy-start.1 = (bf16[256,2,128]{2,1,0:T(2,128)(2,1)S(1)}, bf16[256,2,128]{2,1,0:T(2,128)(2,1)}, u32[]{:S(2)}) copy-start(bf16[256,2,128]{2,1,0:T(2,128)(2,1)} %param.8) | copy-start | bytes 393220
  12.6 9.1 %collective-permute-start.2 = (bf16[256,4,128]{2,0,1:T(8,128)(2,1)S(1)}, bf16[256,4,128]{2,0,1:T(8,128)(2,1)S(1)}, u32[]{:S(2)}, u32[]{:S(2)}) collective-permute-start(bf16[256,4,128]{2,0,1:T(8,128)(2,1)S(1)} %collective-permute-done), channel_id=1, source_target_pairs={{8,16},{12,20},{16,24},{20,28},{9,17},{13,21},{17,25},{21,29},{10,... | collective-permute-start | bytes 786440 | tf_op jit(solution)/shard_map/ppermute | solution.py:95
  13.9 13.8 %collective-permute-start.3 = (bf16[256,4,128]{2,0,1:T(8,128)(2,1)S(1)}, bf16[256,4,128]{2,0,1:T(8,128)(2,1)S(1)}, u32[]{:S(2)}, u32[]{:S(2)}) collective-permute-start(bf16[256,4,128]{2,0,1:T(8,128)(2,1)S(1)} %collective-permute-done), channel_id=1, source_target_pairs={{8,12},{16,20},{24,28},{12,8},{20,16},{28,24},{9,13},{17,21},{25,2... | collective-permute-start | bytes 786440 | tf_op jit(solution)/shard_map/ppermute | solution.py:96
  21.7 12.3 %collective-permute-start.6 = (bf16[256,4,128]{2,0,1:T(8,128)(2,1)S(1)}, bf16[256,4,128]{2,0,1:T(8,128)(2,1)S(1)}, u32[]{:S(2)}, u32[]{:S(2)}) collective-permute-start(bf16[256,4,128]{2,0,1:T(8,128)(2,1)S(1)} %collective-permute-done.2), channel_id=1, source_target_pairs={{16,20},{24,28},{20,16},{28,24},{17,21},{25,29},{21,17},{29,25},{1... | collective-permute-start | bytes 786440 | tf_op jit(solution)/shard_map/ppermute | solution.py:96
  25.1 11.6 %collective-permute-start.5 = (bf16[256,4,128]{2,0,1:T(8,128)(2,1)S(1)}, bf16[256,4,128]{2,0,1:T(8,128)(2,1)S(1)}, u32[]{:S(2)}, u32[]{:S(2)}) collective-permute-start(bf16[256,4,128]{2,0,1:T(8,128)(2,1)S(1)} %collective-permute-done.2), channel_id=1, source_target_pairs={{16,28},{20,24},{17,29},{21,25},{18,30},{22,26},{19,31},{23,27}} | collective-permute-start | bytes 786440 | tf_op jit(solution)/shard_map/ppermute | solution.py:98
  26.4 12.2 %collective-permute-start.4 = (bf16[256,4,128]{2,0,1:T(8,128)(2,1)S(1)}, bf16[256,4,128]{2,0,1:T(8,128)(2,1)S(1)}, u32[]{:S(2)}, u32[]{:S(2)}) collective-permute-start(bf16[256,4,128]{2,0,1:T(8,128)(2,1)S(1)} %collective-permute-done.2), channel_id=1, source_target_pairs={{16,24},{20,28},{17,25},{21,29},{18,26},{22,30},{19,27},{23,31}} | collective-permute-start | bytes 786440 | tf_op jit(solution)/shard_map/ppermute | solution.py:95
  39.1 2.8 %copy-start = (bf16[16,128,768]{2,1,0:T(8,128)(2,1)S(1)}, bf16[16,128,768]{2,1,0:T(8,128)(2,1)}, u32[]{:S(2)}) copy-start(bf16[16,128,768]{2,1,0:T(8,128)(2,1)} %param.10) | copy-start | bytes 9437188
  40.2 8.8 %collective-permute-start.8 = (bf16[2,2,256,128]{3,2,1,0:T(8,128)(2,1)S(1)}, bf16[2,2,256,128]{3,2,1,0:T(8,128)(2,1)S(1)}, u32[]{:S(2)}, u32[]{:S(2)}) collective-permute-start(bf16[2,2,256,128]{3,2,1,0:T(8,128)(2,1)S(1)} %fusion.47), channel_id=1, source_target_pairs={{0,1},{1,0},{2,3},{3,2},{4,5},{5,4},{6,7},{7,6},{8,9},{9,8},{10,11... | collective-permute-start | bytes 786440 | tf_op jit(solution)/shard_map/ppermute | solution.py:117
  40.3 8.7 %collective-permute-start.7 = (bf16[2,2,256,128]{3,2,1,0:T(8,128)(2,1)S(1)}, bf16[2,2,256,128]{3,2,1,0:T(8,128)(2,1)S(1)}, u32[]{:S(2)}, u32[]{:S(2)}) collective-permute-start(bf16[2,2,256,128]{3,2,1,0:T(8,128)(2,1)S(1)} %fusion.47), channel_id=1, source_target_pairs={{0,2},{1,3},{2,0},{3,1},{4,6},{5,7},{6,4},{7,5},{8,10},{9,11},{10,... | collective-permute-start | bytes 786440 | tf_op jit(solution)/shard_map/ppermute | solution.py:117
  49.0 1.5 %collective-permute-start.9 = (bf16[2,2,256,128]{3,2,1,0:T(8,128)(2,1)S(1)}, bf16[2,2,256,128]{3,2,1,0:T(8,128)(2,1)S(1)}, u32[]{:S(2)}, u32[]{:S(2)}) collective-permute-start(bf16[2,2,256,128]{3,2,1,0:T(8,128)(2,1)S(1)} %collective-permute-done.7), channel_id=1, source_target_pairs={{0,1},{1,0},{2,3},{3,2},{4,5},{5,4},{6,7},{7,6},{8,9},{9,8},{10,11... | collective-permute-start | bytes 786440 | tf_op jit(solution)/shard_map/ppermute | solution.py:117
  49.4 3.5 %copy-start.3 = (bf16[768]{0:T(1024)(128)(2,1)S(1)}, bf16[768]{0:T(1024)(128)(2,1)}, u32[]{:S(2)}) copy-start(bf16[768]{0:T(1024)(128)(2,1)} %param.11) | copy-start | bytes 4612
  49.4 6.5 %copy-start.2 = (bf16[256,768]{1,0:T(8,128)(2,1)S(1)}, bf16[256,768]{1,0:T(8,128)(2,1)}, u32[]{:S(2)}) copy-start(bf16[256,768]{1,0:T(8,128)(2,1)} %param.9) | copy-start | bytes 1179652
  51.0 3.1 %collective-permute-start.12 = (f32[256]{0:T(256)S(1)}, f32[256]{0:T(256)S(1)}, u32[]{:S(2)}, u32[]{:S(2)}) collective-permute-start(f32[256]{0:T(256)S(1)} %get-tuple-element.31), channel_id=1, source_target_pairs={{0,3},{1,2},{2,1},{3,0},{4,7},{5,6},{6,5},{7,4},{8,11},{9,10},{10,... | collective-permute-start | bytes 3080 | tf_op jit(solution)/shard_map/ppermute | solution.py:125
  52.3 3.6 %collective-permute-start.11 = (f32[256]{0:T(256)S(1)}, f32[256]{0:T(256)S(1)}, u32[]{:S(2)}, u32[]{:S(2)}) collective-permute-start(f32[256]{0:T(256)S(1)} %get-tuple-element.31), channel_id=1, source_target_pairs={{0,2},{1,3},{2,0},{3,1},{4,6},{5,7},{6,4},{7,5},{8,10},{9,11},{10,... | collective-permute-start | bytes 3080 | tf_op jit(solution)/shard_map/ppermute | solution.py:125
  52.9 3.0 %collective-permute-start.10 = (f32[256]{0:T(256)S(1)}, f32[256]{0:T(256)S(1)}, u32[]{:S(2)}, u32[]{:S(2)}) collective-permute-start(f32[256]{0:T(256)S(1)} %get-tuple-element.31), channel_id=1, source_target_pairs={{0,1},{1,0},{2,3},{3,2},{4,5},{5,4},{6,7},{7,6},{8,9},{9,8},{10,11... | collective-permute-start | bytes 3080 | tf_op jit(solution)/shard_map/ppermute | solution.py:125

commit v16 on v8

--- a/solution.py
+++ b/solution.py
@@ -27,6 +27,24 @@
     sine_part = jnp.sin(angles)
     first_half = values_in[..., :half_width]
     second_half = values_in[..., half_width:]
+    return jnp.concatenate(
+        [
+            first_half * cosine - second_half * sine_part,
+            second_half * cosine + first_half * sine_part,
+        ],
+        axis=-1,
+    )
+
+
+def rotate_halves(values_in, positions):
+    half_width = values_in.shape[-1] // 2
+    steps_half = jnp.arange(half_width, dtype=jnp.float32)
+    inverse = rope_base ** (-2.0 * steps_half / values_in.shape[-1])
+    angles = positions.astype(jnp.float32)[..., None] * inverse
+    cosine = jnp.cos(angles)
+    sine_part = jnp.sin(angles)
+    first_half = values_in[..., :half_width].astype(jnp.float32)
+    second_half = values_in[..., half_width:].astype(jnp.float32)
     return jnp.concatenate(
         [
             first_half * cosine - second_half * sine_part,
@@ -137,7 +155,7 @@
     positions = (device_index * rows + jnp.arange(rows, dtype=jnp.int32))[:, None]
     rotary_queries = rotate(queries.astype(jnp.float32), positions).astype(jnp.bfloat16)
     rotary_queries = rotary_queries.reshape(rows, kv_heads, heads_per_group, head_size)
-    rotary_keys = rotate(keys.astype(jnp.float32), positions).astype(jnp.bfloat16)
+    rotary_keys = rotate_halves(keys, positions).astype(jnp.bfloat16)
     reach = min((WINDOW_TOKENS + rows - 2) // rows, cycle_size - 1)
     state = (
         jnp.zeros((kv_heads, heads_per_group, rows, head_size), jnp.float32),

time: 55.5 us -> 55.7 us (level)
  local copies, waits for them, and re-layouts: 1.31 us -> 2.53 us
  other arithmetic: 4.53 us -> 3.53 us
    slice x0 -> x1, local copies, waits for them, and re-layouts: none -> 1.23 us  [rotate_halves(): first_half = values_in[..., :half_width].astype(jnp.float32)]
    convert_element_type x1 -> x0, other arithmetic: 0.93 us -> none  [local(): keys.astype(jnp.float32)]
where the time goes in v16:
time: 55.7 us; the launch traced here: 55.4 us
  waiting for transfers between devices  21.6 us (39%)
  starting transfers between devices  19 us (34%)
  matrix products  8.3 us (15%)
  other arithmetic  3.53 us (6%)
  local copies, waits for them, and re-layouts  2.53 us (5%)
    ppermute x3, starting transfers between devices, along_lines(): crossed = lax.ppermute(line, 'ctx', across(step))  10.3 us
    ppermute x3, waiting for transfers between devices, exchanged(): lax.ppermute(held, 'tp', pairs)  7.25 us
    ppermute x3, waiting for transfers between devices, along_lines(): arrived = lax.ppermute(line, 'ctx', forward(step))  7.25 us
    ppermute x1, waiting for transfers between devices, along_lines(): lax.ppermute(line, 'ctx', [(source, 2 * (source // 2) + 3 - source % 2) f...  4.14 us
    dot_general x8, matrix products, attend_block(): jnp.einsum('sgrh,kgh->grsk', rotary_queries, key_block, preferred_element...  3.91 us
    ppermute x3, starting transfers between devices, along_lines(): arrived = lax.ppermute(line, 'ctx', forward(step))  3.86 us
    ppermute x3, waiting for transfers between devices, summed(): lax.ppermute(partial, 'tp', [(source, source ^ offset) for source in rang...  2.95 us
    dot_general x8, matrix products, attend_block(): jnp.einsum('grsk,kgh->grsh', weights.astype(jnp.bfloat16), value_block, p...  2.83 us
  transfers between devices with their start and end apart: 13, of which 8 were waited for; matrix products, arithmetic and copies ran while one was open for 15% of the time, Pallas kernels for 0%

profile of v16, /device:TPU:24, one launch (start us, length us, event | category | flops | bytes accessed | tf_op | source)
XLA Modules:
  0.0 55.4 jit_solution(7983258949401697555)
XLA Ops:
  0.0 0.9 %copy.13 = bf16[256,2,128]{2,0,1:T(8,128)(2,1)S(1)} copy(bf16[256,2,128]{2,1,0:T(2,128)(2,1)} %param.8) | data formatting | bytes 262144 | tf_op args[2]
  1.0 1.2 %fusion.72 = (bf16[256,2,64]{2,1,0:T(2,128)(2,1)S(1)}, bf16[256,2,64]{2,1,0:T(2,128)(2,1)S(1)}) fusion(bf16[256,2,128]{2,1,0:T(2,128)(2,1)} %param.7), kind=kLoop, calls=%fused_computation.125 | loop fusion | bytes 262144 | tf_op jit(solution)/shard_map/slice | solution.py:46
  2.2 0.5 multiply_cosine_fusion
  2.7 0.1 fusion.61
  2.8 0.1 pad_maximum_fusion.1
  2.9 1.3 %collective-permute-start.1 = (bf16[256,4,128]{2,0,1:T(8,128)(2,1)S(1)}, bf16[256,4,128]{2,0,1:T(8,128)(2,1)S(1)}, u32[]{:S(2)}, u32[]{:S(2)}) collective-permute-start(bf16[256,4,128]{2,0,1:T(8,128)(2,1)S(1)} %pad_maximum_fusion.1), channel_id=1, source_target_pairs={{0,8},{4,12},{8,16},{12,20},{16,24},{20,28},{1,9},{5,13},{9,17},{1... | collective-permute-start | bytes 786440 | tf_op jit(solution)/shard_map/ppermute | solution.py:113
  4.2 3.4 %collective-permute-start = (bf16[256,4,128]{2,0,1:T(8,128)(2,1)S(1)}, bf16[256,4,128]{2,0,1:T(8,128)(2,1)S(1)}, u32[]{:S(2)}, u32[]{:S(2)}) collective-permute-start(bf16[256,4,128]{2,0,1:T(8,128)(2,1)S(1)} %pad_maximum_fusion.1), channel_id=1, source_target_pairs={{0,4},{8,12},{16,20},{24,28},{1,5},{9,13},{17,21},{25,29},{2,6},{1... | collective-permute-start | bytes 786440 | tf_op jit(solution)/shard_map/ppermute | solution.py:114
  7.7 1.0 %convert_element_type.62 = f32[256,4,128]{2,1,0:T(4,128)S(1)} convert(bf16[256,4,128]{2,1,0:T(4,128)(2,1)} %param.6) | non-fusion elementwise | flops 131072 | bytes 786432 | tf_op jit(solution)/shard_map/convert_element_type | solution.py:156
  8.7 0.0 copy-start.1
  8.7 0.5 subtract_convert_fusion
  9.3 0.1 pad_maximum_fusion
  9.5 0.1 fusion.65
  9.6 0.5 fusion.79
  10.2 0.0 copy-done.1
  10.2 0.3 fusion.58
  10.6 2.2 %collective-permute-done.1 = bf16[256,4,128]{2,0,1:T(8,128)(2,1)S(1)} collective-permute-done((bf16[256,4,128]{2,0,1:T(8,128)(2,1)S(1)}, bf16[256,4,128]{2,0,1:T(8,128)(2,1)S(1)}, u32[]{:S(2)}, u32[]{:S(2)}) %collective-permute-start.1) | collective-permute-done | bytes 262176 | tf_op jit(solution)/shard_map/ppermute | solution.py:113
  12.9 1.3 %collective-permute-start.3 = (bf16[256,4,128]{2,0,1:T(8,128)(2,1)S(1)}, bf16[256,4,128]{2,0,1:T(8,128)(2,1)S(1)}, u32[]{:S(2)}, u32[]{:S(2)}) collective-permute-start(bf16[256,4,128]{2,0,1:T(8,128)(2,1)S(1)} %collective-permute-done.1), channel_id=1, source_target_pairs={{8,16},{12,20},{16,24},{20,28},{9,17},{13,21},{17,25},{21,29},{10,... | collective-permute-start | bytes 786440 | tf_op jit(solution)/shard_map/ppermute | solution.py:113
  14.2 3.4 %collective-permute-start.2 = (bf16[256,4,128]{2,0,1:T(8,128)(2,1)S(1)}, bf16[256,4,128]{2,0,1:T(8,128)(2,1)S(1)}, u32[]{:S(2)}, u32[]{:S(2)}) collective-permute-start(bf16[256,4,128]{2,0,1:T(8,128)(2,1)S(1)} %collective-permute-done.1), channel_id=1, source_target_pairs={{8,12},{16,20},{24,28},{12,8},{20,16},{28,24},{9,13},{17,21},{25,2... | collective-permute-start | bytes 786440 | tf_op jit(solution)/shard_map/ppermute | solution.py:114
  17.6 0.5 fusion.78
  18.1 0.0 collective-permute-done
  18.1 0.5 fusion.80
  18.6 0.3 convolution_add_fusion.3
  18.9 0.3 convolution_add_fusion.2
  19.3 2.6 %collective-permute-done.3 = bf16[256,4,128]{2,0,1:T(8,128)(2,1)S(1)} collective-permute-done((bf16[256,4,128]{2,0,1:T(8,128)(2,1)S(1)}, bf16[256,4,128]{2,0,1:T(8,128)(2,1)S(1)}, u32[]{:S(2)}, u32[]{:S(2)}) %collective-permute-start.3) | collective-permute-done | bytes 262176 | tf_op jit(solution)/shard_map/ppermute | solution.py:113
  21.9 1.3 %collective-permute-start.6 = (bf16[256,4,128]{2,0,1:T(8,128)(2,1)S(1)}, bf16[256,4,128]{2,0,1:T(8,128)(2,1)S(1)}, u32[]{:S(2)}, u32[]{:S(2)}) collective-permute-start(bf16[256,4,128]{2,0,1:T(8,128)(2,1)S(1)} %collective-permute-done.3), channel_id=1, source_target_pairs={{16,28},{20,24},{17,29},{21,25},{18,30},{22,26},{19,31},{23,27}} | collective-permute-start | bytes 786440 | tf_op jit(solution)/shard_map/ppermute | solution.py:116
  23.2 1.3 %collective-permute-start.5 = (bf16[256,4,128]{2,0,1:T(8,128)(2,1)S(1)}, bf16[256,4,128]{2,0,1:T(8,128)(2,1)S(1)}, u32[]{:S(2)}, u32[]{:S(2)}) collective-permute-start(bf16[256,4,128]{2,0,1:T(8,128)(2,1)S(1)} %collective-permute-done.3), channel_id=1, source_target_pairs={{16,24},{20,28},{17,25},{21,29},{18,26},{22,30},{19,27},{23,31}} | collective-permute-start | bytes 786440 | tf_op jit(solution)/shard_map/ppermute | solution.py:113
  24.5 3.4 %collective-permute-start.4 = (bf16[256,4,128]{2,0,1:T(8,128)(2,1)S(1)}, bf16[256,4,128]{2,0,1:T(8,128)(2,1)S(1)}, u32[]{:S(2)}, u32[]{:S(2)}) collective-permute-start(bf16[256,4,128]{2,0,1:T(8,128)(2,1)S(1)} %collective-permute-done.3), channel_id=1, source_target_pairs={{16,20},{24,28},{20,16},{28,24},{17,21},{25,29},{21,17},{29,25},{1... | collective-permute-start | bytes 786440 | tf_op jit(solution)/shard_map/ppermute | solution.py:114
  28.0 0.5 fusion.76
  28.4 0.3 fusion.53
  28.8 0.0 collective-permute-done.2
  28.8 0.5 fusion.77
  29.3 0.4 fusion.46
  29.7 4.1 %collective-permute-done.6 = bf16[256,4,128]{2,0,1:T(8,128)(2,1)S(1)} collective-permute-done((bf16[256,4,128]{2,0,1:T(8,128)(2,1)S(1)}, bf16[256,4,128]{2,0,1:T(8,128)(2,1)S(1)}, u32[]{:S(2)}, u32[]{:S(2)}) %collective-permute-start.6) | collective-permute-done | bytes 262176 | tf_op jit(solution)/shard_map/ppermute | solution.py:116
  33.8 0.5 fusion.73
  34.3 2.4 %collective-permute-done.5 = bf16[256,4,128]{2,0,1:T(8,128)(2,1)S(1)} collective-permute-done((bf16[256,4,128]{2,0,1:T(8,128)(2,1)S(1)}, bf16[256,4,128]{2,0,1:T(8,128)(2,1)S(1)}, u32[]{:S(2)}, u32[]{:S(2)}) %collective-permute-start.5) | collective-permute-done | bytes 262176 | tf_op jit(solution)/shard_map/ppermute | solution.py:113
  36.6 0.5 fusion.74
  37.1 0.0 collective-permute-done.4
  37.1 0.5 fusion.75
  37.6 0.0 copy-start
  37.7 0.3 fusion.48
  38.0 0.3 fusion.50
  38.4 0.4 fusion.47
  38.8 0.1 collective-permute-start.8
  38.8 1.6 %collective-permute-start.7 = (bf16[2,2,256,128]{3,2,1,0:T(8,128)(2,1)S(1)}, bf16[2,2,256,128]{3,2,1,0:T(8,128)(2,1)S(1)}, u32[]{:S(2)}, u32[]{:S(2)}) collective-permute-start(bf16[2,2,256,128]{3,2,1,0:T(8,128)(2,1)S(1)} %fusion.47), channel_id=1, source_target_pairs={{0,2},{1,3},{2,0},{3,1},{4,6},{5,7},{6,4},{7,5},{8,10},{9,11},{10,... | collective-permute-start | bytes 786440 | tf_op jit(solution)/shard_map/ppermute | solution.py:135
  40.4 0.0 copy-done
  40.4 0.3 constant_dynamic-slice_fusion
  40.7 0.4 convolution_bitcast_fusion.3
  41.1 6.5 %collective-permute-done.7 = bf16[2,2,256,128]{3,2,1,0:T(8,128)(2,1)S(1)} collective-permute-done((bf16[2,2,256,128]{3,2,1,0:T(8,128)(2,1)S(1)}, bf16[2,2,256,128]{3,2,1,0:T(8,128)(2,1)S(1)}, u32[]{:S(2)}, u32[]{:S(2)}) %collective-permute-start.7) | collective-permute-done | bytes 262176 | tf_op jit(solution)/shard_map/ppermute | solution.py:135
  47.6 0.0 collective-permute-start.9
  47.6 0.0 collective-permute-done.8
  47.6 0.4 convolution_bitcast_fusion.1
  47.9 0.0 copy-start.3
  48.0 0.0 copy-start.2
  48.0 0.4 fusion.41
  48.3 0.7 %collective-permute-done.9 = bf16[2,2,256,128]{3,2,1,0:T(8,128)(2,1)S(1)} collective-permute-done((bf16[2,2,256,128]{3,2,1,0:T(8,128)(2,1)S(1)}, bf16[2,2,256,128]{3,2,1,0:T(8,128)(2,1)S(1)}, u32[]{:S(2)}, u32[]{:S(2)}) %collective-permute-start.9) | collective-permute-done | bytes 262176 | tf_op jit(solution)/shard_map/ppermute | solution.py:135
  49.1 0.5 multiply_reduce_fusion
  49.5 1.3 %collective-permute-start.12 = (f32[256]{0:T(256)S(1)}, f32[256]{0:T(256)S(1)}, u32[]{:S(2)}, u32[]{:S(2)}) collective-permute-start(f32[256]{0:T(256)S(1)} %get-tuple-element.33), channel_id=1, source_target_pairs={{0,3},{1,2},{2,1},{3,0},{4,7},{5,6},{6,5},{7,4},{8,11},{9,10},{10,... | collective-permute-start | bytes 3080 | tf_op jit(solution)/shard_map/ppermute | solution.py:143
  50.8 0.6 collective-permute-start.11
  51.4 0.1 collective-permute-start.10
  51.5 0.0 copy-done.3
  51.5 1.1 %collective-permute-done.12 = f32[256]{0:T(256)S(1)} collective-permute-done((f32[256]{0:T(256)S(1)}, f32[256]{0:T(256)S(1)}, u32[]{:S(2)}, u32[]{:S(2)}) %collective-permute-start.12) | collective-permute-done | bytes 1056 | tf_op jit(solution)/shard_map/ppermute | solution.py:143
  52.6 1.8 %collective-permute-done.11 = f32[256]{0:T(256)S(1)} collective-permute-done((f32[256]{0:T(256)S(1)}, f32[256]{0:T(256)S(1)}, u32[]{:S(2)}, u32[]{:S(2)}) %collective-permute-start.11) | collective-permute-done | bytes 1056 | tf_op jit(solution)/shard_map/ppermute | solution.py:143
  54.4 0.0 collective-permute-done.10
  54.4 0.9 %add_convert_fusion = bf16[256,768]{1,0:T(8,128)(2,1)} fusion(f32[256,768]{1,0:T(8,128)S(1)} %get-tuple-element.34, bf16[256,768]{1,0:T(8,128)(2,1)S(1)} %copy-done.2, f32[768]{0:T(1024)S(1)} %convert_element_type.72, f32[256]{0:T(256)S(1)} %add_rsqrt_fusion), kind=kLoop, calls=%fused_computation.64 | loop fusion | flops 983040 | bytes 1576960 | tf_op jit(solution)/shard_map/convert_element_type | solution.py:218
  (9 shorter events, 0.1 us)
Async XLA Ops:
  2.9 9.9 %collective-permute-start.1 = (bf16[256,4,128]{2,0,1:T(8,128)(2,1)S(1)}, bf16[256,4,128]{2,0,1:T(8,128)(2,1)S(1)}, u32[]{:S(2)}, u32[]{:S(2)}) collective-permute-start(bf16[256,4,128]{2,0,1:T(8,128)(2,1)S(1)} %pad_maximum_fusion.1), channel_id=1, source_target_pairs={{0,8},{4,12},{8,16},{12,20},{16,24},{20,28},{1,9},{5,13},{9,17},{1... | collective-permute-start | bytes 786440 | tf_op jit(solution)/shard_map/ppermute | solution.py:113
  4.2 13.8 %collective-permute-start = (bf16[256,4,128]{2,0,1:T(8,128)(2,1)S(1)}, bf16[256,4,128]{2,0,1:T(8,128)(2,1)S(1)}, u32[]{:S(2)}, u32[]{:S(2)}) collective-permute-start(bf16[256,4,128]{2,0,1:T(8,128)(2,1)S(1)} %pad_maximum_fusion.1), channel_id=1, source_target_pairs={{0,4},{8,12},{16,20},{24,28},{1,5},{9,13},{17,21},{25,29},{2,6},{1... | collective-permute-start | bytes 786440 | tf_op jit(solution)/shard_map/ppermute | solution.py:114
  8.7 1.5 %copy-start.1 = (bf16[256,2,128]{2,1,0:T(2,128)(2,1)S(1)}, bf16[256,2,128]{2,1,0:T(2,128)(2,1)}, u32[]{:S(2)}) copy-start(bf16[256,2,128]{2,1,0:T(2,128)(2,1)} %param.8) | copy-start | bytes 393220
  12.9 9.1 %collective-permute-start.3 = (bf16[256,4,128]{2,0,1:T(8,128)(2,1)S(1)}, bf16[256,4,128]{2,0,1:T(8,128)(2,1)S(1)}, u32[]{:S(2)}, u32[]{:S(2)}) collective-permute-start(bf16[256,4,128]{2,0,1:T(8,128)(2,1)S(1)} %collective-permute-done.1), channel_id=1, source_target_pairs={{8,16},{12,20},{16,24},{20,28},{9,17},{13,21},{17,25},{21,29},{10,... | collective-permute-start | bytes 786440 | tf_op jit(solution)/shard_map/ppermute | solution.py:113
  14.2 14.6 %collective-permute-start.2 = (bf16[256,4,128]{2,0,1:T(8,128)(2,1)S(1)}, bf16[256,4,128]{2,0,1:T(8,128)(2,1)S(1)}, u32[]{:S(2)}, u32[]{:S(2)}) collective-permute-start(bf16[256,4,128]{2,0,1:T(8,128)(2,1)S(1)} %collective-permute-done.1), channel_id=1, source_target_pairs={{8,12},{16,20},{24,28},{12,8},{20,16},{28,24},{9,13},{17,21},{25,2... | collective-permute-start | bytes 786440 | tf_op jit(solution)/shard_map/ppermute | solution.py:114
  21.9 11.9 %collective-permute-start.6 = (bf16[256,4,128]{2,0,1:T(8,128)(2,1)S(1)}, bf16[256,4,128]{2,0,1:T(8,128)(2,1)S(1)}, u32[]{:S(2)}, u32[]{:S(2)}) collective-permute-start(bf16[256,4,128]{2,0,1:T(8,128)(2,1)S(1)} %collective-permute-done.3), channel_id=1, source_target_pairs={{16,28},{20,24},{17,29},{21,25},{18,30},{22,26},{19,31},{23,27}} | collective-permute-start | bytes 786440 | tf_op jit(solution)/shard_map/ppermute | solution.py:116
  23.2 13.4 %collective-permute-start.5 = (bf16[256,4,128]{2,0,1:T(8,128)(2,1)S(1)}, bf16[256,4,128]{2,0,1:T(8,128)(2,1)S(1)}, u32[]{:S(2)}, u32[]{:S(2)}) collective-permute-start(bf16[256,4,128]{2,0,1:T(8,128)(2,1)S(1)} %collective-permute-done.3), channel_id=1, source_target_pairs={{16,24},{20,28},{17,25},{21,29},{18,26},{22,30},{19,27},{23,31}} | collective-permute-start | bytes 786440 | tf_op jit(solution)/shard_map/ppermute | solution.py:113
  24.5 12.6 %collective-permute-start.4 = (bf16[256,4,128]{2,0,1:T(8,128)(2,1)S(1)}, bf16[256,4,128]{2,0,1:T(8,128)(2,1)S(1)}, u32[]{:S(2)}, u32[]{:S(2)}) collective-permute-start(bf16[256,4,128]{2,0,1:T(8,128)(2,1)S(1)} %collective-permute-done.3), channel_id=1, source_target_pairs={{16,20},{24,28},{20,16},{28,24},{17,21},{25,29},{21,17},{29,25},{1... | collective-permute-start | bytes 786440 | tf_op jit(solution)/shard_map/ppermute | solution.py:114
  37.6 2.8 %copy-start = (bf16[16,128,768]{2,1,0:T(8,128)(2,1)S(1)}, bf16[16,128,768]{2,1,0:T(8,128)(2,1)}, u32[]{:S(2)}) copy-start(bf16[16,128,768]{2,1,0:T(8,128)(2,1)} %param.10) | copy-start | bytes 9437188
  38.8 8.8 %collective-permute-start.8 = (bf16[2,2,256,128]{3,2,1,0:T(8,128)(2,1)S(1)}, bf16[2,2,256,128]{3,2,1,0:T(8,128)(2,1)S(1)}, u32[]{:S(2)}, u32[]{:S(2)}) collective-permute-start(bf16[2,2,256,128]{3,2,1,0:T(8,128)(2,1)S(1)} %fusion.47), channel_id=1, source_target_pairs={{0,1},{1,0},{2,3},{3,2},{4,5},{5,4},{6,7},{7,6},{8,9},{9,8},{10,11... | collective-permute-start | bytes 786440 | tf_op jit(solution)/shard_map/ppermute | solution.py:135
  38.8 8.7 %collective-permute-start.7 = (bf16[2,2,256,128]{3,2,1,0:T(8,128)(2,1)S(1)}, bf16[2,2,256,128]{3,2,1,0:T(8,128)(2,1)S(1)}, u32[]{:S(2)}, u32[]{:S(2)}) collective-permute-start(bf16[2,2,256,128]{3,2,1,0:T(8,128)(2,1)S(1)} %fusion.47), channel_id=1, source_target_pairs={{0,2},{1,3},{2,0},{3,1},{4,6},{5,7},{6,4},{7,5},{8,10},{9,11},{10,... | collective-permute-start | bytes 786440 | tf_op jit(solution)/shard_map/ppermute | solution.py:135
  47.6 1.5 %collective-permute-start.9 = (bf16[2,2,256,128]{3,2,1,0:T(8,128)(2,1)S(1)}, bf16[2,2,256,128]{3,2,1,0:T(8,128)(2,1)S(1)}, u32[]{:S(2)}, u32[]{:S(2)}) collective-permute-start(bf16[2,2,256,128]{3,2,1,0:T(8,128)(2,1)S(1)} %collective-permute-done.7), channel_id=1, source_target_pairs={{0,1},{1,0},{2,3},{3,2},{4,5},{5,4},{6,7},{7,6},{8,9},{9,8},{10,11... | collective-permute-start | bytes 786440 | tf_op jit(solution)/shard_map/ppermute | solution.py:135
  47.9 3.5 %copy-start.3 = (bf16[768]{0:T(1024)(128)(2,1)S(1)}, bf16[768]{0:T(1024)(128)(2,1)}, u32[]{:S(2)}) copy-start(bf16[768]{0:T(1024)(128)(2,1)} %param.11) | copy-start | bytes 4612
  48.0 6.5 %copy-start.2 = (bf16[256,768]{1,0:T(8,128)(2,1)S(1)}, bf16[256,768]{1,0:T(8,128)(2,1)}, u32[]{:S(2)}) copy-start(bf16[256,768]{1,0:T(8,128)(2,1)} %param.9) | copy-start | bytes 1179652
  49.5 3.1 %collective-permute-start.12 = (f32[256]{0:T(256)S(1)}, f32[256]{0:T(256)S(1)}, u32[]{:S(2)}, u32[]{:S(2)}) collective-permute-start(f32[256]{0:T(256)S(1)} %get-tuple-element.33), channel_id=1, source_target_pairs={{0,3},{1,2},{2,1},{3,0},{4,7},{5,6},{6,5},{7,4},{8,11},{9,10},{10,... | collective-permute-start | bytes 3080 | tf_op jit(solution)/shard_map/ppermute | solution.py:143
  50.8 3.6 %collective-permute-start.11 = (f32[256]{0:T(256)S(1)}, f32[256]{0:T(256)S(1)}, u32[]{:S(2)}, u32[]{:S(2)}) collective-permute-start(f32[256]{0:T(256)S(1)} %get-tuple-element.33), channel_id=1, source_target_pairs={{0,2},{1,3},{2,0},{3,1},{4,6},{5,7},{6,4},{7,5},{8,10},{9,11},{10,... | collective-permute-start | bytes 3080 | tf_op jit(solution)/shard_map/ppermute | solution.py:143
  51.4 3.0 %collective-permute-start.10 = (f32[256]{0:T(256)S(1)}, f32[256]{0:T(256)S(1)}, u32[]{:S(2)}, u32[]{:S(2)}) collective-permute-start(f32[256]{0:T(256)S(1)} %get-tuple-element.33), channel_id=1, source_target_pairs={{0,1},{1,0},{2,3},{3,2},{4,5},{5,4},{6,7},{7,6},{8,9},{9,8},{10,11... | collective-permute-start | bytes 3080 | tf_op jit(solution)/shard_map/ppermute | solution.py:143

commit v17 on v16

--- a/solution.py
+++ b/solution.py
@@ -138,10 +138,11 @@
 
 
 def summed(partial, count):
-    total = partial
-    for offset in range(1, count):
-        total = total + lax.ppermute(partial, "tp", [(source, source ^ offset) for source in range(count)])
-    return total
+    bit = 1
+    while bit < count:
+        partial = partial + lax.ppermute(partial, "tp", [(source, source ^ bit) for source in range(count)])
+        bit *= 2
+    return partial
 
 
 def local(queries, keys, values, residual, out_weight, post_gain):

time: 55.7 us -> 55.6 us (level)
    ppermute x3 -> x2, starting transfers between devices: 1.92 us -> 1.69 us  [summed(): lax.ppermute(partial, 'tp', [(source, source ^ bit) for source in range(c...]
    ppermute x3 -> x2, waiting for transfers between devices: 2.95 us -> 3.08 us  [summed(): lax.ppermute(partial, 'tp', [(source, source ^ bit) for source in range(c...]
  transfers between devices with their start and end apart: 13 -> 12, of which waited for: 8 -> 8; matrix products, arithmetic and copies ran while one was open for 15% -> 15% of each run, Pallas kernels for 0% -> 0%
where the time goes in v17:
time: 55.6 us; the launch traced here: 55.3 us
  waiting for transfers between devices  21.7 us (39%)
  starting transfers between devices  18.8 us (34%)
  matrix products  8.3 us (15%)
  other arithmetic  3.54 us (6%)
  local copies, waits for them, and re-layouts  2.53 us (5%)
    ppermute x3, starting transfers between devices, along_lines(): crossed = lax.ppermute(line, 'ctx', across(step))  10.3 us
    ppermute x3, waiting for transfers between devices, exchanged(): lax.ppermute(held, 'tp', pairs)  7.25 us
    ppermute x3, waiting for transfers between devices, along_lines(): arrived = lax.ppermute(line, 'ctx', forward(step))  7.25 us
    ppermute x1, waiting for transfers between devices, along_lines(): lax.ppermute(line, 'ctx', [(source, 2 * (source // 2) + 3 - source % 2) f...  4.14 us
    dot_general x8, matrix products, attend_block(): jnp.einsum('sgrh,kgh->grsk', rotary_queries, key_block, preferred_element...  3.91 us
    ppermute x3, starting transfers between devices, along_lines(): arrived = lax.ppermute(line, 'ctx', forward(step))  3.86 us
    ppermute x2, waiting for transfers between devices, summed(): lax.ppermute(partial, 'tp', [(source, source ^ bit) for source in range(c...  3.08 us
    dot_general x8, matrix products, attend_block(): jnp.einsum('grsk,kgh->grsh', weights.astype(jnp.bfloat16), value_block, p...  2.83 us
  transfers between devices with their start and end apart: 12, of which 8 were waited for; matrix products, arithmetic and copies ran while one was open for 15% of the time, Pallas kernels for 0%

profile of v17, /device:TPU:24, one launch (start us, length us, event | category | flops | bytes accessed | tf_op | source)
XLA Modules:
  0.0 55.3 jit_solution(4322688864966552849)
XLA Ops:
  0.0 0.9 %copy.13 = bf16[256,2,128]{2,0,1:T(8,128)(2,1)S(1)} copy(bf16[256,2,128]{2,1,0:T(2,128)(2,1)} %param.8) | data formatting | bytes 262144 | tf_op args[2]
  1.0 1.2 %fusion.72 = (bf16[256,2,64]{2,1,0:T(2,128)(2,1)S(1)}, bf16[256,2,64]{2,1,0:T(2,128)(2,1)S(1)}) fusion(bf16[256,2,128]{2,1,0:T(2,128)(2,1)} %param.7), kind=kLoop, calls=%fused_computation.125 | loop fusion | bytes 262144 | tf_op jit(solution)/shard_map/slice | solution.py:46
  2.2 0.5 multiply_cosine_fusion
  2.7 0.1 fusion.61
  2.8 0.1 pad_maximum_fusion.1
  2.9 1.3 %collective-permute-start.1 = (bf16[256,4,128]{2,0,1:T(8,128)(2,1)S(1)}, bf16[256,4,128]{2,0,1:T(8,128)(2,1)S(1)}, u32[]{:S(2)}, u32[]{:S(2)}) collective-permute-start(bf16[256,4,128]{2,0,1:T(8,128)(2,1)S(1)} %pad_maximum_fusion.1), channel_id=1, source_target_pairs={{0,8},{4,12},{8,16},{12,20},{16,24},{20,28},{1,9},{5,13},{9,17},{1... | collective-permute-start | bytes 786440 | tf_op jit(solution)/shard_map/ppermute | solution.py:113
  4.2 3.4 %collective-permute-start = (bf16[256,4,128]{2,0,1:T(8,128)(2,1)S(1)}, bf16[256,4,128]{2,0,1:T(8,128)(2,1)S(1)}, u32[]{:S(2)}, u32[]{:S(2)}) collective-permute-start(bf16[256,4,128]{2,0,1:T(8,128)(2,1)S(1)} %pad_maximum_fusion.1), channel_id=1, source_target_pairs={{0,4},{8,12},{16,20},{24,28},{1,5},{9,13},{17,21},{25,29},{2,6},{1... | collective-permute-start | bytes 786440 | tf_op jit(solution)/shard_map/ppermute | solution.py:114
  7.7 1.0 %convert_element_type.62 = f32[256,4,128]{2,1,0:T(4,128)S(1)} convert(bf16[256,4,128]{2,1,0:T(4,128)(2,1)} %param.6) | non-fusion elementwise | flops 131072 | bytes 786432 | tf_op jit(solution)/shard_map/convert_element_type | solution.py:157
  8.7 0.0 copy-start.1
  8.7 0.5 subtract_convert_fusion
  9.3 0.1 pad_maximum_fusion
  9.5 0.1 fusion.65
  9.6 0.5 fusion.79
  10.2 0.0 copy-done.1
  10.2 0.3 fusion.58
  10.6 2.2 %collective-permute-done.1 = bf16[256,4,128]{2,0,1:T(8,128)(2,1)S(1)} collective-permute-done((bf16[256,4,128]{2,0,1:T(8,128)(2,1)S(1)}, bf16[256,4,128]{2,0,1:T(8,128)(2,1)S(1)}, u32[]{:S(2)}, u32[]{:S(2)}) %collective-permute-start.1) | collective-permute-done | bytes 262176 | tf_op jit(solution)/shard_map/ppermute | solution.py:113
  12.9 1.3 %collective-permute-start.3 = (bf16[256,4,128]{2,0,1:T(8,128)(2,1)S(1)}, bf16[256,4,128]{2,0,1:T(8,128)(2,1)S(1)}, u32[]{:S(2)}, u32[]{:S(2)}) collective-permute-start(bf16[256,4,128]{2,0,1:T(8,128)(2,1)S(1)} %collective-permute-done.1), channel_id=1, source_target_pairs={{8,16},{12,20},{16,24},{20,28},{9,17},{13,21},{17,25},{21,29},{10,... | collective-permute-start | bytes 786440 | tf_op jit(solution)/shard_map/ppermute | solution.py:113
  14.2 3.4 %collective-permute-start.2 = (bf16[256,4,128]{2,0,1:T(8,128)(2,1)S(1)}, bf16[256,4,128]{2,0,1:T(8,128)(2,1)S(1)}, u32[]{:S(2)}, u32[]{:S(2)}) collective-permute-start(bf16[256,4,128]{2,0,1:T(8,128)(2,1)S(1)} %collective-permute-done.1), channel_id=1, source_target_pairs={{8,12},{16,20},{24,28},{12,8},{20,16},{28,24},{9,13},{17,21},{25,2... | collective-permute-start | bytes 786440 | tf_op jit(solution)/shard_map/ppermute | solution.py:114
  17.6 0.5 fusion.78
  18.1 0.0 collective-permute-done
  18.1 0.5 fusion.80
  18.6 0.3 convolution_add_fusion.3
  18.9 0.3 convolution_add_fusion.2
  19.3 2.6 %collective-permute-done.3 = bf16[256,4,128]{2,0,1:T(8,128)(2,1)S(1)} collective-permute-done((bf16[256,4,128]{2,0,1:T(8,128)(2,1)S(1)}, bf16[256,4,128]{2,0,1:T(8,128)(2,1)S(1)}, u32[]{:S(2)}, u32[]{:S(2)}) %collective-permute-start.3) | collective-permute-done | bytes 262176 | tf_op jit(solution)/shard_map/ppermute | solution.py:113
  21.9 1.3 %collective-permute-start.6 = (bf16[256,4,128]{2,0,1:T(8,128)(2,1)S(1)}, bf16[256,4,128]{2,0,1:T(8,128)(2,1)S(1)}, u32[]{:S(2)}, u32[]{:S(2)}) collective-permute-start(bf16[256,4,128]{2,0,1:T(8,128)(2,1)S(1)} %collective-permute-done.3), channel_id=1, source_target_pairs={{16,28},{20,24},{17,29},{21,25},{18,30},{22,26},{19,31},{23,27}} | collective-permute-start | bytes 786440 | tf_op jit(solution)/shard_map/ppermute | solution.py:116
  23.2 1.3 %collective-permute-start.5 = (bf16[256,4,128]{2,0,1:T(8,128)(2,1)S(1)}, bf16[256,4,128]{2,0,1:T(8,128)(2,1)S(1)}, u32[]{:S(2)}, u32[]{:S(2)}) collective-permute-start(bf16[256,4,128]{2,0,1:T(8,128)(2,1)S(1)} %collective-permute-done.3), channel_id=1, source_target_pairs={{16,24},{20,28},{17,25},{21,29},{18,26},{22,30},{19,27},{23,31}} | collective-permute-start | bytes 786440 | tf_op jit(solution)/shard_map/ppermute | solution.py:113
  24.5 3.4 %collective-permute-start.4 = (bf16[256,4,128]{2,0,1:T(8,128)(2,1)S(1)}, bf16[256,4,128]{2,0,1:T(8,128)(2,1)S(1)}, u32[]{:S(2)}, u32[]{:S(2)}) collective-permute-start(bf16[256,4,128]{2,0,1:T(8,128)(2,1)S(1)} %collective-permute-done.3), channel_id=1, source_target_pairs={{16,20},{24,28},{20,16},{28,24},{17,21},{25,29},{21,17},{29,25},{1... | collective-permute-start | bytes 786440 | tf_op jit(solution)/shard_map/ppermute | solution.py:114
  28.0 0.5 fusion.76
  28.4 0.3 fusion.53
  28.8 0.0 collective-permute-done.2
  28.8 0.5 fusion.77
  29.3 0.4 fusion.46
  29.7 4.1 %collective-permute-done.6 = bf16[256,4,128]{2,0,1:T(8,128)(2,1)S(1)} collective-permute-done((bf16[256,4,128]{2,0,1:T(8,128)(2,1)S(1)}, bf16[256,4,128]{2,0,1:T(8,128)(2,1)S(1)}, u32[]{:S(2)}, u32[]{:S(2)}) %collective-permute-start.6) | collective-permute-done | bytes 262176 | tf_op jit(solution)/shard_map/ppermute | solution.py:116
  33.8 0.5 fusion.73
  34.3 2.4 %collective-permute-done.5 = bf16[256,4,128]{2,0,1:T(8,128)(2,1)S(1)} collective-permute-done((bf16[256,4,128]{2,0,1:T(8,128)(2,1)S(1)}, bf16[256,4,128]{2,0,1:T(8,128)(2,1)S(1)}, u32[]{:S(2)}, u32[]{:S(2)}) %collective-permute-start.5) | collective-permute-done | bytes 262176 | tf_op jit(solution)/shard_map/ppermute | solution.py:113
  36.6 0.5 fusion.74
  37.1 0.0 collective-permute-done.4
  37.1 0.5 fusion.75
  37.6 0.0 copy-start
  37.7 0.3 fusion.48
  38.0 0.3 fusion.50
  38.4 0.4 fusion.47
  38.8 0.1 collective-permute-start.8
  38.8 1.6 %collective-permute-start.7 = (bf16[2,2,256,128]{3,2,1,0:T(8,128)(2,1)S(1)}, bf16[2,2,256,128]{3,2,1,0:T(8,128)(2,1)S(1)}, u32[]{:S(2)}, u32[]{:S(2)}) collective-permute-start(bf16[2,2,256,128]{3,2,1,0:T(8,128)(2,1)S(1)} %fusion.47), channel_id=1, source_target_pairs={{0,2},{1,3},{2,0},{3,1},{4,6},{5,7},{6,4},{7,5},{8,10},{9,11},{10,... | collective-permute-start | bytes 786440 | tf_op jit(solution)/shard_map/ppermute | solution.py:135
  40.4 0.0 copy-done
  40.4 0.3 constant_dynamic-slice_fusion
  40.7 0.4 convolution_bitcast_fusion.3
  41.1 6.5 %collective-permute-done.7 = bf16[2,2,256,128]{3,2,1,0:T(8,128)(2,1)S(1)} collective-permute-done((bf16[2,2,256,128]{3,2,1,0:T(8,128)(2,1)S(1)}, bf16[2,2,256,128]{3,2,1,0:T(8,128)(2,1)S(1)}, u32[]{:S(2)}, u32[]{:S(2)}) %collective-permute-start.7) | collective-permute-done | bytes 262176 | tf_op jit(solution)/shard_map/ppermute | solution.py:135
  47.6 0.0 collective-permute-start.9
  47.6 0.0 collective-permute-done.8
  47.6 0.4 convolution_bitcast_fusion.1
  47.9 0.0 copy-start.3
  48.0 0.0 copy-start.2
  48.0 0.4 fusion.41
  48.3 0.7 %collective-permute-done.9 = bf16[2,2,256,128]{3,2,1,0:T(8,128)(2,1)S(1)} collective-permute-done((bf16[2,2,256,128]{3,2,1,0:T(8,128)(2,1)S(1)}, bf16[2,2,256,128]{3,2,1,0:T(8,128)(2,1)S(1)}, u32[]{:S(2)}, u32[]{:S(2)}) %collective-permute-start.9) | collective-permute-done | bytes 262176 | tf_op jit(solution)/shard_map/ppermute | solution.py:135
  49.1 0.5 multiply_reduce_fusion
  49.5 0.2 collective-permute-start.10
  49.7 1.0 %collective-permute-done.10 = f32[256]{0:T(256)S(1)} collective-permute-done((f32[256]{0:T(256)S(1)}, f32[256]{0:T(256)S(1)}, u32[]{:S(2)}, u32[]{:S(2)}) %collective-permute-start.10) | collective-permute-done | bytes 1056 | tf_op jit(solution)/shard_map/ppermute | solution.py:143
  50.8 1.5 %collective-permute-start.11 = (f32[256]{0:T(256)S(1)}, f32[256]{0:T(256)S(1)}, u32[]{:S(2)}, u32[]{:S(2)}) collective-permute-start(f32[256]{0:T(256)S(1)} %add.206), channel_id=1, source_target_pairs={{0,2},{1,3},{2,0},{3,1},{4,6},{5,7},{6,4},{7,5},{8,10},{9,11},{10,... | collective-permute-start | bytes 3080 | tf_op jit(solution)/shard_map/ppermute | solution.py:143
  52.2 0.0 copy-done.3
  52.2 2.1 %collective-permute-done.11 = f32[256]{0:T(256)S(1)} collective-permute-done((f32[256]{0:T(256)S(1)}, f32[256]{0:T(256)S(1)}, u32[]{:S(2)}, u32[]{:S(2)}) %collective-permute-start.11) | collective-permute-done | bytes 1056 | tf_op jit(solution)/shard_map/ppermute | solution.py:143
  54.3 0.0 copy-done.2
  54.3 0.9 %add_convert_fusion = bf16[256,768]{1,0:T(8,128)(2,1)} fusion(f32[256,768]{1,0:T(8,128)S(1)} %get-tuple-element.34, bf16[256,768]{1,0:T(8,128)(2,1)S(1)} %copy-done.2, f32[768]{0:T(1024)S(1)} %convert_element_type.72, f32[256]{0:T(256)S(1)} %add_rsqrt_fusion), kind=kLoop, calls=%fused_computation.64 | loop fusion | flops 983040 | bytes 1576960 | tf_op jit(solution)/shard_map/convert_element_type | solution.py:219
  (9 shorter events, 0.1 us)
Async XLA Ops:
  2.9 9.9 %collective-permute-start.1 = (bf16[256,4,128]{2,0,1:T(8,128)(2,1)S(1)}, bf16[256,4,128]{2,0,1:T(8,128)(2,1)S(1)}, u32[]{:S(2)}, u32[]{:S(2)}) collective-permute-start(bf16[256,4,128]{2,0,1:T(8,128)(2,1)S(1)} %pad_maximum_fusion.1), channel_id=1, source_target_pairs={{0,8},{4,12},{8,16},{12,20},{16,24},{20,28},{1,9},{5,13},{9,17},{1... | collective-permute-start | bytes 786440 | tf_op jit(solution)/shard_map/ppermute | solution.py:113
  4.2 13.8 %collective-permute-start = (bf16[256,4,128]{2,0,1:T(8,128)(2,1)S(1)}, bf16[256,4,128]{2,0,1:T(8,128)(2,1)S(1)}, u32[]{:S(2)}, u32[]{:S(2)}) collective-permute-start(bf16[256,4,128]{2,0,1:T(8,128)(2,1)S(1)} %pad_maximum_fusion.1), channel_id=1, source_target_pairs={{0,4},{8,12},{16,20},{24,28},{1,5},{9,13},{17,21},{25,29},{2,6},{1... | collective-permute-start | bytes 786440 | tf_op jit(solution)/shard_map/ppermute | solution.py:114
  8.7 1.5 %copy-start.1 = (bf16[256,2,128]{2,1,0:T(2,128)(2,1)S(1)}, bf16[256,2,128]{2,1,0:T(2,128)(2,1)}, u32[]{:S(2)}) copy-start(bf16[256,2,128]{2,1,0:T(2,128)(2,1)} %param.8) | copy-start | bytes 393220
  12.9 9.1 %collective-permute-start.3 = (bf16[256,4,128]{2,0,1:T(8,128)(2,1)S(1)}, bf16[256,4,128]{2,0,1:T(8,128)(2,1)S(1)}, u32[]{:S(2)}, u32[]{:S(2)}) collective-permute-start(bf16[256,4,128]{2,0,1:T(8,128)(2,1)S(1)} %collective-permute-done.1), channel_id=1, source_target_pairs={{8,16},{12,20},{16,24},{20,28},{9,17},{13,21},{17,25},{21,29},{10,... | collective-permute-start | bytes 786440 | tf_op jit(solution)/shard_map/ppermute | solution.py:113
  14.2 14.6 %collective-permute-start.2 = (bf16[256,4,128]{2,0,1:T(8,128)(2,1)S(1)}, bf16[256,4,128]{2,0,1:T(8,128)(2,1)S(1)}, u32[]{:S(2)}, u32[]{:S(2)}) collective-permute-start(bf16[256,4,128]{2,0,1:T(8,128)(2,1)S(1)} %collective-permute-done.1), channel_id=1, source_target_pairs={{8,12},{16,20},{24,28},{12,8},{20,16},{28,24},{9,13},{17,21},{25,2... | collective-permute-start | bytes 786440 | tf_op jit(solution)/shard_map/ppermute | solution.py:114
  21.9 11.9 %collective-permute-start.6 = (bf16[256,4,128]{2,0,1:T(8,128)(2,1)S(1)}, bf16[256,4,128]{2,0,1:T(8,128)(2,1)S(1)}, u32[]{:S(2)}, u32[]{:S(2)}) collective-permute-start(bf16[256,4,128]{2,0,1:T(8,128)(2,1)S(1)} %collective-permute-done.3), channel_id=1, source_target_pairs={{16,28},{20,24},{17,29},{21,25},{18,30},{22,26},{19,31},{23,27}} | collective-permute-start | bytes 786440 | tf_op jit(solution)/shard_map/ppermute | solution.py:116
  23.2 13.4 %collective-permute-start.5 = (bf16[256,4,128]{2,0,1:T(8,128)(2,1)S(1)}, bf16[256,4,128]{2,0,1:T(8,128)(2,1)S(1)}, u32[]{:S(2)}, u32[]{:S(2)}) collective-permute-start(bf16[256,4,128]{2,0,1:T(8,128)(2,1)S(1)} %collective-permute-done.3), channel_id=1, source_target_pairs={{16,24},{20,28},{17,25},{21,29},{18,26},{22,30},{19,27},{23,31}} | collective-permute-start | bytes 786440 | tf_op jit(solution)/shard_map/ppermute | solution.py:113
  24.5 12.6 %collective-permute-start.4 = (bf16[256,4,128]{2,0,1:T(8,128)(2,1)S(1)}, bf16[256,4,128]{2,0,1:T(8,128)(2,1)S(1)}, u32[]{:S(2)}, u32[]{:S(2)}) collective-permute-start(bf16[256,4,128]{2,0,1:T(8,128)(2,1)S(1)} %collective-permute-done.3), channel_id=1, source_target_pairs={{16,20},{24,28},{20,16},{28,24},{17,21},{25,29},{21,17},{29,25},{1... | collective-permute-start | bytes 786440 | tf_op jit(solution)/shard_map/ppermute | solution.py:114
  37.6 2.8 %copy-start = (bf16[16,128,768]{2,1,0:T(8,128)(2,1)S(1)}, bf16[16,128,768]{2,1,0:T(8,128)(2,1)}, u32[]{:S(2)}) copy-start(bf16[16,128,768]{2,1,0:T(8,128)(2,1)} %param.10) | copy-start | bytes 9437188
  38.8 8.8 %collective-permute-start.8 = (bf16[2,2,256,128]{3,2,1,0:T(8,128)(2,1)S(1)}, bf16[2,2,256,128]{3,2,1,0:T(8,128)(2,1)S(1)}, u32[]{:S(2)}, u32[]{:S(2)}) collective-permute-start(bf16[2,2,256,128]{3,2,1,0:T(8,128)(2,1)S(1)} %fusion.47), channel_id=1, source_target_pairs={{0,1},{1,0},{2,3},{3,2},{4,5},{5,4},{6,7},{7,6},{8,9},{9,8},{10,11... | collective-permute-start | bytes 786440 | tf_op jit(solution)/shard_map/ppermute | solution.py:135
  38.8 8.7 %collective-permute-start.7 = (bf16[2,2,256,128]{3,2,1,0:T(8,128)(2,1)S(1)}, bf16[2,2,256,128]{3,2,1,0:T(8,128)(2,1)S(1)}, u32[]{:S(2)}, u32[]{:S(2)}) collective-permute-start(bf16[2,2,256,128]{3,2,1,0:T(8,128)(2,1)S(1)} %fusion.47), channel_id=1, source_target_pairs={{0,2},{1,3},{2,0},{3,1},{4,6},{5,7},{6,4},{7,5},{8,10},{9,11},{10,... | collective-permute-start | bytes 786440 | tf_op jit(solution)/shard_map/ppermute | solution.py:135
  47.6 1.5 %collective-permute-start.9 = (bf16[2,2,256,128]{3,2,1,0:T(8,128)(2,1)S(1)}, bf16[2,2,256,128]{3,2,1,0:T(8,128)(2,1)S(1)}, u32[]{:S(2)}, u32[]{:S(2)}) collective-permute-start(bf16[2,2,256,128]{3,2,1,0:T(8,128)(2,1)S(1)} %collective-permute-done.7), channel_id=1, source_target_pairs={{0,1},{1,0},{2,3},{3,2},{4,5},{5,4},{6,7},{7,6},{8,9},{9,8},{10,11... | collective-permute-start | bytes 786440 | tf_op jit(solution)/shard_map/ppermute | solution.py:135
  47.9 4.3 %copy-start.3 = (bf16[768]{0:T(1024)(128)(2,1)S(1)}, bf16[768]{0:T(1024)(128)(2,1)}, u32[]{:S(2)}) copy-start(bf16[768]{0:T(1024)(128)(2,1)} %param.11) | copy-start | bytes 4612
  48.0 6.4 %copy-start.2 = (bf16[256,768]{1,0:T(8,128)(2,1)S(1)}, bf16[256,768]{1,0:T(8,128)(2,1)}, u32[]{:S(2)}) copy-start(bf16[256,768]{1,0:T(8,128)(2,1)} %param.9) | copy-start | bytes 1179652
  49.5 1.2 %collective-permute-start.10 = (f32[256]{0:T(256)S(1)}, f32[256]{0:T(256)S(1)}, u32[]{:S(2)}, u32[]{:S(2)}) collective-permute-start(f32[256]{0:T(256)S(1)} %get-tuple-element.33), channel_id=1, source_target_pairs={{0,1},{1,0},{2,3},{3,2},{4,5},{5,4},{6,7},{7,6},{8,9},{9,8},{10,11... | collective-permute-start | bytes 3080 | tf_op jit(solution)/shard_map/ppermute | solution.py:143
  50.8 3.6 %collective-permute-start.11 = (f32[256]{0:T(256)S(1)}, f32[256]{0:T(256)S(1)}, u32[]{:S(2)}, u32[]{:S(2)}) collective-permute-start(f32[256]{0:T(256)S(1)} %add.206), channel_id=1, source_target_pairs={{0,2},{1,3},{2,0},{3,1},{4,6},{5,7},{6,4},{7,5},{8,10},{9,11},{10,... | collective-permute-start | bytes 3080 | tf_op jit(solution)/shard_map/ppermute | solution.py:143
